TPU v7x, 32 devices: a whole 2x2x4 slice. The times are simulated.
32 devices in a mesh: section: 4 (over x, core), expert: 8 (over z, y).
Axes of the slice: x: 2, y: 2, z: 4, core: 2. Of those that a mesh axis runs over, the one named last changes fastest.
Arguments:
- w_in: bfloat16 [2, 4, 8, 2048, 512], P(None, 'section', 'expert'), as said below
- w_out: bfloat16 [2, 4, 8, 256, 2048], P(None, 'section', 'expert'), as said below
- grads: bfloat16 [2, 4, 768, 2048], P(None, 'section', 'expert'), may hold values from -6 to 6
- fresh: bfloat16 [1, 2, 768, 2048], P(None, None, 'expert'), may hold values from -6 to 6
- saved: bfloat16 [2, 2, 4, 8, 192, 2048], P(None, None, 'section', 'expert'), may hold values from -6 to 6
- probs: float32 [2, 2, 4, 768], P(None, None, 'section', 'expert'), may hold values from 0.25 to 1
- routes: int32 [2, 2, 4, 768], P(None, None, 'section', 'expert'), may hold values from 0 to 7, as said below
- counts: int32 [2, 2, 4, 8, 8], P(None, None, 'section', 'expert'), may hold values from 0 to 24, as said below
Outputs:
- out_grads: bfloat16 [2, 4, 768, 2048], P(None, 'section', 'expert')
- grad_in: bfloat16 [4, 8, 2048, 512], P('section', 'expert')
- grad_out: bfloat16 [4, 8, 256, 2048], P('section', 'expert')
Inputs may be any that keep to these rules, and one draw needn't show every extreme that they name: `routes`: rows of one source device in a slot are in order of expert: row r goes to expert e when the counts of experts below e sum to r or less and those up to e to more than r. The counts of one source device in a slot sum to 96; in every slot some expert gets 24 rows from every source device. w_in[1, s] equals w_in[0, 3 - s]. w_out[1, s] equals w_out[0, 3 - s].
All inputs are finite; a program needn't handle non-finite values.
Results may differ from a plain program's by a relative error of at most 0.0066.
Values may be sent and summed in bfloat16 or wider, within the bound.
No kernel may reach another device: no remote copies, remote signals or barrier semaphores. Data moves between devices by JAX's collectives and lax.ppermute only.
A program may use at most 128 MiB of HBM per device.

v0:
```python
import jax
import jax.numpy as jnp
from jax import lax
from jax.sharding import PartitionSpec as P


def passed_along(block, axis, distance):
    devices = range(lax.axis_size(axis))
    route = [(i - distance, i) for i in devices if i - distance in devices]
    return lax.ppermute(block, axis, route)


def slot_index(route_ids, count_table, capacity):
    experts = count_table.shape[0]
    offset = jnp.cumsum(count_table) - count_table
    labels = lax.iota(jnp.int32, experts)
    first_slot = jnp.sum(
        jnp.where(route_ids[:, None] == labels[None, :], offset[None, :], 0), axis=1
    )
    return route_ids * capacity + lax.iota(jnp.int32, route_ids.shape[0]) - first_slot


def left_product(left, right):
    return lax.dot_general(
        left, right, (((0,), (0,)), ((), ())), preferred_element_type=jnp.float32
    )


def right_product(left, right):
    return lax.dot_general(
        left, right, (((1,), (1,)), ((), ())), preferred_element_type=jnp.float32
    )


def expert_pass(gradient, prob_rows, route_ids, count_table, saved_rows, weight_in, weight_out):
    tokens, model_width = gradient.shape
    experts = count_table.shape[0]
    capacity = 2 * tokens // experts
    hidden_width = weight_out.shape[0]
    slot_ids = slot_index(route_ids, count_table, capacity)
    scaled = (prob_rows[:, None] * gradient.astype(jnp.float32)).astype(jnp.bfloat16)
    outgoing = jnp.zeros((experts * capacity, model_width), jnp.bfloat16).at[slot_ids].set(scaled)
    arrived = lax.all_to_all(
        outgoing.reshape(experts, capacity, model_width),
        "expert",
        split_axis=0,
        concat_axis=0,
        tiled=True,
    )
    slope_rows = arrived.reshape(-1, model_width)
    gate_up = jnp.dot(saved_rows, weight_in, preferred_element_type=jnp.float32)
    gate_part = gate_up[:, :hidden_width]
    upward = gate_up[:, hidden_width:]
    sigmoid_gate = jax.nn.sigmoid(gate_part)
    active = gate_part * sigmoid_gate
    hidden = (active * upward).astype(jnp.bfloat16)
    hidden_grad = right_product(slope_rows, weight_out)
    gate_grad = hidden_grad * upward * sigmoid_gate * (1.0 + gate_part * (1.0 - sigmoid_gate))
    pair_grad = jnp.concatenate([gate_grad, hidden_grad * active], axis=1).astype(jnp.bfloat16)
    input_grad = right_product(pair_grad, weight_in).astype(jnp.bfloat16)
    returned = lax.all_to_all(
        input_grad.reshape(experts, capacity, model_width),
        "expert",
        split_axis=0,
        concat_axis=0,
        tiled=True,
    )
    back_rows = jnp.take(returned.reshape(-1, model_width), slot_ids, axis=0)
    updated = (gradient.astype(jnp.float32) + back_rows.astype(jnp.float32)).astype(jnp.bfloat16)
    return (updated, slope_rows, hidden, pair_grad)


def pack_partial(partial_in, partial_out, model_width):
    return jnp.concatenate(
        [
            partial_in.astype(jnp.bfloat16).reshape(-1, model_width),
            partial_out.astype(jnp.bfloat16),
        ],
        axis=0,
    )


def unpack_partial(flat, model_width, hidden_width):
    return (
        flat[: 2 * hidden_width].reshape(model_width, 2 * hidden_width),
        flat[2 * hidden_width :],
    )


def on_device(w_in, w_out, grads, fresh, saved, probs, routes, counts):
    sections = lax.axis_size("section")
    section_id = lax.axis_index("section")
    model_width = grads.shape[-1]
    hidden_width = w_out.shape[-2]
    ticks = saved.shape[0]
    current = [grads[0, 0], grads[1, 0]]
    finished = [grads[0, 0], grads[1, 0]]
    zeros_in = jnp.zeros((model_width, 2 * hidden_width), jnp.float32)
    zeros_out = jnp.zeros((hidden_width, model_width), jnp.float32)
    totals_in = [zeros_in, zeros_in]
    totals_out = [zeros_out, zeros_out]
    for tick_id in range(ticks):
        for way_id in range(2):
            saved_rows = saved[tick_id, way_id, 0, 0]
            updated, slope_rows, hidden, pair_grad = expert_pass(
                current[way_id],
                probs[tick_id, way_id, 0],
                routes[tick_id, way_id, 0],
                counts[tick_id, way_id, 0, 0],
                saved_rows,
                w_in[way_id, 0, 0],
                w_out[way_id, 0, 0],
            )
            finished[way_id] = updated
            totals_in[way_id] = totals_in[way_id] + left_product(saved_rows, pair_grad)
            totals_out[way_id] = totals_out[way_id] + left_product(hidden, slope_rows)
        if tick_id + 1 < ticks:
            from_above = passed_along(finished[0], "section", -1)
            from_below = passed_along(finished[1], "section", 1)
            current = [
                jnp.where(section_id == sections - 1, fresh[tick_id, 0], from_above),
                jnp.where(section_id == 0, fresh[tick_id, 1], from_below),
            ]
    flat = pack_partial(totals_in[1], totals_out[1], model_width)
    spread = lax.all_to_all(
        flat.reshape(sections, -1, model_width), "section", split_axis=0, concat_axis=0, tiled=True
    )
    gathered = lax.all_to_all(
        jnp.flip(spread, 0), "section", split_axis=0, concat_axis=0, tiled=True
    )
    mirror_in, mirror_out = unpack_partial(
        gathered.reshape(-1, model_width), model_width, hidden_width
    )
    grad_in = (totals_in[0] + mirror_in.astype(jnp.float32)).astype(jnp.bfloat16)
    grad_out = (totals_out[0] + mirror_out.astype(jnp.float32)).astype(jnp.bfloat16)
    return (jnp.stack(finished)[:, None], grad_in[None, None], grad_out[None, None])


def solution(mesh):
    return jax.shard_map(
        on_device,
        mesh=mesh,
        in_specs=(
            P(None, "section", "expert", None, None),
            P(None, "section", "expert", None, None),
            P(None, "section", "expert", None),
            P(None, None, "expert", None),
            P(None, None, "section", "expert", None, None),
            P(None, None, "section", "expert"),
            P(None, None, "section", "expert"),
            P(None, None, "section", "expert", None),
        ),
        out_specs=(
            P(None, "section", "expert", None),
            P("section", "expert", None, None),
            P("section", "expert", None, None),
        ),
        check_vma=False,
    )
```

profile of v0, /device:TPU:1, one launch (start us, length us, event | category | flops | bytes accessed | tf_op | source)
XLA Modules:
  0.0 320.8 jit_solution(10715235979612608093)
XLA Ops:
  8.3 6.4 %all-to-all-start.4 = ((bf16[8,24,2048]{2,1,0:T(8,128)(2,1)}), bf16[8,24,2048]{2,1,0:T(8,128)(2,1)S(1)}, u32[]{:S(2)}, u32[]{:S(2)}) async-start(bf16[8,24,2048]{2,1,0:T(8,128)(2,1)} %bitcast.43), calls=%async_computation.4 | async-start | bytes 1572864 | tf_op jit(solution)/shard_map/all_to_all | solution.py:43
  17.3 16.4 %all-to-all-done.4 = bf16[8,24,2048]{2,1,0:T(8,128)(2,1)S(1)} async-done(((bf16[8,24,2048]{2,1,0:T(8,128)(2,1)}), bf16[8,24,2048]{2,1,0:T(8,128)(2,1)S(1)}, u32[]{:S(2)}, u32[]{:S(2)}) %all-to-all-start.4) | async-done | bytes 786464 | tf_op jit(solution)/shard_map/all_to_all | solution.py:43
  33.7 4.8 %all-to-all-start = ((bf16[8,24,2048]{2,1,0:T(8,128)(2,1)}), bf16[8,24,2048]{2,1,0:T(8,128)(2,1)S(1)}, u32[]{:S(2)}, u32[]{:S(2)}) async-start(bf16[8,24,2048]{2,1,0:T(8,128)(2,1)} %bitcast.11), calls=%async_computation | async-start | bytes 1572864 | tf_op jit(solution)/shard_map/all_to_all | solution.py:43
  45.4 12.5 %all-to-all-done = bf16[8,24,2048]{2,1,0:T(8,128)(2,1)S(1)} async-done(((bf16[8,24,2048]{2,1,0:T(8,128)(2,1)}), bf16[8,24,2048]{2,1,0:T(8,128)(2,1)S(1)}, u32[]{:S(2)}, u32[]{:S(2)}) %all-to-all-start) | async-done | bytes 786464 | tf_op jit(solution)/shard_map/all_to_all | solution.py:43
  57.9 4.6 %all-to-all-start.5 = ((bf16[8,24,2048]{2,1,0:T(8,128)(2,1)}), bf16[8,24,2048]{2,1,0:T(8,128)(2,1)S(1)}, u32[]{:S(2)}, u32[]{:S(2)}) async-start(bf16[8,24,2048]{2,1,0:T(8,128)(2,1)} %bitcast.48), calls=%async_computation.5 | async-start | bytes 1572864 | tf_op jit(solution)/shard_map/all_to_all | solution.py:61
  69.4 12.4 %all-to-all-done.5 = bf16[8,24,2048]{2,1,0:T(8,128)(2,1)S(1)} async-done(((bf16[8,24,2048]{2,1,0:T(8,128)(2,1)}), bf16[8,24,2048]{2,1,0:T(8,128)(2,1)S(1)}, u32[]{:S(2)}, u32[]{:S(2)}) %all-to-all-start.5) | async-done | bytes 786464 | tf_op jit(solution)/shard_map/all_to_all | solution.py:61
  81.8 4.6 %all-to-all-start.1 = ((bf16[8,24,2048]{2,1,0:T(8,128)(2,1)}), bf16[8,24,2048]{2,1,0:T(8,128)(2,1)S(1)}, u32[]{:S(2)}, u32[]{:S(2)}) async-start(bf16[8,24,2048]{2,1,0:T(8,128)(2,1)} %bitcast.16), calls=%async_computation.1 | async-start | bytes 1572864 | tf_op jit(solution)/shard_map/all_to_all | solution.py:61
  87.8 17.9 %all-to-all-done.1 = bf16[8,24,2048]{2,1,0:T(8,128)(2,1)S(1)} async-done(((bf16[8,24,2048]{2,1,0:T(8,128)(2,1)}), bf16[8,24,2048]{2,1,0:T(8,128)(2,1)S(1)}, u32[]{:S(2)}, u32[]{:S(2)}) %all-to-all-start.1) | async-done | bytes 786464 | tf_op jit(solution)/shard_map/all_to_all | solution.py:61
  107.5 3.7 %collective-permute-start = (bf16[96,2048]{1,0:T(8,128)(2,1)S(1)}, bf16[96,2048]{1,0:T(8,128)(2,1)S(1)}, u32[]{:S(2)}, u32[]{:S(2)}) collective-permute-start(bf16[96,2048]{1,0:T(8,128)(2,1)S(1)} %get-tuple-element.23), channel_id=1, source_target_pairs={{8,0},{16,8},{24,16},{9,1},{17,9},{25,17},{10,2},{18,10},{26,18},{... | collective-permute-start | bytes 1179656 | tf_op jit(solution)/shard_map/ppermute | solution.py:10
  111.3 6.5 %collective-permute-done = bf16[96,2048]{1,0:T(8,128)(2,1)S(1)} collective-permute-done((bf16[96,2048]{1,0:T(8,128)(2,1)S(1)}, bf16[96,2048]{1,0:T(8,128)(2,1)S(1)}, u32[]{:S(2)}, u32[]{:S(2)}) %collective-permute-start) | collective-permute-done | bytes 393248 | tf_op jit(solution)/shard_map/ppermute | solution.py:10
  120.6 4.2 %all-to-all-start.2 = ((bf16[8,24,2048]{2,1,0:T(8,128)(2,1)}), bf16[8,24,2048]{2,1,0:T(8,128)(2,1)}, u32[]{:S(2)}, u32[]{:S(2)}) async-start(bf16[8,24,2048]{2,1,0:T(8,128)(2,1)} %bitcast.231), calls=%async_computation.2 | async-start | bytes 1572864 | tf_op jit(solution)/shard_map/all_to_all | solution.py:43
  126.7 5.0 %collective-permute-done.1 = bf16[96,2048]{1,0:T(8,128)(2,1)} collective-permute-done((bf16[96,2048]{1,0:T(8,128)(2,1)}, bf16[96,2048]{1,0:T(8,128)(2,1)}, u32[]{:S(2)}, u32[]{:S(2)}) %collective-permute-start.1) | collective-permute-done | bytes 393248 | tf_op jit(solution)/shard_map/ppermute | solution.py:10
  134.5 6.5 %all-to-all-done.2 = bf16[8,24,2048]{2,1,0:T(8,128)(2,1)} async-done(((bf16[8,24,2048]{2,1,0:T(8,128)(2,1)}), bf16[8,24,2048]{2,1,0:T(8,128)(2,1)}, u32[]{:S(2)}, u32[]{:S(2)}) %all-to-all-start.2) | async-done | bytes 786464 | tf_op jit(solution)/shard_map/all_to_all | solution.py:43
  141.0 4.2 %all-to-all-start.6 = ((bf16[8,24,2048]{2,1,0:T(8,128)(2,1)}), bf16[8,24,2048]{2,1,0:T(8,128)(2,1)}, u32[]{:S(2)}, u32[]{:S(2)}) async-start(bf16[8,24,2048]{2,1,0:T(8,128)(2,1)} %bitcast.232), calls=%async_computation.6 | async-start | bytes 1572864 | tf_op jit(solution)/shard_map/all_to_all | solution.py:43
  155.5 9.6 %all-to-all-done.6 = bf16[8,24,2048]{2,1,0:T(8,128)(2,1)} async-done(((bf16[8,24,2048]{2,1,0:T(8,128)(2,1)}), bf16[8,24,2048]{2,1,0:T(8,128)(2,1)}, u32[]{:S(2)}, u32[]{:S(2)}) %all-to-all-start.6) | async-done | bytes 786464 | tf_op jit(solution)/shard_map/all_to_all | solution.py:43
  165.2 3.7 %all-to-all-start.3 = ((bf16[8,24,2048]{2,1,0:T(8,128)(2,1)}), bf16[8,24,2048]{2,1,0:T(8,128)(2,1)S(1)}, u32[]{:S(2)}, u32[]{:S(2)}) async-start(bf16[8,24,2048]{2,1,0:T(8,128)(2,1)} %bitcast.29), calls=%async_computation.3 | async-start | bytes 1572864 | tf_op jit(solution)/shard_map/all_to_all | solution.py:61
  177.4 3.1 reshape.387
  185.0 3.4 %all-to-all-done.3 = bf16[8,24,2048]{2,1,0:T(8,128)(2,1)S(1)} async-done(((bf16[8,24,2048]{2,1,0:T(8,128)(2,1)}), bf16[8,24,2048]{2,1,0:T(8,128)(2,1)S(1)}, u32[]{:S(2)}, u32[]{:S(2)}) %all-to-all-start.3) | async-done | bytes 786464 | tf_op jit(solution)/shard_map/all_to_all | solution.py:61
  188.4 6.0 %all-to-all-start.8 = ((bf16[4,192,2048]{2,1,0:T(8,128)(2,1)}), bf16[4,192,2048]{2,1,0:T(8,128)(2,1)}, u32[]{:S(2)}, u32[]{:S(2)}) async-start(bf16[4,192,2048]{2,1,0:T(8,128)(2,1)} %bitcast.230), calls=%async_computation.8 | async-start | bytes 6291456 | tf_op jit(solution)/shard_map/all_to_all | solution.py:125
  194.4 3.3 %convolution_convert_fusion = bf16[192,2048]{1,0:T(8,128)(2,1)} fusion(bf16[2,1,1,2048,512]{4,3,2,1,0:T(8,128)(2,1)} %param.10, bf16[192,256]{1,0:T(8,128)(2,1)S(1)} %get-tuple-element.30, bf16[192,256]{1,0:T(8,128)(2,1)S(1)} %get-tuple-element.29), kind=kOutput, calls=%fused_computation.19 | convolution fusion | flops 403439616 | bytes 3080192 | tf_op jit(solution)/shard_map/dot_general | solution.py:30
  197.7 32.7 %all-to-all-done.8 = bf16[4,192,2048]{2,1,0:T(8,128)(2,1)} async-done(((bf16[4,192,2048]{2,1,0:T(8,128)(2,1)}), bf16[4,192,2048]{2,1,0:T(8,128)(2,1)}, u32[]{:S(2)}, u32[]{:S(2)}) %all-to-all-start.8) | async-done | bytes 3145760 | tf_op jit(solution)/shard_map/all_to_all | solution.py:125
  230.4 3.5 %all-to-all-start.7 = ((bf16[8,24,2048]{2,1,0:T(8,128)(2,1)}), bf16[8,24,2048]{2,1,0:T(8,128)(2,1)S(1)}, u32[]{:S(2)}, u32[]{:S(2)}) async-start(bf16[8,24,2048]{2,1,0:T(8,128)(2,1)} %bitcast.61), calls=%async_computation.7 | async-start | bytes 1572864 | tf_op jit(solution)/shard_map/all_to_all | solution.py:61
  234.0 3.9 %rev.4 = bf16[4,192,2048]{2,1,0:T(8,128)(2,1)} reverse(bf16[4,192,2048]{2,1,0:T(8,128)(2,1)} %all-to-all-done.8), dimensions={0} | reverse | bytes 6291456 | tf_op jit(solution)/shard_map/jit(_flip)/rev | solution.py:129
  237.9 15.0 %all-to-all-done.7 = bf16[8,24,2048]{2,1,0:T(8,128)(2,1)S(1)} async-done(((bf16[8,24,2048]{2,1,0:T(8,128)(2,1)}), bf16[8,24,2048]{2,1,0:T(8,128)(2,1)S(1)}, u32[]{:S(2)}, u32[]{:S(2)}) %all-to-all-start.7) | async-done | bytes 786464 | tf_op jit(solution)/shard_map/all_to_all | solution.py:61
  253.0 6.8 %all-to-all-start.9 = ((bf16[4,192,2048]{2,1,0:T(8,128)(2,1)}), bf16[4,192,2048]{2,1,0:T(8,128)(2,1)}, u32[]{:S(2)}, u32[]{:S(2)}) async-start(bf16[4,192,2048]{2,1,0:T(8,128)(2,1)} %rev.4), calls=%async_computation.9 | async-start | bytes 6291456 | tf_op jit(solution)/shard_map/all_to_all | solution.py:128
  261.6 3.9 %fusion.54 = f32[512,2048]{1,0:T(8,128)} fusion(bf16[2,2,1,1,192,2048]{5,4,3,2,1,0:T(8,128)(2,1)} %param.14, bf16[192,256]{1,0:T(8,128)(2,1)S(1)} %copy-done.13, bf16[192,256]{1,0:T(8,128)(2,1)S(1)} %copy-done.11), kind=kOutput, calls=%fused_computation.81 | convolution fusion | flops 403046400 | bytes 5177344 | tf_op jit(solution)/shard_map/dot_general | solution.py:24
  270.4 25.4 %all-to-all-done.9 = bf16[4,192,2048]{2,1,0:T(8,128)(2,1)} async-done(((bf16[4,192,2048]{2,1,0:T(8,128)(2,1)}), bf16[4,192,2048]{2,1,0:T(8,128)(2,1)}, u32[]{:S(2)}, u32[]{:S(2)}) %all-to-all-start.9) | async-done | bytes 3145760 | tf_op jit(solution)/shard_map/all_to_all | solution.py:128
  295.8 4.3 %slice_convert_fusion = f32[512,2048]{1,0:T(8,128)} fusion(bf16[768,2048]{1,0:T(8,128)(2,1)} %bitcast.69), kind=kLoop, calls=%fused_computation.24 | loop fusion | flops 1048576 | bytes 6291456 | tf_op jit(solution)/shard_map/convert_element_type | solution.py:134
  300.1 3.0 fusion.6
  303.0 5.2 %reshape.392 = f32[2048,512]{1,0:T(8,128)} reshape(f32[512,2048]{1,0:T(8,128)} %slice_convert_fusion) | data formatting | bytes 8388608 | tf_op jit(solution)/shard_map/convert_element_type | solution.py:134
  308.3 5.5 %copy.18 = f32[2048,512]{0,1:T(8,128)} copy(f32[2048,512]{1,0:T(8,128)} %reshape.392) | data formatting | bytes 8388608 | tf_op jit(solution)/shard_map/convert_element_type | solution.py:134
  313.8 4.4 %fusion.2 = bf16[1,1,2048,512]{2,3,1,0:T(8,128)(2,1)S(1)} fusion(f32[2048,512]{0,1:T(8,128)} %copy.18, f32[512,2048]{1,0:T(8,128)} %fusion.54, bf16[2,2,1,1,192,2048]{5,4,3,2,1,0:T(8,128)(2,1)} %param.14, bf16[192,256]{1,0:T(8,128)(2,1)S(1)} %copy-done.21, bf16[192,256]{1,0:T(8,128)(2,1)S(1)} %copy-done.19), kind=kOutput, calls=%fused_computation.13 | convolution fusion | flops 406192128 | bytes 11468800 | tf_op jit(solution)/shard_map/dot_general | solution.py:24
  (119 shorter events, 67.0 us)
Async XLA Ops:
  8.3 25.5 %all-to-all-start.4 = ((bf16[8,24,2048]{2,1,0:T(8,128)(2,1)}), bf16[8,24,2048]{2,1,0:T(8,128)(2,1)S(1)}, u32[]{:S(2)}, u32[]{:S(2)}) async-start(bf16[8,24,2048]{2,1,0:T(8,128)(2,1)} %bitcast.43), calls=%async_computation.4 | async-start | bytes 1572864 | tf_op jit(solution)/shard_map/all_to_all | solution.py:43
  33.7 9.3 %copy-start.5 = (bf16[8,24,2048]{2,1,0:T(8,128)(2,1)}, bf16[8,24,2048]{2,1,0:T(8,128)(2,1)S(1)}, u32[]{:S(2)}) copy-start(bf16[8,24,2048]{2,1,0:T(8,128)(2,1)S(1)} %all-to-all-done.4) | copy-start | bytes 2359300
  33.7 24.2 %all-to-all-start = ((bf16[8,24,2048]{2,1,0:T(8,128)(2,1)}), bf16[8,24,2048]{2,1,0:T(8,128)(2,1)S(1)}, u32[]{:S(2)}, u32[]{:S(2)}) async-start(bf16[8,24,2048]{2,1,0:T(8,128)(2,1)} %bitcast.11), calls=%async_computation | async-start | bytes 1572864 | tf_op jit(solution)/shard_map/all_to_all | solution.py:43
  38.6 5.2 %copy-start.32 = (bf16[2,1,1,2048,512]{4,3,2,1,0:T(8,128)(2,1)S(1)}, bf16[2,1,1,2048,512]{4,3,2,1,0:T(8,128)(2,1)}, u32[]{:S(2)}) copy-start(bf16[2,1,1,2048,512]{4,3,2,1,0:T(8,128)(2,1)} %param.10) | copy-start | bytes 12582916
  57.9 9.1 %copy-start.3 = (bf16[8,24,2048]{2,1,0:T(8,128)(2,1)}, bf16[8,24,2048]{2,1,0:T(8,128)(2,1)S(1)}, u32[]{:S(2)}) copy-start(bf16[8,24,2048]{2,1,0:T(8,128)(2,1)S(1)} %all-to-all-done) | copy-start | bytes 2359300
  57.9 23.9 %all-to-all-start.5 = ((bf16[8,24,2048]{2,1,0:T(8,128)(2,1)}), bf16[8,24,2048]{2,1,0:T(8,128)(2,1)S(1)}, u32[]{:S(2)}, u32[]{:S(2)}) async-start(bf16[8,24,2048]{2,1,0:T(8,128)(2,1)} %bitcast.48), calls=%async_computation.5 | async-start | bytes 1572864 | tf_op jit(solution)/shard_map/all_to_all | solution.py:61
  62.5 5.2 %copy-start.33 = (bf16[2,1,1,2048,512]{4,3,2,1,0:T(8,128)(2,1)S(1)}, bf16[2,1,1,2048,512]{4,3,2,1,0:T(8,128)(2,1)}, u32[]{:S(2)}) copy-start(bf16[2,1,1,2048,512]{4,3,2,1,0:T(8,128)(2,1)} %param.10) | copy-start | bytes 12582916
  67.0 19.4 %copy-start.29 = (s32[2,2,1,96]{3,2,1,0:T(1,128)S(1)}, s32[2,2,1,96]{3,2,1,0:T(1,128)}, u32[]{:S(2)}) copy-start(s32[2,2,1,96]{3,2,1,0:T(1,128)} %param.16) | copy-start | bytes 4612
  81.8 23.9 %all-to-all-start.1 = ((bf16[8,24,2048]{2,1,0:T(8,128)(2,1)}), bf16[8,24,2048]{2,1,0:T(8,128)(2,1)S(1)}, u32[]{:S(2)}, u32[]{:S(2)}) async-start(bf16[8,24,2048]{2,1,0:T(8,128)(2,1)} %bitcast.16), calls=%async_computation.1 | async-start | bytes 1572864 | tf_op jit(solution)/shard_map/all_to_all | solution.py:61
  86.9 19.6 %copy-start.7 = (bf16[2,1,96,2048]{3,2,1,0:T(8,128)(2,1)S(1)}, bf16[2,1,96,2048]{3,2,1,0:T(8,128)(2,1)}, u32[]{:S(2)}) copy-start(bf16[2,1,96,2048]{3,2,1,0:T(8,128)(2,1)} %param.12) | copy-start | bytes 2359300
  107.5 10.3 %collective-permute-start = (bf16[96,2048]{1,0:T(8,128)(2,1)S(1)}, bf16[96,2048]{1,0:T(8,128)(2,1)S(1)}, u32[]{:S(2)}, u32[]{:S(2)}) collective-permute-start(bf16[96,2048]{1,0:T(8,128)(2,1)S(1)} %get-tuple-element.23), channel_id=1, source_target_pairs={{8,0},{16,8},{24,16},{9,1},{17,9},{25,17},{10,2},{18,10},{26,18},{... | collective-permute-start | bytes 1179656 | tf_op jit(solution)/shard_map/ppermute | solution.py:10
  117.8 27.4 %copy-start.2 = (bf16[2,2,1,1,192,2048]{5,4,3,2,1,0:T(8,128)(2,1)S(1)}, bf16[2,2,1,1,192,2048]{5,4,3,2,1,0:T(8,128)(2,1)}, u32[]{:S(2)}) copy-start(bf16[2,2,1,1,192,2048]{5,4,3,2,1,0:T(8,128)(2,1)} %param.14) | copy-start | bytes 9437188
  120.6 20.4 %all-to-all-start.2 = ((bf16[8,24,2048]{2,1,0:T(8,128)(2,1)}), bf16[8,24,2048]{2,1,0:T(8,128)(2,1)}, u32[]{:S(2)}, u32[]{:S(2)}) async-start(bf16[8,24,2048]{2,1,0:T(8,128)(2,1)} %bitcast.231), calls=%async_computation.2 | async-start | bytes 1572864 | tf_op jit(solution)/shard_map/all_to_all | solution.py:43
  124.8 6.9 %collective-permute-start.1 = (bf16[96,2048]{1,0:T(8,128)(2,1)}, bf16[96,2048]{1,0:T(8,128)(2,1)}, u32[]{:S(2)}, u32[]{:S(2)}) collective-permute-start(bf16[96,2048]{1,0:T(8,128)(2,1)} %get-tuple-element.24), channel_id=1, source_target_pairs={{0,8},{8,16},{16,24},{1,9},{9,17},{17,25},{2,10},{10,18},{18,26},{... | collective-permute-start | bytes 1179656 | tf_op jit(solution)/shard_map/ppermute | solution.py:10
  141.0 24.2 %all-to-all-start.6 = ((bf16[8,24,2048]{2,1,0:T(8,128)(2,1)}), bf16[8,24,2048]{2,1,0:T(8,128)(2,1)}, u32[]{:S(2)}, u32[]{:S(2)}) async-start(bf16[8,24,2048]{2,1,0:T(8,128)(2,1)} %bitcast.232), calls=%async_computation.6 | async-start | bytes 1572864 | tf_op jit(solution)/shard_map/all_to_all | solution.py:43
  153.8 17.0 %copy-start.18 = (bf16[192,256]{1,0:T(8,128)(2,1)}, bf16[192,256]{1,0:T(8,128)(2,1)S(1)}, u32[]{:S(2)}) copy-start(bf16[192,256]{1,0:T(8,128)(2,1)S(1)} %get-tuple-element.25) | copy-start | bytes 294916
  153.8 17.0 %copy-start.20 = (bf16[192,256]{1,0:T(8,128)(2,1)}, bf16[192,256]{1,0:T(8,128)(2,1)S(1)}, u32[]{:S(2)}) copy-start(bf16[192,256]{1,0:T(8,128)(2,1)S(1)} %get-tuple-element.26) | copy-start | bytes 294916
  153.8 15.1 %copy-start.6 = (bf16[8,24,2048]{2,1,0:T(8,128)(2,1)S(1)}, bf16[8,24,2048]{2,1,0:T(8,128)(2,1)}, u32[]{:S(2)}) copy-start(bf16[8,24,2048]{2,1,0:T(8,128)(2,1)} %copy-done.5) | copy-start | bytes 2359300
  153.8 15.1 %copy-start.28 = (f32[192,512]{1,0:T(8,128)S(1)}, f32[192,512]{1,0:T(8,128)}, u32[]{:S(2)}) copy-start(f32[192,512]{1,0:T(8,128)} %copy-done.27) | copy-start | bytes 1179652
  155.5 15.2 %copy-start.24 = (f32[192,512]{1,0:T(8,128)S(1)}, f32[192,512]{1,0:T(8,128)}, u32[]{:S(2)}) copy-start(f32[192,512]{1,0:T(8,128)} %fusion.8) | copy-start | bytes 1179652
  165.2 23.2 %all-to-all-start.3 = ((bf16[8,24,2048]{2,1,0:T(8,128)(2,1)}), bf16[8,24,2048]{2,1,0:T(8,128)(2,1)S(1)}, u32[]{:S(2)}, u32[]{:S(2)}) async-start(bf16[8,24,2048]{2,1,0:T(8,128)(2,1)} %bitcast.29), calls=%async_computation.3 | async-start | bytes 1572864 | tf_op jit(solution)/shard_map/all_to_all | solution.py:61
  188.4 42.0 %all-to-all-start.8 = ((bf16[4,192,2048]{2,1,0:T(8,128)(2,1)}), bf16[4,192,2048]{2,1,0:T(8,128)(2,1)}, u32[]{:S(2)}, u32[]{:S(2)}) async-start(bf16[4,192,2048]{2,1,0:T(8,128)(2,1)} %bitcast.230), calls=%async_computation.8 | async-start | bytes 6291456 | tf_op jit(solution)/shard_map/all_to_all | solution.py:125
  230.4 22.5 %all-to-all-start.7 = ((bf16[8,24,2048]{2,1,0:T(8,128)(2,1)}), bf16[8,24,2048]{2,1,0:T(8,128)(2,1)S(1)}, u32[]{:S(2)}, u32[]{:S(2)}) async-start(bf16[8,24,2048]{2,1,0:T(8,128)(2,1)} %bitcast.61), calls=%async_computation.7 | async-start | bytes 1572864 | tf_op jit(solution)/shard_map/all_to_all | solution.py:61
  237.9 21.8 %copy-start.4 = (bf16[8,24,2048]{2,1,0:T(8,128)(2,1)S(1)}, bf16[8,24,2048]{2,1,0:T(8,128)(2,1)}, u32[]{:S(2)}) copy-start(bf16[8,24,2048]{2,1,0:T(8,128)(2,1)} %copy-done.3) | copy-start | bytes 2359300
  237.9 21.8 %copy-start.26 = (f32[192,512]{1,0:T(8,128)S(1)}, f32[192,512]{1,0:T(8,128)}, u32[]{:S(2)}) copy-start(f32[192,512]{1,0:T(8,128)} %copy-done.25) | copy-start | bytes 1179652
  237.9 23.6 %copy-start.11 = (bf16[192,256]{1,0:T(8,128)(2,1)S(1)}, bf16[192,256]{1,0:T(8,128)(2,1)}, u32[]{:S(2)}) copy-start(bf16[192,256]{1,0:T(8,128)(2,1)} %copy-done.10) | copy-start | bytes 294916
  237.9 23.6 %copy-start.13 = (bf16[192,256]{1,0:T(8,128)(2,1)S(1)}, bf16[192,256]{1,0:T(8,128)(2,1)}, u32[]{:S(2)}) copy-start(bf16[192,256]{1,0:T(8,128)(2,1)} %copy-done.12) | copy-start | bytes 294916
  253.0 42.8 %all-to-all-start.9 = ((bf16[4,192,2048]{2,1,0:T(8,128)(2,1)}), bf16[4,192,2048]{2,1,0:T(8,128)(2,1)}, u32[]{:S(2)}, u32[]{:S(2)}) async-start(bf16[4,192,2048]{2,1,0:T(8,128)(2,1)} %rev.4), calls=%async_computation.9 | async-start | bytes 6291456 | tf_op jit(solution)/shard_map/all_to_all | solution.py:128
  295.8 4.3 %copy-start.1 = (f32[256,2048]{1,0:T(8,128)S(1)}, f32[256,2048]{1,0:T(8,128)}, u32[]{:S(2)}) copy-start(f32[256,2048]{1,0:T(8,128)} %fusion.92) | copy-start | bytes 6291460
  295.8 4.3 %copy-start.23 = (f32[192,512]{1,0:T(8,128)S(1)}, f32[192,512]{1,0:T(8,128)}, u32[]{:S(2)}) copy-start(f32[192,512]{1,0:T(8,128)} %copy-done.22) | copy-start | bytes 1179652
  308.3 5.5 %copy-start.19 = (bf16[192,256]{1,0:T(8,128)(2,1)S(1)}, bf16[192,256]{1,0:T(8,128)(2,1)}, u32[]{:S(2)}) copy-start(bf16[192,256]{1,0:T(8,128)(2,1)} %copy-done.18) | copy-start | bytes 294916
  308.3 5.5 %copy-start.21 = (bf16[192,256]{1,0:T(8,128)(2,1)S(1)}, bf16[192,256]{1,0:T(8,128)(2,1)}, u32[]{:S(2)}) copy-start(bf16[192,256]{1,0:T(8,128)(2,1)} %copy-done.20) | copy-start | bytes 294916
  (16 other events, 31.2 us)
where the time goes:
time: 323 us; the launch traced here: 321 us
  waiting for transfers between devices  163 us (50%)
  starting transfers between devices  54.5 us (17%)
  matrix products  46.8 us (14%)
  local copies, waits for them, and re-layouts  31.1 us (10%)
  other arithmetic  23.8 us (7%)
    all_to_all x4, waiting for transfers between devices, expert_pass(): lax.all_to_all(input_grad.reshape(experts, capacity, model_width), 'exper...  48.8 us
    all_to_all x4, waiting for transfers between devices, expert_pass(): lax.all_to_all(outgoing.reshape(experts, capacity, model_width), 'expert'...  45 us
    all_to_all x1, waiting for transfers between devices, on_device(): lax.all_to_all(flat.reshape(sections, -1, model_width), 'section', split_...  32.7 us
    all_to_all x1, waiting for transfers between devices, on_device(): lax.all_to_all(jnp.flip(spread, 0), 'section', split_axis=0, concat_axis=...  25.4 us
    dot_general x8, matrix products, left_product(): lax.dot_general(left, right, (((0,), (0,)), ((), ())), preferred_element_...  22 us
    all_to_all x4, starting transfers between devices, expert_pass(): lax.all_to_all(outgoing.reshape(experts, capacity, model_width), 'expert'...  19.6 us
    all_to_all x4, starting transfers between devices, expert_pass(): lax.all_to_all(input_grad.reshape(experts, capacity, model_width), 'exper...  16.5 us
    dot_general x8, matrix products, right_product(): lax.dot_general(left, right, (((1,), (1,)), ((), ())), preferred_element_...  16 us
  transfers between devices with their start and end apart: 12, of which 12 were waited for; matrix products, arithmetic and copies ran while one was open for 19% of the time, Pallas kernels for 0%

commit v1 on v0

v1 whole, which is shorter than its diff:
```python
import jax
import jax.numpy as jnp
from jax import lax
from jax.sharding import PartitionSpec as P


def passed_along(block, axis, distance):
    devices = range(lax.axis_size(axis))
    route = [(i - distance, i) for i in devices if i - distance in devices]
    return lax.ppermute(block, axis, route)


def mirrored(block, axis):
    count = lax.axis_size(axis)
    return lax.ppermute(block, axis, [(i, count - 1 - i) for i in range(count)])


def slot_index(route_ids, count_table, capacity):
    experts = count_table.shape[0]
    offset = jnp.cumsum(count_table) - count_table
    labels = lax.iota(jnp.int32, experts)
    first_slot = jnp.sum(
        jnp.where(route_ids[:, None] == labels[None, :], offset[None, :], 0), axis=1
    )
    return route_ids * capacity + lax.iota(jnp.int32, route_ids.shape[0]) - first_slot


def left_product(left, right):
    return lax.dot_general(
        left, right, (((0,), (0,)), ((), ())), preferred_element_type=jnp.float32
    )


def right_product(left, right):
    return lax.dot_general(
        left, right, (((1,), (1,)), ((), ())), preferred_element_type=jnp.float32
    )


def dispatch(gradient, prob_rows, route_ids, count_table):
    tokens, model_width = gradient.shape
    experts = count_table.shape[0]
    capacity = 2 * tokens // experts
    slot_ids = slot_index(route_ids, count_table, capacity)
    scaled = (prob_rows[:, None] * gradient.astype(jnp.float32)).astype(jnp.bfloat16)
    outgoing = jnp.zeros((experts * capacity, model_width), jnp.bfloat16).at[slot_ids].set(scaled)
    arrived = lax.all_to_all(
        outgoing.reshape(experts, capacity, model_width),
        "expert",
        split_axis=0,
        concat_axis=0,
        tiled=True,
    )
    return arrived.reshape(-1, model_width), slot_ids


def expert_grads(slope_rows, saved_rows, weight_in, weight_out):
    hidden_width = weight_out.shape[0]
    gate_up = jnp.dot(saved_rows, weight_in, preferred_element_type=jnp.float32)
    gate_part = gate_up[:, :hidden_width]
    upward = gate_up[:, hidden_width:]
    sigmoid_gate = jax.nn.sigmoid(gate_part)
    active = gate_part * sigmoid_gate
    hidden = (active * upward).astype(jnp.bfloat16)
    hidden_grad = right_product(slope_rows, weight_out)
    gate_grad = hidden_grad * upward * sigmoid_gate * (1.0 + gate_part * (1.0 - sigmoid_gate))
    pair_grad = jnp.concatenate([gate_grad, hidden_grad * active], axis=1).astype(jnp.bfloat16)
    return hidden, pair_grad


def combine(gradient, pair_grad, weight_in, slot_ids):
    experts_rows, model_width = pair_grad.shape[0], gradient.shape[1]
    experts = lax.axis_size("expert")
    input_grad = right_product(pair_grad, weight_in).astype(jnp.bfloat16)
    returned = lax.all_to_all(
        input_grad.reshape(experts, experts_rows // experts, model_width),
        "expert",
        split_axis=0,
        concat_axis=0,
        tiled=True,
    )
    back_rows = jnp.take(returned.reshape(-1, model_width), slot_ids, axis=0)
    return (gradient.astype(jnp.float32) + back_rows.astype(jnp.float32)).astype(jnp.bfloat16)


def weight_terms(saved_rows, slope_rows, hidden, pair_grad):
    return left_product(saved_rows, pair_grad), left_product(hidden, slope_rows)


def on_device(w_in, w_out, grads, fresh, saved, probs, routes, counts):
    sections = lax.axis_size("section")
    section_id = lax.axis_index("section")
    model_width = grads.shape[-1]
    hidden_width = w_out.shape[-2]
    ticks = saved.shape[0]
    saved_mirror = mirrored(saved[:, 1, 0, 0], "section")
    current = [grads[0, 0], grads[1, 0]]
    finished = [grads[0, 0], grads[1, 0]]
    zeros_in = jnp.zeros((model_width, 2 * hidden_width), jnp.float32)
    zeros_out = jnp.zeros((hidden_width, model_width), jnp.float32)
    own_in, own_out = zeros_in, zeros_out
    mirror_in, mirror_out = zeros_in, zeros_out
    for tick_id in range(ticks):
        for way_id in range(2):
            saved_rows = saved[tick_id, way_id, 0, 0]
            slope_rows, slot_ids = dispatch(
                current[way_id],
                probs[tick_id, way_id, 0],
                routes[tick_id, way_id, 0],
                counts[tick_id, way_id, 0, 0],
            )
            hidden, pair_grad = expert_grads(
                slope_rows, saved_rows, w_in[way_id, 0, 0], w_out[way_id, 0, 0]
            )
            finished[way_id] = combine(current[way_id], pair_grad, w_in[way_id, 0, 0], slot_ids)
            if way_id == 0:
                part_in, part_out = weight_terms(saved_rows, slope_rows, hidden, pair_grad)
                own_in = own_in + part_in
                own_out = own_out + part_out
            else:
                slope_mirror = mirrored(slope_rows, "section")
                hidden_m, pair_grad_m = expert_grads(
                    slope_mirror, saved_mirror[tick_id], w_in[0, 0, 0], w_out[0, 0, 0]
                )
                part_in, part_out = weight_terms(
                    saved_mirror[tick_id], slope_mirror, hidden_m, pair_grad_m
                )
                mirror_in = mirror_in + part_in
                mirror_out = mirror_out + part_out
        if tick_id + 1 < ticks:
            from_above = passed_along(finished[0], "section", -1)
            from_below = passed_along(finished[1], "section", 1)
            current = [
                jnp.where(section_id == sections - 1, fresh[tick_id, 0], from_above),
                jnp.where(section_id == 0, fresh[tick_id, 1], from_below),
            ]
    mirror_in = mirror_in.astype(jnp.bfloat16).astype(jnp.float32)
    mirror_out = mirror_out.astype(jnp.bfloat16).astype(jnp.float32)
    grad_in = (own_in + mirror_in).astype(jnp.bfloat16)
    grad_out = (own_out + mirror_out).astype(jnp.bfloat16)
    return (jnp.stack(finished)[:, None], grad_in[None, None], grad_out[None, None])


def solution(mesh):
    return jax.shard_map(
        on_device,
        mesh=mesh,
        in_specs=(
            P(None, "section", "expert", None, None),
            P(None, "section", "expert", None, None),
            P(None, "section", "expert", None),
            P(None, None, "expert", None),
            P(None, None, "section", "expert", None, None),
            P(None, None, "section", "expert"),
            P(None, None, "section", "expert"),
            P(None, None, "section", "expert", None),
        ),
        out_specs=(
            P(None, "section", "expert", None),
            P("section", "expert", None, None),
            P("section", "expert", None, None),
        ),
        check_vma=False,
    )
```

time: 323 us -> 249 us (0.77)
  waiting for transfers between devices: 163 us -> 113 us
  local copies, waits for them, and re-layouts: 31.1 us -> 15.9 us
  starting transfers between devices: 54.5 us -> 45.4 us
  matrix products: 46.8 us -> 54.6 us
  other arithmetic: 23.8 us -> 18 us
    all_to_all x10 -> x8, waiting for transfers between devices: 152 us -> 76.4 us  [the longest x4 39.1 us: dispatch(): lax.all_to_all(outgoing.reshape(experts, capacity, model_width), 'expert'...]
    ppermute x2, waiting for transfers between devices: 11.5 us -> 36.7 us  [passed_along(): return lax.ppermute(block, axis, route)]
    convert_element_type x3 -> x0, local copies, waits for them, and re-layouts: 13.3 us -> none  [the longest x2 10.7 us: on_device(): mirror_in.astype(jnp.float32)]
    all_to_all x10 -> x8, starting transfers between devices: 48.8 us -> 36.1 us  [the longest x4 19.1 us: dispatch(): lax.all_to_all(outgoing.reshape(experts, capacity, model_width), 'expert'...]
    dot_general x4 -> x6, matrix products: 8.76 us -> 14.8 us  [expert_grads(): gate_up = jnp.dot(saved_rows, weight_in, preferred_element_type=jnp.float32)]
    convert_element_type x2 -> x1, other arithmetic: 5.23 us -> 1.17 us  [combine(): (gradient.astype(jnp.float32) + back_rows.astype(jnp.float32)).astype(jnp...]
    rev x1 -> x0, local copies, waits for them, and re-layouts: 3.94 us -> none  [on_device(): jnp.flip(spread, 0)]
    dot_general x8 -> x10, matrix products: 16 us -> 19.5 us  [right_product(): lax.dot_general(left, right, (((1,), (1,)), ((), ())), preferred_element_...]
  transfers between devices with their start and end apart: 12 -> 13, of which waited for: 12 -> 8; matrix products, arithmetic and copies ran while one was open for 19% -> 29% of each run, Pallas kernels for 0% -> 0%
where the time goes in v1:
time: 249 us; the launch traced here: 248 us
  waiting for transfers between devices  113 us (45%)
  matrix products  54.6 us (22%)
  starting transfers between devices  45.4 us (18%)
  other arithmetic  18 us (7%)
  local copies, waits for them, and re-layouts  15.9 us (6%)
    all_to_all x4, waiting for transfers between devices, dispatch(): lax.all_to_all(outgoing.reshape(experts, capacity, model_width), 'expert'...  39.1 us
    all_to_all x4, waiting for transfers between devices, combine(): lax.all_to_all(input_grad.reshape(experts, experts_rows // experts, model...  37.3 us
    ppermute x2, waiting for transfers between devices, passed_along(): return lax.ppermute(block, axis, route)  36.7 us
    dot_general x8, matrix products, left_product(): lax.dot_general(left, right, (((0,), (0,)), ((), ())), preferred_element_...  20.3 us
    dot_general x10, matrix products, right_product(): lax.dot_general(left, right, (((1,), (1,)), ((), ())), preferred_element_...  19.5 us
    all_to_all x4, starting transfers between devices, dispatch(): lax.all_to_all(outgoing.reshape(experts, capacity, model_width), 'expert'...  19.1 us
    all_to_all x4, starting transfers between devices, combine(): lax.all_to_all(input_grad.reshape(experts, experts_rows // experts, model...  16.9 us
    dot_general x6, matrix products, expert_grads(): gate_up = jnp.dot(saved_rows, weight_in, preferred_element_type=jnp.float32)  14.8 us
  transfers between devices with their start and end apart: 13, of which 8 were waited for; matrix products, arithmetic and copies ran while one was open for 29% of the time, Pallas kernels for 0%

profile of v1, /device:TPU:1, one launch (start us, length us, event | category | flops | bytes accessed | tf_op | source)
XLA Modules:
  0.0 248.1 jit_solution(12819093050950173504)
XLA Ops:
  5.7 2.6 %scatter_custom_fusion.2 = bf16[192,2048]{1,0:T(8,128)(2,1)} fusion(s32[96]{0:T(128)S(1)} %get-tuple-element.47, f32[96]{0:T(128)S(1)} %get-tuple-element.43, bf16[]{:T(256)} %constant.7.clone.1, bf16[2,1,96,2048]{3,2,1,0:T(8,128)(2,1)} %param.12), kind=kCustom, calls=%fused_computation.101 | custom fusion | flops 589824 | bytes 1180672 | tf_op jit(solution)/shard_map/scatter | solution.py:46
  8.3 6.4 %all-to-all-start.4 = ((bf16[8,24,2048]{2,1,0:T(8,128)(2,1)}), bf16[8,24,2048]{2,1,0:T(8,128)(2,1)}, u32[]{:S(2)}, u32[]{:S(2)}) async-start(bf16[8,24,2048]{2,1,0:T(8,128)(2,1)} %bitcast.43), calls=%async_computation.4 | async-start | bytes 1572864 | tf_op jit(solution)/shard_map/all_to_all | solution.py:47
  16.9 17.0 %all-to-all-done.4 = bf16[8,24,2048]{2,1,0:T(8,128)(2,1)} async-done(((bf16[8,24,2048]{2,1,0:T(8,128)(2,1)}), bf16[8,24,2048]{2,1,0:T(8,128)(2,1)}, u32[]{:S(2)}, u32[]{:S(2)}) %all-to-all-start.4) | async-done | bytes 786464 | tf_op jit(solution)/shard_map/all_to_all | solution.py:47
  33.9 4.8 %all-to-all-start = ((bf16[8,24,2048]{2,1,0:T(8,128)(2,1)}), bf16[8,24,2048]{2,1,0:T(8,128)(2,1)S(1)}, u32[]{:S(2)}, u32[]{:S(2)}) async-start(bf16[8,24,2048]{2,1,0:T(8,128)(2,1)} %bitcast.11), calls=%async_computation | async-start | bytes 1572864 | tf_op jit(solution)/shard_map/all_to_all | solution.py:47
  38.7 2.5 %fusion.10 = f32[192,512]{1,0:T(8,128)S(1)} fusion(bf16[2,1,1,2048,512]{4,3,2,1,0:T(8,128)(2,1)} %param.10, bf16[2,2,1,1,192,2048]{5,4,3,2,1,0:T(8,128)(2,1)} %param.14), kind=kOutput, calls=%fused_computation.26 | convolution fusion | flops 402653184 | bytes 3276800 | tf_op jit(solution)/shard_map/dot_general | solution.py:59
  45.0 13.0 %all-to-all-done = bf16[8,24,2048]{2,1,0:T(8,128)(2,1)S(1)} async-done(((bf16[8,24,2048]{2,1,0:T(8,128)(2,1)}), bf16[8,24,2048]{2,1,0:T(8,128)(2,1)S(1)}, u32[]{:S(2)}, u32[]{:S(2)}) %all-to-all-start) | async-done | bytes 786464 | tf_op jit(solution)/shard_map/all_to_all | solution.py:47
  58.1 4.6 %all-to-all-start.5 = ((bf16[8,24,2048]{2,1,0:T(8,128)(2,1)}), bf16[8,24,2048]{2,1,0:T(8,128)(2,1)S(1)}, u32[]{:S(2)}, u32[]{:S(2)}) async-start(bf16[8,24,2048]{2,1,0:T(8,128)(2,1)} %bitcast.48), calls=%async_computation.5 | async-start | bytes 1572864 | tf_op jit(solution)/shard_map/all_to_all | solution.py:75
  62.7 2.5 %fusion.20 = f32[192,512]{1,0:T(8,128)S(1)} fusion(bf16[2,1,1,2048,512]{4,3,2,1,0:T(8,128)(2,1)} %param.10, bf16[2,2,1,1,192,2048]{5,4,3,2,1,0:T(8,128)(2,1)} %param.14), kind=kOutput, calls=%fused_computation.36 | convolution fusion | flops 402653184 | bytes 3276800 | tf_op jit(solution)/shard_map/dot_general | solution.py:59
  69.6 12.4 %all-to-all-done.5 = bf16[8,24,2048]{2,1,0:T(8,128)(2,1)S(1)} async-done(((bf16[8,24,2048]{2,1,0:T(8,128)(2,1)}), bf16[8,24,2048]{2,1,0:T(8,128)(2,1)S(1)}, u32[]{:S(2)}, u32[]{:S(2)}) %all-to-all-start.5) | async-done | bytes 786464 | tf_op jit(solution)/shard_map/all_to_all | solution.py:75
  82.0 4.6 %all-to-all-start.1 = ((bf16[8,24,2048]{2,1,0:T(8,128)(2,1)}), bf16[8,24,2048]{2,1,0:T(8,128)(2,1)S(1)}, u32[]{:S(2)}, u32[]{:S(2)}) async-start(bf16[8,24,2048]{2,1,0:T(8,128)(2,1)} %bitcast.16), calls=%async_computation.1 | async-start | bytes 1572864 | tf_op jit(solution)/shard_map/all_to_all | solution.py:75
  88.0 17.9 %all-to-all-done.1 = bf16[8,24,2048]{2,1,0:T(8,128)(2,1)S(1)} async-done(((bf16[8,24,2048]{2,1,0:T(8,128)(2,1)}), bf16[8,24,2048]{2,1,0:T(8,128)(2,1)S(1)}, u32[]{:S(2)}, u32[]{:S(2)}) %all-to-all-start.1) | async-done | bytes 786464 | tf_op jit(solution)/shard_map/all_to_all | solution.py:75
  107.9 4.8 %collective-permute-start.1 = (bf16[96,2048]{1,0:T(8,128)(2,1)}, bf16[96,2048]{1,0:T(8,128)(2,1)S(1)}, u32[]{:S(2)}, u32[]{:S(2)}) collective-permute-start(bf16[96,2048]{1,0:T(8,128)(2,1)} %get-tuple-element.21), channel_id=1, source_target_pairs={{0,8},{8,16},{16,24},{1,9},{9,17},{17,25},{2,10},{10,18},{18,26},{... | collective-permute-start | bytes 1179656 | tf_op jit(solution)/shard_map/ppermute | solution.py:10
  112.8 2.7 %slice_bitcast_fusion = bf16[2,192,2048]{2,1,0:T(8,128)(2,1)} fusion(bf16[2,2,1,1,192,2048]{5,4,3,2,1,0:T(8,128)(2,1)} %param.14), kind=kLoop, calls=%fused_computation.38 | loop fusion | bytes 3145728 | tf_op jit(solution)/shard_map/squeeze | solution.py:96
  116.3 4.4 %collective-permute-done.1 = bf16[96,2048]{1,0:T(8,128)(2,1)S(1)} collective-permute-done((bf16[96,2048]{1,0:T(8,128)(2,1)}, bf16[96,2048]{1,0:T(8,128)(2,1)S(1)}, u32[]{:S(2)}, u32[]{:S(2)}) %collective-permute-start.1) | collective-permute-done | bytes 393248 | tf_op jit(solution)/shard_map/ppermute | solution.py:10
  120.7 2.6 %scatter_custom_fusion.3 = bf16[192,2048]{1,0:T(8,128)(2,1)} fusion(s32[96]{0:T(128)} %get-tuple-element.46, f32[96]{0:T(128)S(1)} %get-tuple-element.42, bf16[]{:T(256)} %constant.7.clone.1, bf16[96,2048]{1,0:T(8,128)(2,1)S(1)} %collective-permute-done.1, bf16[1,2,96,2048]{3,2,1,0:T(8,128)(2,1)} %param.13, pred[]{:T(512)S(6)} %eq.75), kind=kCustom, calls=%fused_computation.104 | custom fusion | flops 786432 | bytes 1573761 | tf_op jit(solution)/shard_map/scatter | solution.py:46
  123.4 4.2 %all-to-all-start.6 = ((bf16[8,24,2048]{2,1,0:T(8,128)(2,1)}), bf16[8,24,2048]{2,1,0:T(8,128)(2,1)}, u32[]{:S(2)}, u32[]{:S(2)}) async-start(bf16[8,24,2048]{2,1,0:T(8,128)(2,1)} %bitcast.245), calls=%async_computation.6 | async-start | bytes 1572864 | tf_op jit(solution)/shard_map/all_to_all | solution.py:47
  127.6 3.1 %fusion.17 = f32[192,512]{1,0:T(8,128)} fusion(bf16[2,1,1,2048,512]{4,3,2,1,0:T(8,128)(2,1)} %param.10, bf16[2,2,1,1,192,2048]{5,4,3,2,1,0:T(8,128)(2,1)S(1)} %copy-done.2), kind=kOutput, calls=%fused_computation.33 | convolution fusion | flops 402653184 | bytes 3276800 | tf_op jit(solution)/shard_map/dot_general | solution.py:59
  132.1 2.4 collective-permute-start.2
  136.6 2.7 %fusion.59 = f32[512,2048]{1,0:T(8,128)} fusion(bf16[2,2,1,1,192,2048]{5,4,3,2,1,0:T(8,128)(2,1)S(1)} %copy-done.2, bf16[192,256]{1,0:T(8,128)(2,1)S(1)} %copy-done.15, bf16[192,256]{1,0:T(8,128)(2,1)S(1)} %copy-done.13), kind=kOutput, calls=%fused_computation.87 | convolution fusion | flops 403046400 | bytes 5177344 | tf_op jit(solution)/shard_map/dot_general | solution.py:29
  139.8 32.3 %collective-permute-done = bf16[96,2048]{1,0:T(8,128)(2,1)} collective-permute-done((bf16[96,2048]{1,0:T(8,128)(2,1)S(1)}, bf16[96,2048]{1,0:T(8,128)(2,1)}, u32[]{:S(2)}, u32[]{:S(2)}) %collective-permute-start) | collective-permute-done | bytes 393248 | tf_op jit(solution)/shard_map/ppermute | solution.py:10
  172.1 2.7 %scatter_custom_fusion.1 = bf16[192,2048]{1,0:T(8,128)(2,1)} fusion(s32[96]{0:T(128)} %get-tuple-element.45, f32[96]{0:T(128)S(1)} %get-tuple-element.41, bf16[]{:T(256)} %constant.7.clone.1, bf16[96,2048]{1,0:T(8,128)(2,1)} %collective-permute-done, bf16[1,2,96,2048]{3,2,1,0:T(8,128)(2,1)S(1)} %copy-done.8, pred[]{:T(512)S(6)} %eq.66), kind=kCustom, calls=%fused_computation.106 | custom fusion | flops 786432 | bytes 1573889 | tf_op jit(solution)/shard_map/scatter | solution.py:46
  174.8 3.7 %all-to-all-start.2 = ((bf16[8,24,2048]{2,1,0:T(8,128)(2,1)}), bf16[8,24,2048]{2,1,0:T(8,128)(2,1)S(1)}, u32[]{:S(2)}, u32[]{:S(2)}) async-start(bf16[8,24,2048]{2,1,0:T(8,128)(2,1)} %bitcast.244), calls=%async_computation.2 | async-start | bytes 1572864 | tf_op jit(solution)/shard_map/all_to_all | solution.py:47
  178.5 3.3 %fusion.12 = f32[192,512]{1,0:T(8,128)} fusion(bf16[2,1,1,2048,512]{4,3,2,1,0:T(8,128)(2,1)} %param.10, bf16[2,192,2048]{2,1,0:T(8,128)(2,1)} %collective-permute-done.3), kind=kOutput, calls=%fused_computation.28 | convolution fusion | flops 402653184 | bytes 3276800 | tf_op jit(solution)/shard_map/dot_general | solution.py:59
  189.1 9.1 %all-to-all-done.2 = bf16[8,24,2048]{2,1,0:T(8,128)(2,1)S(1)} async-done(((bf16[8,24,2048]{2,1,0:T(8,128)(2,1)}), bf16[8,24,2048]{2,1,0:T(8,128)(2,1)S(1)}, u32[]{:S(2)}, u32[]{:S(2)}) %all-to-all-start.2) | async-done | bytes 786464 | tf_op jit(solution)/shard_map/all_to_all | solution.py:47
  199.0 4.1 %all-to-all-start.7 = ((bf16[8,24,2048]{2,1,0:T(8,128)(2,1)}), bf16[8,24,2048]{2,1,0:T(8,128)(2,1)S(1)}, u32[]{:S(2)}, u32[]{:S(2)}) async-start(bf16[8,24,2048]{2,1,0:T(8,128)(2,1)} %bitcast.248), calls=%async_computation.7 | async-start | bytes 1572864 | tf_op jit(solution)/shard_map/all_to_all | solution.py:75
  205.2 3.3 %convolution_convert_fusion.2 = bf16[192,2048]{1,0:T(8,128)(2,1)} fusion(bf16[2,1,1,2048,512]{4,3,2,1,0:T(8,128)(2,1)} %param.10, bf16[192,256]{1,0:T(8,128)(2,1)S(1)} %get-tuple-element.27, bf16[192,256]{1,0:T(8,128)(2,1)S(1)} %get-tuple-element.26), kind=kOutput, calls=%fused_computation.19 | convolution fusion | flops 403439616 | bytes 3080192 | tf_op jit(solution)/shard_map/dot_general | solution.py:35
  208.5 4.0 %fusion.56 = f32[512,2048]{1,0:T(8,128)} fusion(bf16[2,2,1,1,192,2048]{5,4,3,2,1,0:T(8,128)(2,1)} %param.14, bf16[192,256]{1,0:T(8,128)(2,1)S(1)} %get-tuple-element.27, bf16[192,256]{1,0:T(8,128)(2,1)S(1)} %get-tuple-element.26), kind=kOutput, calls=%fused_computation.84 | convolution fusion | flops 403046400 | bytes 5177344 | tf_op jit(solution)/shard_map/dot_general | solution.py:29
  216.5 7.0 %all-to-all-done.7 = bf16[8,24,2048]{2,1,0:T(8,128)(2,1)S(1)} async-done(((bf16[8,24,2048]{2,1,0:T(8,128)(2,1)}), bf16[8,24,2048]{2,1,0:T(8,128)(2,1)S(1)}, u32[]{:S(2)}, u32[]{:S(2)}) %all-to-all-start.7) | async-done | bytes 786464 | tf_op jit(solution)/shard_map/all_to_all | solution.py:75
  223.5 3.7 %all-to-all-start.3 = ((bf16[8,24,2048]{2,1,0:T(8,128)(2,1)}), bf16[8,24,2048]{2,1,0:T(8,128)(2,1)S(1)}, u32[]{:S(2)}, u32[]{:S(2)}) async-start(bf16[8,24,2048]{2,1,0:T(8,128)(2,1)} %bitcast.29), calls=%async_computation.3 | async-start | bytes 1572864 | tf_op jit(solution)/shard_map/all_to_all | solution.py:75
  229.6 4.9 %fusion.4 = bf16[1,1,2048,512]{2,3,1,0:T(8,128)(2,1)} fusion(f32[512,2048]{1,0:T(8,128)S(1)} %fusion.64, f32[512,2048]{1,0:T(8,128)S(1)} %copy-done, f32[512,2048]{1,0:T(8,128)} %fusion.56, bf16[2,192,2048]{2,1,0:T(8,128)(2,1)} %collective-permute-done.3, bf16[192,256]{1,0:T(8,128)(2,1)S(1)} %get-tuple-element.23, bf16[192,256]{1,0:T(8,128)(2,1)S(1)} %get-tuple-element.22), kind=kOutput, calls=%fused_computation.16 | convolution fusion | flops 409337856 | bytes 15663104 | tf_op jit(solution)/shard_map/dot_general | solution.py:29
  234.4 4.0 %copy.14 = bf16[1,1,2048,512]{3,2,1,0:T(8,128)(2,1)} copy(bf16[1,1,2048,512]{2,3,1,0:T(8,128)(2,1)} %fusion.4) | data formatting | bytes 4194304
  240.3 2.6 %fusion.5 = bf16[1,1,256,2048]{3,2,1,0:T(8,128)(2,1)} fusion(f32[256,2048]{1,0:T(8,128)S(1)} %copy-done.1, f32[256,2048]{1,0:T(8,128)S(1)} %fusion.118, bf16[192,2048]{1,0:T(8,128)(2,1)} %collective-permute-done.2, f32[192,512]{1,0:T(8,128)S(1)} %copy-done.18), kind=kOutput, calls=%fused_computation.21 | convolution fusion | flops 204242944 | bytes 6422528 | tf_op jit(solution)/shard_map/dot_general | solution.py:29
  (113 shorter events, 46.9 us)
Async XLA Ops:
  0.6 14.1 %copy-start.7 = (bf16[2,1,96,2048]{3,2,1,0:T(8,128)(2,1)S(1)}, bf16[2,1,96,2048]{3,2,1,0:T(8,128)(2,1)}, u32[]{:S(2)}) copy-start(bf16[2,1,96,2048]{3,2,1,0:T(8,128)(2,1)} %param.12) | copy-start | bytes 2359300
  8.3 25.6 %all-to-all-start.4 = ((bf16[8,24,2048]{2,1,0:T(8,128)(2,1)}), bf16[8,24,2048]{2,1,0:T(8,128)(2,1)}, u32[]{:S(2)}, u32[]{:S(2)}) async-start(bf16[8,24,2048]{2,1,0:T(8,128)(2,1)} %bitcast.43), calls=%async_computation.4 | async-start | bytes 1572864 | tf_op jit(solution)/shard_map/all_to_all | solution.py:47
  33.9 24.2 %all-to-all-start = ((bf16[8,24,2048]{2,1,0:T(8,128)(2,1)}), bf16[8,24,2048]{2,1,0:T(8,128)(2,1)S(1)}, u32[]{:S(2)}, u32[]{:S(2)}) async-start(bf16[8,24,2048]{2,1,0:T(8,128)(2,1)} %bitcast.11), calls=%async_computation | async-start | bytes 1572864 | tf_op jit(solution)/shard_map/all_to_all | solution.py:47
  38.7 4.5 %copy-start.26 = (bf16[2,1,1,2048,512]{4,3,2,1,0:T(8,128)(2,1)S(1)}, bf16[2,1,1,2048,512]{4,3,2,1,0:T(8,128)(2,1)}, u32[]{:S(2)}) copy-start(bf16[2,1,1,2048,512]{4,3,2,1,0:T(8,128)(2,1)} %param.10) | copy-start | bytes 12582916
  58.1 7.2 %copy-start.5 = (bf16[8,24,2048]{2,1,0:T(8,128)(2,1)}, bf16[8,24,2048]{2,1,0:T(8,128)(2,1)S(1)}, u32[]{:S(2)}) copy-start(bf16[8,24,2048]{2,1,0:T(8,128)(2,1)S(1)} %all-to-all-done) | copy-start | bytes 2359300
  58.1 23.9 %all-to-all-start.5 = ((bf16[8,24,2048]{2,1,0:T(8,128)(2,1)}), bf16[8,24,2048]{2,1,0:T(8,128)(2,1)S(1)}, u32[]{:S(2)}, u32[]{:S(2)}) async-start(bf16[8,24,2048]{2,1,0:T(8,128)(2,1)} %bitcast.48), calls=%async_computation.5 | async-start | bytes 1572864 | tf_op jit(solution)/shard_map/all_to_all | solution.py:75
  62.7 5.2 %copy-start.27 = (bf16[2,1,1,2048,512]{4,3,2,1,0:T(8,128)(2,1)S(1)}, bf16[2,1,1,2048,512]{4,3,2,1,0:T(8,128)(2,1)}, u32[]{:S(2)}) copy-start(bf16[2,1,1,2048,512]{4,3,2,1,0:T(8,128)(2,1)} %param.10) | copy-start | bytes 12582916
  67.8 18.8 %copy-start.23 = (s32[2,2,1,96]{3,2,1,0:T(1,128)S(1)}, s32[2,2,1,96]{3,2,1,0:T(1,128)}, u32[]{:S(2)}) copy-start(s32[2,2,1,96]{3,2,1,0:T(1,128)} %param.16) | copy-start | bytes 4612
  82.0 23.9 %all-to-all-start.1 = ((bf16[8,24,2048]{2,1,0:T(8,128)(2,1)}), bf16[8,24,2048]{2,1,0:T(8,128)(2,1)S(1)}, u32[]{:S(2)}, u32[]{:S(2)}) async-start(bf16[8,24,2048]{2,1,0:T(8,128)(2,1)} %bitcast.16), calls=%async_computation.1 | async-start | bytes 1572864 | tf_op jit(solution)/shard_map/all_to_all | solution.py:75
  107.9 12.8 %collective-permute-start.1 = (bf16[96,2048]{1,0:T(8,128)(2,1)}, bf16[96,2048]{1,0:T(8,128)(2,1)S(1)}, u32[]{:S(2)}, u32[]{:S(2)}) collective-permute-start(bf16[96,2048]{1,0:T(8,128)(2,1)} %get-tuple-element.21), channel_id=1, source_target_pairs={{0,8},{8,16},{16,24},{1,9},{9,17},{17,25},{2,10},{10,18},{18,26},{... | collective-permute-start | bytes 1179656 | tf_op jit(solution)/shard_map/ppermute | solution.py:10
  115.5 12.1 %copy-start.2 = (bf16[2,2,1,1,192,2048]{5,4,3,2,1,0:T(8,128)(2,1)S(1)}, bf16[2,2,1,1,192,2048]{5,4,3,2,1,0:T(8,128)(2,1)}, u32[]{:S(2)}) copy-start(bf16[2,2,1,1,192,2048]{5,4,3,2,1,0:T(8,128)(2,1)} %param.14) | copy-start | bytes 9437188
  115.5 63.0 %collective-permute-start.3 = (bf16[2,192,2048]{2,1,0:T(8,128)(2,1)}, bf16[2,192,2048]{2,1,0:T(8,128)(2,1)}, u32[]{:S(2)}, u32[]{:S(2)}) collective-permute-start(bf16[2,192,2048]{2,1,0:T(8,128)(2,1)} %slice_bitcast_fusion), channel_id=1, source_target_pairs={{0,24},{8,16},{16,8},{24,0},{1,25},{9,17},{17,9},{25,1},{2,26},{10... | collective-permute-start | bytes 4718600 | tf_op jit(solution)/shard_map/ppermute | solution.py:15
  123.4 51.4 %all-to-all-start.6 = ((bf16[8,24,2048]{2,1,0:T(8,128)(2,1)}), bf16[8,24,2048]{2,1,0:T(8,128)(2,1)}, u32[]{:S(2)}, u32[]{:S(2)}) async-start(bf16[8,24,2048]{2,1,0:T(8,128)(2,1)} %bitcast.245), calls=%async_computation.6 | async-start | bytes 1572864 | tf_op jit(solution)/shard_map/all_to_all | solution.py:47
  127.6 3.1 %copy-start.28 = (bf16[2,1,1,2048,512]{4,3,2,1,0:T(8,128)(2,1)S(1)}, bf16[2,1,1,2048,512]{4,3,2,1,0:T(8,128)(2,1)}, u32[]{:S(2)}) copy-start(bf16[2,1,1,2048,512]{4,3,2,1,0:T(8,128)(2,1)} %param.10) | copy-start | bytes 12582916
  130.8 3.7 %copy-start.11 = (bf16[96,2048]{1,0:T(8,128)(2,1)S(1)}, bf16[96,2048]{1,0:T(8,128)(2,1)}, u32[]{:S(2)}) copy-start(bf16[96,2048]{1,0:T(8,128)(2,1)} %get-tuple-element.20) | copy-start | bytes 1179652
  130.8 5.8 %copy-start.13 = (bf16[192,256]{1,0:T(8,128)(2,1)S(1)}, bf16[192,256]{1,0:T(8,128)(2,1)}, u32[]{:S(2)}) copy-start(bf16[192,256]{1,0:T(8,128)(2,1)} %copy-done.12) | copy-start | bytes 294916
  130.8 5.8 %copy-start.15 = (bf16[192,256]{1,0:T(8,128)(2,1)S(1)}, bf16[192,256]{1,0:T(8,128)(2,1)}, u32[]{:S(2)}) copy-start(bf16[192,256]{1,0:T(8,128)(2,1)} %copy-done.14) | copy-start | bytes 294916
  132.1 51.7 %collective-permute-start.2 = (bf16[192,2048]{1,0:T(8,128)(2,1)}, bf16[192,2048]{1,0:T(8,128)(2,1)}, u32[]{:S(2)}, u32[]{:S(2)}) collective-permute-start(bf16[192,2048]{1,0:T(8,128)(2,1)} %bitcast.44), channel_id=1, source_target_pairs={{0,24},{8,16},{16,8},{24,0},{1,25},{9,17},{17,9},{25,1},{2,26},{10... | collective-permute-start | bytes 2359304 | tf_op jit(solution)/shard_map/ppermute | solution.py:15
  134.5 4.8 %copy-start.6 = (bf16[8,24,2048]{2,1,0:T(8,128)(2,1)S(1)}, bf16[8,24,2048]{2,1,0:T(8,128)(2,1)}, u32[]{:S(2)}) copy-start(bf16[8,24,2048]{2,1,0:T(8,128)(2,1)} %copy-done.5) | copy-start | bytes 2359300
  134.5 4.8 %copy-start.20 = (f32[192,512]{1,0:T(8,128)S(1)}, f32[192,512]{1,0:T(8,128)}, u32[]{:S(2)}) copy-start(f32[192,512]{1,0:T(8,128)} %copy-done.19) | copy-start | bytes 1179652
  134.5 37.6 %collective-permute-start = (bf16[96,2048]{1,0:T(8,128)(2,1)S(1)}, bf16[96,2048]{1,0:T(8,128)(2,1)}, u32[]{:S(2)}, u32[]{:S(2)}) collective-permute-start(bf16[96,2048]{1,0:T(8,128)(2,1)S(1)} %copy-done.11), channel_id=1, source_target_pairs={{8,0},{16,8},{24,16},{9,1},{17,9},{25,17},{10,2},{18,10},{26,18},{... | collective-permute-start | bytes 1179656 | tf_op jit(solution)/shard_map/ppermute | solution.py:10
  139.3 32.8 %copy-start.8 = (bf16[1,2,96,2048]{3,2,1,0:T(8,128)(2,1)S(1)}, bf16[1,2,96,2048]{3,2,1,0:T(8,128)(2,1)}, u32[]{:S(2)}) copy-start(bf16[1,2,96,2048]{3,2,1,0:T(8,128)(2,1)} %param.13) | copy-start | bytes 2359300
  174.8 23.4 %all-to-all-start.2 = ((bf16[8,24,2048]{2,1,0:T(8,128)(2,1)}), bf16[8,24,2048]{2,1,0:T(8,128)(2,1)S(1)}, u32[]{:S(2)}, u32[]{:S(2)}) async-start(bf16[8,24,2048]{2,1,0:T(8,128)(2,1)} %bitcast.244), calls=%async_computation.2 | async-start | bytes 1572864 | tf_op jit(solution)/shard_map/all_to_all | solution.py:47
  178.5 3.3 %copy-start.29 = (bf16[2,1,1,2048,512]{4,3,2,1,0:T(8,128)(2,1)S(1)}, bf16[2,1,1,2048,512]{4,3,2,1,0:T(8,128)(2,1)}, u32[]{:S(2)}) copy-start(bf16[2,1,1,2048,512]{4,3,2,1,0:T(8,128)(2,1)} %param.10) | copy-start | bytes 12582916
  183.7 3.6 %copy-start.17 = (f32[192,512]{1,0:T(8,128)}, f32[192,512]{1,0:T(8,128)S(1)}, u32[]{:S(2)}) copy-start(f32[192,512]{1,0:T(8,128)S(1)} %fusion.14) | copy-start | bytes 1179652
  185.6 28.8 %collective-permute-start.4 = (bf16[192,2048]{1,0:T(8,128)(2,1)}, bf16[192,2048]{1,0:T(8,128)(2,1)}, u32[]{:S(2)}, u32[]{:S(2)}) collective-permute-start(bf16[192,2048]{1,0:T(8,128)(2,1)} %bitcast.59), channel_id=1, source_target_pairs={{0,24},{8,16},{16,8},{24,0},{1,25},{9,17},{17,9},{25,1},{2,26},{10... | collective-permute-start | bytes 2359304 | tf_op jit(solution)/shard_map/ppermute | solution.py:15
  199.0 24.5 %all-to-all-start.7 = ((bf16[8,24,2048]{2,1,0:T(8,128)(2,1)}), bf16[8,24,2048]{2,1,0:T(8,128)(2,1)S(1)}, u32[]{:S(2)}, u32[]{:S(2)}) async-start(bf16[8,24,2048]{2,1,0:T(8,128)(2,1)} %bitcast.248), calls=%async_computation.7 | async-start | bytes 1572864 | tf_op jit(solution)/shard_map/all_to_all | solution.py:75
  208.5 4.0 %copy-start.4 = (bf16[8,24,2048]{2,1,0:T(8,128)(2,1)S(1)}, bf16[8,24,2048]{2,1,0:T(8,128)(2,1)}, u32[]{:S(2)}) copy-start(bf16[8,24,2048]{2,1,0:T(8,128)(2,1)} %copy-done.3) | copy-start | bytes 2359300
  208.5 4.0 %copy-start.16 = (f32[192,512]{1,0:T(8,128)S(1)}, f32[192,512]{1,0:T(8,128)}, u32[]{:S(2)}) copy-start(f32[192,512]{1,0:T(8,128)} %fusion.17) | copy-start | bytes 1179652
  223.5 21.0 %all-to-all-start.3 = ((bf16[8,24,2048]{2,1,0:T(8,128)(2,1)}), bf16[8,24,2048]{2,1,0:T(8,128)(2,1)S(1)}, u32[]{:S(2)}, u32[]{:S(2)}) async-start(bf16[8,24,2048]{2,1,0:T(8,128)(2,1)} %bitcast.29), calls=%async_computation.3 | async-start | bytes 1572864 | tf_op jit(solution)/shard_map/all_to_all | solution.py:75
  227.1 2.4 copy-start
  234.4 4.0 %copy-start.22 = (f32[192,512]{1,0:T(8,128)S(1)}, f32[192,512]{1,0:T(8,128)}, u32[]{:S(2)}) copy-start(f32[192,512]{1,0:T(8,128)} %fusion.12) | copy-start | bytes 1179652
  (14 other events, 20.7 us)

commit v2 on v1

--- a/solution.py
+++ b/solution.py
@@ -68,10 +68,11 @@
     return hidden, pair_grad
 
 
-def combine(gradient, pair_grad, weight_in, slot_ids):
+def combine(gradient, pair_grad, weight_in, slot_ids, held):
     experts_rows, model_width = pair_grad.shape[0], gradient.shape[1]
     experts = lax.axis_size("expert")
     input_grad = right_product(pair_grad, weight_in).astype(jnp.bfloat16)
+    input_grad, held = lax.optimization_barrier((input_grad, held))
     returned = lax.all_to_all(
         input_grad.reshape(experts, experts_rows // experts, model_width),
         "expert",
@@ -80,7 +81,8 @@
         tiled=True,
     )
     back_rows = jnp.take(returned.reshape(-1, model_width), slot_ids, axis=0)
-    return (gradient.astype(jnp.float32) + back_rows.astype(jnp.float32)).astype(jnp.bfloat16)
+    updated = (gradient.astype(jnp.float32) + back_rows.astype(jnp.float32)).astype(jnp.bfloat16)
+    return updated, held
 
 
 def weight_terms(saved_rows, slope_rows, hidden, pair_grad):
@@ -112,13 +114,18 @@
             hidden, pair_grad = expert_grads(
                 slope_rows, saved_rows, w_in[way_id, 0, 0], w_out[way_id, 0, 0]
             )
-            finished[way_id] = combine(current[way_id], pair_grad, w_in[way_id, 0, 0], slot_ids)
             if way_id == 0:
+                finished[0], saved_mirror = combine(
+                    current[0], pair_grad, w_in[0, 0, 0], slot_ids, saved_mirror
+                )
                 part_in, part_out = weight_terms(saved_rows, slope_rows, hidden, pair_grad)
                 own_in = own_in + part_in
                 own_out = own_out + part_out
             else:
                 slope_mirror = mirrored(slope_rows, "section")
+                finished[1], slope_mirror = combine(
+                    current[1], pair_grad, w_in[1, 0, 0], slot_ids, slope_mirror
+                )
                 hidden_m, pair_grad_m = expert_grads(
                     slope_mirror, saved_mirror[tick_id], w_in[0, 0, 0], w_out[0, 0, 0]
                 )

time: 249 us -> 226 us (0.908)
  waiting for transfers between devices: 113 us -> 89.4 us
  starting transfers between devices: 45.4 us -> 48.9 us
  matrix products: 54.6 us -> 51.5 us
    ppermute x3, waiting for transfers between devices: 0.01 us -> 36.3 us  [mirrored(): return lax.ppermute(block, axis, [(i, count - 1 - i) for i in range(count)])]
    ppermute x2, waiting for transfers between devices: 36.7 us -> 5.58 us  [passed_along(): return lax.ppermute(block, axis, route)]
    all_to_all x4, waiting for transfers between devices: 37.3 us -> 21.1 us  [combine(): lax.all_to_all(input_grad.reshape(experts, experts_rows // experts, model...]
    all_to_all x4, waiting for transfers between devices: 39.1 us -> 26.4 us  [dispatch(): lax.all_to_all(outgoing.reshape(experts, capacity, model_width), 'expert'...]
    dot_general x10, matrix products: 19.5 us -> 15.7 us  [right_product(): lax.dot_general(left, right, (((1,), (1,)), ((), ())), preferred_element_...]
    all_to_all x4, starting transfers between devices: 16.9 us -> 19.5 us  [combine(): lax.all_to_all(input_grad.reshape(experts, experts_rows // experts, model...]
    unnamed x67 -> x69, local copies, waits for them, and re-layouts: 6.9 us -> 6.39 us
  transfers between devices with their start and end apart: 13 -> 13, of which waited for: 8 -> 11; matrix products, arithmetic and copies ran while one was open for 29% -> 30% of each run, Pallas kernels for 0% -> 0%
where the time goes in v2:
time: 226 us; the launch traced here: 223 us
  waiting for transfers between devices  89.4 us (40%)
  matrix products  51.5 us (23%)
  starting transfers between devices  48.9 us (22%)
  other arithmetic  17.9 us (8%)
  local copies, waits for them, and re-layouts  14.6 us (6%)
    ppermute x3, waiting for transfers between devices, mirrored(): return lax.ppermute(block, axis, [(i, count - 1 - i) for i in range(count)])  36.3 us
    all_to_all x4, waiting for transfers between devices, dispatch(): lax.all_to_all(outgoing.reshape(experts, capacity, model_width), 'expert'...  26.4 us
    dot_general x8, matrix products, left_product(): lax.dot_general(left, right, (((0,), (0,)), ((), ())), preferred_element_...  21.8 us
    all_to_all x4, waiting for transfers between devices, combine(): lax.all_to_all(input_grad.reshape(experts, experts_rows // experts, model...  21.1 us
    all_to_all x4, starting transfers between devices, combine(): lax.all_to_all(input_grad.reshape(experts, experts_rows // experts, model...  19.5 us
    all_to_all x4, starting transfers between devices, dispatch(): lax.all_to_all(outgoing.reshape(experts, capacity, model_width), 'expert'...  19.3 us
    dot_general x10, matrix products, right_product(): lax.dot_general(left, right, (((1,), (1,)), ((), ())), preferred_element_...  15.7 us
    dot_general x6, matrix products, expert_grads(): gate_up = jnp.dot(saved_rows, weight_in, preferred_element_type=jnp.float32)  13.9 us
  transfers between devices with their start and end apart: 13, of which 11 were waited for; matrix products, arithmetic and copies ran while one was open for 30% of the time, Pallas kernels for 0%

profile of v2, /device:TPU:1, one launch (start us, length us, event | category | flops | bytes accessed | tf_op | source)
XLA Modules:
  0.0 223.3 jit_solution(6463834727153803462)
XLA Ops:
  5.6 2.6 %scatter_custom_fusion = bf16[192,2048]{1,0:T(8,128)(2,1)} fusion(s32[96]{0:T(128)S(1)} %get-tuple-element.60, f32[96]{0:T(128)S(1)} %get-tuple-element.56, bf16[]{:T(256)} %constant.7.clone.1, bf16[2,1,96,2048]{3,2,1,0:T(8,128)(2,1)} %param.12), kind=kCustom, calls=%fused_computation.108 | custom fusion | flops 589824 | bytes 1180672 | tf_op jit(solution)/shard_map/scatter | solution.py:46
  8.3 6.5 %all-to-all-start = ((bf16[8,24,2048]{2,1,0:T(8,128)(2,1)}), bf16[8,24,2048]{2,1,0:T(8,128)(2,1)S(1)}, u32[]{:S(2)}, u32[]{:S(2)}) async-start(bf16[8,24,2048]{2,1,0:T(8,128)(2,1)} %bitcast.11), calls=%async_computation | async-start | bytes 1572864 | tf_op jit(solution)/shard_map/all_to_all | solution.py:47
  14.8 2.7 %slice_bitcast_fusion = bf16[2,192,2048]{2,1,0:T(8,128)(2,1)} fusion(bf16[2,2,1,1,192,2048]{5,4,3,2,1,0:T(8,128)(2,1)} %param.14), kind=kLoop, calls=%fused_computation.39 | loop fusion | bytes 3145728 | tf_op jit(solution)/shard_map/squeeze | solution.py:98
  21.8 12.1 %all-to-all-done = bf16[8,24,2048]{2,1,0:T(8,128)(2,1)S(1)} async-done(((bf16[8,24,2048]{2,1,0:T(8,128)(2,1)}), bf16[8,24,2048]{2,1,0:T(8,128)(2,1)S(1)}, u32[]{:S(2)}, u32[]{:S(2)}) %all-to-all-start) | async-done | bytes 786464 | tf_op jit(solution)/shard_map/all_to_all | solution.py:47
  33.9 4.8 %all-to-all-start.4 = ((bf16[8,24,2048]{2,1,0:T(8,128)(2,1)}), bf16[8,24,2048]{2,1,0:T(8,128)(2,1)S(1)}, u32[]{:S(2)}, u32[]{:S(2)}) async-start(bf16[8,24,2048]{2,1,0:T(8,128)(2,1)} %bitcast.44), calls=%async_computation.4 | async-start | bytes 1572864 | tf_op jit(solution)/shard_map/all_to_all | solution.py:47
  38.7 2.5 %fusion.21 = f32[192,512]{1,0:T(8,128)S(1)} fusion(bf16[2,1,1,2048,512]{4,3,2,1,0:T(8,128)(2,1)} %param.10, bf16[2,2,1,1,192,2048]{5,4,3,2,1,0:T(8,128)(2,1)} %param.14), kind=kOutput, calls=%fused_computation.37 | convolution fusion | flops 402653184 | bytes 3276800 | tf_op jit(solution)/shard_map/dot_general | solution.py:59
  44.9 10.1 %collective-permute-done = bf16[2,192,2048]{2,1,0:T(8,128)(2,1)} collective-permute-done((bf16[2,192,2048]{2,1,0:T(8,128)(2,1)}, bf16[2,192,2048]{2,1,0:T(8,128)(2,1)}, u32[]{:S(2)}, u32[]{:S(2)}) %collective-permute-start) | collective-permute-done | bytes 1572896 | tf_op jit(solution)/shard_map/ppermute | solution.py:15
  55.0 3.0 %all-to-all-done.4 = bf16[8,24,2048]{2,1,0:T(8,128)(2,1)S(1)} async-done(((bf16[8,24,2048]{2,1,0:T(8,128)(2,1)}), bf16[8,24,2048]{2,1,0:T(8,128)(2,1)S(1)}, u32[]{:S(2)}, u32[]{:S(2)}) %all-to-all-start.4) | async-done | bytes 786464 | tf_op jit(solution)/shard_map/all_to_all | solution.py:47
  58.0 4.6 %all-to-all-start.1 = ((bf16[8,24,2048]{2,1,0:T(8,128)(2,1)}), bf16[8,24,2048]{2,1,0:T(8,128)(2,1)S(1)}, u32[]{:S(2)}, u32[]{:S(2)}) async-start(bf16[8,24,2048]{2,1,0:T(8,128)(2,1)} %bitcast.17), calls=%async_computation.1 | async-start | bytes 1572864 | tf_op jit(solution)/shard_map/all_to_all | solution.py:76
  69.4 13.5 %collective-permute-done.2 = bf16[192,2048]{1,0:T(8,128)(2,1)S(1)} collective-permute-done((bf16[192,2048]{1,0:T(8,128)(2,1)S(1)}, bf16[192,2048]{1,0:T(8,128)(2,1)S(1)}, u32[]{:S(2)}, u32[]{:S(2)}) %collective-permute-start.2) | collective-permute-done | bytes 786464 | tf_op jit(solution)/shard_map/ppermute | solution.py:15
  83.8 5.6 %all-to-all-start.5 = ((bf16[8,24,2048]{2,1,0:T(8,128)(2,1)}), bf16[8,24,2048]{2,1,0:T(8,128)(2,1)S(1)}, u32[]{:S(2)}, u32[]{:S(2)}) async-start(bf16[8,24,2048]{2,1,0:T(8,128)(2,1)} %bitcast.255), calls=%async_computation.5 | async-start | bytes 1572864 | tf_op jit(solution)/shard_map/all_to_all | solution.py:76
  90.8 17.9 %all-to-all-done.5 = bf16[8,24,2048]{2,1,0:T(8,128)(2,1)S(1)} async-done(((bf16[8,24,2048]{2,1,0:T(8,128)(2,1)}), bf16[8,24,2048]{2,1,0:T(8,128)(2,1)S(1)}, u32[]{:S(2)}, u32[]{:S(2)}) %all-to-all-start.5) | async-done | bytes 786464 | tf_op jit(solution)/shard_map/all_to_all | solution.py:76
  110.8 3.9 %collective-permute-start.1 = (bf16[96,2048]{1,0:T(8,128)(2,1)}, bf16[96,2048]{1,0:T(8,128)(2,1)S(1)}, u32[]{:S(2)}, u32[]{:S(2)}) collective-permute-start(bf16[96,2048]{1,0:T(8,128)(2,1)} %get-tuple-element.36), channel_id=1, source_target_pairs={{8,0},{16,8},{24,16},{9,1},{17,9},{25,17},{10,2},{18,10},{26,18},{... | collective-permute-start | bytes 1179656 | tf_op jit(solution)/shard_map/ppermute | solution.py:10
  115.3 5.5 %collective-permute-done.1 = bf16[96,2048]{1,0:T(8,128)(2,1)S(1)} collective-permute-done((bf16[96,2048]{1,0:T(8,128)(2,1)}, bf16[96,2048]{1,0:T(8,128)(2,1)S(1)}, u32[]{:S(2)}, u32[]{:S(2)}) %collective-permute-start.1) | collective-permute-done | bytes 393248 | tf_op jit(solution)/shard_map/ppermute | solution.py:10
  120.8 2.7 %scatter_custom_fusion.1 = bf16[192,2048]{1,0:T(8,128)(2,1)} fusion(s32[96]{0:T(128)} %get-tuple-element.61, f32[96]{0:T(128)S(1)} %get-tuple-element.57, bf16[]{:T(256)} %constant.7.clone.1, bf16[96,2048]{1,0:T(8,128)(2,1)S(1)} %collective-permute-done.1, bf16[1,2,96,2048]{3,2,1,0:T(8,128)(2,1)} %param.13, pred[]{:T(512)S(6)} %eq.66), kind=kCustom, calls=%fused_computation.112 | custom fusion | flops 786432 | bytes 1573761 | tf_op jit(solution)/shard_map/scatter | solution.py:46
  123.5 4.2 %all-to-all-start.2 = ((bf16[8,24,2048]{2,1,0:T(8,128)(2,1)}), bf16[8,24,2048]{2,1,0:T(8,128)(2,1)}, u32[]{:S(2)}, u32[]{:S(2)}) async-start(bf16[8,24,2048]{2,1,0:T(8,128)(2,1)} %bitcast.248), calls=%async_computation.2 | async-start | bytes 1572864 | tf_op jit(solution)/shard_map/all_to_all | solution.py:47
  127.7 3.1 %fusion.18 = f32[192,512]{1,0:T(8,128)} fusion(bf16[2,1,1,2048,512]{4,3,2,1,0:T(8,128)(2,1)} %param.10, bf16[2,2,1,1,192,2048]{5,4,3,2,1,0:T(8,128)(2,1)S(1)} %copy-done.2), kind=kOutput, calls=%fused_computation.34 | convolution fusion | flops 402653184 | bytes 3276800 | tf_op jit(solution)/shard_map/dot_general | solution.py:59
  136.2 2.7 %fusion.64 = f32[512,2048]{1,0:T(8,128)} fusion(bf16[2,2,1,1,192,2048]{5,4,3,2,1,0:T(8,128)(2,1)S(1)} %copy-done.2, bf16[192,256]{1,0:T(8,128)(2,1)S(1)} %copy-done.13, bf16[192,256]{1,0:T(8,128)(2,1)S(1)} %copy-done.11), kind=kOutput, calls=%fused_computation.90 | convolution fusion | flops 403046400 | bytes 5177344 | tf_op jit(solution)/shard_map/dot_general | solution.py:29
  139.0 2.8 %scatter_custom_fusion.3 = bf16[192,2048]{1,0:T(8,128)(2,1)} fusion(s32[96]{0:T(128)} %get-tuple-element.62, f32[96]{0:T(128)S(1)} %get-tuple-element.58, bf16[]{:T(256)} %constant.7.clone.1, bf16[96,2048]{1,0:T(8,128)(2,1)} %collective-permute-done.3, bf16[1,2,96,2048]{3,2,1,0:T(8,128)(2,1)} %param.13, pred[]{:T(512)S(6)} %eq.75), kind=kCustom, calls=%fused_computation.110 | custom fusion | flops 786432 | bytes 1573761 | tf_op jit(solution)/shard_map/scatter | solution.py:46
  141.8 2.7 %all-to-all-done.2 = bf16[8,24,2048]{2,1,0:T(8,128)(2,1)} async-done(((bf16[8,24,2048]{2,1,0:T(8,128)(2,1)}), bf16[8,24,2048]{2,1,0:T(8,128)(2,1)}, u32[]{:S(2)}, u32[]{:S(2)}) %all-to-all-start.2) | async-done | bytes 786464 | tf_op jit(solution)/shard_map/all_to_all | solution.py:47
  144.5 3.7 %all-to-all-start.6 = ((bf16[8,24,2048]{2,1,0:T(8,128)(2,1)}), bf16[8,24,2048]{2,1,0:T(8,128)(2,1)S(1)}, u32[]{:S(2)}, u32[]{:S(2)}) async-start(bf16[8,24,2048]{2,1,0:T(8,128)(2,1)} %bitcast.59), calls=%async_computation.6 | async-start | bytes 1572864 | tf_op jit(solution)/shard_map/all_to_all | solution.py:47
  151.7 4.1 %fusion.57 = f32[2048,512]{0,1:T(8,128)} fusion(bf16[2,192,2048]{2,1,0:T(8,128)(2,1)} %collective-permute-done, bf16[192,256]{1,0:T(8,128)(2,1)S(1)} %get-tuple-element.41, bf16[192,256]{1,0:T(8,128)(2,1)S(1)} %get-tuple-element.40), kind=kOutput, calls=%fused_computation.83 | convolution fusion | flops 403046400 | bytes 5177344 | tf_op jit(solution)/shard_map/dot_general | solution.py:29
  159.2 8.6 %all-to-all-done.6 = bf16[8,24,2048]{2,1,0:T(8,128)(2,1)S(1)} async-done(((bf16[8,24,2048]{2,1,0:T(8,128)(2,1)}), bf16[8,24,2048]{2,1,0:T(8,128)(2,1)S(1)}, u32[]{:S(2)}, u32[]{:S(2)}) %all-to-all-start.6) | async-done | bytes 786464 | tf_op jit(solution)/shard_map/all_to_all | solution.py:47
  167.8 4.2 %all-to-all-start.3 = ((bf16[8,24,2048]{2,1,0:T(8,128)(2,1)}), bf16[8,24,2048]{2,1,0:T(8,128)(2,1)S(1)}, u32[]{:S(2)}, u32[]{:S(2)}) async-start(bf16[8,24,2048]{2,1,0:T(8,128)(2,1)} %bitcast.30), calls=%async_computation.3 | async-start | bytes 1572864 | tf_op jit(solution)/shard_map/all_to_all | solution.py:76
  173.9 3.5 %convolution_convert_fusion = bf16[192,2048]{1,0:T(8,128)(2,1)} fusion(bf16[2,1,1,2048,512]{4,3,2,1,0:T(8,128)(2,1)} %param.10, bf16[192,256]{1,0:T(8,128)(2,1)S(1)} %get-tuple-element.47, bf16[192,256]{1,0:T(8,128)(2,1)S(1)} %get-tuple-element.46), kind=kOutput, calls=%fused_computation.18 | convolution fusion | flops 403439616 | bytes 3080192 | tf_op jit(solution)/shard_map/dot_general | solution.py:35
  179.3 12.6 %collective-permute-done.4 = bf16[192,2048]{1,0:T(8,128)(2,1)S(1)} collective-permute-done((bf16[192,2048]{1,0:T(8,128)(2,1)S(1)}, bf16[192,2048]{1,0:T(8,128)(2,1)S(1)}, u32[]{:S(2)}, u32[]{:S(2)}) %collective-permute-start.4) | collective-permute-done | bytes 786464 | tf_op jit(solution)/shard_map/ppermute | solution.py:15
  192.5 3.3 %add_convert_fusion = bf16[2048,512]{0,1:T(8,128)(2,1)} fusion(f32[2048,512]{0,1:T(8,128)S(1)} %copy-done, bf16[2,192,2048]{2,1,0:T(8,128)(2,1)} %collective-permute-done, bf16[192,256]{1,0:T(8,128)(2,1)S(1)} %get-tuple-element.39, bf16[192,256]{1,0:T(8,128)(2,1)S(1)} %get-tuple-element.38), kind=kOutput, calls=%fused_computation.10 | convolution fusion | flops 405143552 | bytes 7274496 | tf_op jit(solution)/shard_map/dot_general | solution.py:29
  195.7 5.2 %all-to-all-start.7 = ((bf16[8,24,2048]{2,1,0:T(8,128)(2,1)}), bf16[8,24,2048]{2,1,0:T(8,128)(2,1)S(1)}, u32[]{:S(2)}, u32[]{:S(2)}) async-start(bf16[8,24,2048]{2,1,0:T(8,128)(2,1)} %bitcast.62), calls=%async_computation.7 | async-start | bytes 1572864 | tf_op jit(solution)/shard_map/all_to_all | solution.py:76
  200.9 5.3 %fusion.1 = bf16[1,1,2048,512]{2,3,1,0:T(8,128)(2,1)} fusion(bf16[2048,512]{0,1:T(8,128)(2,1)} %add_convert_fusion, f32[512,2048]{1,0:T(8,128)} %fusion.64, bf16[2,2,1,1,192,2048]{5,4,3,2,1,0:T(8,128)(2,1)} %param.14, bf16[192,256]{1,0:T(8,128)(2,1)} %copy-done.15, bf16[192,256]{1,0:T(8,128)(2,1)} %copy-done.14), kind=kOutput, calls=%fused_computation.11 | convolution fusion | flops 407240704 | bytes 9371648 | tf_op jit(solution)/shard_map/dot_general | solution.py:29
  206.2 3.9 %copy.18 = bf16[1,1,2048,512]{3,2,1,0:T(8,128)(2,1)} copy(bf16[1,1,2048,512]{2,3,1,0:T(8,128)(2,1)} %fusion.1) | data formatting | bytes 4194304
  213.3 2.6 %fusion.6 = bf16[1,1,256,2048]{3,2,1,0:T(8,128)(2,1)} fusion(f32[256,2048]{1,0:T(8,128)S(1)} %fusion.5, f32[256,2048]{1,0:T(8,128)S(1)} %copy-done.1, bf16[192,2048]{1,0:T(8,128)(2,1)} %bitcast.28, f32[192,512]{1,0:T(8,128)S(1)} %copy-done.17), kind=kOutput, calls=%fused_computation.22 | convolution fusion | flops 203194368 | bytes 6422528 | tf_op jit(solution)/shard_map/dot_general | solution.py:29
  216.8 3.2 %all-to-all-done.7 = bf16[8,24,2048]{2,1,0:T(8,128)(2,1)S(1)} async-done(((bf16[8,24,2048]{2,1,0:T(8,128)(2,1)}), bf16[8,24,2048]{2,1,0:T(8,128)(2,1)S(1)}, u32[]{:S(2)}, u32[]{:S(2)}) %all-to-all-start.7) | async-done | bytes 786464 | tf_op jit(solution)/shard_map/all_to_all | solution.py:76
  (115 shorter events, 48.4 us)
Async XLA Ops:
  8.3 11.3 %copy-start.5 = (bf16[2,1,96,2048]{3,2,1,0:T(8,128)(2,1)S(1)}, bf16[2,1,96,2048]{3,2,1,0:T(8,128)(2,1)}, u32[]{:S(2)}) copy-start(bf16[2,1,96,2048]{3,2,1,0:T(8,128)(2,1)} %param.12) | copy-start | bytes 2359300
  8.3 25.6 %all-to-all-start = ((bf16[8,24,2048]{2,1,0:T(8,128)(2,1)}), bf16[8,24,2048]{2,1,0:T(8,128)(2,1)S(1)}, u32[]{:S(2)}, u32[]{:S(2)}) async-start(bf16[8,24,2048]{2,1,0:T(8,128)(2,1)} %bitcast.11), calls=%async_computation | async-start | bytes 1572864 | tf_op jit(solution)/shard_map/all_to_all | solution.py:47
  17.5 37.5 %collective-permute-start = (bf16[2,192,2048]{2,1,0:T(8,128)(2,1)}, bf16[2,192,2048]{2,1,0:T(8,128)(2,1)}, u32[]{:S(2)}, u32[]{:S(2)}) collective-permute-start(bf16[2,192,2048]{2,1,0:T(8,128)(2,1)} %slice_bitcast_fusion), channel_id=1, source_target_pairs={{0,24},{8,16},{16,8},{24,0},{1,25},{9,17},{17,9},{25,1},{2,26},{10... | collective-permute-start | bytes 4718600 | tf_op jit(solution)/shard_map/ppermute | solution.py:15
  33.9 7.4 %copy-start.3 = (bf16[8,24,2048]{2,1,0:T(8,128)(2,1)}, bf16[8,24,2048]{2,1,0:T(8,128)(2,1)S(1)}, u32[]{:S(2)}) copy-start(bf16[8,24,2048]{2,1,0:T(8,128)(2,1)S(1)} %all-to-all-done) | copy-start | bytes 2359300
  33.9 24.2 %all-to-all-start.4 = ((bf16[8,24,2048]{2,1,0:T(8,128)(2,1)}), bf16[8,24,2048]{2,1,0:T(8,128)(2,1)S(1)}, u32[]{:S(2)}, u32[]{:S(2)}) async-start(bf16[8,24,2048]{2,1,0:T(8,128)(2,1)} %bitcast.44), calls=%async_computation.4 | async-start | bytes 1572864 | tf_op jit(solution)/shard_map/all_to_all | solution.py:47
  38.7 4.5 %copy-start.26 = (bf16[2,1,1,2048,512]{4,3,2,1,0:T(8,128)(2,1)S(1)}, bf16[2,1,1,2048,512]{4,3,2,1,0:T(8,128)(2,1)}, u32[]{:S(2)}) copy-start(bf16[2,1,1,2048,512]{4,3,2,1,0:T(8,128)(2,1)} %param.10) | copy-start | bytes 12582916
  43.2 14.9 %copy-start.10 = (bf16[192,256]{1,0:T(8,128)(2,1)}, bf16[192,256]{1,0:T(8,128)(2,1)S(1)}, u32[]{:S(2)}) copy-start(bf16[192,256]{1,0:T(8,128)(2,1)S(1)} %get-tuple-element.44) | copy-start | bytes 294916
  43.2 14.9 %copy-start.12 = (bf16[192,256]{1,0:T(8,128)(2,1)}, bf16[192,256]{1,0:T(8,128)(2,1)S(1)}, u32[]{:S(2)}) copy-start(bf16[192,256]{1,0:T(8,128)(2,1)S(1)} %get-tuple-element.45) | copy-start | bytes 294916
  58.0 24.9 %all-to-all-start.1 = ((bf16[8,24,2048]{2,1,0:T(8,128)(2,1)}), bf16[8,24,2048]{2,1,0:T(8,128)(2,1)S(1)}, u32[]{:S(2)}, u32[]{:S(2)}) async-start(bf16[8,24,2048]{2,1,0:T(8,128)(2,1)} %bitcast.17), calls=%async_computation.1 | async-start | bytes 1572864 | tf_op jit(solution)/shard_map/all_to_all | solution.py:76
  62.6 4.5 %copy-start.31 = (bf16[2,1,1,256,2048]{4,3,2,1,0:T(8,128)(2,1)S(1)}, bf16[2,1,1,256,2048]{4,3,2,1,0:T(8,128)(2,1)}, u32[]{:S(2)}) copy-start(bf16[2,1,1,256,2048]{4,3,2,1,0:T(8,128)(2,1)} %param.11) | copy-start | bytes 6291460
  62.7 20.3 %collective-permute-start.2 = (bf16[192,2048]{1,0:T(8,128)(2,1)S(1)}, bf16[192,2048]{1,0:T(8,128)(2,1)S(1)}, u32[]{:S(2)}, u32[]{:S(2)}) collective-permute-start(bf16[192,2048]{1,0:T(8,128)(2,1)S(1)} %bitcast.253), channel_id=1, source_target_pairs={{0,24},{8,16},{16,8},{24,0},{1,25},{9,17},{17,9},{25,1},{2,26},{10... | collective-permute-start | bytes 2359304 | tf_op jit(solution)/shard_map/ppermute | solution.py:15
  67.7 21.7 %copy-start.23 = (s32[2,2,1,96]{3,2,1,0:T(1,128)S(1)}, s32[2,2,1,96]{3,2,1,0:T(1,128)}, u32[]{:S(2)}) copy-start(s32[2,2,1,96]{3,2,1,0:T(1,128)} %param.16) | copy-start | bytes 4612
  83.8 24.9 %all-to-all-start.5 = ((bf16[8,24,2048]{2,1,0:T(8,128)(2,1)}), bf16[8,24,2048]{2,1,0:T(8,128)(2,1)S(1)}, u32[]{:S(2)}, u32[]{:S(2)}) async-start(bf16[8,24,2048]{2,1,0:T(8,128)(2,1)} %bitcast.255), calls=%async_computation.5 | async-start | bytes 1572864 | tf_op jit(solution)/shard_map/all_to_all | solution.py:76
  110.8 16.9 %copy-start.2 = (bf16[2,2,1,1,192,2048]{5,4,3,2,1,0:T(8,128)(2,1)S(1)}, bf16[2,2,1,1,192,2048]{5,4,3,2,1,0:T(8,128)(2,1)}, u32[]{:S(2)}) copy-start(bf16[2,2,1,1,192,2048]{5,4,3,2,1,0:T(8,128)(2,1)} %param.14) | copy-start | bytes 9437188
  110.8 10.1 %collective-permute-start.1 = (bf16[96,2048]{1,0:T(8,128)(2,1)}, bf16[96,2048]{1,0:T(8,128)(2,1)S(1)}, u32[]{:S(2)}, u32[]{:S(2)}) collective-permute-start(bf16[96,2048]{1,0:T(8,128)(2,1)} %get-tuple-element.36), channel_id=1, source_target_pairs={{8,0},{16,8},{24,16},{9,1},{17,9},{25,17},{10,2},{18,10},{26,18},{... | collective-permute-start | bytes 1179656 | tf_op jit(solution)/shard_map/ppermute | solution.py:10
  123.5 21.0 %all-to-all-start.2 = ((bf16[8,24,2048]{2,1,0:T(8,128)(2,1)}), bf16[8,24,2048]{2,1,0:T(8,128)(2,1)}, u32[]{:S(2)}, u32[]{:S(2)}) async-start(bf16[8,24,2048]{2,1,0:T(8,128)(2,1)} %bitcast.248), calls=%async_computation.2 | async-start | bytes 1572864 | tf_op jit(solution)/shard_map/all_to_all | solution.py:47
  132.2 6.8 %collective-permute-start.3 = (bf16[96,2048]{1,0:T(8,128)(2,1)S(1)}, bf16[96,2048]{1,0:T(8,128)(2,1)}, u32[]{:S(2)}, u32[]{:S(2)}) collective-permute-start(bf16[96,2048]{1,0:T(8,128)(2,1)S(1)} %copy-done.9), channel_id=1, source_target_pairs={{0,8},{8,16},{16,24},{1,9},{9,17},{17,25},{2,10},{10,18},{18,26},{... | collective-permute-start | bytes 1179656 | tf_op jit(solution)/shard_map/ppermute | solution.py:10
  144.5 23.3 %all-to-all-start.6 = ((bf16[8,24,2048]{2,1,0:T(8,128)(2,1)}), bf16[8,24,2048]{2,1,0:T(8,128)(2,1)S(1)}, u32[]{:S(2)}, u32[]{:S(2)}) async-start(bf16[8,24,2048]{2,1,0:T(8,128)(2,1)} %bitcast.59), calls=%async_computation.6 | async-start | bytes 1572864 | tf_op jit(solution)/shard_map/all_to_all | solution.py:47
  151.7 4.1 %copy-start.16 = (f32[192,512]{1,0:T(8,128)S(1)}, f32[192,512]{1,0:T(8,128)}, u32[]{:S(2)}) copy-start(f32[192,512]{1,0:T(8,128)} %fusion.18) | copy-start | bytes 1179652
  151.7 5.8 %copy-start.29 = (bf16[2,1,1,2048,512]{4,3,2,1,0:T(8,128)(2,1)S(1)}, bf16[2,1,1,2048,512]{4,3,2,1,0:T(8,128)(2,1)}, u32[]{:S(2)}) copy-start(bf16[2,1,1,2048,512]{4,3,2,1,0:T(8,128)(2,1)} %param.10) | copy-start | bytes 12582916
  157.4 10.3 %copy-start.14 = (bf16[192,256]{1,0:T(8,128)(2,1)}, bf16[192,256]{1,0:T(8,128)(2,1)S(1)}, u32[]{:S(2)}) copy-start(bf16[192,256]{1,0:T(8,128)(2,1)S(1)} %get-tuple-element.42) | copy-start | bytes 294916
  157.4 10.3 %copy-start.15 = (bf16[192,256]{1,0:T(8,128)(2,1)}, bf16[192,256]{1,0:T(8,128)(2,1)S(1)}, u32[]{:S(2)}) copy-start(bf16[192,256]{1,0:T(8,128)(2,1)S(1)} %get-tuple-element.43) | copy-start | bytes 294916
  167.8 28.0 %all-to-all-start.3 = ((bf16[8,24,2048]{2,1,0:T(8,128)(2,1)}), bf16[8,24,2048]{2,1,0:T(8,128)(2,1)S(1)}, u32[]{:S(2)}, u32[]{:S(2)}) async-start(bf16[8,24,2048]{2,1,0:T(8,128)(2,1)} %bitcast.30), calls=%async_computation.3 | async-start | bytes 1572864 | tf_op jit(solution)/shard_map/all_to_all | solution.py:76
  171.9 20.0 %collective-permute-start.4 = (bf16[192,2048]{1,0:T(8,128)(2,1)S(1)}, bf16[192,2048]{1,0:T(8,128)(2,1)S(1)}, u32[]{:S(2)}, u32[]{:S(2)}) collective-permute-start(bf16[192,2048]{1,0:T(8,128)(2,1)S(1)} %bitcast.251), channel_id=1, source_target_pairs={{0,24},{8,16},{16,8},{24,0},{1,25},{9,17},{17,9},{25,1},{2,26},{10... | collective-permute-start | bytes 2359304 | tf_op jit(solution)/shard_map/ppermute | solution.py:15
  171.9 5.5 %copy-start.30 = (bf16[2,1,1,2048,512]{4,3,2,1,0:T(8,128)(2,1)S(1)}, bf16[2,1,1,2048,512]{4,3,2,1,0:T(8,128)(2,1)}, u32[]{:S(2)}) copy-start(bf16[2,1,1,2048,512]{4,3,2,1,0:T(8,128)(2,1)} %param.10) | copy-start | bytes 12582916
  173.9 18.0 %copy-start.33 = (bf16[2,1,1,256,2048]{4,3,2,1,0:T(8,128)(2,1)S(1)}, bf16[2,1,1,256,2048]{4,3,2,1,0:T(8,128)(2,1)}, u32[]{:S(2)}) copy-start(bf16[2,1,1,256,2048]{4,3,2,1,0:T(8,128)(2,1)} %param.11) | copy-start | bytes 6291460
  177.4 15.1 %copy-start = (f32[2048,512]{0,1:T(8,128)S(1)}, f32[2048,512]{0,1:T(8,128)}, u32[]{:S(2)}) copy-start(f32[2048,512]{0,1:T(8,128)} %fusion.57) | copy-start | bytes 12582916
  179.3 12.7 %copy-start.22 = (f32[192,512]{1,0:T(8,128)}, f32[192,512]{1,0:T(8,128)S(1)}, u32[]{:S(2)}) copy-start(f32[192,512]{1,0:T(8,128)S(1)} %fusion.13) | copy-start | bytes 1179652
  195.7 24.3 %all-to-all-start.7 = ((bf16[8,24,2048]{2,1,0:T(8,128)(2,1)}), bf16[8,24,2048]{2,1,0:T(8,128)(2,1)S(1)}, u32[]{:S(2)}, u32[]{:S(2)}) async-start(bf16[8,24,2048]{2,1,0:T(8,128)(2,1)} %bitcast.62), calls=%async_computation.7 | async-start | bytes 1572864 | tf_op jit(solution)/shard_map/all_to_all | solution.py:76
  216.8 4.1 %copy-start.6 = (bf16[1,2,96,2048]{3,2,1,0:T(8,128)(2,1)S(1)}, bf16[1,2,96,2048]{3,2,1,0:T(8,128)(2,1)}, u32[]{:S(2)}) copy-start(bf16[1,2,96,2048]{3,2,1,0:T(8,128)(2,1)} %param.13) | copy-start | bytes 2359300
  216.8 4.1 %copy-start.24 = (pred[96]{0:T(512)(128)(4,1)S(1)}, pred[96]{0:T(512)(128)(4,1)}, u32[]{:S(2)}) copy-start(pred[96]{0:T(512)(128)(4,1)} %get-tuple-element.26) | copy-start | bytes 292
  216.8 4.1 %copy-start.25 = (pred[96]{0:T(512)(128)(4,1)S(1)}, pred[96]{0:T(512)(128)(4,1)}, u32[]{:S(2)}) copy-start(pred[96]{0:T(512)(128)(4,1)} %get-tuple-element.50) | copy-start | bytes 292
  (15 other events, 37.8 us)

commit v3 on v1

--- a/solution.py
+++ b/solution.py
@@ -37,21 +37,20 @@
     )
 
 
-def dispatch(gradient, prob_rows, route_ids, count_table):
+def outgoing_rows(gradient, prob_rows, route_ids, count_table):
     tokens, model_width = gradient.shape
     experts = count_table.shape[0]
     capacity = 2 * tokens // experts
     slot_ids = slot_index(route_ids, count_table, capacity)
     scaled = (prob_rows[:, None] * gradient.astype(jnp.float32)).astype(jnp.bfloat16)
     outgoing = jnp.zeros((experts * capacity, model_width), jnp.bfloat16).at[slot_ids].set(scaled)
-    arrived = lax.all_to_all(
-        outgoing.reshape(experts, capacity, model_width),
-        "expert",
-        split_axis=0,
-        concat_axis=0,
-        tiled=True,
-    )
-    return arrived.reshape(-1, model_width), slot_ids
+    return outgoing.reshape(experts, 1, capacity, model_width), slot_ids
+
+
+def exchange(blocks):
+    experts, ways, capacity, model_width = blocks.shape
+    arrived = lax.all_to_all(blocks, "expert", split_axis=0, concat_axis=0, tiled=True)
+    return [arrived[:, way_id].reshape(experts * capacity, model_width) for way_id in range(ways)]
 
 
 def expert_grads(slope_rows, saved_rows, weight_in, weight_out):
@@ -68,21 +67,6 @@
     return hidden, pair_grad
 
 
-def combine(gradient, pair_grad, weight_in, slot_ids):
-    experts_rows, model_width = pair_grad.shape[0], gradient.shape[1]
-    experts = lax.axis_size("expert")
-    input_grad = right_product(pair_grad, weight_in).astype(jnp.bfloat16)
-    returned = lax.all_to_all(
-        input_grad.reshape(experts, experts_rows // experts, model_width),
-        "expert",
-        split_axis=0,
-        concat_axis=0,
-        tiled=True,
-    )
-    back_rows = jnp.take(returned.reshape(-1, model_width), slot_ids, axis=0)
-    return (gradient.astype(jnp.float32) + back_rows.astype(jnp.float32)).astype(jnp.bfloat16)
-
-
 def weight_terms(saved_rows, slope_rows, hidden, pair_grad):
     return left_product(saved_rows, pair_grad), left_product(hidden, slope_rows)
 
@@ -90,43 +74,64 @@
 def on_device(w_in, w_out, grads, fresh, saved, probs, routes, counts):
     sections = lax.axis_size("section")
     section_id = lax.axis_index("section")
+    experts = lax.axis_size("expert")
     model_width = grads.shape[-1]
     hidden_width = w_out.shape[-2]
     ticks = saved.shape[0]
     saved_mirror = mirrored(saved[:, 1, 0, 0], "section")
     current = [grads[0, 0], grads[1, 0]]
-    finished = [grads[0, 0], grads[1, 0]]
     zeros_in = jnp.zeros((model_width, 2 * hidden_width), jnp.float32)
     zeros_out = jnp.zeros((hidden_width, model_width), jnp.float32)
     own_in, own_out = zeros_in, zeros_out
     mirror_in, mirror_out = zeros_in, zeros_out
+    slope_mirror = None
     for tick_id in range(ticks):
-        for way_id in range(2):
-            saved_rows = saved[tick_id, way_id, 0, 0]
-            slope_rows, slot_ids = dispatch(
+        sent = [
+            outgoing_rows(
                 current[way_id],
                 probs[tick_id, way_id, 0],
                 routes[tick_id, way_id, 0],
                 counts[tick_id, way_id, 0, 0],
             )
+            for way_id in range(2)
+        ]
+        blocks = jnp.concatenate([sent[0][0], sent[1][0]], axis=1)
+        if slope_mirror is not None:
+            blocks, slope_mirror = lax.optimization_barrier((blocks, slope_mirror))
+            hidden_m, pair_grad_m = expert_grads(
+                slope_mirror, saved_mirror[tick_id - 1], w_in[0, 0, 0], w_out[0, 0, 0]
+            )
+            part_in, part_out = weight_terms(
+                saved_mirror[tick_id - 1], slope_mirror, hidden_m, pair_grad_m
+            )
+            mirror_in = mirror_in + part_in
+            mirror_out = mirror_out + part_out
+        slopes = exchange(blocks)
+        input_grads = []
+        for way_id in range(2):
+            saved_rows = saved[tick_id, way_id, 0, 0]
             hidden, pair_grad = expert_grads(
-                slope_rows, saved_rows, w_in[way_id, 0, 0], w_out[way_id, 0, 0]
+                slopes[way_id], saved_rows, w_in[way_id, 0, 0], w_out[way_id, 0, 0]
             )
-            finished[way_id] = combine(current[way_id], pair_grad, w_in[way_id, 0, 0], slot_ids)
+            input_grad = right_product(pair_grad, w_in[way_id, 0, 0]).astype(jnp.bfloat16)
+            input_grads.append(input_grad.reshape(experts, 1, -1, model_width))
             if way_id == 0:
-                part_in, part_out = weight_terms(saved_rows, slope_rows, hidden, pair_grad)
+                part_in, part_out = weight_terms(saved_rows, slopes[0], hidden, pair_grad)
                 own_in = own_in + part_in
                 own_out = own_out + part_out
-            else:
-                slope_mirror = mirrored(slope_rows, "section")
-                hidden_m, pair_grad_m = expert_grads(
-                    slope_mirror, saved_mirror[tick_id], w_in[0, 0, 0], w_out[0, 0, 0]
+        slope_mirror = mirrored(slopes[1], "section")
+        back_blocks = jnp.concatenate(input_grads, axis=1)
+        if tick_id == 0:
+            back_blocks, saved_mirror = lax.optimization_barrier((back_blocks, saved_mirror))
+        returned = exchange(back_blocks)
+        finished = []
+        for way_id in range(2):
+            back_rows = jnp.take(returned[way_id], sent[way_id][1], axis=0)
+            finished.append(
+                (current[way_id].astype(jnp.float32) + back_rows.astype(jnp.float32)).astype(
+                    jnp.bfloat16
                 )
-                part_in, part_out = weight_terms(
-                    saved_mirror[tick_id], slope_mirror, hidden_m, pair_grad_m
-                )
-                mirror_in = mirror_in + part_in
-                mirror_out = mirror_out + part_out
+            )
         if tick_id + 1 < ticks:
             from_above = passed_along(finished[0], "section", -1)
             from_below = passed_along(finished[1], "section", 1)
@@ -134,8 +139,12 @@
                 jnp.where(section_id == sections - 1, fresh[tick_id, 0], from_above),
                 jnp.where(section_id == 0, fresh[tick_id, 1], from_below),
             ]
-    mirror_in = mirror_in.astype(jnp.bfloat16).astype(jnp.float32)
-    mirror_out = mirror_out.astype(jnp.bfloat16).astype(jnp.float32)
+    hidden_m, pair_grad_m = expert_grads(
+        slope_mirror, saved_mirror[ticks - 1], w_in[0, 0, 0], w_out[0, 0, 0]
+    )
+    part_in, part_out = weight_terms(saved_mirror[ticks - 1], slope_mirror, hidden_m, pair_grad_m)
+    mirror_in = (mirror_in + part_in).astype(jnp.bfloat16).astype(jnp.float32)
+    mirror_out = (mirror_out + part_out).astype(jnp.bfloat16).astype(jnp.float32)
     grad_in = (own_in + mirror_in).astype(jnp.bfloat16)
     grad_out = (own_out + mirror_out).astype(jnp.bfloat16)
     return (jnp.stack(finished)[:, None], grad_in[None, None], grad_out[None, None])

time: 249 us -> 215 us (0.86)
  starting transfers between devices: 45.4 us -> 29.7 us
  matrix products: 54.6 us -> 39 us
  waiting for transfers between devices: 113 us -> 102 us
  local copies, waits for them, and re-layouts: 15.9 us -> 23.2 us
    ppermute x2, waiting for transfers between devices: 36.7 us -> 5.52 us  [passed_along(): return lax.ppermute(block, axis, route)]
    all_to_all x8 -> x4, waiting for transfers between devices: 76.4 us -> 94.8 us  [exchange(): lax.all_to_all(blocks, 'expert', split_axis=0, concat_axis=0, tiled=True)]
    all_to_all x8 -> x4, starting transfers between devices: 36.1 us -> 19.2 us  [exchange(): lax.all_to_all(blocks, 'expert', split_axis=0, concat_axis=0, tiled=True)]
    dot_general x10, matrix products: 19.5 us -> 10.1 us  [right_product(): lax.dot_general(left, right, (((1,), (1,)), ((), ())), preferred_element_...]
    dot_general x8, matrix products: 20.3 us -> 14.6 us  [left_product(): lax.dot_general(left, right, (((0,), (0,)), ((), ())), preferred_element_...]
    concatenate x0 -> x4, other arithmetic: none -> 5.26 us  [the longest x2 2.68 us: on_device(): back_blocks = jnp.concatenate(input_grads, axis=1)]
    unnamed x67 -> x83, local copies, waits for them, and re-layouts: 6.9 us -> 9.99 us
    scatter x4, other arithmetic: 10.1 us -> 7.16 us  [outgoing_rows(): jnp.zeros((experts * capacity, model_width), jnp.bfloat16).at[slot_ids]]
  transfers between devices with their start and end apart: 13 -> 9, of which waited for: 8 -> 7; matrix products, arithmetic and copies ran while one was open for 29% -> 26% of each run, Pallas kernels for 0% -> 0%
where the time goes in v3:
time: 215 us; the launch traced here: 214 us
  waiting for transfers between devices  102 us (47%)
  matrix products  39 us (18%)
  starting transfers between devices  29.7 us (14%)
  local copies, waits for them, and re-layouts  23.2 us (11%)
  other arithmetic  18.8 us (9%)
    all_to_all x4, waiting for transfers between devices, exchange(): lax.all_to_all(blocks, 'expert', split_axis=0, concat_axis=0, tiled=True)  94.8 us
    all_to_all x4, starting transfers between devices, exchange(): lax.all_to_all(blocks, 'expert', split_axis=0, concat_axis=0, tiled=True)  19.2 us
    dot_general x8, matrix products, left_product(): lax.dot_general(left, right, (((0,), (0,)), ((), ())), preferred_element_...  14.6 us
    dot_general x6, matrix products, expert_grads(): gate_up = jnp.dot(saved_rows, weight_in, preferred_element_type=jnp.float32)  14.3 us
    dot_general x10, matrix products, right_product(): lax.dot_general(left, right, (((1,), (1,)), ((), ())), preferred_element_...  10.1 us
    unnamed x83, local copies, waits for them, and re-layouts  9.99 us
    scatter x4, other arithmetic, outgoing_rows(): jnp.zeros((experts * capacity, model_width), jnp.bfloat16).at[slot_ids]  7.16 us
    ppermute x2, starting transfers between devices, passed_along(): return lax.ppermute(block, axis, route)  6.5 us
  transfers between devices with their start and end apart: 9, of which 7 were waited for; matrix products, arithmetic and copies ran while one was open for 26% of the time, Pallas kernels for 0%

profile of v3, /device:TPU:1, one launch (start us, length us, event | category | flops | bytes accessed | tf_op | source)
XLA Modules:
  0.0 214.1 jit_solution(15100089199858005204)
XLA Ops:
  6.2 2.0 scatter_custom_fusion.1
  8.1 2.0 scatter_custom_fusion
  11.4 6.4 %all-to-all-start = ((bf16[8,2,24,2048]{3,2,1,0:T(8,128)(2,1)}), bf16[8,2,24,2048]{3,2,1,0:T(8,128)(2,1)S(1)}, u32[]{:S(2)}, u32[]{:S(2)}) async-start(bf16[8,2,24,2048]{3,2,1,0:T(8,128)(2,1)} %pad_maximum_fusion), calls=%async_computation | async-start | bytes 3145728 | tf_op jit(solution)/shard_map/all_to_all | solution.py:52
  17.8 2.9 %slice_bitcast_fusion = bf16[2,192,2048]{2,1,0:T(8,128)(2,1)} fusion(bf16[2,2,1,1,192,2048]{5,4,3,2,1,0:T(8,128)(2,1)} %param.14), kind=kLoop, calls=%fused_computation.43 | loop fusion | bytes 3145728 | tf_op jit(solution)/shard_map/squeeze | solution.py:81
  20.7 2.1 collective-permute-start
  22.8 2.2 %fusion.21 = f32[192,512]{1,0:T(8,128)S(1)} fusion(bf16[2,1,1,2048,512]{4,3,2,1,0:T(8,128)(2,1)} %param.10, bf16[2,2,1,1,192,2048]{5,4,3,2,1,0:T(8,128)(2,1)S(1)} %copy-done.1), kind=kOutput, calls=%fused_computation.37 | convolution fusion | flops 402653184 | bytes 3276800 | tf_op jit(solution)/shard_map/dot_general | solution.py:58
  26.3 27.7 %all-to-all-done = bf16[8,2,24,2048]{3,2,1,0:T(8,128)(2,1)S(1)} async-done(((bf16[8,2,24,2048]{3,2,1,0:T(8,128)(2,1)}), bf16[8,2,24,2048]{3,2,1,0:T(8,128)(2,1)S(1)}, u32[]{:S(2)}, u32[]{:S(2)}) %all-to-all-start) | async-done | bytes 1572896 | tf_op jit(solution)/shard_map/all_to_all | solution.py:52
  54.1 2.0 copy-done.36
  61.4 4.8 %all-to-all-start.1 = ((bf16[8,2,24,2048]{3,2,1,0:T(8,128)(2,1)}), bf16[8,2,24,2048]{3,2,1,0:T(8,128)(2,1)S(1)}, u32[]{:S(2)}, u32[]{:S(2)}) async-start(bf16[8,2,24,2048]{3,2,1,0:T(8,128)(2,1)} %pad_maximum_fusion.1), calls=%async_computation.1 | async-start | bytes 3145728 | tf_op jit(solution)/shard_map/all_to_all | solution.py:52
  66.8 1.9 collective-permute-start.3
  68.8 33.8 %all-to-all-done.1 = bf16[8,2,24,2048]{3,2,1,0:T(8,128)(2,1)S(1)} async-done(((bf16[8,2,24,2048]{3,2,1,0:T(8,128)(2,1)}), bf16[8,2,24,2048]{3,2,1,0:T(8,128)(2,1)S(1)}, u32[]{:S(2)}, u32[]{:S(2)}) %all-to-all-start.1) | async-done | bytes 1572896 | tf_op jit(solution)/shard_map/all_to_all | solution.py:52
  105.0 4.6 %collective-permute-start.2 = (bf16[96,2048]{1,0:T(8,128)(2,1)S(1)}, bf16[96,2048]{1,0:T(8,128)(2,1)S(1)}, u32[]{:S(2)}, u32[]{:S(2)}) collective-permute-start(bf16[96,2048]{1,0:T(8,128)(2,1)S(1)} %get-tuple-element.40), channel_id=1, source_target_pairs={{0,8},{8,16},{16,24},{1,9},{9,17},{17,25},{2,10},{10,18},{18,26},{... | collective-permute-start | bytes 1179656 | tf_op jit(solution)/shard_map/ppermute | solution.py:10
  109.6 1.9 collective-permute-start.1
  111.6 2.8 %collective-permute-done.2 = bf16[96,2048]{1,0:T(8,128)(2,1)S(1)} collective-permute-done((bf16[96,2048]{1,0:T(8,128)(2,1)S(1)}, bf16[96,2048]{1,0:T(8,128)(2,1)S(1)}, u32[]{:S(2)}, u32[]{:S(2)}) %collective-permute-start.2) | collective-permute-done | bytes 393248 | tf_op jit(solution)/shard_map/ppermute | solution.py:10
  116.0 2.8 %collective-permute-done.1 = bf16[96,2048]{1,0:T(8,128)(2,1)S(1)} collective-permute-done((bf16[96,2048]{1,0:T(8,128)(2,1)S(1)}, bf16[96,2048]{1,0:T(8,128)(2,1)S(1)}, u32[]{:S(2)}, u32[]{:S(2)}) %collective-permute-start.1) | collective-permute-done | bytes 393248 | tf_op jit(solution)/shard_map/ppermute | solution.py:10
  121.7 3.8 %all-to-all-start.2 = ((bf16[8,2,24,2048]{3,2,1,0:T(8,128)(2,1)}), bf16[8,2,24,2048]{3,2,1,0:T(8,128)(2,1)S(1)}, u32[]{:S(2)}, u32[]{:S(2)}) async-start(bf16[8,2,24,2048]{3,2,1,0:T(8,128)(2,1)} %pad_maximum_fusion.2), calls=%async_computation.2 | async-start | bytes 3145728 | tf_op jit(solution)/shard_map/all_to_all | solution.py:52
  125.5 3.3 %fusion.18 = f32[192,512]{1,0:T(8,128)} fusion(bf16[2,1,1,2048,512]{4,3,2,1,0:T(8,128)(2,1)} %param.10, bf16[2,2,1,1,192,2048]{5,4,3,2,1,0:T(8,128)(2,1)} %param.14), kind=kOutput, calls=%fused_computation.34 | convolution fusion | flops 402653184 | bytes 3276800 | tf_op jit(solution)/shard_map/dot_general | solution.py:58
  128.8 3.0 %fusion.8 = f32[192,512]{1,0:T(8,128)} fusion(bf16[2,1,1,2048,512]{4,3,2,1,0:T(8,128)(2,1)} %param.10, bf16[2,2,1,1,192,2048]{5,4,3,2,1,0:T(8,128)(2,1)S(1)} %copy-done.2), kind=kOutput, calls=%fused_computation.24 | convolution fusion | flops 402653184 | bytes 3276800 | tf_op jit(solution)/shard_map/dot_general | solution.py:58
  131.9 3.1 %fusion.13 = f32[192,512]{1,0:T(8,128)} fusion(bf16[2,1,1,2048,512]{4,3,2,1,0:T(8,128)(2,1)} %param.10, bf16[2,192,2048]{2,1,0:T(8,128)(2,1)S(1)} %copy-done.8), kind=kOutput, calls=%fused_computation.29 | convolution fusion | flops 402653184 | bytes 3276800 | tf_op jit(solution)/shard_map/dot_general | solution.py:58
  136.3 2.7 %fusion.64 = f32[512,2048]{1,0:T(8,128)} fusion(bf16[2,2,1,1,192,2048]{5,4,3,2,1,0:T(8,128)(2,1)S(1)} %copy-done.2, bf16[192,256]{1,0:T(8,128)(2,1)S(1)} %copy-done.16, bf16[192,256]{1,0:T(8,128)(2,1)S(1)} %copy-done.14), kind=kOutput, calls=%fused_computation.94 | convolution fusion | flops 403046400 | bytes 5177344 | tf_op jit(solution)/shard_map/dot_general | solution.py:29
  139.0 19.0 %all-to-all-done.2 = bf16[8,2,24,2048]{3,2,1,0:T(8,128)(2,1)S(1)} async-done(((bf16[8,2,24,2048]{3,2,1,0:T(8,128)(2,1)}), bf16[8,2,24,2048]{3,2,1,0:T(8,128)(2,1)S(1)}, u32[]{:S(2)}, u32[]{:S(2)}) %all-to-all-start.2) | async-done | bytes 1572896 | tf_op jit(solution)/shard_map/all_to_all | solution.py:52
  159.9 1.8 fusion.105
  165.4 4.3 %all-to-all-start.3 = ((bf16[8,2,24,2048]{3,2,1,0:T(8,128)(2,1)}), bf16[8,2,24,2048]{3,2,1,0:T(8,128)(2,1)}, u32[]{:S(2)}, u32[]{:S(2)}) async-start(bf16[8,2,24,2048]{3,2,1,0:T(8,128)(2,1)} %pad_maximum_fusion.3), calls=%async_computation.3 | async-start | bytes 3145728 | tf_op jit(solution)/shard_map/all_to_all | solution.py:52
  169.7 2.0 fusion.125
  171.9 1.8 multiply_convert_fusion.7
  174.4 2.0 collective-permute-done.4
  176.5 1.6 multiply_convert_fusion.5
  180.3 3.3 %fusion.1 = bf16[1,1,2048,512]{2,3,1,0:T(8,128)(2,1)} fusion(bf16[2048,512]{0,1:T(8,128)(2,1)S(1)} %add_convert_fusion, f32[512,2048]{1,0:T(8,128)S(1)} %copy-done, bf16[2,2,1,1,192,2048]{5,4,3,2,1,0:T(8,128)(2,1)} %param.14, bf16[192,256]{1,0:T(8,128)(2,1)S(1)} %get-tuple-element.46, bf16[192,256]{1,0:T(8,128)(2,1)S(1)} %get-tuple-element.45), kind=kOutput, calls=%fused_computation.11 | convolution fusion | flops 407240704 | bytes 9371648 | tf_op jit(solution)/shard_map/dot_general | solution.py:29
  183.6 3.9 %copy.30 = bf16[1,1,2048,512]{3,2,1,0:T(8,128)(2,1)} copy(bf16[1,1,2048,512]{2,3,1,0:T(8,128)(2,1)} %fusion.1) | data formatting | bytes 4194304
  187.5 1.9 fusion.126
  189.4 1.7 fusion.5
  192.6 14.3 %all-to-all-done.3 = bf16[8,2,24,2048]{3,2,1,0:T(8,128)(2,1)} async-done(((bf16[8,2,24,2048]{3,2,1,0:T(8,128)(2,1)}), bf16[8,2,24,2048]{3,2,1,0:T(8,128)(2,1)}, u32[]{:S(2)}, u32[]{:S(2)}) %all-to-all-start.3) | async-done | bytes 1572896 | tf_op jit(solution)/shard_map/all_to_all | solution.py:52
  (129 shorter events, 39.8 us)
Async XLA Ops:
  11.4 42.6 %all-to-all-start = ((bf16[8,2,24,2048]{3,2,1,0:T(8,128)(2,1)}), bf16[8,2,24,2048]{3,2,1,0:T(8,128)(2,1)S(1)}, u32[]{:S(2)}, u32[]{:S(2)}) async-start(bf16[8,2,24,2048]{3,2,1,0:T(8,128)(2,1)} %pad_maximum_fusion), calls=%async_computation | async-start | bytes 3145728 | tf_op jit(solution)/shard_map/all_to_all | solution.py:52
  17.8 5.0 %copy-start.1 = (bf16[2,2,1,1,192,2048]{5,4,3,2,1,0:T(8,128)(2,1)S(1)}, bf16[2,2,1,1,192,2048]{5,4,3,2,1,0:T(8,128)(2,1)}, u32[]{:S(2)}) copy-start(bf16[2,2,1,1,192,2048]{5,4,3,2,1,0:T(8,128)(2,1)} %param.14) | copy-start | bytes 9437188
  20.7 4.3 %copy-start.32 = (bf16[2,1,1,2048,512]{4,3,2,1,0:T(8,128)(2,1)S(1)}, bf16[2,1,1,2048,512]{4,3,2,1,0:T(8,128)(2,1)}, u32[]{:S(2)}) copy-start(bf16[2,1,1,2048,512]{4,3,2,1,0:T(8,128)(2,1)} %param.10) | copy-start | bytes 12582916
  20.7 40.7 %collective-permute-start = (bf16[2,192,2048]{2,1,0:T(8,128)(2,1)}, bf16[2,192,2048]{2,1,0:T(8,128)(2,1)S(1)}, u32[]{:S(2)}, u32[]{:S(2)}) collective-permute-start(bf16[2,192,2048]{2,1,0:T(8,128)(2,1)} %slice_bitcast_fusion), channel_id=1, source_target_pairs={{0,24},{8,16},{16,8},{24,0},{1,25},{9,17},{17,9},{25,1},{2,26},{10... | collective-permute-start | bytes 4718600 | tf_op jit(solution)/shard_map/ppermute | solution.py:15
  25.0 31.7 %copy-start.21 = (f32[192,512]{1,0:T(8,128)}, f32[192,512]{1,0:T(8,128)S(1)}, u32[]{:S(2)}) copy-start(f32[192,512]{1,0:T(8,128)S(1)} %fusion.21) | copy-start | bytes 1179652
  54.1 3.1 %copy-start.6 = (bf16[8,1,24,2048]{3,2,1,0:T(8,128)(2,1)}, bf16[8,1,24,2048]{3,2,1,0:T(8,128)(2,1)S(1)}, u32[]{:S(2)}) copy-start(bf16[8,1,24,2048]{3,2,1,0:T(8,128)(2,1)S(1)} %get-tuple-element.35) | copy-start | bytes 2359300
  54.1 3.1 %copy-start.12 = (bf16[8,1,24,2048]{3,2,1,0:T(8,128)(2,1)}, bf16[8,1,24,2048]{3,2,1,0:T(8,128)(2,1)S(1)}, u32[]{:S(2)}) copy-start(bf16[8,1,24,2048]{3,2,1,0:T(8,128)(2,1)S(1)} %get-tuple-element.36) | copy-start | bytes 2359300
  56.2 2.3 %copy-start.33 = (bf16[2,1,1,2048,512]{4,3,2,1,0:T(8,128)(2,1)S(1)}, bf16[2,1,1,2048,512]{4,3,2,1,0:T(8,128)(2,1)}, u32[]{:S(2)}) copy-start(bf16[2,1,1,2048,512]{4,3,2,1,0:T(8,128)(2,1)} %param.10) | copy-start | bytes 12582916
  57.2 2.9 %copy-start.13 = (bf16[192,256]{1,0:T(8,128)(2,1)}, bf16[192,256]{1,0:T(8,128)(2,1)S(1)}, u32[]{:S(2)}) copy-start(bf16[192,256]{1,0:T(8,128)(2,1)S(1)} %get-tuple-element.49) | copy-start | bytes 294916
  57.2 2.9 %copy-start.15 = (bf16[192,256]{1,0:T(8,128)(2,1)}, bf16[192,256]{1,0:T(8,128)(2,1)S(1)}, u32[]{:S(2)}) copy-start(bf16[192,256]{1,0:T(8,128)(2,1)S(1)} %get-tuple-element.50) | copy-start | bytes 294916
  61.4 4.8 %copy-start.23 = (s32[2,2,1,96]{3,2,1,0:T(1,128)S(1)}, s32[2,2,1,96]{3,2,1,0:T(1,128)}, u32[]{:S(2)}) copy-start(s32[2,2,1,96]{3,2,1,0:T(1,128)} %param.16) | copy-start | bytes 4612
  61.4 7.3 %copy-start.7 = (bf16[2,192,2048]{2,1,0:T(8,128)(2,1)}, bf16[2,192,2048]{2,1,0:T(8,128)(2,1)S(1)}, u32[]{:S(2)}) copy-start(bf16[2,192,2048]{2,1,0:T(8,128)(2,1)S(1)} %collective-permute-done) | copy-start | bytes 4718596
  61.4 41.1 %all-to-all-start.1 = ((bf16[8,2,24,2048]{3,2,1,0:T(8,128)(2,1)}), bf16[8,2,24,2048]{3,2,1,0:T(8,128)(2,1)S(1)}, u32[]{:S(2)}, u32[]{:S(2)}) async-start(bf16[8,2,24,2048]{3,2,1,0:T(8,128)(2,1)} %pad_maximum_fusion.1), calls=%async_computation.1 | async-start | bytes 3145728 | tf_op jit(solution)/shard_map/all_to_all | solution.py:52
  66.8 54.8 %collective-permute-start.3 = (bf16[192,2048]{1,0:T(8,128)(2,1)}, bf16[192,2048]{1,0:T(8,128)(2,1)}, u32[]{:S(2)}, u32[]{:S(2)}) collective-permute-start(bf16[192,2048]{1,0:T(8,128)(2,1)} %bitcast.265), channel_id=1, source_target_pairs={{0,24},{8,16},{16,8},{24,0},{1,25},{9,17},{17,9},{25,1},{2,26},{10... | collective-permute-start | bytes 2359304 | tf_op jit(solution)/shard_map/ppermute | solution.py:15
  103.6 10.7 %copy-start.4 = (bf16[1,2,96,2048]{3,2,1,0:T(8,128)(2,1)S(1)}, bf16[1,2,96,2048]{3,2,1,0:T(8,128)(2,1)}, u32[]{:S(2)}) copy-start(bf16[1,2,96,2048]{3,2,1,0:T(8,128)(2,1)} %param.13) | copy-start | bytes 2359300
  103.6 10.7 %copy-start.25 = (f32[96]{0:T(128)S(1)}, f32[96]{0:T(128)}, u32[]{:S(2)}) copy-start(f32[96]{0:T(128)} %get-tuple-element.62) | copy-start | bytes 1156
  104.5 14.2 %copy-start.24 = (f32[96]{0:T(128)S(1)}, f32[96]{0:T(128)}, u32[]{:S(2)}) copy-start(f32[96]{0:T(128)} %get-tuple-element.59) | copy-start | bytes 1156
  105.0 9.3 %collective-permute-start.2 = (bf16[96,2048]{1,0:T(8,128)(2,1)S(1)}, bf16[96,2048]{1,0:T(8,128)(2,1)S(1)}, u32[]{:S(2)}, u32[]{:S(2)}) collective-permute-start(bf16[96,2048]{1,0:T(8,128)(2,1)S(1)} %get-tuple-element.40), channel_id=1, source_target_pairs={{0,8},{8,16},{16,24},{1,9},{9,17},{17,25},{2,10},{10,18},{18,26},{... | collective-permute-start | bytes 1179656 | tf_op jit(solution)/shard_map/ppermute | solution.py:10
  109.6 9.1 %collective-permute-start.1 = (bf16[96,2048]{1,0:T(8,128)(2,1)S(1)}, bf16[96,2048]{1,0:T(8,128)(2,1)S(1)}, u32[]{:S(2)}, u32[]{:S(2)}) collective-permute-start(bf16[96,2048]{1,0:T(8,128)(2,1)S(1)} %get-tuple-element.39), channel_id=1, source_target_pairs={{8,0},{16,8},{24,16},{9,1},{17,9},{25,17},{10,2},{18,10},{26,18},{... | collective-permute-start | bytes 1179656 | tf_op jit(solution)/shard_map/ppermute | solution.py:10
  118.7 2.9 %copy-start.10 = (bf16[96,2048]{1,0:T(8,128)(2,1)}, bf16[96,2048]{1,0:T(8,128)(2,1)S(1)}, u32[]{:S(2)}) copy-start(bf16[96,2048]{1,0:T(8,128)(2,1)S(1)} %collective-permute-done.1) | copy-start | bytes 1179652
  121.6 3.8 %copy-start.27 = (s32[96]{0:T(128)S(1)}, s32[96]{0:T(128)}, u32[]{:S(2)}) copy-start(s32[96]{0:T(128)} %get-tuple-element.22) | copy-start | bytes 1156
  121.7 3.8 %copy-start.26 = (s32[96]{0:T(128)S(1)}, s32[96]{0:T(128)}, u32[]{:S(2)}) copy-start(s32[96]{0:T(128)} %get-tuple-element.54) | copy-start | bytes 1156
  121.7 36.4 %all-to-all-start.2 = ((bf16[8,2,24,2048]{3,2,1,0:T(8,128)(2,1)}), bf16[8,2,24,2048]{3,2,1,0:T(8,128)(2,1)S(1)}, u32[]{:S(2)}, u32[]{:S(2)}) async-start(bf16[8,2,24,2048]{3,2,1,0:T(8,128)(2,1)} %pad_maximum_fusion.2), calls=%async_computation.2 | async-start | bytes 3145728 | tf_op jit(solution)/shard_map/all_to_all | solution.py:52
  125.5 3.3 %copy-start.2 = (bf16[2,2,1,1,192,2048]{5,4,3,2,1,0:T(8,128)(2,1)S(1)}, bf16[2,2,1,1,192,2048]{5,4,3,2,1,0:T(8,128)(2,1)}, u32[]{:S(2)}) copy-start(bf16[2,2,1,1,192,2048]{5,4,3,2,1,0:T(8,128)(2,1)} %param.14) | copy-start | bytes 9437188
  128.8 3.1 %copy-start.8 = (bf16[2,192,2048]{2,1,0:T(8,128)(2,1)S(1)}, bf16[2,192,2048]{2,1,0:T(8,128)(2,1)}, u32[]{:S(2)}) copy-start(bf16[2,192,2048]{2,1,0:T(8,128)(2,1)} %copy-done.7) | copy-start | bytes 4718596
  131.9 3.1 %copy-start.34 = (bf16[2,1,1,2048,512]{4,3,2,1,0:T(8,128)(2,1)S(1)}, bf16[2,1,1,2048,512]{4,3,2,1,0:T(8,128)(2,1)}, u32[]{:S(2)}) copy-start(bf16[2,1,1,2048,512]{4,3,2,1,0:T(8,128)(2,1)} %param.10) | copy-start | bytes 12582916
  139.0 20.0 %copy-start.39 = (f32[192,512]{1,0:T(8,128)S(1)}, f32[192,512]{1,0:T(8,128)}, u32[]{:S(2)}) copy-start(f32[192,512]{1,0:T(8,128)} %fusion.8) | copy-start | bytes 1179652
  159.0 2.7 %copy-start.17 = (f32[192,512]{1,0:T(8,128)S(1)}, f32[192,512]{1,0:T(8,128)}, u32[]{:S(2)}) copy-start(f32[192,512]{1,0:T(8,128)} %fusion.18) | copy-start | bytes 1179652
  159.0 17.4 %collective-permute-start.4 = (bf16[192,2048]{1,0:T(8,128)(2,1)}, bf16[192,2048]{1,0:T(8,128)(2,1)}, u32[]{:S(2)}, u32[]{:S(2)}) collective-permute-start(bf16[192,2048]{1,0:T(8,128)(2,1)} %bitcast.61), channel_id=1, source_target_pairs={{0,24},{8,16},{16,8},{24,0},{1,25},{9,17},{17,9},{25,1},{2,26},{10... | collective-permute-start | bytes 2359304 | tf_op jit(solution)/shard_map/ppermute | solution.py:15
  159.9 2.5 %copy-start.35 = (bf16[2,1,1,2048,512]{4,3,2,1,0:T(8,128)(2,1)S(1)}, bf16[2,1,1,2048,512]{4,3,2,1,0:T(8,128)(2,1)}, u32[]{:S(2)}) copy-start(bf16[2,1,1,2048,512]{4,3,2,1,0:T(8,128)(2,1)} %param.10) | copy-start | bytes 12582916
  165.4 41.5 %all-to-all-start.3 = ((bf16[8,2,24,2048]{3,2,1,0:T(8,128)(2,1)}), bf16[8,2,24,2048]{3,2,1,0:T(8,128)(2,1)}, u32[]{:S(2)}, u32[]{:S(2)}) async-start(bf16[8,2,24,2048]{3,2,1,0:T(8,128)(2,1)} %pad_maximum_fusion.3), calls=%async_computation.3 | async-start | bytes 3145728 | tf_op jit(solution)/shard_map/all_to_all | solution.py:52
  173.7 2.8 %copy-start.22 = (f32[192,512]{1,0:T(8,128)S(1)}, f32[192,512]{1,0:T(8,128)}, u32[]{:S(2)}) copy-start(f32[192,512]{1,0:T(8,128)} %fusion.13) | copy-start | bytes 1179652
  (18 other events, 30.3 us)

commit v4 on v3

--- a/solution.py
+++ b/solution.py
@@ -15,16 +15,6 @@
     return lax.ppermute(block, axis, [(i, count - 1 - i) for i in range(count)])
 
 
-def slot_index(route_ids, count_table, capacity):
-    experts = count_table.shape[0]
-    offset = jnp.cumsum(count_table) - count_table
-    labels = lax.iota(jnp.int32, experts)
-    first_slot = jnp.sum(
-        jnp.where(route_ids[:, None] == labels[None, :], offset[None, :], 0), axis=1
-    )
-    return route_ids * capacity + lax.iota(jnp.int32, route_ids.shape[0]) - first_slot
-
-
 def left_product(left, right):
     return lax.dot_general(
         left, right, (((0,), (0,)), ((), ())), preferred_element_type=jnp.float32
@@ -37,14 +27,25 @@
     )
 
 
-def outgoing_rows(gradient, prob_rows, route_ids, count_table):
-    tokens, model_width = gradient.shape
+def slot_table(route_ids, count_table, capacity, way_id, ways):
     experts = count_table.shape[0]
-    capacity = 2 * tokens // experts
-    slot_ids = slot_index(route_ids, count_table, capacity)
-    scaled = (prob_rows[:, None] * gradient.astype(jnp.float32)).astype(jnp.bfloat16)
-    outgoing = jnp.zeros((experts * capacity, model_width), jnp.bfloat16).at[slot_ids].set(scaled)
-    return outgoing.reshape(experts, 1, capacity, model_width), slot_ids
+    labels = lax.iota(jnp.int32, experts)
+    below = jnp.sum(
+        jnp.where(labels[None, :] < labels[:, None], count_table[None, :], 0), axis=1
+    )
+    first_slot = jnp.sum(jnp.where(route_ids[:, None] == labels[None, :], below[None, :], 0), axis=1)
+    within = lax.iota(jnp.int32, route_ids.shape[0]) - first_slot
+    return (route_ids * ways + way_id) * capacity + within
+
+
+def placement(route_ids, count_tables, capacity):
+    ways, tokens = route_ids.shape
+    experts = count_tables.shape[1]
+    slots = jnp.concatenate(
+        [slot_table(route_ids[w], count_tables[w], capacity, w, ways) for w in range(ways)]
+    )
+    rows = lax.iota(jnp.int32, ways * experts * capacity)
+    return (rows[:, None] == slots[None, :]).astype(jnp.bfloat16)
 
 
 def exchange(blocks):
@@ -76,26 +77,22 @@
     section_id = lax.axis_index("section")
     experts = lax.axis_size("expert")
     model_width = grads.shape[-1]
+    tokens = grads.shape[2]
+    capacity = 2 * tokens // experts
     hidden_width = w_out.shape[-2]
     ticks = saved.shape[0]
     saved_mirror = mirrored(saved[:, 1, 0, 0], "section")
-    current = [grads[0, 0], grads[1, 0]]
+    current = grads[:, 0]
     zeros_in = jnp.zeros((model_width, 2 * hidden_width), jnp.float32)
     zeros_out = jnp.zeros((hidden_width, model_width), jnp.float32)
     own_in, own_out = zeros_in, zeros_out
     mirror_in, mirror_out = zeros_in, zeros_out
     slope_mirror = None
     for tick_id in range(ticks):
-        sent = [
-            outgoing_rows(
-                current[way_id],
-                probs[tick_id, way_id, 0],
-                routes[tick_id, way_id, 0],
-                counts[tick_id, way_id, 0, 0],
-            )
-            for way_id in range(2)
-        ]
-        blocks = jnp.concatenate([sent[0][0], sent[1][0]], axis=1)
+        one_hot = placement(routes[tick_id, :, 0], counts[tick_id, :, 0, 0], capacity)
+        scaled = (probs[tick_id, :, 0][:, :, None] * current.astype(jnp.float32)).astype(jnp.bfloat16)
+        blocks = jnp.dot(one_hot, scaled.reshape(-1, model_width), preferred_element_type=jnp.float32)
+        blocks = blocks.astype(jnp.bfloat16).reshape(experts, 2, capacity, model_width)
         if slope_mirror is not None:
             blocks, slope_mirror = lax.optimization_barrier((blocks, slope_mirror))
             hidden_m, pair_grad_m = expert_grads(
@@ -114,7 +111,7 @@
                 slopes[way_id], saved_rows, w_in[way_id, 0, 0], w_out[way_id, 0, 0]
             )
             input_grad = right_product(pair_grad, w_in[way_id, 0, 0]).astype(jnp.bfloat16)
-            input_grads.append(input_grad.reshape(experts, 1, -1, model_width))
+            input_grads.append(input_grad.reshape(experts, 1, capacity, model_width))
             if way_id == 0:
                 part_in, part_out = weight_terms(saved_rows, slopes[0], hidden, pair_grad)
                 own_in = own_in + part_in
@@ -123,22 +120,18 @@
         back_blocks = jnp.concatenate(input_grads, axis=1)
         if tick_id == 0:
             back_blocks, saved_mirror = lax.optimization_barrier((back_blocks, saved_mirror))
-        returned = exchange(back_blocks)
-        finished = []
-        for way_id in range(2):
-            back_rows = jnp.take(returned[way_id], sent[way_id][1], axis=0)
-            finished.append(
-                (current[way_id].astype(jnp.float32) + back_rows.astype(jnp.float32)).astype(
-                    jnp.bfloat16
-                )
-            )
+        returned = lax.all_to_all(back_blocks, "expert", split_axis=0, concat_axis=0, tiled=True)
+        back_rows = left_product(one_hot, returned.reshape(-1, model_width))
+        finished = (current.astype(jnp.float32) + back_rows.reshape(2, tokens, model_width)).astype(
+            jnp.bfloat16
+        )
         if tick_id + 1 < ticks:
             from_above = passed_along(finished[0], "section", -1)
             from_below = passed_along(finished[1], "section", 1)
-            current = [
+            current = jnp.stack([
                 jnp.where(section_id == sections - 1, fresh[tick_id, 0], from_above),
                 jnp.where(section_id == 0, fresh[tick_id, 1], from_below),
-            ]
+            ])
     hidden_m, pair_grad_m = expert_grads(
         slope_mirror, saved_mirror[ticks - 1], w_in[0, 0, 0], w_out[0, 0, 0]
     )
@@ -147,7 +140,7 @@
     mirror_out = (mirror_out + part_out).astype(jnp.bfloat16).astype(jnp.float32)
     grad_in = (own_in + mirror_in).astype(jnp.bfloat16)
     grad_out = (own_out + mirror_out).astype(jnp.bfloat16)
-    return (jnp.stack(finished)[:, None], grad_in[None, None], grad_out[None, None])
+    return (finished[:, None], grad_in[None, None], grad_out[None, None])
 
 
 def solution(mesh):

time: 215 us -> 222 us (1.033)
  waiting for transfers between devices: 102 us -> 122 us
  other arithmetic: 18.8 us -> 5.6 us
  matrix products: 39 us -> 45.8 us
  local copies, waits for them, and re-layouts: 23.2 us -> 17.5 us
    all_to_all x0 -> x2, waiting for transfers between devices: none -> 49.5 us  [on_device(): lax.all_to_all(back_blocks, 'expert', split_axis=0, concat_axis=0, tiled=...]
    all_to_all x4 -> x2, waiting for transfers between devices: 94.8 us -> 50 us  [exchange(): lax.all_to_all(blocks, 'expert', split_axis=0, concat_axis=0, tiled=True)]
    ppermute x3, waiting for transfers between devices: 2.02 us -> 14.6 us  [mirrored(): return lax.ppermute(block, axis, [(i, count - 1 - i) for i in range(count)])]
    all_to_all x4 -> x2, starting transfers between devices: 19.2 us -> 9.95 us  [exchange(): lax.all_to_all(blocks, 'expert', split_axis=0, concat_axis=0, tiled=True)]
    all_to_all x0 -> x2, starting transfers between devices: none -> 9.1 us  [on_device(): lax.all_to_all(back_blocks, 'expert', split_axis=0, concat_axis=0, tiled=...]
    scatter x4 -> x0, other arithmetic: 7.16 us -> none  [outgoing_rows(): jnp.zeros((experts * capacity, model_width), jnp.bfloat16).at[slot_ids]]
    gather x4 -> x0, local copies, waits for them, and re-layouts: 4.84 us -> none  [on_device(): back_rows = jnp.take(returned[way_id], sent[way_id][1], axis=0)]
    dot_general x0 -> x2, matrix products: none -> 3.43 us  [on_device(): jnp.dot(one_hot, scaled.reshape(-1, model_width), preferred_element_type=...]
  transfers between devices with their start and end apart: 9 -> 9, of which waited for: 7 -> 8; matrix products, arithmetic and copies ran while one was open for 26% -> 23% of each run, Pallas kernels for 0% -> 0%
where the time goes in v4:
time: 222 us; the launch traced here: 220 us
  waiting for transfers between devices  122 us (55%)
  matrix products  45.8 us (21%)
  starting transfers between devices  28.2 us (13%)
  local copies, waits for them, and re-layouts  17.5 us (8%)
  other arithmetic  5.6 us (3%)
    all_to_all x2, waiting for transfers between devices, exchange(): lax.all_to_all(blocks, 'expert', split_axis=0, concat_axis=0, tiled=True)  50 us
    all_to_all x2, waiting for transfers between devices, on_device(): lax.all_to_all(back_blocks, 'expert', split_axis=0, concat_axis=0, tiled=...  49.5 us
    dot_general x10, matrix products, left_product(): lax.dot_general(left, right, (((0,), (0,)), ((), ())), preferred_element_...  18 us
    ppermute x3, waiting for transfers between devices, mirrored(): return lax.ppermute(block, axis, [(i, count - 1 - i) for i in range(count)])  14.6 us
    dot_general x6, matrix products, expert_grads(): gate_up = jnp.dot(saved_rows, weight_in, preferred_element_type=jnp.float32)  14.3 us
    unnamed x55, local copies, waits for them, and re-layouts  11 us
    dot_general x10, matrix products, right_product(): lax.dot_general(left, right, (((1,), (1,)), ((), ())), preferred_element_...  10.1 us
    all_to_all x2, starting transfers between devices, exchange(): lax.all_to_all(blocks, 'expert', split_axis=0, concat_axis=0, tiled=True)  9.95 us
  transfers between devices with their start and end apart: 9, of which 8 were waited for; matrix products, arithmetic and copies ran while one was open for 23% of the time, Pallas kernels for 0%

profile of v4, /device:TPU:1, one launch (start us, length us, event | category | flops | bytes accessed | tf_op | source)
XLA Modules:
  0.0 220.2 jit_solution(16105184950177676775)
XLA Ops:
  5.2 1.7 convolution_convert_fusion.1
  7.0 6.4 %all-to-all-start = ((bf16[8,2,24,2048]{3,2,1,0:T(8,128)(2,1)}), bf16[8,2,24,2048]{3,2,1,0:T(8,128)(2,1)S(1)}, u32[]{:S(2)}, u32[]{:S(2)}) async-start(bf16[8,2,24,2048]{3,2,1,0:T(8,128)(2,1)} %bitcast.13), calls=%async_computation | async-start | bytes 3145728 | tf_op jit(solution)/shard_map/all_to_all | solution.py:53
  13.3 2.9 %slice_bitcast_fusion = bf16[2,192,2048]{2,1,0:T(8,128)(2,1)} fusion(bf16[2,2,1,1,192,2048]{5,4,3,2,1,0:T(8,128)(2,1)} %param.12), kind=kLoop, calls=%fused_computation.44 | loop fusion | bytes 3145728 | tf_op jit(solution)/shard_map/squeeze | solution.py:84
  16.2 2.1 collective-permute-start
  18.3 2.9 %fusion.24 = f32[192,512]{1,0:T(8,128)} fusion(bf16[2,1,1,2048,512]{4,3,2,1,0:T(8,128)(2,1)} %param.8, bf16[2,2,1,1,192,2048]{5,4,3,2,1,0:T(8,128)(2,1)S(1)} %copy-done.1), kind=kOutput, calls=%fused_computation.36 | convolution fusion | flops 402653184 | bytes 3276800 | tf_op jit(solution)/shard_map/dot_general | solution.py:59
  22.6 26.9 %all-to-all-done = bf16[8,2,24,2048]{3,2,1,0:T(8,128)(2,1)S(1)} async-done(((bf16[8,2,24,2048]{3,2,1,0:T(8,128)(2,1)}), bf16[8,2,24,2048]{3,2,1,0:T(8,128)(2,1)S(1)}, u32[]{:S(2)}, u32[]{:S(2)}) %all-to-all-start) | async-done | bytes 1572896 | tf_op jit(solution)/shard_map/all_to_all | solution.py:53
  49.7 2.0 copy-done.22
  58.1 4.6 %all-to-all-start.1 = ((bf16[8,2,24,2048]{3,2,1,0:T(8,128)(2,1)}), bf16[8,2,24,2048]{3,2,1,0:T(8,128)(2,1)S(1)}, u32[]{:S(2)}, u32[]{:S(2)}) async-start(bf16[8,2,24,2048]{3,2,1,0:T(8,128)(2,1)} %pad_maximum_fusion), calls=%async_computation.1 | async-start | bytes 3145728 | tf_op jit(solution)/shard_map/all_to_all | solution.py:123
  63.0 36.1 %all-to-all-done.1 = bf16[8,2,24,2048]{3,2,1,0:T(8,128)(2,1)S(1)} async-done(((bf16[8,2,24,2048]{3,2,1,0:T(8,128)(2,1)}), bf16[8,2,24,2048]{3,2,1,0:T(8,128)(2,1)S(1)}, u32[]{:S(2)}, u32[]{:S(2)}) %all-to-all-start.1) | async-done | bytes 1572896 | tf_op jit(solution)/shard_map/all_to_all | solution.py:123
  99.8 3.5 %collective-permute-start.1 = (bf16[96,2048]{1,0:T(8,128)(2,1)S(1)}, bf16[96,2048]{1,0:T(8,128)(2,1)S(1)}, u32[]{:S(2)}, u32[]{:S(2)}) collective-permute-start(bf16[96,2048]{1,0:T(8,128)(2,1)S(1)} %get-tuple-element.28), channel_id=1, source_target_pairs={{8,0},{16,8},{24,16},{9,1},{17,9},{25,17},{10,2},{18,10},{26,18},{... | collective-permute-start | bytes 1179656 | tf_op jit(solution)/shard_map/ppermute | solution.py:10
  103.3 3.0 %collective-permute-start.2 = (bf16[96,2048]{1,0:T(8,128)(2,1)S(1)}, bf16[96,2048]{1,0:T(8,128)(2,1)S(1)}, u32[]{:S(2)}, u32[]{:S(2)}) collective-permute-start(bf16[96,2048]{1,0:T(8,128)(2,1)S(1)} %get-tuple-element.29), channel_id=1, source_target_pairs={{0,8},{8,16},{16,24},{1,9},{9,17},{17,25},{2,10},{10,18},{18,26},{... | collective-permute-start | bytes 1179656 | tf_op jit(solution)/shard_map/ppermute | solution.py:10
  106.9 4.8 %collective-permute-done.1 = bf16[96,2048]{1,0:T(8,128)(2,1)S(1)} collective-permute-done((bf16[96,2048]{1,0:T(8,128)(2,1)S(1)}, bf16[96,2048]{1,0:T(8,128)(2,1)S(1)}, u32[]{:S(2)}, u32[]{:S(2)}) %collective-permute-start.1) | collective-permute-done | bytes 393248 | tf_op jit(solution)/shard_map/ppermute | solution.py:10
  111.7 3.1 %collective-permute-done.2 = bf16[96,2048]{1,0:T(8,128)(2,1)S(1)} collective-permute-done((bf16[96,2048]{1,0:T(8,128)(2,1)S(1)}, bf16[96,2048]{1,0:T(8,128)(2,1)S(1)}, u32[]{:S(2)}, u32[]{:S(2)}) %collective-permute-start.2) | collective-permute-done | bytes 393248 | tf_op jit(solution)/shard_map/ppermute | solution.py:10
  115.2 1.7 convolution_convert_fusion
  116.9 11.1 %collective-permute-done.3 = bf16[192,2048]{1,0:T(8,128)(2,1)} collective-permute-done((bf16[192,2048]{1,0:T(8,128)(2,1)}, bf16[192,2048]{1,0:T(8,128)(2,1)}, u32[]{:S(2)}, u32[]{:S(2)}) %collective-permute-start.3) | collective-permute-done | bytes 786464 | tf_op jit(solution)/shard_map/ppermute | solution.py:15
  128.0 3.6 %all-to-all-start.2 = ((bf16[8,2,24,2048]{3,2,1,0:T(8,128)(2,1)}), bf16[8,2,24,2048]{3,2,1,0:T(8,128)(2,1)S(1)}, u32[]{:S(2)}, u32[]{:S(2)}) async-start(bf16[8,2,24,2048]{3,2,1,0:T(8,128)(2,1)} %bitcast.44), calls=%async_computation.2 | async-start | bytes 3145728 | tf_op jit(solution)/shard_map/all_to_all | solution.py:53
  131.8 2.5 %fusion.21 = f32[192,512]{1,0:T(8,128)S(1)} fusion(bf16[2,1,1,2048,512]{4,3,2,1,0:T(8,128)(2,1)} %param.8, bf16[2,2,1,1,192,2048]{5,4,3,2,1,0:T(8,128)(2,1)} %param.12), kind=kOutput, calls=%fused_computation.33 | convolution fusion | flops 402653184 | bytes 3276800 | tf_op jit(solution)/shard_map/dot_general | solution.py:59
  134.5 3.1 %fusion.11 = f32[192,512]{1,0:T(8,128)} fusion(bf16[2,1,1,2048,512]{4,3,2,1,0:T(8,128)(2,1)} %param.8, bf16[2,2,1,1,192,2048]{5,4,3,2,1,0:T(8,128)(2,1)S(1)} %copy-done.2), kind=kOutput, calls=%fused_computation.23 | convolution fusion | flops 402653184 | bytes 3276800 | tf_op jit(solution)/shard_map/dot_general | solution.py:59
  137.6 3.1 %fusion.16 = f32[192,512]{1,0:T(8,128)} fusion(bf16[2,1,1,2048,512]{4,3,2,1,0:T(8,128)(2,1)} %param.8, bf16[2,192,2048]{2,1,0:T(8,128)(2,1)S(1)} %copy-done.8), kind=kOutput, calls=%fused_computation.28 | convolution fusion | flops 402653184 | bytes 3276800 | tf_op jit(solution)/shard_map/dot_general | solution.py:59
  142.0 2.7 %fusion.61 = f32[512,2048]{1,0:T(8,128)} fusion(bf16[2,2,1,1,192,2048]{5,4,3,2,1,0:T(8,128)(2,1)S(1)} %copy-done.2, bf16[192,256]{1,0:T(8,128)(2,1)S(1)} %get-tuple-element.39, bf16[192,256]{1,0:T(8,128)(2,1)S(1)} %get-tuple-element.38), kind=kOutput, calls=%fused_computation.79 | convolution fusion | flops 403046400 | bytes 5177344 | tf_op jit(solution)/shard_map/dot_general | solution.py:19
  144.7 23.0 %all-to-all-done.2 = bf16[8,2,24,2048]{3,2,1,0:T(8,128)(2,1)S(1)} async-done(((bf16[8,2,24,2048]{3,2,1,0:T(8,128)(2,1)}), bf16[8,2,24,2048]{3,2,1,0:T(8,128)(2,1)S(1)}, u32[]{:S(2)}, u32[]{:S(2)}) %all-to-all-start.2) | async-done | bytes 1572896 | tf_op jit(solution)/shard_map/all_to_all | solution.py:53
  169.6 1.8 fusion.82
  175.1 4.5 %all-to-all-start.3 = ((bf16[8,2,24,2048]{3,2,1,0:T(8,128)(2,1)}), bf16[8,2,24,2048]{3,2,1,0:T(8,128)(2,1)}, u32[]{:S(2)}, u32[]{:S(2)}) async-start(bf16[8,2,24,2048]{3,2,1,0:T(8,128)(2,1)} %pad_maximum_fusion.1), calls=%async_computation.3 | async-start | bytes 3145728 | tf_op jit(solution)/shard_map/all_to_all | solution.py:123
  179.6 2.0 fusion.104
  181.8 1.8 multiply_convert_fusion.7
  184.3 3.5 %collective-permute-done.4 = bf16[192,2048]{1,0:T(8,128)(2,1)} collective-permute-done((bf16[192,2048]{1,0:T(8,128)(2,1)}, bf16[192,2048]{1,0:T(8,128)(2,1)}, u32[]{:S(2)}, u32[]{:S(2)}) %collective-permute-start.4) | collective-permute-done | bytes 786464 | tf_op jit(solution)/shard_map/ppermute | solution.py:15
  191.7 3.2 %fusion.1 = bf16[1,1,2048,512]{2,3,1,0:T(8,128)(2,1)} fusion(bf16[2048,512]{0,1:T(8,128)(2,1)S(1)} %add_convert_fusion, f32[512,2048]{1,0:T(8,128)S(1)} %copy-done, bf16[2,2,1,1,192,2048]{5,4,3,2,1,0:T(8,128)(2,1)} %param.12, bf16[192,256]{1,0:T(8,128)(2,1)S(1)} %get-tuple-element.35, bf16[192,256]{1,0:T(8,128)(2,1)S(1)} %get-tuple-element.34), kind=kOutput, calls=%fused_computation.5 | convolution fusion | flops 407240704 | bytes 9371648 | tf_op jit(solution)/shard_map/dot_general | solution.py:19
  194.9 3.9 %copy.35 = bf16[1,1,2048,512]{3,2,1,0:T(8,128)(2,1)} copy(bf16[1,1,2048,512]{2,3,1,0:T(8,128)(2,1)} %fusion.1) | data formatting | bytes 4194304
  198.9 1.8 fusion.105
  200.7 1.7 fusion.5
  204.0 13.3 %all-to-all-done.3 = bf16[8,2,24,2048]{3,2,1,0:T(8,128)(2,1)} async-done(((bf16[8,2,24,2048]{3,2,1,0:T(8,128)(2,1)}), bf16[8,2,24,2048]{3,2,1,0:T(8,128)(2,1)}, u32[]{:S(2)}, u32[]{:S(2)}) %all-to-all-start.3) | async-done | bytes 1572896 | tf_op jit(solution)/shard_map/all_to_all | solution.py:123
  217.3 2.9 %fusion.9 = bf16[2,1,96,2048]{3,2,1,0:T(8,128)(2,1)} fusion(pred[2,96,384]{2,1,0:T(32,128)(4,1)S(1)} %bitcast.221, bf16[384,2048,1]{1,0,2:T(8,128)(2,1)} %bitcast.54, bf16[1,96,2048]{2,1,0:T(8,128)(2,1)S(1)} %get-tuple-element.27, bf16[1,96,2048]{2,1,0:T(8,128)(2,1)S(1)} %get-tuple-element.26), kind=kOutput, calls=%fused_computation.21 | convolution fusion | flops 303562752 | bytes 3219456 | tf_op jit(solution)/shard_map/dot_general | solution.py:19
  (101 shorter events, 27.8 us)
Async XLA Ops:
  3.3 1.8 copy-start.17
  7.0 42.6 %all-to-all-start = ((bf16[8,2,24,2048]{3,2,1,0:T(8,128)(2,1)}), bf16[8,2,24,2048]{3,2,1,0:T(8,128)(2,1)S(1)}, u32[]{:S(2)}, u32[]{:S(2)}) async-start(bf16[8,2,24,2048]{3,2,1,0:T(8,128)(2,1)} %bitcast.13), calls=%async_computation | async-start | bytes 3145728 | tf_op jit(solution)/shard_map/all_to_all | solution.py:53
  13.3 5.0 %copy-start.1 = (bf16[2,2,1,1,192,2048]{5,4,3,2,1,0:T(8,128)(2,1)S(1)}, bf16[2,2,1,1,192,2048]{5,4,3,2,1,0:T(8,128)(2,1)}, u32[]{:S(2)}) copy-start(bf16[2,2,1,1,192,2048]{5,4,3,2,1,0:T(8,128)(2,1)} %param.12) | copy-start | bytes 9437188
  16.2 5.0 %copy-start.18 = (bf16[2,1,1,2048,512]{4,3,2,1,0:T(8,128)(2,1)S(1)}, bf16[2,1,1,2048,512]{4,3,2,1,0:T(8,128)(2,1)}, u32[]{:S(2)}) copy-start(bf16[2,1,1,2048,512]{4,3,2,1,0:T(8,128)(2,1)} %param.8) | copy-start | bytes 12582916
  16.2 40.7 %collective-permute-start = (bf16[2,192,2048]{2,1,0:T(8,128)(2,1)}, bf16[2,192,2048]{2,1,0:T(8,128)(2,1)S(1)}, u32[]{:S(2)}, u32[]{:S(2)}) collective-permute-start(bf16[2,192,2048]{2,1,0:T(8,128)(2,1)} %slice_bitcast_fusion), channel_id=1, source_target_pairs={{0,24},{8,16},{16,8},{24,0},{1,25},{9,17},{17,9},{25,1},{2,26},{10... | collective-permute-start | bytes 4718600 | tf_op jit(solution)/shard_map/ppermute | solution.py:15
  49.5 2.2 copy-start.22
  49.5 2.2 copy-start.26
  49.6 3.1 %copy-start.6 = (bf16[8,1,24,2048]{3,2,1,0:T(8,128)(2,1)}, bf16[8,1,24,2048]{3,2,1,0:T(8,128)(2,1)S(1)}, u32[]{:S(2)}) copy-start(bf16[8,1,24,2048]{3,2,1,0:T(8,128)(2,1)S(1)} %get-tuple-element.24) | copy-start | bytes 2359300
  49.6 3.1 %copy-start.11 = (bf16[8,1,24,2048]{3,2,1,0:T(8,128)(2,1)}, bf16[8,1,24,2048]{3,2,1,0:T(8,128)(2,1)S(1)}, u32[]{:S(2)}) copy-start(bf16[8,1,24,2048]{3,2,1,0:T(8,128)(2,1)S(1)} %get-tuple-element.25) | copy-start | bytes 2359300
  49.7 2.6 %copy-start.15 = (f32[192,512]{1,0:T(8,128)S(1)}, f32[192,512]{1,0:T(8,128)}, u32[]{:S(2)}) copy-start(f32[192,512]{1,0:T(8,128)} %fusion.24) | copy-start | bytes 1179652
  51.7 2.2 %copy-start.19 = (bf16[2,1,1,2048,512]{4,3,2,1,0:T(8,128)(2,1)S(1)}, bf16[2,1,1,2048,512]{4,3,2,1,0:T(8,128)(2,1)}, u32[]{:S(2)}) copy-start(bf16[2,1,1,2048,512]{4,3,2,1,0:T(8,128)(2,1)} %param.8) | copy-start | bytes 12582916
  56.9 42.2 %copy-start.5 = (bf16[2,1,96,2048]{3,2,1,0:T(8,128)(2,1)S(1)}, bf16[2,1,96,2048]{3,2,1,0:T(8,128)(2,1)}, u32[]{:S(2)}) copy-start(bf16[2,1,96,2048]{3,2,1,0:T(8,128)(2,1)} %param.10) | copy-start | bytes 2359300
  58.1 41.0 %all-to-all-start.1 = ((bf16[8,2,24,2048]{3,2,1,0:T(8,128)(2,1)}), bf16[8,2,24,2048]{3,2,1,0:T(8,128)(2,1)S(1)}, u32[]{:S(2)}, u32[]{:S(2)}) async-start(bf16[8,2,24,2048]{3,2,1,0:T(8,128)(2,1)} %pad_maximum_fusion), calls=%async_computation.1 | async-start | bytes 3145728 | tf_op jit(solution)/shard_map/all_to_all | solution.py:123
  99.1 15.7 %copy-start.10 = (bf16[1,2,96,2048]{3,2,1,0:T(8,128)(2,1)S(1)}, bf16[1,2,96,2048]{3,2,1,0:T(8,128)(2,1)}, u32[]{:S(2)}) copy-start(bf16[1,2,96,2048]{3,2,1,0:T(8,128)(2,1)} %param.11) | copy-start | bytes 2359300
  99.8 11.9 %collective-permute-start.1 = (bf16[96,2048]{1,0:T(8,128)(2,1)S(1)}, bf16[96,2048]{1,0:T(8,128)(2,1)S(1)}, u32[]{:S(2)}, u32[]{:S(2)}) collective-permute-start(bf16[96,2048]{1,0:T(8,128)(2,1)S(1)} %get-tuple-element.28), channel_id=1, source_target_pairs={{8,0},{16,8},{24,16},{9,1},{17,9},{25,17},{10,2},{18,10},{26,18},{... | collective-permute-start | bytes 1179656 | tf_op jit(solution)/shard_map/ppermute | solution.py:10
  103.3 11.5 %collective-permute-start.2 = (bf16[96,2048]{1,0:T(8,128)(2,1)S(1)}, bf16[96,2048]{1,0:T(8,128)(2,1)S(1)}, u32[]{:S(2)}, u32[]{:S(2)}) collective-permute-start(bf16[96,2048]{1,0:T(8,128)(2,1)S(1)} %get-tuple-element.29), channel_id=1, source_target_pairs={{0,8},{8,16},{16,24},{1,9},{9,17},{17,25},{2,10},{10,18},{18,26},{... | collective-permute-start | bytes 1179656 | tf_op jit(solution)/shard_map/ppermute | solution.py:10
  106.4 21.6 %collective-permute-start.3 = (bf16[192,2048]{1,0:T(8,128)(2,1)}, bf16[192,2048]{1,0:T(8,128)(2,1)}, u32[]{:S(2)}, u32[]{:S(2)}) collective-permute-start(bf16[192,2048]{1,0:T(8,128)(2,1)} %bitcast.216), channel_id=1, source_target_pairs={{0,24},{8,16},{16,8},{24,0},{1,25},{9,17},{17,9},{25,1},{2,26},{10... | collective-permute-start | bytes 2359304 | tf_op jit(solution)/shard_map/ppermute | solution.py:15
  128.0 39.8 %all-to-all-start.2 = ((bf16[8,2,24,2048]{3,2,1,0:T(8,128)(2,1)}), bf16[8,2,24,2048]{3,2,1,0:T(8,128)(2,1)S(1)}, u32[]{:S(2)}, u32[]{:S(2)}) async-start(bf16[8,2,24,2048]{3,2,1,0:T(8,128)(2,1)} %bitcast.44), calls=%async_computation.2 | async-start | bytes 3145728 | tf_op jit(solution)/shard_map/all_to_all | solution.py:53
  131.7 2.8 %copy-start.2 = (bf16[2,2,1,1,192,2048]{5,4,3,2,1,0:T(8,128)(2,1)S(1)}, bf16[2,2,1,1,192,2048]{5,4,3,2,1,0:T(8,128)(2,1)}, u32[]{:S(2)}) copy-start(bf16[2,2,1,1,192,2048]{5,4,3,2,1,0:T(8,128)(2,1)} %param.12) | copy-start | bytes 9437188
  134.5 37.0 %copy-start.12 = (f32[192,512]{1,0:T(8,128)}, f32[192,512]{1,0:T(8,128)S(1)}, u32[]{:S(2)}) copy-start(f32[192,512]{1,0:T(8,128)S(1)} %fusion.21) | copy-start | bytes 1179652
  134.5 3.1 %copy-start.8 = (bf16[2,192,2048]{2,1,0:T(8,128)(2,1)S(1)}, bf16[2,192,2048]{2,1,0:T(8,128)(2,1)}, u32[]{:S(2)}) copy-start(bf16[2,192,2048]{2,1,0:T(8,128)(2,1)} %copy-done.7) | copy-start | bytes 4718596
  137.6 3.1 %copy-start.20 = (bf16[2,1,1,2048,512]{4,3,2,1,0:T(8,128)(2,1)S(1)}, bf16[2,1,1,2048,512]{4,3,2,1,0:T(8,128)(2,1)}, u32[]{:S(2)}) copy-start(bf16[2,1,1,2048,512]{4,3,2,1,0:T(8,128)(2,1)} %param.8) | copy-start | bytes 12582916
  144.7 24.1 %copy-start.25 = (f32[192,512]{1,0:T(8,128)S(1)}, f32[192,512]{1,0:T(8,128)}, u32[]{:S(2)}) copy-start(f32[192,512]{1,0:T(8,128)} %fusion.11) | copy-start | bytes 1179652
  167.8 1.9 copy-start.23
  168.8 3.2 %copy-start.3 = (bf16[8,1,24,2048]{3,2,1,0:T(8,128)(2,1)}, bf16[8,1,24,2048]{3,2,1,0:T(8,128)(2,1)S(1)}, u32[]{:S(2)}) copy-start(bf16[8,1,24,2048]{3,2,1,0:T(8,128)(2,1)S(1)} %get-tuple-element.22) | copy-start | bytes 2359300
  168.8 19.1 %collective-permute-start.4 = (bf16[192,2048]{1,0:T(8,128)(2,1)}, bf16[192,2048]{1,0:T(8,128)(2,1)}, u32[]{:S(2)}, u32[]{:S(2)}) collective-permute-start(bf16[192,2048]{1,0:T(8,128)(2,1)} %bitcast.49), channel_id=1, source_target_pairs={{0,24},{8,16},{16,8},{24,0},{1,25},{9,17},{17,9},{25,1},{2,26},{10... | collective-permute-start | bytes 2359304 | tf_op jit(solution)/shard_map/ppermute | solution.py:15
  169.6 2.4 %copy-start.21 = (bf16[2,1,1,2048,512]{4,3,2,1,0:T(8,128)(2,1)S(1)}, bf16[2,1,1,2048,512]{4,3,2,1,0:T(8,128)(2,1)}, u32[]{:S(2)}) copy-start(bf16[2,1,1,2048,512]{4,3,2,1,0:T(8,128)(2,1)} %param.8) | copy-start | bytes 12582916
  175.1 42.2 %all-to-all-start.3 = ((bf16[8,2,24,2048]{3,2,1,0:T(8,128)(2,1)}), bf16[8,2,24,2048]{3,2,1,0:T(8,128)(2,1)}, u32[]{:S(2)}, u32[]{:S(2)}) async-start(bf16[8,2,24,2048]{3,2,1,0:T(8,128)(2,1)} %pad_maximum_fusion.1), calls=%async_computation.3 | async-start | bytes 3145728 | tf_op jit(solution)/shard_map/all_to_all | solution.py:123
  179.6 2.0 copy-start.14
  179.6 2.1 copy-start.24
  183.6 4.3 %copy-start.16 = (f32[192,512]{1,0:T(8,128)S(1)}, f32[192,512]{1,0:T(8,128)}, u32[]{:S(2)}) copy-start(f32[192,512]{1,0:T(8,128)} %fusion.16) | copy-start | bytes 1179652
  189.5 2.2 copy-start
  (4 other events, 6.5 us)

commit v5 on v4

--- a/solution.py
+++ b/solution.py
@@ -94,7 +94,6 @@
         blocks = jnp.dot(one_hot, scaled.reshape(-1, model_width), preferred_element_type=jnp.float32)
         blocks = blocks.astype(jnp.bfloat16).reshape(experts, 2, capacity, model_width)
         if slope_mirror is not None:
-            blocks, slope_mirror = lax.optimization_barrier((blocks, slope_mirror))
             hidden_m, pair_grad_m = expert_grads(
                 slope_mirror, saved_mirror[tick_id - 1], w_in[0, 0, 0], w_out[0, 0, 0]
             )
@@ -121,6 +120,8 @@
         if tick_id == 0:
             back_blocks, saved_mirror = lax.optimization_barrier((back_blocks, saved_mirror))
         returned = lax.all_to_all(back_blocks, "expert", split_axis=0, concat_axis=0, tiled=True)
+        if tick_id + 1 < ticks:
+            returned, slope_mirror = lax.optimization_barrier((returned, slope_mirror))
         back_rows = left_product(one_hot, returned.reshape(-1, model_width))
         finished = (current.astype(jnp.float32) + back_rows.reshape(2, tokens, model_width)).astype(
             jnp.bfloat16

time: 222 us -> 205 us (0.923)
  waiting for transfers between devices: 122 us -> 105 us
    all_to_all x2, waiting for transfers between devices: 49.5 us -> 31.2 us  [on_device(): lax.all_to_all(back_blocks, 'expert', split_axis=0, concat_axis=0, tiled=...]
    ppermute x3, waiting for transfers between devices: 14.6 us -> 20.5 us  [mirrored(): return lax.ppermute(block, axis, [(i, count - 1 - i) for i in range(count)])]
    ppermute x2, waiting for transfers between devices: 7.9 us -> 4.61 us  [passed_along(): return lax.ppermute(block, axis, route)]
    unnamed x55 -> x61, local copies, waits for them, and re-layouts: 11 us -> 10.9 us
where the time goes in v5:
time: 205 us; the launch traced here: 204 us
  waiting for transfers between devices  105 us (51%)
  matrix products  44.7 us (22%)
  starting transfers between devices  30.4 us (15%)
  local copies, waits for them, and re-layouts  17.4 us (8%)
  other arithmetic  5.58 us (3%)
    all_to_all x2, waiting for transfers between devices, exchange(): lax.all_to_all(blocks, 'expert', split_axis=0, concat_axis=0, tiled=True)  48.1 us
    all_to_all x2, waiting for transfers between devices, on_device(): lax.all_to_all(back_blocks, 'expert', split_axis=0, concat_axis=0, tiled=...  31.2 us
    ppermute x3, waiting for transfers between devices, mirrored(): return lax.ppermute(block, axis, [(i, count - 1 - i) for i in range(count)])  20.5 us
    dot_general x10, matrix products, left_product(): lax.dot_general(left, right, (((0,), (0,)), ((), ())), preferred_element_...  16.7 us
    dot_general x6, matrix products, expert_grads(): gate_up = jnp.dot(saved_rows, weight_in, preferred_element_type=jnp.float32)  14.3 us
    unnamed x61, local copies, waits for them, and re-layouts  10.9 us
    dot_general x10, matrix products, right_product(): lax.dot_general(left, right, (((1,), (1,)), ((), ())), preferred_element_...  10.2 us
    all_to_all x2, starting transfers between devices, exchange(): lax.all_to_all(blocks, 'expert', split_axis=0, concat_axis=0, tiled=True)  9.95 us
  transfers between devices with their start and end apart: 9, of which 8 were waited for; matrix products, arithmetic and copies ran while one was open for 23% of the time, Pallas kernels for 0%

profile of v5, /device:TPU:1, one launch (start us, length us, event | category | flops | bytes accessed | tf_op | source)
XLA Modules:
  0.0 203.7 jit_solution(17280610309743925888)
XLA Ops:
  5.2 1.7 convolution_convert_fusion.1
  7.0 6.4 %all-to-all-start = ((bf16[8,2,24,2048]{3,2,1,0:T(8,128)(2,1)}), bf16[8,2,24,2048]{3,2,1,0:T(8,128)(2,1)S(1)}, u32[]{:S(2)}, u32[]{:S(2)}) async-start(bf16[8,2,24,2048]{3,2,1,0:T(8,128)(2,1)} %bitcast.13), calls=%async_computation | async-start | bytes 3145728 | tf_op jit(solution)/shard_map/all_to_all | solution.py:53
  13.3 2.9 %slice_bitcast_fusion = bf16[2,192,2048]{2,1,0:T(8,128)(2,1)} fusion(bf16[2,2,1,1,192,2048]{5,4,3,2,1,0:T(8,128)(2,1)} %param.12), kind=kLoop, calls=%fused_computation.44 | loop fusion | bytes 3145728 | tf_op jit(solution)/shard_map/squeeze | solution.py:84
  16.2 2.1 %collective-permute-start = (bf16[2,192,2048]{2,1,0:T(8,128)(2,1)}, bf16[2,192,2048]{2,1,0:T(8,128)(2,1)S(1)}, u32[]{:S(2)}, u32[]{:S(2)}) collective-permute-start(bf16[2,192,2048]{2,1,0:T(8,128)(2,1)} %slice_bitcast_fusion), channel_id=1, source_target_pairs={{0,24},{8,16},{16,8},{24,0},{1,25},{9,17},{17,9},{25,1},{2,26},{10... | collective-permute-start | bytes 4718600 | tf_op jit(solution)/shard_map/ppermute | solution.py:15
  18.3 2.9 %fusion.24 = f32[192,512]{1,0:T(8,128)} fusion(bf16[2,1,1,2048,512]{4,3,2,1,0:T(8,128)(2,1)} %param.8, bf16[2,2,1,1,192,2048]{5,4,3,2,1,0:T(8,128)(2,1)S(1)} %copy-done.1), kind=kOutput, calls=%fused_computation.36 | convolution fusion | flops 402653184 | bytes 3276800 | tf_op jit(solution)/shard_map/dot_general | solution.py:59
  22.6 27.0 %all-to-all-done = bf16[8,2,24,2048]{3,2,1,0:T(8,128)(2,1)S(1)} async-done(((bf16[8,2,24,2048]{3,2,1,0:T(8,128)(2,1)}), bf16[8,2,24,2048]{3,2,1,0:T(8,128)(2,1)S(1)}, u32[]{:S(2)}, u32[]{:S(2)}) %all-to-all-start) | async-done | bytes 1572896 | tf_op jit(solution)/shard_map/all_to_all | solution.py:53
  49.7 2.0 copy-done.25
  58.1 4.6 %all-to-all-start.1 = ((bf16[8,2,24,2048]{3,2,1,0:T(8,128)(2,1)}), bf16[8,2,24,2048]{3,2,1,0:T(8,128)(2,1)S(1)}, u32[]{:S(2)}, u32[]{:S(2)}) async-start(bf16[8,2,24,2048]{3,2,1,0:T(8,128)(2,1)} %pad_maximum_fusion), calls=%async_computation.1 | async-start | bytes 3145728 | tf_op jit(solution)/shard_map/all_to_all | solution.py:122
  62.7 1.9 collective-permute-start.1
  64.9 18.3 %collective-permute-done.1 = bf16[192,2048]{1,0:T(8,128)(2,1)S(1)} collective-permute-done((bf16[192,2048]{1,0:T(8,128)(2,1)}, bf16[192,2048]{1,0:T(8,128)(2,1)S(1)}, u32[]{:S(2)}, u32[]{:S(2)}) %collective-permute-start.1) | collective-permute-done | bytes 786464 | tf_op jit(solution)/shard_map/ppermute | solution.py:15
  83.2 15.9 %all-to-all-done.1 = bf16[8,2,24,2048]{3,2,1,0:T(8,128)(2,1)S(1)} async-done(((bf16[8,2,24,2048]{3,2,1,0:T(8,128)(2,1)}), bf16[8,2,24,2048]{3,2,1,0:T(8,128)(2,1)S(1)}, u32[]{:S(2)}, u32[]{:S(2)}) %all-to-all-start.1) | async-done | bytes 1572896 | tf_op jit(solution)/shard_map/all_to_all | solution.py:122
  99.8 3.6 %collective-permute-start.2 = (bf16[96,2048]{1,0:T(8,128)(2,1)S(1)}, bf16[96,2048]{1,0:T(8,128)(2,1)S(1)}, u32[]{:S(2)}, u32[]{:S(2)}) collective-permute-start(bf16[96,2048]{1,0:T(8,128)(2,1)S(1)} %get-tuple-element.28), channel_id=1, source_target_pairs={{8,0},{16,8},{24,16},{9,1},{17,9},{25,17},{10,2},{18,10},{26,18},{... | collective-permute-start | bytes 1179656 | tf_op jit(solution)/shard_map/ppermute | solution.py:10
  103.4 3.0 %collective-permute-start.3 = (bf16[96,2048]{1,0:T(8,128)(2,1)S(1)}, bf16[96,2048]{1,0:T(8,128)(2,1)S(1)}, u32[]{:S(2)}, u32[]{:S(2)}) collective-permute-start(bf16[96,2048]{1,0:T(8,128)(2,1)S(1)} %get-tuple-element.29), channel_id=1, source_target_pairs={{0,8},{8,16},{16,24},{1,9},{9,17},{17,25},{2,10},{10,18},{18,26},{... | collective-permute-start | bytes 1179656 | tf_op jit(solution)/shard_map/ppermute | solution.py:10
  106.5 3.4 %collective-permute-done.2 = bf16[96,2048]{1,0:T(8,128)(2,1)S(1)} collective-permute-done((bf16[96,2048]{1,0:T(8,128)(2,1)S(1)}, bf16[96,2048]{1,0:T(8,128)(2,1)S(1)}, u32[]{:S(2)}, u32[]{:S(2)}) %collective-permute-start.2) | collective-permute-done | bytes 393248 | tf_op jit(solution)/shard_map/ppermute | solution.py:10
  111.5 1.7 convolution_convert_fusion
  113.2 3.6 %all-to-all-start.2 = ((bf16[8,2,24,2048]{3,2,1,0:T(8,128)(2,1)}), bf16[8,2,24,2048]{3,2,1,0:T(8,128)(2,1)S(1)}, u32[]{:S(2)}, u32[]{:S(2)}) async-start(bf16[8,2,24,2048]{3,2,1,0:T(8,128)(2,1)} %bitcast.44), calls=%async_computation.2 | async-start | bytes 3145728 | tf_op jit(solution)/shard_map/all_to_all | solution.py:53
  117.0 2.5 %fusion.21 = f32[192,512]{1,0:T(8,128)S(1)} fusion(bf16[2,1,1,2048,512]{4,3,2,1,0:T(8,128)(2,1)} %param.8, bf16[2,2,1,1,192,2048]{5,4,3,2,1,0:T(8,128)(2,1)} %param.12), kind=kOutput, calls=%fused_computation.33 | convolution fusion | flops 402653184 | bytes 3276800 | tf_op jit(solution)/shard_map/dot_general | solution.py:59
  119.8 3.1 %fusion.11 = f32[192,512]{1,0:T(8,128)} fusion(bf16[2,1,1,2048,512]{4,3,2,1,0:T(8,128)(2,1)} %param.8, bf16[2,2,1,1,192,2048]{5,4,3,2,1,0:T(8,128)(2,1)S(1)} %copy-done.2), kind=kOutput, calls=%fused_computation.23 | convolution fusion | flops 402653184 | bytes 3276800 | tf_op jit(solution)/shard_map/dot_general | solution.py:59
  122.9 3.1 %fusion.16 = f32[192,512]{1,0:T(8,128)} fusion(bf16[2,1,1,2048,512]{4,3,2,1,0:T(8,128)(2,1)} %param.8, bf16[2,192,2048]{2,1,0:T(8,128)(2,1)S(1)} %copy-done.8), kind=kOutput, calls=%fused_computation.28 | convolution fusion | flops 402653184 | bytes 3276800 | tf_op jit(solution)/shard_map/dot_general | solution.py:59
  127.3 2.7 %fusion.61 = f32[512,2048]{1,0:T(8,128)} fusion(bf16[2,2,1,1,192,2048]{5,4,3,2,1,0:T(8,128)(2,1)S(1)} %copy-done.2, bf16[192,256]{1,0:T(8,128)(2,1)S(1)} %get-tuple-element.39, bf16[192,256]{1,0:T(8,128)(2,1)S(1)} %get-tuple-element.38), kind=kOutput, calls=%fused_computation.79 | convolution fusion | flops 403046400 | bytes 5177344 | tf_op jit(solution)/shard_map/dot_general | solution.py:19
  130.0 21.2 %all-to-all-done.2 = bf16[8,2,24,2048]{3,2,1,0:T(8,128)(2,1)S(1)} async-done(((bf16[8,2,24,2048]{3,2,1,0:T(8,128)(2,1)}), bf16[8,2,24,2048]{3,2,1,0:T(8,128)(2,1)S(1)}, u32[]{:S(2)}, u32[]{:S(2)}) %all-to-all-start.2) | async-done | bytes 1572896 | tf_op jit(solution)/shard_map/all_to_all | solution.py:53
  153.0 1.8 fusion.82
  158.5 4.5 %all-to-all-start.3 = ((bf16[8,2,24,2048]{3,2,1,0:T(8,128)(2,1)}), bf16[8,2,24,2048]{3,2,1,0:T(8,128)(2,1)}, u32[]{:S(2)}, u32[]{:S(2)}) async-start(bf16[8,2,24,2048]{3,2,1,0:T(8,128)(2,1)} %pad_maximum_fusion.1), calls=%async_computation.3 | async-start | bytes 3145728 | tf_op jit(solution)/shard_map/all_to_all | solution.py:122
  163.0 1.9 fusion.104
  164.9 1.9 multiply_convert_fusion.7
  167.6 2.2 %collective-permute-done.4 = bf16[192,2048]{1,0:T(8,128)(2,1)} collective-permute-done((bf16[192,2048]{1,0:T(8,128)(2,1)}, bf16[192,2048]{1,0:T(8,128)(2,1)}, u32[]{:S(2)}, u32[]{:S(2)}) %collective-permute-start.4) | collective-permute-done | bytes 786464 | tf_op jit(solution)/shard_map/ppermute | solution.py:15
  169.8 1.6 multiply_convert_fusion.5
  173.6 3.2 %fusion.1 = bf16[1,1,2048,512]{2,3,1,0:T(8,128)(2,1)} fusion(bf16[2048,512]{0,1:T(8,128)(2,1)S(1)} %add_convert_fusion, f32[512,2048]{1,0:T(8,128)S(1)} %copy-done, bf16[2,2,1,1,192,2048]{5,4,3,2,1,0:T(8,128)(2,1)} %param.12, bf16[192,256]{1,0:T(8,128)(2,1)S(1)} %get-tuple-element.35, bf16[192,256]{1,0:T(8,128)(2,1)S(1)} %get-tuple-element.34), kind=kOutput, calls=%fused_computation.5 | convolution fusion | flops 407240704 | bytes 9371648 | tf_op jit(solution)/shard_map/dot_general | solution.py:19
  176.9 3.9 %copy.35 = bf16[1,1,2048,512]{3,2,1,0:T(8,128)(2,1)} copy(bf16[1,1,2048,512]{2,3,1,0:T(8,128)(2,1)} %fusion.1) | data formatting | bytes 4194304
  180.8 1.9 fusion.105
  185.5 15.3 %all-to-all-done.3 = bf16[8,2,24,2048]{3,2,1,0:T(8,128)(2,1)} async-done(((bf16[8,2,24,2048]{3,2,1,0:T(8,128)(2,1)}), bf16[8,2,24,2048]{3,2,1,0:T(8,128)(2,1)}, u32[]{:S(2)}, u32[]{:S(2)}) %all-to-all-start.3) | async-done | bytes 1572896 | tf_op jit(solution)/shard_map/all_to_all | solution.py:122
  200.8 2.9 %fusion.9 = bf16[2,1,96,2048]{3,2,1,0:T(8,128)(2,1)} fusion(pred[2,96,384]{2,1,0:T(32,128)(4,1)S(1)} %bitcast.221, bf16[384,2048,1]{1,0,2:T(8,128)(2,1)} %bitcast.54, bf16[1,96,2048]{2,1,0:T(8,128)(2,1)S(1)} %get-tuple-element.27, bf16[1,96,2048]{2,1,0:T(8,128)(2,1)S(1)} %get-tuple-element.26), kind=kOutput, calls=%fused_computation.21 | convolution fusion | flops 303562752 | bytes 3219456 | tf_op jit(solution)/shard_map/dot_general | solution.py:19
  (107 shorter events, 27.8 us)
Async XLA Ops:
  7.0 42.6 %all-to-all-start = ((bf16[8,2,24,2048]{3,2,1,0:T(8,128)(2,1)}), bf16[8,2,24,2048]{3,2,1,0:T(8,128)(2,1)S(1)}, u32[]{:S(2)}, u32[]{:S(2)}) async-start(bf16[8,2,24,2048]{3,2,1,0:T(8,128)(2,1)} %bitcast.13), calls=%async_computation | async-start | bytes 3145728 | tf_op jit(solution)/shard_map/all_to_all | solution.py:53
  13.3 5.0 %copy-start.1 = (bf16[2,2,1,1,192,2048]{5,4,3,2,1,0:T(8,128)(2,1)S(1)}, bf16[2,2,1,1,192,2048]{5,4,3,2,1,0:T(8,128)(2,1)}, u32[]{:S(2)}) copy-start(bf16[2,2,1,1,192,2048]{5,4,3,2,1,0:T(8,128)(2,1)} %param.12) | copy-start | bytes 9437188
  16.2 5.0 %copy-start.21 = (bf16[2,1,1,2048,512]{4,3,2,1,0:T(8,128)(2,1)S(1)}, bf16[2,1,1,2048,512]{4,3,2,1,0:T(8,128)(2,1)}, u32[]{:S(2)}) copy-start(bf16[2,1,1,2048,512]{4,3,2,1,0:T(8,128)(2,1)} %param.8) | copy-start | bytes 12582916
  16.2 40.7 %collective-permute-start = (bf16[2,192,2048]{2,1,0:T(8,128)(2,1)}, bf16[2,192,2048]{2,1,0:T(8,128)(2,1)S(1)}, u32[]{:S(2)}, u32[]{:S(2)}) collective-permute-start(bf16[2,192,2048]{2,1,0:T(8,128)(2,1)} %slice_bitcast_fusion), channel_id=1, source_target_pairs={{0,24},{8,16},{16,8},{24,0},{1,25},{9,17},{17,9},{25,1},{2,26},{10... | collective-permute-start | bytes 4718600 | tf_op jit(solution)/shard_map/ppermute | solution.py:15
  49.5 2.2 %copy-start.25 = (bf16[2,1,1,256,2048]{4,3,2,1,0:T(8,128)(2,1)S(1)}, bf16[2,1,1,256,2048]{4,3,2,1,0:T(8,128)(2,1)}, u32[]{:S(2)}) copy-start(bf16[2,1,1,256,2048]{4,3,2,1,0:T(8,128)(2,1)} %param.9) | copy-start | bytes 6291460
  49.5 2.2 %copy-start.29 = (f32[192,512]{1,0:T(8,128)S(1)}, f32[192,512]{1,0:T(8,128)}, u32[]{:S(2)}) copy-start(f32[192,512]{1,0:T(8,128)} %fusion.14) | copy-start | bytes 1179652
  49.6 3.1 %copy-start.6 = (bf16[8,1,24,2048]{3,2,1,0:T(8,128)(2,1)}, bf16[8,1,24,2048]{3,2,1,0:T(8,128)(2,1)S(1)}, u32[]{:S(2)}) copy-start(bf16[8,1,24,2048]{3,2,1,0:T(8,128)(2,1)S(1)} %get-tuple-element.24) | copy-start | bytes 2359300
  49.6 3.1 %copy-start.14 = (bf16[8,1,24,2048]{3,2,1,0:T(8,128)(2,1)}, bf16[8,1,24,2048]{3,2,1,0:T(8,128)(2,1)S(1)}, u32[]{:S(2)}) copy-start(bf16[8,1,24,2048]{3,2,1,0:T(8,128)(2,1)S(1)} %get-tuple-element.25) | copy-start | bytes 2359300
  49.7 2.6 %copy-start.18 = (f32[192,512]{1,0:T(8,128)S(1)}, f32[192,512]{1,0:T(8,128)}, u32[]{:S(2)}) copy-start(f32[192,512]{1,0:T(8,128)} %fusion.24) | copy-start | bytes 1179652
  51.7 2.2 %copy-start.22 = (bf16[2,1,1,2048,512]{4,3,2,1,0:T(8,128)(2,1)S(1)}, bf16[2,1,1,2048,512]{4,3,2,1,0:T(8,128)(2,1)}, u32[]{:S(2)}) copy-start(bf16[2,1,1,2048,512]{4,3,2,1,0:T(8,128)(2,1)} %param.8) | copy-start | bytes 12582916
  56.9 42.2 %copy-start.5 = (bf16[2,1,96,2048]{3,2,1,0:T(8,128)(2,1)S(1)}, bf16[2,1,96,2048]{3,2,1,0:T(8,128)(2,1)}, u32[]{:S(2)}) copy-start(bf16[2,1,96,2048]{3,2,1,0:T(8,128)(2,1)} %param.10) | copy-start | bytes 2359300
  58.1 41.0 %all-to-all-start.1 = ((bf16[8,2,24,2048]{3,2,1,0:T(8,128)(2,1)}), bf16[8,2,24,2048]{3,2,1,0:T(8,128)(2,1)S(1)}, u32[]{:S(2)}, u32[]{:S(2)}) async-start(bf16[8,2,24,2048]{3,2,1,0:T(8,128)(2,1)} %pad_maximum_fusion), calls=%async_computation.1 | async-start | bytes 3145728 | tf_op jit(solution)/shard_map/all_to_all | solution.py:122
  62.7 20.5 %collective-permute-start.1 = (bf16[192,2048]{1,0:T(8,128)(2,1)}, bf16[192,2048]{1,0:T(8,128)(2,1)S(1)}, u32[]{:S(2)}, u32[]{:S(2)}) collective-permute-start(bf16[192,2048]{1,0:T(8,128)(2,1)} %bitcast.216), channel_id=1, source_target_pairs={{0,24},{8,16},{16,8},{24,0},{1,25},{9,17},{17,9},{25,1},{2,26},{10... | collective-permute-start | bytes 2359304 | tf_op jit(solution)/shard_map/ppermute | solution.py:15
  83.2 16.6 %copy-start.10 = (bf16[192,2048]{1,0:T(8,128)(2,1)}, bf16[192,2048]{1,0:T(8,128)(2,1)S(1)}, u32[]{:S(2)}) copy-start(bf16[192,2048]{1,0:T(8,128)(2,1)S(1)} %collective-permute-done.1) | copy-start | bytes 2359300
  99.7 11.5 %copy-start.13 = (bf16[1,2,96,2048]{3,2,1,0:T(8,128)(2,1)S(1)}, bf16[1,2,96,2048]{3,2,1,0:T(8,128)(2,1)}, u32[]{:S(2)}) copy-start(bf16[1,2,96,2048]{3,2,1,0:T(8,128)(2,1)} %param.11) | copy-start | bytes 2359300
  99.8 10.2 %collective-permute-start.2 = (bf16[96,2048]{1,0:T(8,128)(2,1)S(1)}, bf16[96,2048]{1,0:T(8,128)(2,1)S(1)}, u32[]{:S(2)}, u32[]{:S(2)}) collective-permute-start(bf16[96,2048]{1,0:T(8,128)(2,1)S(1)} %get-tuple-element.28), channel_id=1, source_target_pairs={{8,0},{16,8},{24,16},{9,1},{17,9},{25,17},{10,2},{18,10},{26,18},{... | collective-permute-start | bytes 1179656 | tf_op jit(solution)/shard_map/ppermute | solution.py:10
  103.4 7.7 %collective-permute-start.3 = (bf16[96,2048]{1,0:T(8,128)(2,1)S(1)}, bf16[96,2048]{1,0:T(8,128)(2,1)S(1)}, u32[]{:S(2)}, u32[]{:S(2)}) collective-permute-start(bf16[96,2048]{1,0:T(8,128)(2,1)S(1)} %get-tuple-element.29), channel_id=1, source_target_pairs={{0,8},{8,16},{16,24},{1,9},{9,17},{17,25},{2,10},{10,18},{18,26},{... | collective-permute-start | bytes 1179656 | tf_op jit(solution)/shard_map/ppermute | solution.py:10
  113.2 37.9 %all-to-all-start.2 = ((bf16[8,2,24,2048]{3,2,1,0:T(8,128)(2,1)}), bf16[8,2,24,2048]{3,2,1,0:T(8,128)(2,1)S(1)}, u32[]{:S(2)}, u32[]{:S(2)}) async-start(bf16[8,2,24,2048]{3,2,1,0:T(8,128)(2,1)} %bitcast.44), calls=%async_computation.2 | async-start | bytes 3145728 | tf_op jit(solution)/shard_map/all_to_all | solution.py:53
  117.0 2.8 %copy-start.2 = (bf16[2,2,1,1,192,2048]{5,4,3,2,1,0:T(8,128)(2,1)S(1)}, bf16[2,2,1,1,192,2048]{5,4,3,2,1,0:T(8,128)(2,1)}, u32[]{:S(2)}) copy-start(bf16[2,2,1,1,192,2048]{5,4,3,2,1,0:T(8,128)(2,1)} %param.12) | copy-start | bytes 9437188
  119.8 35.1 %copy-start.15 = (f32[192,512]{1,0:T(8,128)}, f32[192,512]{1,0:T(8,128)S(1)}, u32[]{:S(2)}) copy-start(f32[192,512]{1,0:T(8,128)S(1)} %fusion.21) | copy-start | bytes 1179652
  119.8 3.1 %copy-start.8 = (bf16[2,192,2048]{2,1,0:T(8,128)(2,1)S(1)}, bf16[2,192,2048]{2,1,0:T(8,128)(2,1)}, u32[]{:S(2)}) copy-start(bf16[2,192,2048]{2,1,0:T(8,128)(2,1)} %copy-done.7) | copy-start | bytes 4718596
  122.9 3.1 %copy-start.23 = (bf16[2,1,1,2048,512]{4,3,2,1,0:T(8,128)(2,1)S(1)}, bf16[2,1,1,2048,512]{4,3,2,1,0:T(8,128)(2,1)}, u32[]{:S(2)}) copy-start(bf16[2,1,1,2048,512]{4,3,2,1,0:T(8,128)(2,1)} %param.8) | copy-start | bytes 12582916
  130.0 22.9 %copy-start.28 = (f32[192,512]{1,0:T(8,128)S(1)}, f32[192,512]{1,0:T(8,128)}, u32[]{:S(2)}) copy-start(f32[192,512]{1,0:T(8,128)} %fusion.11) | copy-start | bytes 1179652
  152.1 3.2 %copy-start.3 = (bf16[8,1,24,2048]{3,2,1,0:T(8,128)(2,1)}, bf16[8,1,24,2048]{3,2,1,0:T(8,128)(2,1)S(1)}, u32[]{:S(2)}) copy-start(bf16[8,1,24,2048]{3,2,1,0:T(8,128)(2,1)S(1)} %get-tuple-element.22) | copy-start | bytes 2359300
  152.1 17.7 %collective-permute-start.4 = (bf16[192,2048]{1,0:T(8,128)(2,1)}, bf16[192,2048]{1,0:T(8,128)(2,1)}, u32[]{:S(2)}, u32[]{:S(2)}) collective-permute-start(bf16[192,2048]{1,0:T(8,128)(2,1)} %bitcast.49), channel_id=1, source_target_pairs={{0,24},{8,16},{16,8},{24,0},{1,25},{9,17},{17,9},{25,1},{2,26},{10... | collective-permute-start | bytes 2359304 | tf_op jit(solution)/shard_map/ppermute | solution.py:15
  153.0 2.4 %copy-start.24 = (bf16[2,1,1,2048,512]{4,3,2,1,0:T(8,128)(2,1)S(1)}, bf16[2,1,1,2048,512]{4,3,2,1,0:T(8,128)(2,1)}, u32[]{:S(2)}) copy-start(bf16[2,1,1,2048,512]{4,3,2,1,0:T(8,128)(2,1)} %param.8) | copy-start | bytes 12582916
  158.5 42.3 %all-to-all-start.3 = ((bf16[8,2,24,2048]{3,2,1,0:T(8,128)(2,1)}), bf16[8,2,24,2048]{3,2,1,0:T(8,128)(2,1)}, u32[]{:S(2)}, u32[]{:S(2)}) async-start(bf16[8,2,24,2048]{3,2,1,0:T(8,128)(2,1)} %pad_maximum_fusion.1), calls=%async_computation.3 | async-start | bytes 3145728 | tf_op jit(solution)/shard_map/all_to_all | solution.py:122
  163.0 1.9 copy-start.11
  163.0 1.9 copy-start.17
  166.8 3.0 %copy-start.19 = (f32[192,512]{1,0:T(8,128)S(1)}, f32[192,512]{1,0:T(8,128)}, u32[]{:S(2)}) copy-start(f32[192,512]{1,0:T(8,128)} %fusion.16) | copy-start | bytes 1179652
  166.8 3.0 %copy-start.27 = (bf16[2,1,1,256,2048]{4,3,2,1,0:T(8,128)(2,1)S(1)}, bf16[2,1,1,256,2048]{4,3,2,1,0:T(8,128)(2,1)}, u32[]{:S(2)}) copy-start(bf16[2,1,1,256,2048]{4,3,2,1,0:T(8,128)(2,1)} %param.9) | copy-start | bytes 6291460
  171.4 2.2 %copy-start = (f32[512,2048]{1,0:T(8,128)S(1)}, f32[512,2048]{1,0:T(8,128)}, u32[]{:S(2)}) copy-start(f32[512,2048]{1,0:T(8,128)} %fusion.61) | copy-start | bytes 12582916
  (7 other events, 11.0 us)

commit v6 on v5

--- a/solution.py
+++ b/solution.py
@@ -48,10 +48,14 @@
     return (rows[:, None] == slots[None, :]).astype(jnp.bfloat16)
 
 
-def exchange(blocks):
-    experts, ways, capacity, model_width = blocks.shape
+def exchange(blocks, ways):
+    experts, rows, model_width = blocks.shape
+    capacity = rows // ways
     arrived = lax.all_to_all(blocks, "expert", split_axis=0, concat_axis=0, tiled=True)
-    return [arrived[:, way_id].reshape(experts * capacity, model_width) for way_id in range(ways)]
+    return [
+        arrived[:, way_id * capacity:(way_id + 1) * capacity].reshape(experts * capacity, model_width)
+        for way_id in range(ways)
+    ]
 
 
 def expert_grads(slope_rows, saved_rows, weight_in, weight_out):
@@ -92,7 +96,7 @@
         one_hot = placement(routes[tick_id, :, 0], counts[tick_id, :, 0, 0], capacity)
         scaled = (probs[tick_id, :, 0][:, :, None] * current.astype(jnp.float32)).astype(jnp.bfloat16)
         blocks = jnp.dot(one_hot, scaled.reshape(-1, model_width), preferred_element_type=jnp.float32)
-        blocks = blocks.astype(jnp.bfloat16).reshape(experts, 2, capacity, model_width)
+        blocks = blocks.astype(jnp.bfloat16).reshape(experts, 2 * capacity, model_width)
         if slope_mirror is not None:
             hidden_m, pair_grad_m = expert_grads(
                 slope_mirror, saved_mirror[tick_id - 1], w_in[0, 0, 0], w_out[0, 0, 0]
@@ -102,7 +106,7 @@
             )
             mirror_in = mirror_in + part_in
             mirror_out = mirror_out + part_out
-        slopes = exchange(blocks)
+        slopes = exchange(blocks, 2)
         input_grads = []
         for way_id in range(2):
             saved_rows = saved[tick_id, way_id, 0, 0]
@@ -110,7 +114,7 @@
                 slopes[way_id], saved_rows, w_in[way_id, 0, 0], w_out[way_id, 0, 0]
             )
             input_grad = right_product(pair_grad, w_in[way_id, 0, 0]).astype(jnp.bfloat16)
-            input_grads.append(input_grad.reshape(experts, 1, capacity, model_width))
+            input_grads.append(input_grad.reshape(experts, capacity, model_width))
             if way_id == 0:
                 part_in, part_out = weight_terms(saved_rows, slopes[0], hidden, pair_grad)
                 own_in = own_in + part_in

time: 205 us -> 205 us (level)
  no operation moved by 1% of the time
where the time goes in v6:
time: 205 us; the launch traced here: 204 us
  waiting for transfers between devices  105 us (51%)
  matrix products  44.7 us (22%)
  starting transfers between devices  30.4 us (15%)
  local copies, waits for them, and re-layouts  17.4 us (8%)
  other arithmetic  5.49 us (3%)
    all_to_all x2, waiting for transfers between devices, exchange(): lax.all_to_all(blocks, 'expert', split_axis=0, concat_axis=0, tiled=True)  48.1 us
    all_to_all x2, waiting for transfers between devices, on_device(): lax.all_to_all(back_blocks, 'expert', split_axis=0, concat_axis=0, tiled=...  31.2 us
    ppermute x3, waiting for transfers between devices, mirrored(): return lax.ppermute(block, axis, [(i, count - 1 - i) for i in range(count)])  20.6 us
    dot_general x10, matrix products, left_product(): lax.dot_general(left, right, (((0,), (0,)), ((), ())), preferred_element_...  16.7 us
    dot_general x6, matrix products, expert_grads(): gate_up = jnp.dot(saved_rows, weight_in, preferred_element_type=jnp.float32)  14.3 us
    unnamed x61, local copies, waits for them, and re-layouts  10.9 us
    dot_general x10, matrix products, right_product(): lax.dot_general(left, right, (((1,), (1,)), ((), ())), preferred_element_...  10.2 us
    all_to_all x2, starting transfers between devices, exchange(): lax.all_to_all(blocks, 'expert', split_axis=0, concat_axis=0, tiled=True)  9.95 us
  transfers between devices with their start and end apart: 9, of which 8 were waited for; matrix products, arithmetic and copies ran while one was open for 23% of the time, Pallas kernels for 0%

profile of v6, /device:TPU:1, one launch (start us, length us, event | category | flops | bytes accessed | tf_op | source)
XLA Modules:
  0.0 203.6 jit_solution(10437558092014412760)
XLA Ops:
  5.2 1.7 convolution_convert_fusion.1
  7.0 6.4 %all-to-all-start = ((bf16[8,48,2048]{2,1,0:T(8,128)(2,1)}), bf16[8,48,2048]{2,1,0:T(8,128)(2,1)S(1)}, u32[]{:S(2)}, u32[]{:S(2)}) async-start(bf16[8,48,2048]{2,1,0:T(8,128)(2,1)} %bitcast.13), calls=%async_computation | async-start | bytes 3145728 | tf_op jit(solution)/shard_map/all_to_all | solution.py:54
  13.3 2.9 %slice_bitcast_fusion = bf16[2,192,2048]{2,1,0:T(8,128)(2,1)} fusion(bf16[2,2,1,1,192,2048]{5,4,3,2,1,0:T(8,128)(2,1)} %param.12), kind=kLoop, calls=%fused_computation.44 | loop fusion | bytes 3145728 | tf_op jit(solution)/shard_map/squeeze | solution.py:88
  16.2 2.1 %collective-permute-start = (bf16[2,192,2048]{2,1,0:T(8,128)(2,1)}, bf16[2,192,2048]{2,1,0:T(8,128)(2,1)S(1)}, u32[]{:S(2)}, u32[]{:S(2)}) collective-permute-start(bf16[2,192,2048]{2,1,0:T(8,128)(2,1)} %slice_bitcast_fusion), channel_id=1, source_target_pairs={{0,24},{8,16},{16,8},{24,0},{1,25},{9,17},{17,9},{25,1},{2,26},{10... | collective-permute-start | bytes 4718600 | tf_op jit(solution)/shard_map/ppermute | solution.py:15
  18.3 2.9 %fusion.24 = f32[192,512]{1,0:T(8,128)} fusion(bf16[2,1,1,2048,512]{4,3,2,1,0:T(8,128)(2,1)} %param.8, bf16[2,2,1,1,192,2048]{5,4,3,2,1,0:T(8,128)(2,1)S(1)} %copy-done.1), kind=kOutput, calls=%fused_computation.36 | convolution fusion | flops 402653184 | bytes 3276800 | tf_op jit(solution)/shard_map/dot_general | solution.py:63
  22.6 27.0 %all-to-all-done = bf16[8,48,2048]{2,1,0:T(8,128)(2,1)S(1)} async-done(((bf16[8,48,2048]{2,1,0:T(8,128)(2,1)}), bf16[8,48,2048]{2,1,0:T(8,128)(2,1)S(1)}, u32[]{:S(2)}, u32[]{:S(2)}) %all-to-all-start) | async-done | bytes 1572896 | tf_op jit(solution)/shard_map/all_to_all | solution.py:54
  49.7 2.0 copy-done.25
  58.0 4.6 %all-to-all-start.1 = ((bf16[8,48,2048]{2,1,0:T(8,128)(2,1)}), bf16[8,48,2048]{2,1,0:T(8,128)(2,1)S(1)}, u32[]{:S(2)}, u32[]{:S(2)}) async-start(bf16[8,48,2048]{2,1,0:T(8,128)(2,1)} %pad_maximum_fusion), calls=%async_computation.1 | async-start | bytes 3145728 | tf_op jit(solution)/shard_map/all_to_all | solution.py:126
  62.7 1.9 collective-permute-start.1
  64.8 18.3 %collective-permute-done.1 = bf16[192,2048]{1,0:T(8,128)(2,1)S(1)} collective-permute-done((bf16[192,2048]{1,0:T(8,128)(2,1)}, bf16[192,2048]{1,0:T(8,128)(2,1)S(1)}, u32[]{:S(2)}, u32[]{:S(2)}) %collective-permute-start.1) | collective-permute-done | bytes 786464 | tf_op jit(solution)/shard_map/ppermute | solution.py:15
  83.1 15.9 %all-to-all-done.1 = bf16[8,48,2048]{2,1,0:T(8,128)(2,1)S(1)} async-done(((bf16[8,48,2048]{2,1,0:T(8,128)(2,1)}), bf16[8,48,2048]{2,1,0:T(8,128)(2,1)S(1)}, u32[]{:S(2)}, u32[]{:S(2)}) %all-to-all-start.1) | async-done | bytes 1572896 | tf_op jit(solution)/shard_map/all_to_all | solution.py:126
  99.7 3.6 %collective-permute-start.2 = (bf16[96,2048]{1,0:T(8,128)(2,1)S(1)}, bf16[96,2048]{1,0:T(8,128)(2,1)S(1)}, u32[]{:S(2)}, u32[]{:S(2)}) collective-permute-start(bf16[96,2048]{1,0:T(8,128)(2,1)S(1)} %get-tuple-element.25), channel_id=1, source_target_pairs={{8,0},{16,8},{24,16},{9,1},{17,9},{25,17},{10,2},{18,10},{26,18},{... | collective-permute-start | bytes 1179656 | tf_op jit(solution)/shard_map/ppermute | solution.py:10
  103.4 3.0 %collective-permute-start.3 = (bf16[96,2048]{1,0:T(8,128)(2,1)S(1)}, bf16[96,2048]{1,0:T(8,128)(2,1)S(1)}, u32[]{:S(2)}, u32[]{:S(2)}) collective-permute-start(bf16[96,2048]{1,0:T(8,128)(2,1)S(1)} %get-tuple-element.26), channel_id=1, source_target_pairs={{0,8},{8,16},{16,24},{1,9},{9,17},{17,25},{2,10},{10,18},{18,26},{... | collective-permute-start | bytes 1179656 | tf_op jit(solution)/shard_map/ppermute | solution.py:10
  106.5 3.4 %collective-permute-done.2 = bf16[96,2048]{1,0:T(8,128)(2,1)S(1)} collective-permute-done((bf16[96,2048]{1,0:T(8,128)(2,1)S(1)}, bf16[96,2048]{1,0:T(8,128)(2,1)S(1)}, u32[]{:S(2)}, u32[]{:S(2)}) %collective-permute-start.2) | collective-permute-done | bytes 393248 | tf_op jit(solution)/shard_map/ppermute | solution.py:10
  111.4 1.7 convolution_convert_fusion
  113.2 3.6 %all-to-all-start.2 = ((bf16[8,48,2048]{2,1,0:T(8,128)(2,1)}), bf16[8,48,2048]{2,1,0:T(8,128)(2,1)S(1)}, u32[]{:S(2)}, u32[]{:S(2)}) async-start(bf16[8,48,2048]{2,1,0:T(8,128)(2,1)} %bitcast.42), calls=%async_computation.2 | async-start | bytes 3145728 | tf_op jit(solution)/shard_map/all_to_all | solution.py:54
  117.0 2.5 %fusion.21 = f32[192,512]{1,0:T(8,128)S(1)} fusion(bf16[2,1,1,2048,512]{4,3,2,1,0:T(8,128)(2,1)} %param.8, bf16[2,2,1,1,192,2048]{5,4,3,2,1,0:T(8,128)(2,1)} %param.12), kind=kOutput, calls=%fused_computation.33 | convolution fusion | flops 402653184 | bytes 3276800 | tf_op jit(solution)/shard_map/dot_general | solution.py:63
  119.7 3.1 %fusion.11 = f32[192,512]{1,0:T(8,128)} fusion(bf16[2,1,1,2048,512]{4,3,2,1,0:T(8,128)(2,1)} %param.8, bf16[2,2,1,1,192,2048]{5,4,3,2,1,0:T(8,128)(2,1)S(1)} %copy-done.2), kind=kOutput, calls=%fused_computation.23 | convolution fusion | flops 402653184 | bytes 3276800 | tf_op jit(solution)/shard_map/dot_general | solution.py:63
  122.8 3.1 %fusion.16 = f32[192,512]{1,0:T(8,128)} fusion(bf16[2,1,1,2048,512]{4,3,2,1,0:T(8,128)(2,1)} %param.8, bf16[2,192,2048]{2,1,0:T(8,128)(2,1)S(1)} %copy-done.8), kind=kOutput, calls=%fused_computation.28 | convolution fusion | flops 402653184 | bytes 3276800 | tf_op jit(solution)/shard_map/dot_general | solution.py:63
  127.2 2.7 %fusion.61 = f32[512,2048]{1,0:T(8,128)} fusion(bf16[2,2,1,1,192,2048]{5,4,3,2,1,0:T(8,128)(2,1)S(1)} %copy-done.2, bf16[192,256]{1,0:T(8,128)(2,1)S(1)} %get-tuple-element.36, bf16[192,256]{1,0:T(8,128)(2,1)S(1)} %get-tuple-element.35), kind=kOutput, calls=%fused_computation.79 | convolution fusion | flops 403046400 | bytes 5177344 | tf_op jit(solution)/shard_map/dot_general | solution.py:19
  129.9 21.2 %all-to-all-done.2 = bf16[8,48,2048]{2,1,0:T(8,128)(2,1)S(1)} async-done(((bf16[8,48,2048]{2,1,0:T(8,128)(2,1)}), bf16[8,48,2048]{2,1,0:T(8,128)(2,1)S(1)}, u32[]{:S(2)}, u32[]{:S(2)}) %all-to-all-start.2) | async-done | bytes 1572896 | tf_op jit(solution)/shard_map/all_to_all | solution.py:54
  153.0 1.8 fusion.82
  158.4 4.5 %all-to-all-start.3 = ((bf16[8,48,2048]{2,1,0:T(8,128)(2,1)}), bf16[8,48,2048]{2,1,0:T(8,128)(2,1)}, u32[]{:S(2)}, u32[]{:S(2)}) async-start(bf16[8,48,2048]{2,1,0:T(8,128)(2,1)} %pad_maximum_fusion.1), calls=%async_computation.3 | async-start | bytes 3145728 | tf_op jit(solution)/shard_map/all_to_all | solution.py:126
  162.9 1.9 fusion.104
  164.8 1.9 multiply_convert_fusion.7
  167.5 2.3 %collective-permute-done.4 = bf16[192,2048]{1,0:T(8,128)(2,1)} collective-permute-done((bf16[192,2048]{1,0:T(8,128)(2,1)}, bf16[192,2048]{1,0:T(8,128)(2,1)}, u32[]{:S(2)}, u32[]{:S(2)}) %collective-permute-start.4) | collective-permute-done | bytes 786464 | tf_op jit(solution)/shard_map/ppermute | solution.py:15
  169.8 1.6 multiply_convert_fusion.5
  173.6 3.2 %fusion.1 = bf16[1,1,2048,512]{2,3,1,0:T(8,128)(2,1)} fusion(bf16[2048,512]{0,1:T(8,128)(2,1)S(1)} %add_convert_fusion, f32[512,2048]{1,0:T(8,128)S(1)} %copy-done, bf16[2,2,1,1,192,2048]{5,4,3,2,1,0:T(8,128)(2,1)} %param.12, bf16[192,256]{1,0:T(8,128)(2,1)S(1)} %get-tuple-element.32, bf16[192,256]{1,0:T(8,128)(2,1)S(1)} %get-tuple-element.31), kind=kOutput, calls=%fused_computation.5 | convolution fusion | flops 407240704 | bytes 9371648 | tf_op jit(solution)/shard_map/dot_general | solution.py:19
  176.8 3.9 %copy.20 = bf16[1,1,2048,512]{3,2,1,0:T(8,128)(2,1)} copy(bf16[1,1,2048,512]{2,3,1,0:T(8,128)(2,1)} %fusion.1) | data formatting | bytes 4194304
  180.8 1.9 fusion.105
  185.4 15.3 %all-to-all-done.3 = bf16[8,48,2048]{2,1,0:T(8,128)(2,1)} async-done(((bf16[8,48,2048]{2,1,0:T(8,128)(2,1)}), bf16[8,48,2048]{2,1,0:T(8,128)(2,1)}, u32[]{:S(2)}, u32[]{:S(2)}) %all-to-all-start.3) | async-done | bytes 1572896 | tf_op jit(solution)/shard_map/all_to_all | solution.py:126
  200.7 2.9 %fusion.9 = bf16[2,1,96,2048]{3,2,1,0:T(8,128)(2,1)} fusion(pred[2,96,384]{2,1,0:T(32,128)(4,1)S(1)} %bitcast.213, bf16[384,2048,1]{1,0,2:T(8,128)(2,1)} %bitcast.50, bf16[1,96,2048]{2,1,0:T(8,128)(2,1)S(1)} %get-tuple-element.24, bf16[1,96,2048]{2,1,0:T(8,128)(2,1)S(1)} %get-tuple-element.23), kind=kOutput, calls=%fused_computation.21 | convolution fusion | flops 303562752 | bytes 3219456 | tf_op jit(solution)/shard_map/dot_general | solution.py:19
  (107 shorter events, 27.7 us)
Async XLA Ops:
  7.0 42.6 %all-to-all-start = ((bf16[8,48,2048]{2,1,0:T(8,128)(2,1)}), bf16[8,48,2048]{2,1,0:T(8,128)(2,1)S(1)}, u32[]{:S(2)}, u32[]{:S(2)}) async-start(bf16[8,48,2048]{2,1,0:T(8,128)(2,1)} %bitcast.13), calls=%async_computation | async-start | bytes 3145728 | tf_op jit(solution)/shard_map/all_to_all | solution.py:54
  13.3 5.0 %copy-start.1 = (bf16[2,2,1,1,192,2048]{5,4,3,2,1,0:T(8,128)(2,1)S(1)}, bf16[2,2,1,1,192,2048]{5,4,3,2,1,0:T(8,128)(2,1)}, u32[]{:S(2)}) copy-start(bf16[2,2,1,1,192,2048]{5,4,3,2,1,0:T(8,128)(2,1)} %param.12) | copy-start | bytes 9437188
  16.2 5.0 %copy-start.21 = (bf16[2,1,1,2048,512]{4,3,2,1,0:T(8,128)(2,1)S(1)}, bf16[2,1,1,2048,512]{4,3,2,1,0:T(8,128)(2,1)}, u32[]{:S(2)}) copy-start(bf16[2,1,1,2048,512]{4,3,2,1,0:T(8,128)(2,1)} %param.8) | copy-start | bytes 12582916
  16.2 40.6 %collective-permute-start = (bf16[2,192,2048]{2,1,0:T(8,128)(2,1)}, bf16[2,192,2048]{2,1,0:T(8,128)(2,1)S(1)}, u32[]{:S(2)}, u32[]{:S(2)}) collective-permute-start(bf16[2,192,2048]{2,1,0:T(8,128)(2,1)} %slice_bitcast_fusion), channel_id=1, source_target_pairs={{0,24},{8,16},{16,8},{24,0},{1,25},{9,17},{17,9},{25,1},{2,26},{10... | collective-permute-start | bytes 4718600 | tf_op jit(solution)/shard_map/ppermute | solution.py:15
  49.5 2.2 %copy-start.25 = (bf16[2,1,1,256,2048]{4,3,2,1,0:T(8,128)(2,1)S(1)}, bf16[2,1,1,256,2048]{4,3,2,1,0:T(8,128)(2,1)}, u32[]{:S(2)}) copy-start(bf16[2,1,1,256,2048]{4,3,2,1,0:T(8,128)(2,1)} %param.9) | copy-start | bytes 6291460
  49.5 2.2 %copy-start.29 = (f32[192,512]{1,0:T(8,128)S(1)}, f32[192,512]{1,0:T(8,128)}, u32[]{:S(2)}) copy-start(f32[192,512]{1,0:T(8,128)} %fusion.14) | copy-start | bytes 1179652
  49.6 3.1 %copy-start.6 = (bf16[8,24,2048]{2,1,0:T(8,128)(2,1)}, bf16[8,24,2048]{2,1,0:T(8,128)(2,1)S(1)}, u32[]{:S(2)}) copy-start(bf16[8,24,2048]{2,1,0:T(8,128)(2,1)S(1)} %get-tuple-element.21) | copy-start | bytes 2359300
  49.6 3.1 %copy-start.14 = (bf16[8,24,2048]{2,1,0:T(8,128)(2,1)}, bf16[8,24,2048]{2,1,0:T(8,128)(2,1)S(1)}, u32[]{:S(2)}) copy-start(bf16[8,24,2048]{2,1,0:T(8,128)(2,1)S(1)} %get-tuple-element.22) | copy-start | bytes 2359300
  49.7 2.6 %copy-start.18 = (f32[192,512]{1,0:T(8,128)S(1)}, f32[192,512]{1,0:T(8,128)}, u32[]{:S(2)}) copy-start(f32[192,512]{1,0:T(8,128)} %fusion.24) | copy-start | bytes 1179652
  51.7 2.2 %copy-start.22 = (bf16[2,1,1,2048,512]{4,3,2,1,0:T(8,128)(2,1)S(1)}, bf16[2,1,1,2048,512]{4,3,2,1,0:T(8,128)(2,1)}, u32[]{:S(2)}) copy-start(bf16[2,1,1,2048,512]{4,3,2,1,0:T(8,128)(2,1)} %param.8) | copy-start | bytes 12582916
  56.9 42.2 %copy-start.5 = (bf16[2,1,96,2048]{3,2,1,0:T(8,128)(2,1)S(1)}, bf16[2,1,96,2048]{3,2,1,0:T(8,128)(2,1)}, u32[]{:S(2)}) copy-start(bf16[2,1,96,2048]{3,2,1,0:T(8,128)(2,1)} %param.10) | copy-start | bytes 2359300
  58.0 41.0 %all-to-all-start.1 = ((bf16[8,48,2048]{2,1,0:T(8,128)(2,1)}), bf16[8,48,2048]{2,1,0:T(8,128)(2,1)S(1)}, u32[]{:S(2)}, u32[]{:S(2)}) async-start(bf16[8,48,2048]{2,1,0:T(8,128)(2,1)} %pad_maximum_fusion), calls=%async_computation.1 | async-start | bytes 3145728 | tf_op jit(solution)/shard_map/all_to_all | solution.py:126
  62.7 20.5 %collective-permute-start.1 = (bf16[192,2048]{1,0:T(8,128)(2,1)}, bf16[192,2048]{1,0:T(8,128)(2,1)S(1)}, u32[]{:S(2)}, u32[]{:S(2)}) collective-permute-start(bf16[192,2048]{1,0:T(8,128)(2,1)} %bitcast.208), channel_id=1, source_target_pairs={{0,24},{8,16},{16,8},{24,0},{1,25},{9,17},{17,9},{25,1},{2,26},{10... | collective-permute-start | bytes 2359304 | tf_op jit(solution)/shard_map/ppermute | solution.py:15
  83.1 16.6 %copy-start.10 = (bf16[192,2048]{1,0:T(8,128)(2,1)}, bf16[192,2048]{1,0:T(8,128)(2,1)S(1)}, u32[]{:S(2)}) copy-start(bf16[192,2048]{1,0:T(8,128)(2,1)S(1)} %collective-permute-done.1) | copy-start | bytes 2359300
  99.6 11.5 %copy-start.13 = (bf16[1,2,96,2048]{3,2,1,0:T(8,128)(2,1)S(1)}, bf16[1,2,96,2048]{3,2,1,0:T(8,128)(2,1)}, u32[]{:S(2)}) copy-start(bf16[1,2,96,2048]{3,2,1,0:T(8,128)(2,1)} %param.11) | copy-start | bytes 2359300
  99.7 10.2 %collective-permute-start.2 = (bf16[96,2048]{1,0:T(8,128)(2,1)S(1)}, bf16[96,2048]{1,0:T(8,128)(2,1)S(1)}, u32[]{:S(2)}, u32[]{:S(2)}) collective-permute-start(bf16[96,2048]{1,0:T(8,128)(2,1)S(1)} %get-tuple-element.25), channel_id=1, source_target_pairs={{8,0},{16,8},{24,16},{9,1},{17,9},{25,17},{10,2},{18,10},{26,18},{... | collective-permute-start | bytes 1179656 | tf_op jit(solution)/shard_map/ppermute | solution.py:10
  103.4 7.7 %collective-permute-start.3 = (bf16[96,2048]{1,0:T(8,128)(2,1)S(1)}, bf16[96,2048]{1,0:T(8,128)(2,1)S(1)}, u32[]{:S(2)}, u32[]{:S(2)}) collective-permute-start(bf16[96,2048]{1,0:T(8,128)(2,1)S(1)} %get-tuple-element.26), channel_id=1, source_target_pairs={{0,8},{8,16},{16,24},{1,9},{9,17},{17,25},{2,10},{10,18},{18,26},{... | collective-permute-start | bytes 1179656 | tf_op jit(solution)/shard_map/ppermute | solution.py:10
  113.2 37.9 %all-to-all-start.2 = ((bf16[8,48,2048]{2,1,0:T(8,128)(2,1)}), bf16[8,48,2048]{2,1,0:T(8,128)(2,1)S(1)}, u32[]{:S(2)}, u32[]{:S(2)}) async-start(bf16[8,48,2048]{2,1,0:T(8,128)(2,1)} %bitcast.42), calls=%async_computation.2 | async-start | bytes 3145728 | tf_op jit(solution)/shard_map/all_to_all | solution.py:54
  117.0 2.8 %copy-start.2 = (bf16[2,2,1,1,192,2048]{5,4,3,2,1,0:T(8,128)(2,1)S(1)}, bf16[2,2,1,1,192,2048]{5,4,3,2,1,0:T(8,128)(2,1)}, u32[]{:S(2)}) copy-start(bf16[2,2,1,1,192,2048]{5,4,3,2,1,0:T(8,128)(2,1)} %param.12) | copy-start | bytes 9437188
  119.7 35.1 %copy-start.15 = (f32[192,512]{1,0:T(8,128)}, f32[192,512]{1,0:T(8,128)S(1)}, u32[]{:S(2)}) copy-start(f32[192,512]{1,0:T(8,128)S(1)} %fusion.21) | copy-start | bytes 1179652
  119.7 3.1 %copy-start.8 = (bf16[2,192,2048]{2,1,0:T(8,128)(2,1)S(1)}, bf16[2,192,2048]{2,1,0:T(8,128)(2,1)}, u32[]{:S(2)}) copy-start(bf16[2,192,2048]{2,1,0:T(8,128)(2,1)} %copy-done.7) | copy-start | bytes 4718596
  122.8 3.1 %copy-start.23 = (bf16[2,1,1,2048,512]{4,3,2,1,0:T(8,128)(2,1)S(1)}, bf16[2,1,1,2048,512]{4,3,2,1,0:T(8,128)(2,1)}, u32[]{:S(2)}) copy-start(bf16[2,1,1,2048,512]{4,3,2,1,0:T(8,128)(2,1)} %param.8) | copy-start | bytes 12582916
  129.9 22.9 %copy-start.28 = (f32[192,512]{1,0:T(8,128)S(1)}, f32[192,512]{1,0:T(8,128)}, u32[]{:S(2)}) copy-start(f32[192,512]{1,0:T(8,128)} %fusion.11) | copy-start | bytes 1179652
  152.1 3.2 %copy-start.3 = (bf16[8,24,2048]{2,1,0:T(8,128)(2,1)}, bf16[8,24,2048]{2,1,0:T(8,128)(2,1)S(1)}, u32[]{:S(2)}) copy-start(bf16[8,24,2048]{2,1,0:T(8,128)(2,1)S(1)} %get-tuple-element.19) | copy-start | bytes 2359300
  152.1 17.7 %collective-permute-start.4 = (bf16[192,2048]{1,0:T(8,128)(2,1)}, bf16[192,2048]{1,0:T(8,128)(2,1)}, u32[]{:S(2)}, u32[]{:S(2)}) collective-permute-start(bf16[192,2048]{1,0:T(8,128)(2,1)} %bitcast.46), channel_id=1, source_target_pairs={{0,24},{8,16},{16,8},{24,0},{1,25},{9,17},{17,9},{25,1},{2,26},{10... | collective-permute-start | bytes 2359304 | tf_op jit(solution)/shard_map/ppermute | solution.py:15
  153.0 2.4 %copy-start.24 = (bf16[2,1,1,2048,512]{4,3,2,1,0:T(8,128)(2,1)S(1)}, bf16[2,1,1,2048,512]{4,3,2,1,0:T(8,128)(2,1)}, u32[]{:S(2)}) copy-start(bf16[2,1,1,2048,512]{4,3,2,1,0:T(8,128)(2,1)} %param.8) | copy-start | bytes 12582916
  158.4 42.3 %all-to-all-start.3 = ((bf16[8,48,2048]{2,1,0:T(8,128)(2,1)}), bf16[8,48,2048]{2,1,0:T(8,128)(2,1)}, u32[]{:S(2)}, u32[]{:S(2)}) async-start(bf16[8,48,2048]{2,1,0:T(8,128)(2,1)} %pad_maximum_fusion.1), calls=%async_computation.3 | async-start | bytes 3145728 | tf_op jit(solution)/shard_map/all_to_all | solution.py:126
  162.9 1.9 copy-start.11
  162.9 1.9 copy-start.17
  166.7 3.0 %copy-start.19 = (f32[192,512]{1,0:T(8,128)S(1)}, f32[192,512]{1,0:T(8,128)}, u32[]{:S(2)}) copy-start(f32[192,512]{1,0:T(8,128)} %fusion.16) | copy-start | bytes 1179652
  166.7 3.0 %copy-start.27 = (bf16[2,1,1,256,2048]{4,3,2,1,0:T(8,128)(2,1)S(1)}, bf16[2,1,1,256,2048]{4,3,2,1,0:T(8,128)(2,1)}, u32[]{:S(2)}) copy-start(bf16[2,1,1,256,2048]{4,3,2,1,0:T(8,128)(2,1)} %param.9) | copy-start | bytes 6291460
  171.4 2.2 %copy-start = (f32[512,2048]{1,0:T(8,128)S(1)}, f32[512,2048]{1,0:T(8,128)}, u32[]{:S(2)}) copy-start(f32[512,2048]{1,0:T(8,128)} %fusion.61) | copy-start | bytes 12582916
  (7 other events, 11.0 us)

commit v7 on v6

--- a/solution.py
+++ b/solution.py
@@ -107,6 +107,8 @@
             mirror_in = mirror_in + part_in
             mirror_out = mirror_out + part_out
         slopes = exchange(blocks, 2)
+        if tick_id == 0:
+            slopes, saved_mirror = lax.optimization_barrier((slopes, saved_mirror))
         input_grads = []
         for way_id in range(2):
             saved_rows = saved[tick_id, way_id, 0, 0]
@@ -121,8 +123,6 @@
                 own_out = own_out + part_out
         slope_mirror = mirrored(slopes[1], "section")
         back_blocks = jnp.concatenate(input_grads, axis=1)
-        if tick_id == 0:
-            back_blocks, saved_mirror = lax.optimization_barrier((back_blocks, saved_mirror))
         returned = lax.all_to_all(back_blocks, "expert", split_axis=0, concat_axis=0, tiled=True)
         if tick_id + 1 < ticks:
             returned, slope_mirror = lax.optimization_barrier((returned, slope_mirror))

time: 205 us -> 207 us (level)
  waiting for transfers between devices: 105 us -> 112 us
  matrix products: 44.7 us -> 41.9 us
    ppermute x3, waiting for transfers between devices: 20.6 us -> 27.8 us  [mirrored(): return lax.ppermute(block, axis, [(i, count - 1 - i) for i in range(count)])]
    unnamed x61 -> x69, local copies, waits for them, and re-layouts: 10.9 us -> 8.94 us
  transfers between devices with their start and end apart: 9 -> 9, of which waited for: 8 -> 9; matrix products, arithmetic and copies ran while one was open for 23% -> 20% of each run, Pallas kernels for 0% -> 0%
where the time goes in v7:
time: 207 us; the launch traced here: 206 us
  waiting for transfers between devices  112 us (54%)
  matrix products  41.9 us (20%)
  starting transfers between devices  30.5 us (15%)
  local copies, waits for them, and re-layouts  15.5 us (7%)
  other arithmetic  5.42 us (3%)
    all_to_all x2, waiting for transfers between devices, exchange(): lax.all_to_all(blocks, 'expert', split_axis=0, concat_axis=0, tiled=True)  47.9 us
    all_to_all x2, waiting for transfers between devices, on_device(): lax.all_to_all(back_blocks, 'expert', split_axis=0, concat_axis=0, tiled=...  31.4 us
    ppermute x3, waiting for transfers between devices, mirrored(): return lax.ppermute(block, axis, [(i, count - 1 - i) for i in range(count)])  27.8 us
    dot_general x10, matrix products, left_product(): lax.dot_general(left, right, (((0,), (0,)), ((), ())), preferred_element_...  15.4 us
    dot_general x6, matrix products, expert_grads(): gate_up = jnp.dot(saved_rows, weight_in, preferred_element_type=jnp.float32)  14.2 us
    all_to_all x2, starting transfers between devices, exchange(): lax.all_to_all(blocks, 'expert', split_axis=0, concat_axis=0, tiled=True)  10.7 us
    all_to_all x2, starting transfers between devices, on_device(): lax.all_to_all(back_blocks, 'expert', split_axis=0, concat_axis=0, tiled=...  10.5 us
    unnamed x69, local copies, waits for them, and re-layouts  8.94 us
  transfers between devices with their start and end apart: 9, of which 9 were waited for; matrix products, arithmetic and copies ran while one was open for 20% of the time, Pallas kernels for 0%

profile of v7, /device:TPU:1, one launch (start us, length us, event | category | flops | bytes accessed | tf_op | source)
XLA Modules:
  0.0 206.2 jit_solution(2331825382402490753)
XLA Ops:
  5.2 1.7 convolution_convert_fusion.1
  7.0 6.4 %all-to-all-start = ((bf16[8,48,2048]{2,1,0:T(8,128)(2,1)}), bf16[8,48,2048]{2,1,0:T(8,128)(2,1)S(1)}, u32[]{:S(2)}, u32[]{:S(2)}) async-start(bf16[8,48,2048]{2,1,0:T(8,128)(2,1)} %bitcast.13), calls=%async_computation | async-start | bytes 3145728 | tf_op jit(solution)/shard_map/all_to_all | solution.py:54
  13.3 2.9 %slice_bitcast_fusion = bf16[2,192,2048]{2,1,0:T(8,128)(2,1)} fusion(bf16[2,2,1,1,192,2048]{5,4,3,2,1,0:T(8,128)(2,1)} %param.12), kind=kLoop, calls=%fused_computation.44 | loop fusion | bytes 3145728 | tf_op jit(solution)/shard_map/squeeze | solution.py:88
  16.2 2.1 collective-permute-start
  18.3 2.9 %fusion.24 = f32[192,512]{1,0:T(8,128)} fusion(bf16[2,1,1,2048,512]{4,3,2,1,0:T(8,128)(2,1)} %param.8, bf16[2,2,1,1,192,2048]{5,4,3,2,1,0:T(8,128)(2,1)S(1)} %copy-done.1), kind=kOutput, calls=%fused_computation.36 | convolution fusion | flops 402653184 | bytes 3276800 | tf_op jit(solution)/shard_map/dot_general | solution.py:63
  22.6 26.9 %all-to-all-done = bf16[8,48,2048]{2,1,0:T(8,128)(2,1)S(1)} async-done(((bf16[8,48,2048]{2,1,0:T(8,128)(2,1)}), bf16[8,48,2048]{2,1,0:T(8,128)(2,1)S(1)}, u32[]{:S(2)}, u32[]{:S(2)}) %all-to-all-start) | async-done | bytes 1572896 | tf_op jit(solution)/shard_map/all_to_all | solution.py:54
  49.7 4.0 %collective-permute-done = bf16[2,192,2048]{2,1,0:T(8,128)(2,1)S(1)} collective-permute-done((bf16[2,192,2048]{2,1,0:T(8,128)(2,1)}, bf16[2,192,2048]{2,1,0:T(8,128)(2,1)S(1)}, u32[]{:S(2)}, u32[]{:S(2)}) %collective-permute-start) | collective-permute-done | bytes 1572896 | tf_op jit(solution)/shard_map/ppermute | solution.py:15
  54.9 1.6 copy-done.25
  59.4 5.8 %all-to-all-start.1 = ((bf16[8,48,2048]{2,1,0:T(8,128)(2,1)}), bf16[8,48,2048]{2,1,0:T(8,128)(2,1)S(1)}, u32[]{:S(2)}, u32[]{:S(2)}) async-start(bf16[8,48,2048]{2,1,0:T(8,128)(2,1)} %pad_maximum_fusion), calls=%async_computation.1 | async-start | bytes 3145728 | tf_op jit(solution)/shard_map/all_to_all | solution.py:126
  66.7 18.8 %collective-permute-done.1 = bf16[192,2048]{1,0:T(8,128)(2,1)S(1)} collective-permute-done((bf16[192,2048]{1,0:T(8,128)(2,1)}, bf16[192,2048]{1,0:T(8,128)(2,1)S(1)}, u32[]{:S(2)}, u32[]{:S(2)}) %collective-permute-start.1) | collective-permute-done | bytes 786464 | tf_op jit(solution)/shard_map/ppermute | solution.py:15
  85.5 16.1 %all-to-all-done.1 = bf16[8,48,2048]{2,1,0:T(8,128)(2,1)S(1)} async-done(((bf16[8,48,2048]{2,1,0:T(8,128)(2,1)}), bf16[8,48,2048]{2,1,0:T(8,128)(2,1)S(1)}, u32[]{:S(2)}, u32[]{:S(2)}) %all-to-all-start.1) | async-done | bytes 1572896 | tf_op jit(solution)/shard_map/all_to_all | solution.py:126
  102.4 3.5 %collective-permute-start.2 = (bf16[96,2048]{1,0:T(8,128)(2,1)S(1)}, bf16[96,2048]{1,0:T(8,128)(2,1)S(1)}, u32[]{:S(2)}, u32[]{:S(2)}) collective-permute-start(bf16[96,2048]{1,0:T(8,128)(2,1)S(1)} %get-tuple-element.27), channel_id=1, source_target_pairs={{8,0},{16,8},{24,16},{9,1},{17,9},{25,17},{10,2},{18,10},{26,18},{... | collective-permute-start | bytes 1179656 | tf_op jit(solution)/shard_map/ppermute | solution.py:10
  105.9 2.2 %collective-permute-start.3 = (bf16[96,2048]{1,0:T(8,128)(2,1)S(1)}, bf16[96,2048]{1,0:T(8,128)(2,1)S(1)}, u32[]{:S(2)}, u32[]{:S(2)}) collective-permute-start(bf16[96,2048]{1,0:T(8,128)(2,1)S(1)} %get-tuple-element.28), channel_id=1, source_target_pairs={{0,8},{8,16},{16,24},{1,9},{9,17},{17,25},{2,10},{10,18},{18,26},{... | collective-permute-start | bytes 1179656 | tf_op jit(solution)/shard_map/ppermute | solution.py:10
  108.2 3.4 %collective-permute-done.2 = bf16[96,2048]{1,0:T(8,128)(2,1)S(1)} collective-permute-done((bf16[96,2048]{1,0:T(8,128)(2,1)S(1)}, bf16[96,2048]{1,0:T(8,128)(2,1)S(1)}, u32[]{:S(2)}, u32[]{:S(2)}) %collective-permute-start.2) | collective-permute-done | bytes 393248 | tf_op jit(solution)/shard_map/ppermute | solution.py:10
  113.1 1.7 convolution_convert_fusion
  114.8 4.3 %all-to-all-start.2 = ((bf16[8,48,2048]{2,1,0:T(8,128)(2,1)}), bf16[8,48,2048]{2,1,0:T(8,128)(2,1)S(1)}, u32[]{:S(2)}, u32[]{:S(2)}) async-start(bf16[8,48,2048]{2,1,0:T(8,128)(2,1)} %bitcast.42), calls=%async_computation.2 | async-start | bytes 3145728 | tf_op jit(solution)/shard_map/all_to_all | solution.py:54
  119.4 3.3 %fusion.21 = f32[192,512]{1,0:T(8,128)} fusion(bf16[2,1,1,2048,512]{4,3,2,1,0:T(8,128)(2,1)} %param.8, bf16[2,2,1,1,192,2048]{5,4,3,2,1,0:T(8,128)(2,1)} %param.12), kind=kOutput, calls=%fused_computation.33 | convolution fusion | flops 402653184 | bytes 3276800 | tf_op jit(solution)/shard_map/dot_general | solution.py:63
  122.7 3.0 %fusion.11 = f32[192,512]{1,0:T(8,128)} fusion(bf16[2,1,1,2048,512]{4,3,2,1,0:T(8,128)(2,1)} %param.8, bf16[2,2,1,1,192,2048]{5,4,3,2,1,0:T(8,128)(2,1)S(1)} %copy-done.2), kind=kOutput, calls=%fused_computation.23 | convolution fusion | flops 402653184 | bytes 3276800 | tf_op jit(solution)/shard_map/dot_general | solution.py:63
  125.8 3.1 %fusion.16 = f32[192,512]{1,0:T(8,128)} fusion(bf16[2,1,1,2048,512]{4,3,2,1,0:T(8,128)(2,1)} %param.8, bf16[2,192,2048]{2,1,0:T(8,128)(2,1)S(1)} %copy-done.9), kind=kOutput, calls=%fused_computation.28 | convolution fusion | flops 402653184 | bytes 3276800 | tf_op jit(solution)/shard_map/dot_general | solution.py:63
  129.4 2.7 %fusion.61 = f32[512,2048]{1,0:T(8,128)} fusion(bf16[2,2,1,1,192,2048]{5,4,3,2,1,0:T(8,128)(2,1)S(1)} %copy-done.2, bf16[192,256]{1,0:T(8,128)(2,1)S(1)} %get-tuple-element.38, bf16[192,256]{1,0:T(8,128)(2,1)S(1)} %get-tuple-element.37), kind=kOutput, calls=%fused_computation.79 | convolution fusion | flops 403046400 | bytes 5177344 | tf_op jit(solution)/shard_map/dot_general | solution.py:19
  132.6 21.0 %all-to-all-done.2 = bf16[8,48,2048]{2,1,0:T(8,128)(2,1)S(1)} async-done(((bf16[8,48,2048]{2,1,0:T(8,128)(2,1)}), bf16[8,48,2048]{2,1,0:T(8,128)(2,1)S(1)}, u32[]{:S(2)}, u32[]{:S(2)}) %all-to-all-start.2) | async-done | bytes 1572896 | tf_op jit(solution)/shard_map/all_to_all | solution.py:54
  155.5 1.8 fusion.82
  160.9 4.6 %all-to-all-start.3 = ((bf16[8,48,2048]{2,1,0:T(8,128)(2,1)}), bf16[8,48,2048]{2,1,0:T(8,128)(2,1)}, u32[]{:S(2)}, u32[]{:S(2)}) async-start(bf16[8,48,2048]{2,1,0:T(8,128)(2,1)} %pad_maximum_fusion.1), calls=%async_computation.3 | async-start | bytes 3145728 | tf_op jit(solution)/shard_map/all_to_all | solution.py:126
  167.3 5.0 %collective-permute-done.4 = bf16[192,2048]{1,0:T(8,128)(2,1)} collective-permute-done((bf16[192,2048]{1,0:T(8,128)(2,1)}, bf16[192,2048]{1,0:T(8,128)(2,1)}, u32[]{:S(2)}, u32[]{:S(2)}) %collective-permute-start.4) | collective-permute-done | bytes 786464 | tf_op jit(solution)/shard_map/ppermute | solution.py:15
  172.3 1.7 multiply_convert_fusion.5
  174.8 1.4 copy-done
  176.2 3.3 %fusion.1 = bf16[1,1,2048,512]{2,3,1,0:T(8,128)(2,1)} fusion(bf16[2048,512]{0,1:T(8,128)(2,1)S(1)} %add_convert_fusion, f32[512,2048]{1,0:T(8,128)S(1)} %copy-done, bf16[2,2,1,1,192,2048]{5,4,3,2,1,0:T(8,128)(2,1)} %param.12, bf16[192,256]{1,0:T(8,128)(2,1)S(1)} %get-tuple-element.34, bf16[192,256]{1,0:T(8,128)(2,1)S(1)} %get-tuple-element.33), kind=kOutput, calls=%fused_computation.5 | convolution fusion | flops 407240704 | bytes 9371648 | tf_op jit(solution)/shard_map/dot_general | solution.py:19
  179.5 3.9 %copy.20 = bf16[1,1,2048,512]{3,2,1,0:T(8,128)(2,1)} copy(bf16[1,1,2048,512]{2,3,1,0:T(8,128)(2,1)} %fusion.1) | data formatting | bytes 4194304
  183.4 1.9 fusion.105
  186.5 1.5 fusion.8
  188.1 15.2 %all-to-all-done.3 = bf16[8,48,2048]{2,1,0:T(8,128)(2,1)} async-done(((bf16[8,48,2048]{2,1,0:T(8,128)(2,1)}), bf16[8,48,2048]{2,1,0:T(8,128)(2,1)}, u32[]{:S(2)}, u32[]{:S(2)}) %all-to-all-start.3) | async-done | bytes 1572896 | tf_op jit(solution)/shard_map/all_to_all | solution.py:126
  203.3 2.9 %fusion.9 = bf16[2,1,96,2048]{3,2,1,0:T(8,128)(2,1)} fusion(pred[2,96,384]{2,1,0:T(32,128)(4,1)S(1)} %bitcast.213, bf16[384,2048,1]{1,0,2:T(8,128)(2,1)} %bitcast.50, bf16[1,96,2048]{2,1,0:T(8,128)(2,1)S(1)} %get-tuple-element.26, bf16[1,96,2048]{2,1,0:T(8,128)(2,1)S(1)} %get-tuple-element.25), kind=kOutput, calls=%fused_computation.21 | convolution fusion | flops 303562752 | bytes 3219456 | tf_op jit(solution)/shard_map/dot_general | solution.py:19
  (115 shorter events, 24.3 us)
Async XLA Ops:
  7.0 42.6 %all-to-all-start = ((bf16[8,48,2048]{2,1,0:T(8,128)(2,1)}), bf16[8,48,2048]{2,1,0:T(8,128)(2,1)S(1)}, u32[]{:S(2)}, u32[]{:S(2)}) async-start(bf16[8,48,2048]{2,1,0:T(8,128)(2,1)} %bitcast.13), calls=%async_computation | async-start | bytes 3145728 | tf_op jit(solution)/shard_map/all_to_all | solution.py:54
  13.3 5.0 %copy-start.1 = (bf16[2,2,1,1,192,2048]{5,4,3,2,1,0:T(8,128)(2,1)S(1)}, bf16[2,2,1,1,192,2048]{5,4,3,2,1,0:T(8,128)(2,1)}, u32[]{:S(2)}) copy-start(bf16[2,2,1,1,192,2048]{5,4,3,2,1,0:T(8,128)(2,1)} %param.12) | copy-start | bytes 9437188
  16.2 5.0 %copy-start.24 = (bf16[2,1,1,2048,512]{4,3,2,1,0:T(8,128)(2,1)S(1)}, bf16[2,1,1,2048,512]{4,3,2,1,0:T(8,128)(2,1)}, u32[]{:S(2)}) copy-start(bf16[2,1,1,2048,512]{4,3,2,1,0:T(8,128)(2,1)} %param.8) | copy-start | bytes 12582916
  16.2 37.4 %collective-permute-start = (bf16[2,192,2048]{2,1,0:T(8,128)(2,1)}, bf16[2,192,2048]{2,1,0:T(8,128)(2,1)S(1)}, u32[]{:S(2)}, u32[]{:S(2)}) collective-permute-start(bf16[2,192,2048]{2,1,0:T(8,128)(2,1)} %slice_bitcast_fusion), channel_id=1, source_target_pairs={{0,24},{8,16},{16,8},{24,0},{1,25},{9,17},{17,9},{25,1},{2,26},{10... | collective-permute-start | bytes 4718600 | tf_op jit(solution)/shard_map/ppermute | solution.py:15
  49.5 4.2 %copy-start.28 = (bf16[2,1,1,256,2048]{4,3,2,1,0:T(8,128)(2,1)S(1)}, bf16[2,1,1,256,2048]{4,3,2,1,0:T(8,128)(2,1)}, u32[]{:S(2)}) copy-start(bf16[2,1,1,256,2048]{4,3,2,1,0:T(8,128)(2,1)} %param.9) | copy-start | bytes 6291460
  49.5 4.2 %copy-start.33 = (f32[192,512]{1,0:T(8,128)S(1)}, f32[192,512]{1,0:T(8,128)}, u32[]{:S(2)}) copy-start(f32[192,512]{1,0:T(8,128)} %fusion.14) | copy-start | bytes 1179652
  49.6 5.1 %copy-start.3 = (bf16[8,24,2048]{2,1,0:T(8,128)(2,1)}, bf16[8,24,2048]{2,1,0:T(8,128)(2,1)S(1)}, u32[]{:S(2)}) copy-start(bf16[8,24,2048]{2,1,0:T(8,128)(2,1)S(1)} %get-tuple-element.24) | copy-start | bytes 2359300
  49.6 5.1 %copy-start.15 = (bf16[8,24,2048]{2,1,0:T(8,128)(2,1)}, bf16[8,24,2048]{2,1,0:T(8,128)(2,1)S(1)}, u32[]{:S(2)}) copy-start(bf16[8,24,2048]{2,1,0:T(8,128)(2,1)S(1)} %get-tuple-element.23) | copy-start | bytes 2359300
  49.7 4.6 %copy-start.16 = (f32[192,512]{1,0:T(8,128)S(1)}, f32[192,512]{1,0:T(8,128)}, u32[]{:S(2)}) copy-start(f32[192,512]{1,0:T(8,128)} %fusion.24) | copy-start | bytes 1179652
  53.7 2.8 %copy-start.25 = (bf16[2,1,1,2048,512]{4,3,2,1,0:T(8,128)(2,1)S(1)}, bf16[2,1,1,2048,512]{4,3,2,1,0:T(8,128)(2,1)}, u32[]{:S(2)}) copy-start(bf16[2,1,1,2048,512]{4,3,2,1,0:T(8,128)(2,1)} %param.8) | copy-start | bytes 12582916
  59.4 42.3 %copy-start.5 = (bf16[2,1,96,2048]{3,2,1,0:T(8,128)(2,1)S(1)}, bf16[2,1,96,2048]{3,2,1,0:T(8,128)(2,1)}, u32[]{:S(2)}) copy-start(bf16[2,1,96,2048]{3,2,1,0:T(8,128)(2,1)} %param.10) | copy-start | bytes 2359300
  59.4 42.3 %all-to-all-start.1 = ((bf16[8,48,2048]{2,1,0:T(8,128)(2,1)}), bf16[8,48,2048]{2,1,0:T(8,128)(2,1)S(1)}, u32[]{:S(2)}, u32[]{:S(2)}) async-start(bf16[8,48,2048]{2,1,0:T(8,128)(2,1)} %pad_maximum_fusion), calls=%async_computation.1 | async-start | bytes 3145728 | tf_op jit(solution)/shard_map/all_to_all | solution.py:126
  65.2 20.3 %collective-permute-start.1 = (bf16[192,2048]{1,0:T(8,128)(2,1)}, bf16[192,2048]{1,0:T(8,128)(2,1)S(1)}, u32[]{:S(2)}, u32[]{:S(2)}) collective-permute-start(bf16[192,2048]{1,0:T(8,128)(2,1)} %bitcast.208), channel_id=1, source_target_pairs={{0,24},{8,16},{16,8},{24,0},{1,25},{9,17},{17,9},{25,1},{2,26},{10... | collective-permute-start | bytes 2359304 | tf_op jit(solution)/shard_map/ppermute | solution.py:15
  85.5 46.6 %copy-start.12 = (bf16[192,2048]{1,0:T(8,128)(2,1)}, bf16[192,2048]{1,0:T(8,128)(2,1)S(1)}, u32[]{:S(2)}) copy-start(bf16[192,2048]{1,0:T(8,128)(2,1)S(1)} %collective-permute-done.1) | copy-start | bytes 2359300
  102.3 10.5 %copy-start.14 = (bf16[1,2,96,2048]{3,2,1,0:T(8,128)(2,1)S(1)}, bf16[1,2,96,2048]{3,2,1,0:T(8,128)(2,1)}, u32[]{:S(2)}) copy-start(bf16[1,2,96,2048]{3,2,1,0:T(8,128)(2,1)} %param.11) | copy-start | bytes 2359300
  102.4 9.2 %collective-permute-start.2 = (bf16[96,2048]{1,0:T(8,128)(2,1)S(1)}, bf16[96,2048]{1,0:T(8,128)(2,1)S(1)}, u32[]{:S(2)}, u32[]{:S(2)}) collective-permute-start(bf16[96,2048]{1,0:T(8,128)(2,1)S(1)} %get-tuple-element.27), channel_id=1, source_target_pairs={{8,0},{16,8},{24,16},{9,1},{17,9},{25,17},{10,2},{18,10},{26,18},{... | collective-permute-start | bytes 1179656 | tf_op jit(solution)/shard_map/ppermute | solution.py:10
  105.9 6.9 %collective-permute-start.3 = (bf16[96,2048]{1,0:T(8,128)(2,1)S(1)}, bf16[96,2048]{1,0:T(8,128)(2,1)S(1)}, u32[]{:S(2)}, u32[]{:S(2)}) collective-permute-start(bf16[96,2048]{1,0:T(8,128)(2,1)S(1)} %get-tuple-element.28), channel_id=1, source_target_pairs={{0,8},{8,16},{16,24},{1,9},{9,17},{17,25},{2,10},{10,18},{18,26},{... | collective-permute-start | bytes 1179656 | tf_op jit(solution)/shard_map/ppermute | solution.py:10
  114.8 38.8 %all-to-all-start.2 = ((bf16[8,48,2048]{2,1,0:T(8,128)(2,1)}), bf16[8,48,2048]{2,1,0:T(8,128)(2,1)S(1)}, u32[]{:S(2)}, u32[]{:S(2)}) async-start(bf16[8,48,2048]{2,1,0:T(8,128)(2,1)} %bitcast.42), calls=%async_computation.2 | async-start | bytes 3145728 | tf_op jit(solution)/shard_map/all_to_all | solution.py:54
  119.4 3.3 %copy-start.2 = (bf16[2,2,1,1,192,2048]{5,4,3,2,1,0:T(8,128)(2,1)S(1)}, bf16[2,2,1,1,192,2048]{5,4,3,2,1,0:T(8,128)(2,1)}, u32[]{:S(2)}) copy-start(bf16[2,2,1,1,192,2048]{5,4,3,2,1,0:T(8,128)(2,1)} %param.12) | copy-start | bytes 9437188
  122.7 3.0 %copy-start.9 = (bf16[2,192,2048]{2,1,0:T(8,128)(2,1)S(1)}, bf16[2,192,2048]{2,1,0:T(8,128)(2,1)}, u32[]{:S(2)}) copy-start(bf16[2,192,2048]{2,1,0:T(8,128)(2,1)} %copy-done.8) | copy-start | bytes 4718596
  125.8 3.1 %copy-start.26 = (bf16[2,1,1,2048,512]{4,3,2,1,0:T(8,128)(2,1)S(1)}, bf16[2,1,1,2048,512]{4,3,2,1,0:T(8,128)(2,1)}, u32[]{:S(2)}) copy-start(bf16[2,1,1,2048,512]{4,3,2,1,0:T(8,128)(2,1)} %param.8) | copy-start | bytes 12582916
  129.4 2.7 %copy-start.18 = (f32[192,512]{1,0:T(8,128)}, f32[192,512]{1,0:T(8,128)S(1)}, u32[]{:S(2)}) copy-start(f32[192,512]{1,0:T(8,128)S(1)} %fusion.18) | copy-start | bytes 1179652
  129.4 2.7 %copy-start.29 = (bf16[2,1,1,256,2048]{4,3,2,1,0:T(8,128)(2,1)S(1)}, bf16[2,1,1,256,2048]{4,3,2,1,0:T(8,128)(2,1)}, u32[]{:S(2)}) copy-start(bf16[2,1,1,256,2048]{4,3,2,1,0:T(8,128)(2,1)} %param.9) | copy-start | bytes 6291460
  154.6 3.3 %copy-start.6 = (bf16[8,24,2048]{2,1,0:T(8,128)(2,1)}, bf16[8,24,2048]{2,1,0:T(8,128)(2,1)S(1)}, u32[]{:S(2)}) copy-start(bf16[8,24,2048]{2,1,0:T(8,128)(2,1)S(1)} %get-tuple-element.21) | copy-start | bytes 2359300
  154.6 2.7 %copy-start.21 = (f32[192,512]{1,0:T(8,128)S(1)}, f32[192,512]{1,0:T(8,128)}, u32[]{:S(2)}) copy-start(f32[192,512]{1,0:T(8,128)} %fusion.21) | copy-start | bytes 1179652
  154.7 17.7 %collective-permute-start.4 = (bf16[192,2048]{1,0:T(8,128)(2,1)}, bf16[192,2048]{1,0:T(8,128)(2,1)}, u32[]{:S(2)}, u32[]{:S(2)}) collective-permute-start(bf16[192,2048]{1,0:T(8,128)(2,1)} %bitcast.46), channel_id=1, source_target_pairs={{0,24},{8,16},{16,8},{24,0},{1,25},{9,17},{17,9},{25,1},{2,26},{10... | collective-permute-start | bytes 2359304 | tf_op jit(solution)/shard_map/ppermute | solution.py:15
  155.5 2.5 %copy-start.27 = (bf16[2,1,1,2048,512]{4,3,2,1,0:T(8,128)(2,1)S(1)}, bf16[2,1,1,2048,512]{4,3,2,1,0:T(8,128)(2,1)}, u32[]{:S(2)}) copy-start(bf16[2,1,1,2048,512]{4,3,2,1,0:T(8,128)(2,1)} %param.8) | copy-start | bytes 12582916
  160.9 4.6 %copy-start.10 = (bf16[2,192,2048]{2,1,0:T(8,128)(2,1)S(1)}, bf16[2,192,2048]{2,1,0:T(8,128)(2,1)}, u32[]{:S(2)}) copy-start(bf16[2,192,2048]{2,1,0:T(8,128)(2,1)} %copy-done.8) | copy-start | bytes 4718596
  160.9 42.4 %all-to-all-start.3 = ((bf16[8,48,2048]{2,1,0:T(8,128)(2,1)}), bf16[8,48,2048]{2,1,0:T(8,128)(2,1)}, u32[]{:S(2)}, u32[]{:S(2)}) async-start(bf16[8,48,2048]{2,1,0:T(8,128)(2,1)} %pad_maximum_fusion.1), calls=%async_computation.3 | async-start | bytes 3145728 | tf_op jit(solution)/shard_map/all_to_all | solution.py:126
  166.8 5.5 %copy-start.20 = (f32[192,512]{1,0:T(8,128)S(1)}, f32[192,512]{1,0:T(8,128)}, u32[]{:S(2)}) copy-start(f32[192,512]{1,0:T(8,128)} %fusion.16) | copy-start | bytes 1179652
  166.8 5.5 %copy-start.31 = (bf16[2,1,1,256,2048]{4,3,2,1,0:T(8,128)(2,1)S(1)}, bf16[2,1,1,256,2048]{4,3,2,1,0:T(8,128)(2,1)}, u32[]{:S(2)}) copy-start(bf16[2,1,1,256,2048]{4,3,2,1,0:T(8,128)(2,1)} %param.9) | copy-start | bytes 6291460
  167.3 6.7 %copy-start.11 = (bf16[2,192,2048]{2,1,0:T(8,128)(2,1)S(1)}, bf16[2,192,2048]{2,1,0:T(8,128)(2,1)}, u32[]{:S(2)}) copy-start(bf16[2,192,2048]{2,1,0:T(8,128)(2,1)} %copy-done.8) | copy-start | bytes 4718596
  (11 other events, 17.5 us)

commit v8 on v6

--- a/solution.py
+++ b/solution.py
@@ -58,6 +58,13 @@
     ]
 
 
+def batched(left, right, contract_left, contract_right):
+    return lax.dot_general(
+        left, right, (((contract_left,), (contract_right,)), ((0,), (0,))),
+        preferred_element_type=jnp.float32,
+    )
+
+
 def expert_grads(slope_rows, saved_rows, weight_in, weight_out):
     hidden_width = weight_out.shape[0]
     gate_up = jnp.dot(saved_rows, weight_in, preferred_element_type=jnp.float32)
@@ -106,21 +113,32 @@
             )
             mirror_in = mirror_in + part_in
             mirror_out = mirror_out + part_out
-        slopes = exchange(blocks, 2)
-        input_grads = []
-        for way_id in range(2):
-            saved_rows = saved[tick_id, way_id, 0, 0]
-            hidden, pair_grad = expert_grads(
-                slopes[way_id], saved_rows, w_in[way_id, 0, 0], w_out[way_id, 0, 0]
-            )
-            input_grad = right_product(pair_grad, w_in[way_id, 0, 0]).astype(jnp.bfloat16)
-            input_grads.append(input_grad.reshape(experts, capacity, model_width))
-            if way_id == 0:
-                part_in, part_out = weight_terms(saved_rows, slopes[0], hidden, pair_grad)
-                own_in = own_in + part_in
-                own_out = own_out + part_out
+        arrived = lax.all_to_all(blocks, "expert", split_axis=0, concat_axis=0, tiled=True)
+        slopes = (
+            arrived.reshape(experts, 2, capacity, model_width)
+            .transpose(1, 0, 2, 3)
+            .reshape(2, experts * capacity, model_width)
+        )
+        saved_rows = saved[tick_id, :, 0, 0]
+        gate_up = batched(saved_rows, w_in[:, 0, 0], 2, 1)
+        gate_part = gate_up[..., :hidden_width]
+        upward = gate_up[..., hidden_width:]
+        sigmoid_gate = jax.nn.sigmoid(gate_part)
+        active = gate_part * sigmoid_gate
+        hidden = (active * upward).astype(jnp.bfloat16)
+        hidden_grad = batched(slopes, w_out[:, 0, 0], 2, 2)
+        gate_grad = hidden_grad * upward * sigmoid_gate * (1.0 + gate_part * (1.0 - sigmoid_gate))
+        pair_grad = jnp.concatenate([gate_grad, hidden_grad * active], axis=2).astype(jnp.bfloat16)
+        input_grads = batched(pair_grad, w_in[:, 0, 0], 2, 2).astype(jnp.bfloat16)
+        part_in, part_out = weight_terms(saved_rows[0], slopes[0], hidden[0], pair_grad[0])
+        own_in = own_in + part_in
+        own_out = own_out + part_out
         slope_mirror = mirrored(slopes[1], "section")
-        back_blocks = jnp.concatenate(input_grads, axis=1)
+        back_blocks = (
+            input_grads.reshape(2, experts, capacity, model_width)
+            .transpose(1, 0, 2, 3)
+            .reshape(experts, 2 * capacity, model_width)
+        )
         if tick_id == 0:
             back_blocks, saved_mirror = lax.optimization_barrier((back_blocks, saved_mirror))
         returned = lax.all_to_all(back_blocks, "expert", split_axis=0, concat_axis=0, tiled=True)

time: 205 us -> 206 us (level)
  waiting for transfers between devices: 105 us -> 101 us
  local copies, waits for them, and re-layouts: 17.4 us -> 19.9 us
  matrix products: 44.7 us -> 47.1 us
    dot_general x0 -> x6, matrix products: none -> 15.2 us  [batched(): lax.dot_general(left, right, (((contract_left,), (contract_right,)), ((0,...]
    dot_general x6 -> x2, matrix products: 14.3 us -> 4.94 us  [expert_grads(): gate_up = jnp.dot(saved_rows, weight_in, preferred_element_type=jnp.float32)]
    dot_general x10 -> x2, matrix products: 10.2 us -> 2.15 us  [right_product(): lax.dot_general(left, right, (((1,), (1,)), ((), ())), preferred_element_...]
    dot_general x10, matrix products: 16.7 us -> 21.4 us  [left_product(): lax.dot_general(left, right, (((0,), (0,)), ((), ())), preferred_element_...]
    reshape x0 -> x4, local copies, waits for them, and re-layouts: none -> 2.99 us  [the longest x2 2.72 us: on_device(): input_grads.reshape(2, experts, capacity, model_width).transpose(1, 0, 2, 3)]
    concatenate x2 -> x0, other arithmetic: 2.57 us -> none  [on_device(): back_blocks = jnp.concatenate(input_grads, axis=1)]
    unnamed x61 -> x63, local copies, waits for them, and re-layouts: 10.9 us -> 9.02 us
  transfers between devices with their start and end apart: 9 -> 9, of which waited for: 8 -> 8; matrix products, arithmetic and copies ran while one was open for 23% -> 26% of each run, Pallas kernels for 0% -> 0%
where the time goes in v8:
time: 206 us; the launch traced here: 204 us
  waiting for transfers between devices  101 us (49%)
  matrix products  47.1 us (23%)
  starting transfers between devices  30.3 us (15%)
  local copies, waits for them, and re-layouts  19.9 us (10%)
  other arithmetic  5.28 us (3%)
    all_to_all x2, waiting for transfers between devices, on_device(): lax.all_to_all(blocks, 'expert', split_axis=0, concat_axis=0, tiled=True)  47.2 us
    all_to_all x2, waiting for transfers between devices, on_device(): lax.all_to_all(back_blocks, 'expert', split_axis=0, concat_axis=0, tiled=...  29.9 us
    dot_general x10, matrix products, left_product(): lax.dot_general(left, right, (((0,), (0,)), ((), ())), preferred_element_...  21.4 us
    ppermute x3, waiting for transfers between devices, mirrored(): return lax.ppermute(block, axis, [(i, count - 1 - i) for i in range(count)])  19 us
    dot_general x6, matrix products, batched(): lax.dot_general(left, right, (((contract_left,), (contract_right,)), ((0,...  15.2 us
    all_to_all x2, starting transfers between devices, on_device(): lax.all_to_all(blocks, 'expert', split_axis=0, concat_axis=0, tiled=True)  10.1 us
    all_to_all x2, starting transfers between devices, on_device(): lax.all_to_all(back_blocks, 'expert', split_axis=0, concat_axis=0, tiled=...  9.1 us
    unnamed x63, local copies, waits for them, and re-layouts  9.02 us
  transfers between devices with their start and end apart: 9, of which 8 were waited for; matrix products, arithmetic and copies ran while one was open for 26% of the time, Pallas kernels for 0%

profile of v8, /device:TPU:1, one launch (start us, length us, event | category | flops | bytes accessed | tf_op | source)
XLA Modules:
  0.0 204.3 jit_solution(13615285872310292644)
XLA Ops:
  5.6 1.7 convolution_convert_fusion.1
  7.4 6.4 %all-to-all-start = ((bf16[8,48,2048]{2,1,0:T(8,128)(2,1)}), bf16[8,48,2048]{2,1,0:T(8,128)(2,1)S(1)}, u32[]{:S(2)}, u32[]{:S(2)}) async-start(bf16[8,48,2048]{2,1,0:T(8,128)(2,1)} %bitcast.13), calls=%async_computation | async-start | bytes 3145728 | tf_op jit(solution)/shard_map/all_to_all | solution.py:116
  13.7 2.9 %slice_bitcast_fusion.4 = bf16[2,192,2048]{2,1,0:T(8,128)(2,1)} fusion(bf16[2,2,1,1,192,2048]{5,4,3,2,1,0:T(8,128)(2,1)} %param.12), kind=kLoop, calls=%fused_computation.44 | loop fusion | bytes 3145728 | tf_op jit(solution)/shard_map/squeeze | solution.py:95
  16.6 2.0 %collective-permute-start = (bf16[2,192,2048]{2,1,0:T(8,128)(2,1)}, bf16[2,192,2048]{2,1,0:T(8,128)(2,1)}, u32[]{:S(2)}, u32[]{:S(2)}) collective-permute-start(bf16[2,192,2048]{2,1,0:T(8,128)(2,1)} %slice_bitcast_fusion.4), channel_id=1, source_target_pairs={{0,24},{8,16},{16,8},{24,0},{1,25},{9,17},{17,9},{25,1},{2,26},{10... | collective-permute-start | bytes 4718600 | tf_op jit(solution)/shard_map/ppermute | solution.py:15
  18.7 4.0 %fusion.7 = f32[2,192,512]{2,1,0:T(8,128)} fusion(bf16[2,1,1,2048,512]{4,3,2,1,0:T(8,128)(2,1)} %param.8, bf16[2,2,1,1,192,2048]{5,4,1,3,2,0:T(8,128)(2,1)S(1)} %bitcast.225), kind=kOutput, calls=%fused_computation.8 | convolution fusion | flops 805306368 | bytes 6553600 | tf_op jit(solution)/shard_map/dot_general | solution.py:62
  22.7 27.2 %all-to-all-done = bf16[8,48,2048]{2,1,0:T(8,128)(2,1)S(1)} async-done(((bf16[8,48,2048]{2,1,0:T(8,128)(2,1)}), bf16[8,48,2048]{2,1,0:T(8,128)(2,1)S(1)}, u32[]{:S(2)}, u32[]{:S(2)}) %all-to-all-start) | async-done | bytes 1572896 | tf_op jit(solution)/shard_map/all_to_all | solution.py:116
  51.7 1.7 multiply_convert_fusion.3
  57.0 4.6 %all-to-all-start.1 = ((bf16[8,48,2048]{2,1,0:T(8,128)(2,1)}), bf16[8,48,2048]{2,1,0:T(8,128)(2,1)S(1)}, u32[]{:S(2)}, u32[]{:S(2)}) async-start(bf16[8,48,2048]{2,1,0:T(8,128)(2,1)} %bitcast.23), calls=%async_computation.1 | async-start | bytes 3145728 | tf_op jit(solution)/shard_map/all_to_all | solution.py:144
  62.9 1.9 collective-permute-start.1
  66.2 17.1 %collective-permute-done.1 = bf16[192,2048]{1,0:T(8,128)(2,1)S(1)} collective-permute-done((bf16[192,2048]{1,0:T(8,128)(2,1)}, bf16[192,2048]{1,0:T(8,128)(2,1)S(1)}, u32[]{:S(2)}, u32[]{:S(2)}) %collective-permute-start.1) | collective-permute-done | bytes 786464 | tf_op jit(solution)/shard_map/ppermute | solution.py:15
  83.3 14.7 %all-to-all-done.1 = bf16[8,48,2048]{2,1,0:T(8,128)(2,1)S(1)} async-done(((bf16[8,48,2048]{2,1,0:T(8,128)(2,1)}), bf16[8,48,2048]{2,1,0:T(8,128)(2,1)S(1)}, u32[]{:S(2)}, u32[]{:S(2)}) %all-to-all-start.1) | async-done | bytes 1572896 | tf_op jit(solution)/shard_map/all_to_all | solution.py:144
  98.0 1.8 fusion.20
  99.9 3.5 %collective-permute-start.2 = (bf16[96,2048]{1,0:T(8,128)(2,1)S(1)}, bf16[96,2048]{1,0:T(8,128)(2,1)S(1)}, u32[]{:S(2)}, u32[]{:S(2)}) collective-permute-start(bf16[96,2048]{1,0:T(8,128)(2,1)S(1)} %get-tuple-element.40), channel_id=1, source_target_pairs={{8,0},{16,8},{24,16},{9,1},{17,9},{25,17},{10,2},{18,10},{26,18},{... | collective-permute-start | bytes 1179656 | tf_op jit(solution)/shard_map/ppermute | solution.py:10
  103.4 3.0 %collective-permute-start.3 = (bf16[96,2048]{1,0:T(8,128)(2,1)S(1)}, bf16[96,2048]{1,0:T(8,128)(2,1)S(1)}, u32[]{:S(2)}, u32[]{:S(2)}) collective-permute-start(bf16[96,2048]{1,0:T(8,128)(2,1)S(1)} %get-tuple-element.41), channel_id=1, source_target_pairs={{0,8},{8,16},{16,24},{1,9},{9,17},{17,25},{2,10},{10,18},{18,26},{... | collective-permute-start | bytes 1179656 | tf_op jit(solution)/shard_map/ppermute | solution.py:10
  106.6 3.3 %collective-permute-done.2 = bf16[96,2048]{1,0:T(8,128)(2,1)S(1)} collective-permute-done((bf16[96,2048]{1,0:T(8,128)(2,1)S(1)}, bf16[96,2048]{1,0:T(8,128)(2,1)S(1)}, u32[]{:S(2)}, u32[]{:S(2)}) %collective-permute-start.2) | collective-permute-done | bytes 393248 | tf_op jit(solution)/shard_map/ppermute | solution.py:10
  111.5 1.7 convolution_convert_fusion
  113.2 3.7 %all-to-all-start.2 = ((bf16[8,48,2048]{2,1,0:T(8,128)(2,1)}), bf16[8,48,2048]{2,1,0:T(8,128)(2,1)S(1)}, u32[]{:S(2)}, u32[]{:S(2)}) async-start(bf16[8,48,2048]{2,1,0:T(8,128)(2,1)} %bitcast.43), calls=%async_computation.2 | async-start | bytes 3145728 | tf_op jit(solution)/shard_map/all_to_all | solution.py:116
  117.8 4.7 %fusion.3 = f32[2,192,512]{2,1,0:T(8,128)} fusion(bf16[2,1,1,2048,512]{4,3,2,1,0:T(8,128)(2,1)} %param.8, bf16[2,2,1,1,192,2048]{5,4,1,3,2,0:T(8,128)(2,1)} %bitcast.224), kind=kOutput, calls=%fused_computation.4 | convolution fusion | flops 805306368 | bytes 6553600 | tf_op jit(solution)/shard_map/dot_general | solution.py:62
  122.5 2.5 %fusion.24 = f32[192,512]{1,0:T(8,128)} fusion(bf16[2,1,1,2048,512]{4,3,2,1,0:T(8,128)(2,1)S(1)} %copy-done.1, bf16[2,192,2048]{2,1,0:T(8,128)(2,1)} %collective-permute-done), kind=kOutput, calls=%fused_computation.28 | convolution fusion | flops 402653184 | bytes 3276800 | tf_op jit(solution)/shard_map/dot_general | solution.py:70
  125.0 2.5 %fusion.26 = f32[192,512]{1,0:T(8,128)} fusion(bf16[2,1,1,2048,512]{4,3,2,1,0:T(8,128)(2,1)S(1)} %copy-done.1, bf16[2,192,2048]{2,1,0:T(8,128)(2,1)} %collective-permute-done), kind=kOutput, calls=%fused_computation.30 | convolution fusion | flops 402653184 | bytes 3276800 | tf_op jit(solution)/shard_map/dot_general | solution.py:70
  127.4 3.8 %fusion.48 = f32[512,2048]{1,0:T(8,128)} fusion(bf16[2,2,1,1,192,2048]{5,4,3,2,1,0:T(8,128)(2,1)} %param.12, bf16[2,192,256]{2,1,0:T(8,128)(2,1)S(1)} %get-tuple-element.33, bf16[2,192,256]{2,1,0:T(8,128)(2,1)S(1)} %get-tuple-element.32), kind=kOutput, calls=%fused_computation.58 | convolution fusion | flops 403046400 | bytes 5373952 | tf_op jit(solution)/shard_map/dot_general | solution.py:19
  131.2 20.1 %all-to-all-done.2 = bf16[8,48,2048]{2,1,0:T(8,128)(2,1)S(1)} async-done(((bf16[8,48,2048]{2,1,0:T(8,128)(2,1)}), bf16[8,48,2048]{2,1,0:T(8,128)(2,1)S(1)}, u32[]{:S(2)}, u32[]{:S(2)}) %all-to-all-start.2) | async-done | bytes 1572896 | tf_op jit(solution)/shard_map/all_to_all | solution.py:116
  153.7 1.7 multiply_convert_fusion.1
  159.1 4.5 %all-to-all-start.3 = ((bf16[8,48,2048]{2,1,0:T(8,128)(2,1)}), bf16[8,48,2048]{2,1,0:T(8,128)(2,1)}, u32[]{:S(2)}, u32[]{:S(2)}) async-start(bf16[8,48,2048]{2,1,0:T(8,128)(2,1)} %bitcast.51), calls=%async_computation.3 | async-start | bytes 3145728 | tf_op jit(solution)/shard_map/all_to_all | solution.py:144
  163.6 1.9 fusion.84
  166.5 1.9 fusion.44
  168.5 1.9 collective-permute-done.4
  172.0 2.1 %add_convert_fusion = bf16[2048,512]{0,1:T(8,128)(2,1)S(1)} fusion(f32[2048,512]{0,1:T(8,128)S(1)} %fusion.44, bf16[2,192,2048]{2,1,0:T(8,128)(2,1)} %collective-permute-done, bf16[192,256]{1,0:T(8,128)(2,1)S(1)} %get-tuple-element.43, bf16[192,256]{1,0:T(8,128)(2,1)S(1)} %get-tuple-element.42), kind=kOutput, calls=%fused_computation.10 | convolution fusion | flops 405143552 | bytes 7274496 | tf_op jit(solution)/shard_map/dot_general | solution.py:19
  174.4 3.2 %fusion.15 = bf16[1,1,2048,512]{2,3,1,0:T(8,128)(2,1)} fusion(bf16[2048,512]{0,1:T(8,128)(2,1)S(1)} %add_convert_fusion, f32[512,2048]{1,0:T(8,128)S(1)} %copy-done.3, bf16[2,2,1,1,192,2048]{5,4,3,2,1,0:T(8,128)(2,1)} %param.12, bf16[2,192,256]{2,1,0:T(8,128)(2,1)S(1)} %get-tuple-element.31, bf16[2,192,256]{2,1,0:T(8,128)(2,1)S(1)} %get-tuple-element.30), kind=kOutput, calls=%fused_computation.15 | convolution fusion | flops 407240704 | bytes 9568256 | tf_op jit(solution)/shard_map/dot_general | solution.py:19
  177.6 4.0 %copy.41 = bf16[1,1,2048,512]{3,2,1,0:T(8,128)(2,1)} copy(bf16[1,1,2048,512]{2,3,1,0:T(8,128)(2,1)} %fusion.15) | data formatting | bytes 4194304
  186.2 15.2 %all-to-all-done.3 = bf16[8,48,2048]{2,1,0:T(8,128)(2,1)} async-done(((bf16[8,48,2048]{2,1,0:T(8,128)(2,1)}), bf16[8,48,2048]{2,1,0:T(8,128)(2,1)}, u32[]{:S(2)}, u32[]{:S(2)}) %all-to-all-start.3) | async-done | bytes 1572896 | tf_op jit(solution)/shard_map/all_to_all | solution.py:144
  201.4 2.9 %fusion.23 = bf16[2,1,96,2048]{3,2,1,0:T(8,128)(2,1)} fusion(pred[2,96,384]{2,1,0:T(32,128)(4,1)S(1)} %bitcast.227, bf16[384,2048,1]{1,0,2:T(8,128)(2,1)} %bitcast.53, bf16[1,96,2048]{2,1,0:T(8,128)(2,1)S(1)} %get-tuple-element.39, bf16[1,96,2048]{2,1,0:T(8,128)(2,1)S(1)} %get-tuple-element.38), kind=kOutput, calls=%fused_computation.27 | convolution fusion | flops 303562752 | bytes 3219456 | tf_op jit(solution)/shard_map/dot_general | solution.py:19
  (105 shorter events, 29.1 us)
Async XLA Ops:
  0.6 4.2 %copy-start.17 = (s32[2,2,1,96]{3,2,1,0:T(1,128)S(1)}, s32[2,2,1,96]{3,2,1,0:T(1,128)}, u32[]{:S(2)}) copy-start(s32[2,2,1,96]{3,2,1,0:T(1,128)} %param.14) | copy-start | bytes 4612
  4.8 2.5 %copy-start.20 = (s32[96]{0:T(128)}, s32[96]{0:T(128)S(1)}, u32[]{:S(2)}) copy-start(s32[96]{0:T(128)S(1)} %select_reduce_fusion.6) | copy-start | bytes 1156
  7.4 42.6 %all-to-all-start = ((bf16[8,48,2048]{2,1,0:T(8,128)(2,1)}), bf16[8,48,2048]{2,1,0:T(8,128)(2,1)S(1)}, u32[]{:S(2)}, u32[]{:S(2)}) async-start(bf16[8,48,2048]{2,1,0:T(8,128)(2,1)} %bitcast.13), calls=%async_computation | async-start | bytes 3145728 | tf_op jit(solution)/shard_map/all_to_all | solution.py:116
  13.7 5.0 %copy-start.5 = (bf16[2,2,1,1,192,2048]{5,4,3,2,1,0:T(8,128)(2,1)S(1)}, bf16[2,2,1,1,192,2048]{5,4,3,2,1,0:T(8,128)(2,1)}, u32[]{:S(2)}) copy-start(bf16[2,2,1,1,192,2048]{5,4,3,2,1,0:T(8,128)(2,1)} %param.12) | copy-start | bytes 9437188
  16.6 40.4 %collective-permute-start = (bf16[2,192,2048]{2,1,0:T(8,128)(2,1)}, bf16[2,192,2048]{2,1,0:T(8,128)(2,1)}, u32[]{:S(2)}, u32[]{:S(2)}) collective-permute-start(bf16[2,192,2048]{2,1,0:T(8,128)(2,1)} %slice_bitcast_fusion.4), channel_id=1, source_target_pairs={{0,24},{8,16},{16,8},{24,0},{1,25},{9,17},{17,9},{25,1},{2,26},{10... | collective-permute-start | bytes 4718600 | tf_op jit(solution)/shard_map/ppermute | solution.py:15
  51.7 2.5 %copy-start = (bf16[2,1,1,2048,512]{4,3,2,1,0:T(8,128)(2,1)S(1)}, bf16[2,1,1,2048,512]{4,3,2,1,0:T(8,128)(2,1)}, u32[]{:S(2)}) copy-start(bf16[2,1,1,2048,512]{4,3,2,1,0:T(8,128)(2,1)} %param.8) | copy-start | bytes 12582916
  57.0 41.0 %all-to-all-start.1 = ((bf16[8,48,2048]{2,1,0:T(8,128)(2,1)}), bf16[8,48,2048]{2,1,0:T(8,128)(2,1)S(1)}, u32[]{:S(2)}, u32[]{:S(2)}) async-start(bf16[8,48,2048]{2,1,0:T(8,128)(2,1)} %bitcast.23), calls=%async_computation.1 | async-start | bytes 3145728 | tf_op jit(solution)/shard_map/all_to_all | solution.py:144
  61.6 3.1 %copy-start.19 = (s32[96]{0:T(128)S(1)}, s32[96]{0:T(128)}, u32[]{:S(2)}) copy-start(s32[96]{0:T(128)} %copy-done.18) | copy-start | bytes 1156
  61.6 3.1 %copy-start.21 = (s32[96]{0:T(128)S(1)}, s32[96]{0:T(128)}, u32[]{:S(2)}) copy-start(s32[96]{0:T(128)} %copy-done.20) | copy-start | bytes 1156
  62.9 20.4 %collective-permute-start.1 = (bf16[192,2048]{1,0:T(8,128)(2,1)}, bf16[192,2048]{1,0:T(8,128)(2,1)S(1)}, u32[]{:S(2)}, u32[]{:S(2)}) collective-permute-start(bf16[192,2048]{1,0:T(8,128)(2,1)} %bitcast.25), channel_id=1, source_target_pairs={{0,24},{8,16},{16,8},{24,0},{1,25},{9,17},{17,9},{25,1},{2,26},{10... | collective-permute-start | bytes 2359304 | tf_op jit(solution)/shard_map/ppermute | solution.py:15
  83.3 16.6 %copy-start.6 = (bf16[192,2048]{1,0:T(8,128)(2,1)}, bf16[192,2048]{1,0:T(8,128)(2,1)S(1)}, u32[]{:S(2)}) copy-start(bf16[192,2048]{1,0:T(8,128)(2,1)S(1)} %collective-permute-done.1) | copy-start | bytes 2359300
  98.0 8.5 %copy-start.22 = (s32[96]{0:T(128)S(1)}, s32[96]{0:T(128)}, u32[]{:S(2)}) copy-start(s32[96]{0:T(128)} %get-tuple-element.46) | copy-start | bytes 1156
  98.0 8.5 %copy-start.23 = (s32[96]{0:T(128)S(1)}, s32[96]{0:T(128)}, u32[]{:S(2)}) copy-start(s32[96]{0:T(128)} %get-tuple-element.47) | copy-start | bytes 1156
  98.0 13.1 %copy-start.9 = (bf16[1,2,96,2048]{3,2,1,0:T(8,128)(2,1)S(1)}, bf16[1,2,96,2048]{3,2,1,0:T(8,128)(2,1)}, u32[]{:S(2)}) copy-start(bf16[1,2,96,2048]{3,2,1,0:T(8,128)(2,1)} %param.11) | copy-start | bytes 2359300
  99.9 10.0 %collective-permute-start.2 = (bf16[96,2048]{1,0:T(8,128)(2,1)S(1)}, bf16[96,2048]{1,0:T(8,128)(2,1)S(1)}, u32[]{:S(2)}, u32[]{:S(2)}) collective-permute-start(bf16[96,2048]{1,0:T(8,128)(2,1)S(1)} %get-tuple-element.40), channel_id=1, source_target_pairs={{8,0},{16,8},{24,16},{9,1},{17,9},{25,17},{10,2},{18,10},{26,18},{... | collective-permute-start | bytes 1179656 | tf_op jit(solution)/shard_map/ppermute | solution.py:10
  103.4 7.7 %collective-permute-start.3 = (bf16[96,2048]{1,0:T(8,128)(2,1)S(1)}, bf16[96,2048]{1,0:T(8,128)(2,1)S(1)}, u32[]{:S(2)}, u32[]{:S(2)}) collective-permute-start(bf16[96,2048]{1,0:T(8,128)(2,1)S(1)} %get-tuple-element.41), channel_id=1, source_target_pairs={{0,8},{8,16},{16,24},{1,9},{9,17},{17,25},{2,10},{10,18},{18,26},{... | collective-permute-start | bytes 1179656 | tf_op jit(solution)/shard_map/ppermute | solution.py:10
  113.2 3.7 %copy-start.24 = (s32[1,96,1]{1,2,0:T(1,128)S(1)}, s32[1,96,1]{1,2,0:T(1,128)}, u32[]{:S(2)}) copy-start(s32[1,96,1]{1,2,0:T(1,128)} %get-tuple-element.52) | copy-start | bytes 1156
  113.2 3.7 %copy-start.25 = (s32[1,96,1]{1,2,0:T(1,128)S(1)}, s32[1,96,1]{1,2,0:T(1,128)}, u32[]{:S(2)}) copy-start(s32[1,96,1]{1,2,0:T(1,128)} %get-tuple-element.53) | copy-start | bytes 1156
  113.2 38.1 %all-to-all-start.2 = ((bf16[8,48,2048]{2,1,0:T(8,128)(2,1)}), bf16[8,48,2048]{2,1,0:T(8,128)(2,1)S(1)}, u32[]{:S(2)}, u32[]{:S(2)}) async-start(bf16[8,48,2048]{2,1,0:T(8,128)(2,1)} %bitcast.43), calls=%async_computation.2 | async-start | bytes 3145728 | tf_op jit(solution)/shard_map/all_to_all | solution.py:116
  117.8 4.7 %copy-start.1 = (bf16[2,1,1,2048,512]{4,3,2,1,0:T(8,128)(2,1)S(1)}, bf16[2,1,1,2048,512]{4,3,2,1,0:T(8,128)(2,1)}, u32[]{:S(2)}) copy-start(bf16[2,1,1,2048,512]{4,3,2,1,0:T(8,128)(2,1)} %param.8) | copy-start | bytes 12582916
  151.4 2.2 %copy-start.27 = (bf16[2,1,1,256,2048]{4,3,2,1,0:T(8,128)(2,1)S(1)}, bf16[2,1,1,256,2048]{4,3,2,1,0:T(8,128)(2,1)}, u32[]{:S(2)}) copy-start(bf16[2,1,1,256,2048]{4,3,2,1,0:T(8,128)(2,1)} %param.9) | copy-start | bytes 6291460
  151.4 2.3 %copy-start.29 = (f32[2,192,512]{2,1,0:T(8,128)S(1)}, f32[2,192,512]{2,1,0:T(8,128)}, u32[]{:S(2)}) copy-start(f32[2,192,512]{2,1,0:T(8,128)} %fusion.3) | copy-start | bytes 2359300
  152.7 17.7 %collective-permute-start.4 = (bf16[192,2048]{1,0:T(8,128)(2,1)}, bf16[192,2048]{1,0:T(8,128)(2,1)}, u32[]{:S(2)}, u32[]{:S(2)}) collective-permute-start(bf16[192,2048]{1,0:T(8,128)(2,1)} %bitcast.65), channel_id=1, source_target_pairs={{0,24},{8,16},{16,8},{24,0},{1,25},{9,17},{17,9},{25,1},{2,26},{10... | collective-permute-start | bytes 2359304 | tf_op jit(solution)/shard_map/ppermute | solution.py:15
  153.7 2.5 %copy-start.2 = (bf16[2,1,1,2048,512]{4,3,2,1,0:T(8,128)(2,1)S(1)}, bf16[2,1,1,2048,512]{4,3,2,1,0:T(8,128)(2,1)}, u32[]{:S(2)}) copy-start(bf16[2,1,1,2048,512]{4,3,2,1,0:T(8,128)(2,1)} %param.8) | copy-start | bytes 12582916
  159.1 42.3 %all-to-all-start.3 = ((bf16[8,48,2048]{2,1,0:T(8,128)(2,1)}), bf16[8,48,2048]{2,1,0:T(8,128)(2,1)}, u32[]{:S(2)}, u32[]{:S(2)}) async-start(bf16[8,48,2048]{2,1,0:T(8,128)(2,1)} %bitcast.51), calls=%async_computation.3 | async-start | bytes 3145728 | tf_op jit(solution)/shard_map/all_to_all | solution.py:144
  163.6 2.0 copy-start.7
  163.6 2.0 copy-start.11
  163.6 2.4 %copy-start.28 = (bf16[2,1,1,256,2048]{4,3,2,1,0:T(8,128)(2,1)S(1)}, bf16[2,1,1,256,2048]{4,3,2,1,0:T(8,128)(2,1)}, u32[]{:S(2)}) copy-start(bf16[2,1,1,256,2048]{4,3,2,1,0:T(8,128)(2,1)} %param.9) | copy-start | bytes 6291460
  166.5 3.8 %copy-start.15 = (f32[192,512]{1,0:T(8,128)S(1)}, f32[192,512]{1,0:T(8,128)}, u32[]{:S(2)}) copy-start(f32[192,512]{1,0:T(8,128)} %fusion.24) | copy-start | bytes 1179652
  172.0 2.4 %copy-start.3 = (f32[512,2048]{1,0:T(8,128)S(1)}, f32[512,2048]{1,0:T(8,128)}, u32[]{:S(2)}) copy-start(f32[512,2048]{1,0:T(8,128)} %fusion.48) | copy-start | bytes 12582916
  177.6 4.0 %copy-start.16 = (f32[192,512]{1,0:T(8,128)S(1)}, f32[192,512]{1,0:T(8,128)}, u32[]{:S(2)}) copy-start(f32[192,512]{1,0:T(8,128)} %fusion.24) | copy-start | bytes 1179652
  184.7 16.7 %copy-start.10 = (pred[192,384]{1,0:T(32,128)(4,1)S(1)}, pred[192,384]{1,0:T(32,128)(4,1)}, u32[]{:S(2)}) copy-start(pred[192,384]{1,0:T(32,128)(4,1)} %iota_compare_fusion.4) | copy-start | bytes 221188
  (8 other events, 11.2 us)

commit v9 on v5

--- a/solution.py
+++ b/solution.py
@@ -1,6 +1,7 @@
 import jax
 import jax.numpy as jnp
 from jax import lax
+from jax.experimental import pallas as pl
 from jax.sharding import PartitionSpec as P
 
 
@@ -46,12 +47,6 @@
     )
     rows = lax.iota(jnp.int32, ways * experts * capacity)
     return (rows[:, None] == slots[None, :]).astype(jnp.bfloat16)
-
-
-def exchange(blocks):
-    experts, ways, capacity, model_width = blocks.shape
-    arrived = lax.all_to_all(blocks, "expert", split_axis=0, concat_axis=0, tiled=True)
-    return [arrived[:, way_id].reshape(experts * capacity, model_width) for way_id in range(ways)]
 
 
 def expert_grads(slope_rows, saved_rows, weight_in, weight_out):
@@ -66,6 +61,67 @@
     gate_grad = hidden_grad * upward * sigmoid_gate * (1.0 + gate_part * (1.0 - sigmoid_gate))
     pair_grad = jnp.concatenate([gate_grad, hidden_grad * active], axis=1).astype(jnp.bfloat16)
     return hidden, pair_grad
+
+
+def critical_kernel(slope_ref, factor_ref, active_ref, w_out_ref, w_in_ref, input_ref, pair_ref):
+    experts, _, capacity, width = slope_ref.shape
+    hidden = factor_ref.shape[-1]
+    slope = slope_ref[...].astype(jnp.float32).reshape(experts * capacity, width).astype(jnp.bfloat16)
+    hidden_grad = lax.dot_general(
+        slope, w_out_ref[0], (((1,), (1,)), ((), ())), preferred_element_type=jnp.float32
+    )
+    gate_grad = (hidden_grad * factor_ref[0]).astype(jnp.bfloat16)
+    up_grad = (hidden_grad * active_ref[0]).astype(jnp.bfloat16)
+    pair_ref[0, :, :hidden] = gate_grad
+    pair_ref[0, :, hidden:] = up_grad
+    w_in = w_in_ref[0]
+    input_grad = lax.dot_general(
+        gate_grad, w_in[:, :hidden], (((1,), (1,)), ((), ())), preferred_element_type=jnp.float32
+    ) + lax.dot_general(
+        up_grad, w_in[:, hidden:], (((1,), (1,)), ((), ())), preferred_element_type=jnp.float32
+    )
+    input_ref[...] = input_grad.reshape(experts, 1, capacity, width).astype(input_ref.dtype)
+
+
+def critical(arrived, factor, active, weight_out, weight_in):
+    experts, ways, capacity, width = arrived.shape
+    rows, hidden = factor.shape[1], factor.shape[2]
+    row_block = pl.BlockSpec((experts, 1, capacity, width), lambda w: (0, w, 0, 0))
+    return pl.pallas_call(
+        critical_kernel,
+        grid=(ways,),
+        in_specs=[
+            row_block,
+            pl.BlockSpec((1, rows, hidden), lambda w: (w, 0, 0)),
+            pl.BlockSpec((1, rows, hidden), lambda w: (w, 0, 0)),
+            pl.BlockSpec((1,) + weight_out.shape[1:], lambda w: (w, 0, 0)),
+            pl.BlockSpec((1,) + weight_in.shape[1:], lambda w: (w, 0, 0)),
+        ],
+        out_specs=[row_block, pl.BlockSpec((1, rows, 2 * hidden), lambda w: (w, 0, 0))],
+        out_shape=[
+            jax.ShapeDtypeStruct(arrived.shape, jnp.bfloat16),
+            jax.ShapeDtypeStruct((ways, rows, 2 * hidden), jnp.bfloat16),
+        ],
+        cost_estimate=pl.CostEstimate(
+            flops=2 * ways * rows * width * 3 * hidden,
+            bytes_accessed=2 * arrived.size * 2 + weight_in.size * 2 + weight_out.size * 2
+            + factor.size * 8 + ways * rows * 2 * hidden * 2,
+            transcendentals=0,
+        ),
+    )(arrived, factor, active, weight_out, weight_in)
+
+
+def gate_terms(saved_rows, weight_in, hidden_width):
+    gate_up = lax.dot_general(
+        saved_rows, weight_in, (((2,), (1,)), ((0,), (0,))), preferred_element_type=jnp.float32
+    )
+    gate_part = gate_up[..., :hidden_width]
+    upward = gate_up[..., hidden_width:]
+    sigmoid_gate = jax.nn.sigmoid(gate_part)
+    active = gate_part * sigmoid_gate
+    hidden = (active * upward).astype(jnp.bfloat16)
+    factor = upward * sigmoid_gate * (1.0 + gate_part * (1.0 - sigmoid_gate))
+    return factor, active, hidden
 
 
 def weight_terms(saved_rows, slope_rows, hidden, pair_grad):
@@ -102,21 +158,14 @@
             )
             mirror_in = mirror_in + part_in
             mirror_out = mirror_out + part_out
-        slopes = exchange(blocks)
-        input_grads = []
-        for way_id in range(2):
-            saved_rows = saved[tick_id, way_id, 0, 0]
-            hidden, pair_grad = expert_grads(
-                slopes[way_id], saved_rows, w_in[way_id, 0, 0], w_out[way_id, 0, 0]
-            )
-            input_grad = right_product(pair_grad, w_in[way_id, 0, 0]).astype(jnp.bfloat16)
-            input_grads.append(input_grad.reshape(experts, 1, capacity, model_width))
-            if way_id == 0:
-                part_in, part_out = weight_terms(saved_rows, slopes[0], hidden, pair_grad)
-                own_in = own_in + part_in
-                own_out = own_out + part_out
+        arrived = lax.all_to_all(blocks, "expert", split_axis=0, concat_axis=0, tiled=True)
+        factor, active, hidden = gate_terms(saved[tick_id, :, 0, 0], w_in[:, 0, 0], hidden_width)
+        back_blocks, pair_grad = critical(arrived, factor, active, w_out[:, 0, 0], w_in[:, 0, 0])
+        slopes = [arrived[:, way_id].reshape(experts * capacity, model_width) for way_id in range(2)]
+        part_in, part_out = weight_terms(saved[tick_id, 0, 0, 0], slopes[0], hidden[0], pair_grad[0])
+        own_in = own_in + part_in
+        own_out = own_out + part_out
         slope_mirror = mirrored(slopes[1], "section")
-        back_blocks = jnp.concatenate(input_grads, axis=1)
         if tick_id == 0:
             back_blocks, saved_mirror = lax.optimization_barrier((back_blocks, saved_mirror))
         returned = lax.all_to_all(back_blocks, "expert", split_axis=0, concat_axis=0, tiled=True)

time: 205 us -> 206 us (level)
  Pallas kernels: 0 us -> 13.3 us
  matrix products: 44.7 us -> 36.6 us
  waiting for transfers between devices: 105 us -> 102 us
    all_to_all x2, waiting for transfers between devices: 31.2 us -> 17.4 us  [on_device(): lax.all_to_all(back_blocks, 'expert', split_axis=0, concat_axis=0, tiled=...]
    pallas_call x0 -> x2, Pallas kernels: none -> 13.3 us  [critical(): pl.pallas_call(critical_kernel, grid=(ways,), in_specs=[row_block, pl.Blo...]
    ppermute x3, waiting for transfers between devices: 20.5 us -> 32.6 us  [mirrored(): return lax.ppermute(block, axis, [(i, count - 1 - i) for i in range(count)])]
    dot_general x6 -> x2, matrix products: 14.3 us -> 4.99 us  [expert_grads(): gate_up = jnp.dot(saved_rows, weight_in, preferred_element_type=jnp.float32)]
    dot_general x10 -> x2, matrix products: 10.2 us -> 1.05 us  [right_product(): lax.dot_general(left, right, (((1,), (1,)), ((), ())), preferred_element_...]
    dot_general x0 -> x2, matrix products: none -> 6.96 us  [gate_terms(): lax.dot_general(saved_rows, weight_in, (((2,), (1,)), ((0,), (0,))), pref...]
    dot_general x10, matrix products: 16.7 us -> 20.2 us  [left_product(): lax.dot_general(left, right, (((0,), (0,)), ((), ())), preferred_element_...]
    concatenate x2 -> x0, other arithmetic: 2.65 us -> none  [on_device(): back_blocks = jnp.concatenate(input_grads, axis=1)]
  transfers between devices with their start and end apart: 9 -> 9, of which waited for: 8 -> 8; matrix products, arithmetic and copies ran while one was open for 23% -> 20% of each run, Pallas kernels for 0% -> 3%
where the time goes in v9:
time: 206 us; the launch traced here: 205 us
  waiting for transfers between devices  102 us (50%)
  matrix products  36.6 us (18%)
  starting transfers between devices  30.5 us (15%)
  local copies, waits for them, and re-layouts  16.2 us (8%)
  Pallas kernels  13.3 us (6%)
  other arithmetic  5.11 us (2%)
    all_to_all x2, waiting for transfers between devices, on_device(): lax.all_to_all(blocks, 'expert', split_axis=0, concat_axis=0, tiled=True)  47.4 us
    ppermute x3, waiting for transfers between devices, mirrored(): return lax.ppermute(block, axis, [(i, count - 1 - i) for i in range(count)])  32.6 us
    dot_general x10, matrix products, left_product(): lax.dot_general(left, right, (((0,), (0,)), ((), ())), preferred_element_...  20.2 us
    all_to_all x2, waiting for transfers between devices, on_device(): lax.all_to_all(back_blocks, 'expert', split_axis=0, concat_axis=0, tiled=...  17.4 us
    pallas_call x2, Pallas kernels, critical(): pl.pallas_call(critical_kernel, grid=(ways,), in_specs=[row_block, pl.Blo...  13.3 us
    all_to_all x2, starting transfers between devices, on_device(): lax.all_to_all(blocks, 'expert', split_axis=0, concat_axis=0, tiled=True)  9.95 us
    all_to_all x2, starting transfers between devices, on_device(): lax.all_to_all(back_blocks, 'expert', split_axis=0, concat_axis=0, tiled=...  9.38 us
    unnamed x49, local copies, waits for them, and re-layouts  8.49 us
  transfers between devices with their start and end apart: 9, of which 8 were waited for; matrix products, arithmetic and copies ran while one was open for 20% of the time, Pallas kernels for 3%

profile of v9, /device:TPU:1, one launch (start us, length us, event | category | flops | bytes accessed | tf_op | source)
XLA Modules:
  0.0 204.7 jit_solution(8280721266990737236)
XLA Ops:
  5.2 1.7 convolution_convert_fusion.1
  7.0 6.4 %all-to-all-start = ((bf16[8,2,24,2048]{3,2,1,0:T(8,128)(2,1)}), bf16[8,2,24,2048]{3,2,1,0:T(8,128)(2,1)S(1)}, u32[]{:S(2)}, u32[]{:S(2)}) async-start(bf16[8,2,24,2048]{3,2,1,0:T(8,128)(2,1)} %bitcast.13), calls=%async_computation | async-start | bytes 3145728 | tf_op jit(solution)/shard_map/all_to_all | solution.py:161
  13.3 2.9 %slice_bitcast_fusion.4 = bf16[2,192,2048]{2,1,0:T(8,128)(2,1)} fusion(bf16[2,2,1,1,192,2048]{5,4,3,2,1,0:T(8,128)(2,1)} %param.12), kind=kLoop, calls=%fused_computation.32 | loop fusion | bytes 3145728 | tf_op jit(solution)/shard_map/squeeze | solution.py:140
  16.2 2.1 %collective-permute-start = (bf16[2,192,2048]{2,1,0:T(8,128)(2,1)}, bf16[2,192,2048]{2,1,0:T(8,128)(2,1)}, u32[]{:S(2)}, u32[]{:S(2)}) collective-permute-start(bf16[2,192,2048]{2,1,0:T(8,128)(2,1)} %slice_bitcast_fusion.4), channel_id=1, source_target_pairs={{0,24},{8,16},{16,8},{24,0},{1,25},{9,17},{17,9},{25,1},{2,26},{10... | collective-permute-start | bytes 4718600 | tf_op jit(solution)/shard_map/ppermute | solution.py:16
  18.3 3.2 %fusion.17 = f32[2,192,512]{2,1,0:T(8,128)S(1)} fusion(bf16[2,2,1,1,192,2048]{5,4,1,3,2,0:T(8,128)(2,1)S(1)} %bitcast.182, bf16[2,1,1,2048,512]{4,3,2,1,0:T(8,128)(2,1)} %param.8), kind=kOutput, calls=%fused_computation.27 | convolution fusion | flops 805306368 | bytes 6553600 | tf_op jit(solution)/shard_map/dot_general | solution.py:115
  22.6 26.9 %all-to-all-done.slope_ref = bf16[8,2,24,2048]{3,2,1,0:T(8,128)(2,1)S(1)} async-done(((bf16[8,2,24,2048]{3,2,1,0:T(8,128)(2,1)}), bf16[8,2,24,2048]{3,2,1,0:T(8,128)(2,1)S(1)}, u32[]{:S(2)}, u32[]{:S(2)}) %all-to-all-start) | async-done | bytes 1572896 | tf_op jit(solution)/shard_map/all_to_all | solution.py:161
  50.7 6.7 %shard_map.103 = (bf16[8,2,24,2048]{3,2,1,0:T(8,128)(2,1)}, bf16[2,192,512]{2,1,0:T(8,128)(2,1)}) custom-call(bf16[8,2,24,2048]{3,2,1,0:T(8,128)(2,1)} %copy-done.4, f32[2,192,256]{2,1,0:T(8,128)} %get-tuple-element.35.factor_ref, f32[2,192,256]{2,1,0:T(8,128)} %get-tuple-element.36.active_ref, bf16[2,256,2048]{2,1,0:T(8,128)(2,1)} %bitcast.178, ...), custom_call_target="tpu_custom_call" | custom-call | flops 1207959552 | bytes 10616832 | tf_op jit(solution)/shard_map/pallas_call | solution.py:90
  57.3 4.8 %all-to-all-start.1 = ((bf16[8,2,24,2048]{3,2,1,0:T(8,128)(2,1)}), bf16[8,2,24,2048]{3,2,1,0:T(8,128)(2,1)S(1)}, u32[]{:S(2)}, u32[]{:S(2)}) async-start(bf16[8,2,24,2048]{3,2,1,0:T(8,128)(2,1)} %get-tuple-element.12), calls=%async_computation.1 | async-start | bytes 3145728 | tf_op jit(solution)/shard_map/all_to_all | solution.py:171
  63.4 1.9 collective-permute-start.1
  65.5 18.3 %collective-permute-done.1 = bf16[192,2048]{1,0:T(8,128)(2,1)S(1)} collective-permute-done((bf16[192,2048]{1,0:T(8,128)(2,1)}, bf16[192,2048]{1,0:T(8,128)(2,1)S(1)}, u32[]{:S(2)}, u32[]{:S(2)}) %collective-permute-start.1) | collective-permute-done | bytes 786464 | tf_op jit(solution)/shard_map/ppermute | solution.py:16
  83.8 14.7 %all-to-all-done.1 = bf16[8,2,24,2048]{3,2,1,0:T(8,128)(2,1)S(1)} async-done(((bf16[8,2,24,2048]{3,2,1,0:T(8,128)(2,1)}), bf16[8,2,24,2048]{3,2,1,0:T(8,128)(2,1)S(1)}, u32[]{:S(2)}, u32[]{:S(2)}) %all-to-all-start.1) | async-done | bytes 1572896 | tf_op jit(solution)/shard_map/all_to_all | solution.py:171
  98.5 1.8 fusion.6
  100.4 3.5 %collective-permute-start.2 = (bf16[96,2048]{1,0:T(8,128)(2,1)S(1)}, bf16[96,2048]{1,0:T(8,128)(2,1)S(1)}, u32[]{:S(2)}, u32[]{:S(2)}) collective-permute-start(bf16[96,2048]{1,0:T(8,128)(2,1)S(1)} %get-tuple-element.39), channel_id=1, source_target_pairs={{8,0},{16,8},{24,16},{9,1},{17,9},{25,17},{10,2},{18,10},{26,18},{... | collective-permute-start | bytes 1179656 | tf_op jit(solution)/shard_map/ppermute | solution.py:11
  103.9 3.0 %collective-permute-start.3 = (bf16[96,2048]{1,0:T(8,128)(2,1)S(1)}, bf16[96,2048]{1,0:T(8,128)(2,1)S(1)}, u32[]{:S(2)}, u32[]{:S(2)}) collective-permute-start(bf16[96,2048]{1,0:T(8,128)(2,1)S(1)} %get-tuple-element.40), channel_id=1, source_target_pairs={{0,8},{8,16},{16,24},{1,9},{9,17},{17,25},{2,10},{10,18},{18,26},{... | collective-permute-start | bytes 1179656 | tf_op jit(solution)/shard_map/ppermute | solution.py:11
  107.0 3.4 %collective-permute-done.2 = bf16[96,2048]{1,0:T(8,128)(2,1)S(1)} collective-permute-done((bf16[96,2048]{1,0:T(8,128)(2,1)S(1)}, bf16[96,2048]{1,0:T(8,128)(2,1)S(1)}, u32[]{:S(2)}, u32[]{:S(2)}) %collective-permute-start.2) | collective-permute-done | bytes 393248 | tf_op jit(solution)/shard_map/ppermute | solution.py:11
  111.9 1.7 convolution_convert_fusion
  113.7 3.6 %all-to-all-start.2 = ((bf16[8,2,24,2048]{3,2,1,0:T(8,128)(2,1)}), bf16[8,2,24,2048]{3,2,1,0:T(8,128)(2,1)S(1)}, u32[]{:S(2)}, u32[]{:S(2)}) async-start(bf16[8,2,24,2048]{3,2,1,0:T(8,128)(2,1)} %bitcast.37), calls=%async_computation.2 | async-start | bytes 3145728 | tf_op jit(solution)/shard_map/all_to_all | solution.py:161
  117.5 3.8 %fusion.16 = f32[2,192,512]{2,1,0:T(8,128)S(1)} fusion(bf16[2,2,1,1,192,2048]{5,4,1,3,2,0:T(8,128)(2,1)} %bitcast.181, bf16[2,1,1,2048,512]{4,3,2,1,0:T(8,128)(2,1)} %param.8), kind=kOutput, calls=%fused_computation.25 | convolution fusion | flops 805306368 | bytes 6553600 | tf_op jit(solution)/shard_map/dot_general | solution.py:115
  122.3 2.5 %fusion.10 = f32[192,512]{1,0:T(8,128)} fusion(bf16[2,1,1,2048,512]{4,3,2,1,0:T(8,128)(2,1)S(1)} %copy-done.1, bf16[2,192,2048]{2,1,0:T(8,128)(2,1)} %collective-permute-done), kind=kOutput, calls=%fused_computation.18 | convolution fusion | flops 402653184 | bytes 3276800 | tf_op jit(solution)/shard_map/dot_general | solution.py:54
  124.8 2.5 %fusion.12 = f32[192,512]{1,0:T(8,128)} fusion(bf16[2,1,1,2048,512]{4,3,2,1,0:T(8,128)(2,1)S(1)} %copy-done.1, bf16[2,192,2048]{2,1,0:T(8,128)(2,1)} %collective-permute-done), kind=kOutput, calls=%fused_computation.20 | convolution fusion | flops 402653184 | bytes 3276800 | tf_op jit(solution)/shard_map/dot_general | solution.py:54
  127.3 3.8 %fusion.32 = f32[512,2048]{1,0:T(8,128)} fusion(bf16[2,2,1,1,192,2048]{5,4,3,2,1,0:T(8,128)(2,1)} %param.12, bf16[2,192,512]{2,1,0:T(8,128)(2,1)S(1)} %copy-done.18), kind=kOutput, calls=%fused_computation.46 | convolution fusion | flops 402653184 | bytes 5177344 | tf_op jit(solution)/shard_map/dot_general | solution.py:20
  131.2 20.4 %all-to-all-done.2.slope_ref = bf16[8,2,24,2048]{3,2,1,0:T(8,128)(2,1)S(1)} async-done(((bf16[8,2,24,2048]{3,2,1,0:T(8,128)(2,1)}), bf16[8,2,24,2048]{3,2,1,0:T(8,128)(2,1)S(1)}, u32[]{:S(2)}, u32[]{:S(2)}) %all-to-all-start.2) | async-done | bytes 1572896 | tf_op jit(solution)/shard_map/all_to_all | solution.py:161
  152.7 6.7 %shard_map.104 = (bf16[8,2,24,2048]{3,2,1,0:T(8,128)(2,1)}, bf16[2,192,512]{2,1,0:T(8,128)(2,1)}) custom-call(bf16[8,2,24,2048]{3,2,1,0:T(8,128)(2,1)} %copy-done.2, f32[2,192,256]{2,1,0:T(8,128)} %get-tuple-element.32.factor_ref, f32[2,192,256]{2,1,0:T(8,128)} %get-tuple-element.33.active_ref, bf16[2,256,2048]{2,1,0:T(8,128)(2,1)} %bitcast.179, ...), custom_call_target="tpu_custom_call" | custom-call | flops 1207959552 | bytes 10616832 | tf_op jit(solution)/shard_map/pallas_call | solution.py:90
  159.4 4.6 %all-to-all-start.3 = ((bf16[8,2,24,2048]{3,2,1,0:T(8,128)(2,1)}), bf16[8,2,24,2048]{3,2,1,0:T(8,128)(2,1)}, u32[]{:S(2)}, u32[]{:S(2)}) async-start(bf16[8,2,24,2048]{3,2,1,0:T(8,128)(2,1)} %get-tuple-element.14), calls=%async_computation.3 | async-start | bytes 3145728 | tf_op jit(solution)/shard_map/all_to_all | solution.py:171
  167.6 1.9 fusion.28
  169.5 14.3 %collective-permute-done.4 = bf16[192,2048]{1,0:T(8,128)(2,1)S(1)} collective-permute-done((bf16[192,2048]{1,0:T(8,128)(2,1)S(1)}, bf16[192,2048]{1,0:T(8,128)(2,1)S(1)}, u32[]{:S(2)}, u32[]{:S(2)}) %collective-permute-start.4) | collective-permute-done | bytes 786464 | tf_op jit(solution)/shard_map/ppermute | solution.py:16
  184.7 2.1 %add_convert_fusion = bf16[2048,512]{0,1:T(8,128)(2,1)S(1)} fusion(f32[2048,512]{0,1:T(8,128)S(1)} %fusion.28, bf16[2,192,2048]{2,1,0:T(8,128)(2,1)} %collective-permute-done, bf16[192,256]{1,0:T(8,128)(2,1)S(1)} %get-tuple-element.42, bf16[192,256]{1,0:T(8,128)(2,1)S(1)} %get-tuple-element.41), kind=kOutput, calls=%fused_computation.2 | convolution fusion | flops 405143552 | bytes 7274496 | tf_op jit(solution)/shard_map/dot_general | solution.py:20
  187.2 3.3 %fusion.1 = bf16[1,1,2048,512]{2,3,1,0:T(8,128)(2,1)} fusion(bf16[2048,512]{0,1:T(8,128)(2,1)S(1)} %add_convert_fusion, f32[512,2048]{1,0:T(8,128)S(1)} %copy-done, bf16[2,2,1,1,192,2048]{5,4,3,2,1,0:T(8,128)(2,1)} %param.12, bf16[2,192,512]{2,1,0:T(8,128)(2,1)S(1)} %copy-done.22), kind=kOutput, calls=%fused_computation.5 | convolution fusion | flops 406847488 | bytes 9371648 | tf_op jit(solution)/shard_map/dot_general | solution.py:20
  190.5 3.9 %copy.24 = bf16[1,1,2048,512]{3,2,1,0:T(8,128)(2,1)} copy(bf16[1,1,2048,512]{2,3,1,0:T(8,128)(2,1)} %fusion.1) | data formatting | bytes 4194304
  194.4 1.9 fusion.60
  199.0 2.8 %all-to-all-done.3 = bf16[8,2,24,2048]{3,2,1,0:T(8,128)(2,1)} async-done(((bf16[8,2,24,2048]{3,2,1,0:T(8,128)(2,1)}), bf16[8,2,24,2048]{3,2,1,0:T(8,128)(2,1)}, u32[]{:S(2)}, u32[]{:S(2)}) %all-to-all-start.3) | async-done | bytes 1572896 | tf_op jit(solution)/shard_map/all_to_all | solution.py:171
  201.8 2.9 %fusion.9 = bf16[2,1,96,2048]{3,2,1,0:T(8,128)(2,1)} fusion(pred[2,96,384]{2,1,0:T(32,128)(4,1)S(1)} %bitcast.186, bf16[384,2048,1]{1,0,2:T(8,128)(2,1)} %bitcast.41, bf16[1,96,2048]{2,1,0:T(8,128)(2,1)S(1)} %get-tuple-element.38, bf16[1,96,2048]{2,1,0:T(8,128)(2,1)S(1)} %get-tuple-element.37), kind=kOutput, calls=%fused_computation.17 | convolution fusion | flops 303562752 | bytes 3219456 | tf_op jit(solution)/shard_map/dot_general | solution.py:20
  (87 shorter events, 19.9 us)
Async XLA Ops:
  3.3 1.8 copy-start.23
  7.0 42.6 %all-to-all-start = ((bf16[8,2,24,2048]{3,2,1,0:T(8,128)(2,1)}), bf16[8,2,24,2048]{3,2,1,0:T(8,128)(2,1)S(1)}, u32[]{:S(2)}, u32[]{:S(2)}) async-start(bf16[8,2,24,2048]{3,2,1,0:T(8,128)(2,1)} %bitcast.13), calls=%async_computation | async-start | bytes 3145728 | tf_op jit(solution)/shard_map/all_to_all | solution.py:161
  13.3 5.0 %copy-start.7 = (bf16[2,2,1,1,192,2048]{5,4,3,2,1,0:T(8,128)(2,1)S(1)}, bf16[2,2,1,1,192,2048]{5,4,3,2,1,0:T(8,128)(2,1)}, u32[]{:S(2)}) copy-start(bf16[2,2,1,1,192,2048]{5,4,3,2,1,0:T(8,128)(2,1)} %param.12) | copy-start | bytes 9437188
  16.2 41.1 %collective-permute-start = (bf16[2,192,2048]{2,1,0:T(8,128)(2,1)}, bf16[2,192,2048]{2,1,0:T(8,128)(2,1)}, u32[]{:S(2)}, u32[]{:S(2)}) collective-permute-start(bf16[2,192,2048]{2,1,0:T(8,128)(2,1)} %slice_bitcast_fusion.4), channel_id=1, source_target_pairs={{0,24},{8,16},{16,8},{24,0},{1,25},{9,17},{17,9},{25,1},{2,26},{10... | collective-permute-start | bytes 4718600 | tf_op jit(solution)/shard_map/ppermute | solution.py:16
  49.5 1.1 copy-start.4
  57.3 4.8 %copy-start.5 = (bf16[8,2,24,2048]{3,2,1,0:T(8,128)(2,1)S(1)}, bf16[8,2,24,2048]{3,2,1,0:T(8,128)(2,1)}, u32[]{:S(2)}) copy-start(bf16[8,2,24,2048]{3,2,1,0:T(8,128)(2,1)} %copy-done.4) | copy-start | bytes 4718596
  57.3 41.1 %all-to-all-start.1 = ((bf16[8,2,24,2048]{3,2,1,0:T(8,128)(2,1)}), bf16[8,2,24,2048]{3,2,1,0:T(8,128)(2,1)S(1)}, u32[]{:S(2)}, u32[]{:S(2)}) async-start(bf16[8,2,24,2048]{3,2,1,0:T(8,128)(2,1)} %get-tuple-element.12), calls=%async_computation.1 | async-start | bytes 3145728 | tf_op jit(solution)/shard_map/all_to_all | solution.py:171
  63.4 20.4 %collective-permute-start.1 = (bf16[192,2048]{1,0:T(8,128)(2,1)}, bf16[192,2048]{1,0:T(8,128)(2,1)S(1)}, u32[]{:S(2)}, u32[]{:S(2)}) collective-permute-start(bf16[192,2048]{1,0:T(8,128)(2,1)} %bitcast.19), channel_id=1, source_target_pairs={{0,24},{8,16},{16,8},{24,0},{1,25},{9,17},{17,9},{25,1},{2,26},{10... | collective-permute-start | bytes 2359304 | tf_op jit(solution)/shard_map/ppermute | solution.py:16
  83.8 16.6 %copy-start.13 = (bf16[192,2048]{1,0:T(8,128)(2,1)}, bf16[192,2048]{1,0:T(8,128)(2,1)S(1)}, u32[]{:S(2)}) copy-start(bf16[192,2048]{1,0:T(8,128)(2,1)S(1)} %collective-permute-done.1) | copy-start | bytes 2359300
  98.5 13.1 %copy-start.16 = (bf16[1,2,96,2048]{3,2,1,0:T(8,128)(2,1)S(1)}, bf16[1,2,96,2048]{3,2,1,0:T(8,128)(2,1)}, u32[]{:S(2)}) copy-start(bf16[1,2,96,2048]{3,2,1,0:T(8,128)(2,1)} %param.11) | copy-start | bytes 2359300
  100.4 10.0 %collective-permute-start.2 = (bf16[96,2048]{1,0:T(8,128)(2,1)S(1)}, bf16[96,2048]{1,0:T(8,128)(2,1)S(1)}, u32[]{:S(2)}, u32[]{:S(2)}) collective-permute-start(bf16[96,2048]{1,0:T(8,128)(2,1)S(1)} %get-tuple-element.39), channel_id=1, source_target_pairs={{8,0},{16,8},{24,16},{9,1},{17,9},{25,17},{10,2},{18,10},{26,18},{... | collective-permute-start | bytes 1179656 | tf_op jit(solution)/shard_map/ppermute | solution.py:11
  103.9 7.7 %collective-permute-start.3 = (bf16[96,2048]{1,0:T(8,128)(2,1)S(1)}, bf16[96,2048]{1,0:T(8,128)(2,1)S(1)}, u32[]{:S(2)}, u32[]{:S(2)}) collective-permute-start(bf16[96,2048]{1,0:T(8,128)(2,1)S(1)} %get-tuple-element.40), channel_id=1, source_target_pairs={{0,8},{8,16},{16,24},{1,9},{9,17},{17,25},{2,10},{10,18},{18,26},{... | collective-permute-start | bytes 1179656 | tf_op jit(solution)/shard_map/ppermute | solution.py:11
  113.7 37.9 %all-to-all-start.2 = ((bf16[8,2,24,2048]{3,2,1,0:T(8,128)(2,1)}), bf16[8,2,24,2048]{3,2,1,0:T(8,128)(2,1)S(1)}, u32[]{:S(2)}, u32[]{:S(2)}) async-start(bf16[8,2,24,2048]{3,2,1,0:T(8,128)(2,1)} %bitcast.37), calls=%async_computation.2 | async-start | bytes 3145728 | tf_op jit(solution)/shard_map/all_to_all | solution.py:161
  117.4 4.9 %copy-start.1 = (bf16[2,1,1,2048,512]{4,3,2,1,0:T(8,128)(2,1)S(1)}, bf16[2,1,1,2048,512]{4,3,2,1,0:T(8,128)(2,1)}, u32[]{:S(2)}) copy-start(bf16[2,1,1,2048,512]{4,3,2,1,0:T(8,128)(2,1)} %param.8) | copy-start | bytes 12582916
  124.8 2.5 %copy-start.18 = (bf16[2,192,512]{2,1,0:T(8,128)(2,1)S(1)}, bf16[2,192,512]{2,1,0:T(8,128)(2,1)}, u32[]{:S(2)}) copy-start(bf16[2,192,512]{2,1,0:T(8,128)(2,1)} %get-tuple-element.15) | copy-start | bytes 1179652
  151.6 1.1 copy-start.2
  159.4 4.6 %copy-start.3 = (bf16[8,2,24,2048]{3,2,1,0:T(8,128)(2,1)S(1)}, bf16[8,2,24,2048]{3,2,1,0:T(8,128)(2,1)}, u32[]{:S(2)}) copy-start(bf16[8,2,24,2048]{3,2,1,0:T(8,128)(2,1)} %copy-done.2) | copy-start | bytes 4718596
  159.4 42.4 %all-to-all-start.3 = ((bf16[8,2,24,2048]{3,2,1,0:T(8,128)(2,1)}), bf16[8,2,24,2048]{3,2,1,0:T(8,128)(2,1)}, u32[]{:S(2)}, u32[]{:S(2)}) async-start(bf16[8,2,24,2048]{3,2,1,0:T(8,128)(2,1)} %get-tuple-element.14), calls=%async_computation.3 | async-start | bytes 3145728 | tf_op jit(solution)/shard_map/all_to_all | solution.py:171
  164.0 1.8 copy-start.9
  164.0 1.8 copy-start.11
  164.0 1.8 copy-start.12
  165.1 1.7 copy-start.6
  165.1 1.9 copy-start.14
  165.1 2.0 copy-start.19
  165.1 18.8 %collective-permute-start.4 = (bf16[192,2048]{1,0:T(8,128)(2,1)S(1)}, bf16[192,2048]{1,0:T(8,128)(2,1)S(1)}, u32[]{:S(2)}, u32[]{:S(2)}) collective-permute-start(bf16[192,2048]{1,0:T(8,128)(2,1)S(1)} %bitcast.185), channel_id=1, source_target_pairs={{0,24},{8,16},{16,8},{24,0},{1,25},{9,17},{17,9},{25,1},{2,26},{10... | collective-permute-start | bytes 2359304 | tf_op jit(solution)/shard_map/ppermute | solution.py:16
  167.6 16.2 %copy-start.21 = (f32[192,512]{1,0:T(8,128)S(1)}, f32[192,512]{1,0:T(8,128)}, u32[]{:S(2)}) copy-start(f32[192,512]{1,0:T(8,128)} %fusion.10) | copy-start | bytes 1179652
  184.7 2.4 %copy-start = (f32[512,2048]{1,0:T(8,128)S(1)}, f32[512,2048]{1,0:T(8,128)}, u32[]{:S(2)}) copy-start(f32[512,2048]{1,0:T(8,128)} %fusion.32) | copy-start | bytes 12582916
  184.7 2.5 %copy-start.22 = (bf16[2,192,512]{2,1,0:T(8,128)(2,1)S(1)}, bf16[2,192,512]{2,1,0:T(8,128)(2,1)}, u32[]{:S(2)}) copy-start(bf16[2,192,512]{2,1,0:T(8,128)(2,1)} %get-tuple-element.16) | copy-start | bytes 1179652
  194.4 1.9 copy-start.15
  194.4 1.9 copy-start.20
  196.3 1.1 copy-start.8
  196.3 1.2 copy-start.10
  (1 other events, 0.9 us)

commit v10 on v5

--- a/solution.py
+++ b/solution.py
@@ -81,7 +81,7 @@
     capacity = 2 * tokens // experts
     hidden_width = w_out.shape[-2]
     ticks = saved.shape[0]
-    saved_mirror = mirrored(saved[:, 1, 0, 0], "section")
+    saved_mirror = [mirrored(saved[tick_id, 1, 0, 0], "section") for tick_id in range(saved.shape[0])]
     current = grads[:, 0]
     zeros_in = jnp.zeros((model_width, 2 * hidden_width), jnp.float32)
     zeros_out = jnp.zeros((hidden_width, model_width), jnp.float32)
@@ -103,6 +103,7 @@
             mirror_in = mirror_in + part_in
             mirror_out = mirror_out + part_out
         slopes = exchange(blocks)
+        slopes, saved_mirror[tick_id] = lax.optimization_barrier((slopes, saved_mirror[tick_id]))
         input_grads = []
         for way_id in range(2):
             saved_rows = saved[tick_id, way_id, 0, 0]
@@ -117,8 +118,6 @@
                 own_out = own_out + part_out
         slope_mirror = mirrored(slopes[1], "section")
         back_blocks = jnp.concatenate(input_grads, axis=1)
-        if tick_id == 0:
-            back_blocks, saved_mirror = lax.optimization_barrier((back_blocks, saved_mirror))
         returned = lax.all_to_all(back_blocks, "expert", split_axis=0, concat_axis=0, tiled=True)
         if tick_id + 1 < ticks:
             returned, slope_mirror = lax.optimization_barrier((returned, slope_mirror))

time: 205 us -> 206 us (level)
  starting transfers between devices: 30.4 us -> 33.2 us
  matrix products: 44.7 us -> 42.4 us
    all_to_all x2, waiting for transfers between devices: 31.2 us -> 34.1 us  [on_device(): lax.all_to_all(back_blocks, 'expert', split_axis=0, concat_axis=0, tiled=...]
    ppermute x3 -> x4, starting transfers between devices: 4.69 us -> 7.35 us  [mirrored(): return lax.ppermute(block, axis, [(i, count - 1 - i) for i in range(count)])]
    ppermute x3 -> x4, waiting for transfers between devices: 20.5 us -> 19.1 us  [mirrored(): return lax.ppermute(block, axis, [(i, count - 1 - i) for i in range(count)])]
    unnamed x61 -> x67, local copies, waits for them, and re-layouts: 10.9 us -> 10.3 us
  transfers between devices with their start and end apart: 9 -> 10, of which waited for: 8 -> 8; matrix products, arithmetic and copies ran while one was open for 23% -> 21% of each run, Pallas kernels for 0% -> 0%
where the time goes in v10:
time: 206 us; the launch traced here: 205 us
  waiting for transfers between devices  106 us (51%)
  matrix products  42.4 us (21%)
  starting transfers between devices  33.2 us (16%)
  local copies, waits for them, and re-layouts  16.5 us (8%)
  other arithmetic  5.52 us (3%)
    all_to_all x2, waiting for transfers between devices, exchange(): lax.all_to_all(blocks, 'expert', split_axis=0, concat_axis=0, tiled=True)  48.6 us
    all_to_all x2, waiting for transfers between devices, on_device(): lax.all_to_all(back_blocks, 'expert', split_axis=0, concat_axis=0, tiled=...  34.1 us
    ppermute x4, waiting for transfers between devices, mirrored(): return lax.ppermute(block, axis, [(i, count - 1 - i) for i in range(count)])  19.1 us
    dot_general x10, matrix products, left_product(): lax.dot_general(left, right, (((0,), (0,)), ((), ())), preferred_element_...  17 us
    dot_general x6, matrix products, expert_grads(): gate_up = jnp.dot(saved_rows, weight_in, preferred_element_type=jnp.float32)  12.5 us
    unnamed x67, local copies, waits for them, and re-layouts  10.3 us
    all_to_all x2, starting transfers between devices, exchange(): lax.all_to_all(blocks, 'expert', split_axis=0, concat_axis=0, tiled=True)  9.95 us
    dot_general x10, matrix products, right_product(): lax.dot_general(left, right, (((1,), (1,)), ((), ())), preferred_element_...  9.46 us
  transfers between devices with their start and end apart: 10, of which 8 were waited for; matrix products, arithmetic and copies ran while one was open for 21% of the time, Pallas kernels for 0%

profile of v10, /device:TPU:1, one launch (start us, length us, event | category | flops | bytes accessed | tf_op | source)
XLA Modules:
  0.0 205.1 jit_solution(2792746141822336318)
XLA Ops:
  5.2 1.7 convolution_convert_fusion.1
  7.0 6.4 %all-to-all-start = ((bf16[8,2,24,2048]{3,2,1,0:T(8,128)(2,1)}), bf16[8,2,24,2048]{3,2,1,0:T(8,128)(2,1)S(1)}, u32[]{:S(2)}, u32[]{:S(2)}) async-start(bf16[8,2,24,2048]{3,2,1,0:T(8,128)(2,1)} %bitcast.13), calls=%async_computation | async-start | bytes 3145728 | tf_op jit(solution)/shard_map/all_to_all | solution.py:53
  13.3 2.5 %slice_bitcast_fusion = (bf16[192,2048]{1,0:T(8,128)(2,1)}, bf16[192,2048]{1,0:T(8,128)(2,1)S(1)}) fusion(bf16[2,2,1,1,192,2048]{5,4,3,2,1,0:T(8,128)(2,1)} %param.12), kind=kLoop, calls=%fused_computation.76 | loop fusion | bytes 3145728 | tf_op jit(solution)/shard_map/squeeze | solution.py:84
  15.9 2.1 %collective-permute-start = (bf16[192,2048]{1,0:T(8,128)(2,1)S(1)}, bf16[192,2048]{1,0:T(8,128)(2,1)S(1)}, u32[]{:S(2)}, u32[]{:S(2)}) collective-permute-start(bf16[192,2048]{1,0:T(8,128)(2,1)S(1)} %get-tuple-element.31), channel_id=1, source_target_pairs={{0,24},{8,16},{16,8},{24,0},{1,25},{9,17},{17,9},{25,1},{2,26},{10... | collective-permute-start | bytes 2359304 | tf_op jit(solution)/shard_map/ppermute | solution.py:15
  17.9 3.0 %fusion.24 = f32[192,512]{1,0:T(8,128)} fusion(bf16[2,1,1,2048,512]{4,3,2,1,0:T(8,128)(2,1)} %param.8, bf16[2,2,1,1,192,2048]{5,4,3,2,1,0:T(8,128)(2,1)S(1)} %copy-done.1), kind=kOutput, calls=%fused_computation.36 | convolution fusion | flops 402653184 | bytes 3276800 | tf_op jit(solution)/shard_map/dot_general | solution.py:59
  22.2 27.3 %all-to-all-done = bf16[8,2,24,2048]{3,2,1,0:T(8,128)(2,1)S(1)} async-done(((bf16[8,2,24,2048]{3,2,1,0:T(8,128)(2,1)}), bf16[8,2,24,2048]{3,2,1,0:T(8,128)(2,1)S(1)}, u32[]{:S(2)}, u32[]{:S(2)}) %all-to-all-start) | async-done | bytes 1572896 | tf_op jit(solution)/shard_map/all_to_all | solution.py:53
  49.7 2.3 %copy-done.28 = bf16[2,1,1,256,2048]{4,3,2,1,0:T(8,128)(2,1)S(1)} copy-done((bf16[2,1,1,256,2048]{4,3,2,1,0:T(8,128)(2,1)S(1)}, bf16[2,1,1,256,2048]{4,3,2,1,0:T(8,128)(2,1)}, u32[]{:S(2)}) %copy-start.28) | copy-done | bytes 2097176
  57.2 4.8 %all-to-all-start.1 = ((bf16[8,2,24,2048]{3,2,1,0:T(8,128)(2,1)}), bf16[8,2,24,2048]{3,2,1,0:T(8,128)(2,1)S(1)}, u32[]{:S(2)}, u32[]{:S(2)}) async-start(bf16[8,2,24,2048]{3,2,1,0:T(8,128)(2,1)} %pad_maximum_fusion), calls=%async_computation.1 | async-start | bytes 3145728 | tf_op jit(solution)/shard_map/all_to_all | solution.py:121
  62.0 1.9 collective-permute-start.1
  64.1 18.3 %collective-permute-done.1 = bf16[192,2048]{1,0:T(8,128)(2,1)S(1)} collective-permute-done((bf16[192,2048]{1,0:T(8,128)(2,1)}, bf16[192,2048]{1,0:T(8,128)(2,1)S(1)}, u32[]{:S(2)}, u32[]{:S(2)}) %collective-permute-start.1) | collective-permute-done | bytes 786464 | tf_op jit(solution)/shard_map/ppermute | solution.py:15
  82.4 15.9 %all-to-all-done.1 = bf16[8,2,24,2048]{3,2,1,0:T(8,128)(2,1)S(1)} async-done(((bf16[8,2,24,2048]{3,2,1,0:T(8,128)(2,1)}), bf16[8,2,24,2048]{3,2,1,0:T(8,128)(2,1)S(1)}, u32[]{:S(2)}, u32[]{:S(2)}) %all-to-all-start.1) | async-done | bytes 1572896 | tf_op jit(solution)/shard_map/all_to_all | solution.py:121
  99.0 3.6 %collective-permute-start.2 = (bf16[96,2048]{1,0:T(8,128)(2,1)S(1)}, bf16[96,2048]{1,0:T(8,128)(2,1)S(1)}, u32[]{:S(2)}, u32[]{:S(2)}) collective-permute-start(bf16[96,2048]{1,0:T(8,128)(2,1)S(1)} %get-tuple-element.38), channel_id=1, source_target_pairs={{8,0},{16,8},{24,16},{9,1},{17,9},{25,17},{10,2},{18,10},{26,18},{... | collective-permute-start | bytes 1179656 | tf_op jit(solution)/shard_map/ppermute | solution.py:10
  102.6 3.0 %collective-permute-start.3 = (bf16[96,2048]{1,0:T(8,128)(2,1)S(1)}, bf16[96,2048]{1,0:T(8,128)(2,1)S(1)}, u32[]{:S(2)}, u32[]{:S(2)}) collective-permute-start(bf16[96,2048]{1,0:T(8,128)(2,1)S(1)} %get-tuple-element.39), channel_id=1, source_target_pairs={{0,8},{8,16},{16,24},{1,9},{9,17},{17,25},{2,10},{10,18},{18,26},{... | collective-permute-start | bytes 1179656 | tf_op jit(solution)/shard_map/ppermute | solution.py:10
  105.8 3.4 %collective-permute-done.2 = bf16[96,2048]{1,0:T(8,128)(2,1)S(1)} collective-permute-done((bf16[96,2048]{1,0:T(8,128)(2,1)S(1)}, bf16[96,2048]{1,0:T(8,128)(2,1)S(1)}, u32[]{:S(2)}, u32[]{:S(2)}) %collective-permute-start.2) | collective-permute-done | bytes 393248 | tf_op jit(solution)/shard_map/ppermute | solution.py:10
  110.7 1.7 convolution_convert_fusion
  112.4 3.6 %all-to-all-start.2 = ((bf16[8,2,24,2048]{3,2,1,0:T(8,128)(2,1)}), bf16[8,2,24,2048]{3,2,1,0:T(8,128)(2,1)S(1)}, u32[]{:S(2)}, u32[]{:S(2)}) async-start(bf16[8,2,24,2048]{3,2,1,0:T(8,128)(2,1)} %bitcast.43), calls=%async_computation.2 | async-start | bytes 3145728 | tf_op jit(solution)/shard_map/all_to_all | solution.py:53
  116.0 2.7 %collective-permute-start.4 = (bf16[192,2048]{1,0:T(8,128)(2,1)}, bf16[192,2048]{1,0:T(8,128)(2,1)S(1)}, u32[]{:S(2)}, u32[]{:S(2)}) collective-permute-start(bf16[192,2048]{1,0:T(8,128)(2,1)} %get-tuple-element.30), channel_id=1, source_target_pairs={{0,24},{8,16},{16,8},{24,0},{1,25},{9,17},{17,9},{25,1},{2,26},{10... | collective-permute-start | bytes 2359304 | tf_op jit(solution)/shard_map/ppermute | solution.py:15
  118.9 3.3 %fusion.21 = f32[192,512]{1,0:T(8,128)} fusion(bf16[2,1,1,2048,512]{4,3,2,1,0:T(8,128)(2,1)} %param.8, bf16[2,2,1,1,192,2048]{5,4,3,2,1,0:T(8,128)(2,1)} %param.12), kind=kOutput, calls=%fused_computation.33 | convolution fusion | flops 402653184 | bytes 3276800 | tf_op jit(solution)/shard_map/dot_general | solution.py:59
  122.2 3.0 %fusion.11 = f32[192,512]{1,0:T(8,128)} fusion(bf16[2,1,1,2048,512]{4,3,2,1,0:T(8,128)(2,1)} %param.8, bf16[2,2,1,1,192,2048]{5,4,3,2,1,0:T(8,128)(2,1)S(1)} %copy-done.2), kind=kOutput, calls=%fused_computation.23 | convolution fusion | flops 402653184 | bytes 3276800 | tf_op jit(solution)/shard_map/dot_general | solution.py:59
  125.8 2.7 %fusion.55 = f32[512,2048]{1,0:T(8,128)} fusion(bf16[2,2,1,1,192,2048]{5,4,3,2,1,0:T(8,128)(2,1)S(1)} %copy-done.2, bf16[192,256]{1,0:T(8,128)(2,1)S(1)} %get-tuple-element.49, bf16[192,256]{1,0:T(8,128)(2,1)S(1)} %get-tuple-element.48), kind=kOutput, calls=%fused_computation.72 | convolution fusion | flops 403046400 | bytes 5177344 | tf_op jit(solution)/shard_map/dot_general | solution.py:19
  129.1 21.3 %all-to-all-done.2 = bf16[8,2,24,2048]{3,2,1,0:T(8,128)(2,1)S(1)} async-done(((bf16[8,2,24,2048]{3,2,1,0:T(8,128)(2,1)}), bf16[8,2,24,2048]{3,2,1,0:T(8,128)(2,1)S(1)}, u32[]{:S(2)}, u32[]{:S(2)}) %all-to-all-start.2) | async-done | bytes 1572896 | tf_op jit(solution)/shard_map/all_to_all | solution.py:53
  152.1 2.4 %fusion.70 = (bf16[192,256]{1,0:T(8,128)(2,1)S(1)}, bf16[192,256]{1,0:T(8,128)(2,1)S(1)}) fusion(f32[192,512]{1,0:T(8,128)} %fusion.11, bf16[192,2048]{1,0:T(8,128)(2,1)} %bitcast.45, bf16[2,1,1,256,2048]{4,3,2,1,0:T(8,128)(2,1)} %param.9), kind=kOutput, calls=%fused_computation.99 | convolution fusion | flops 201965568 | bytes 2424832 | tf_op jit(solution)/shard_map/dot_general | solution.py:25
  159.9 4.5 %all-to-all-start.3 = ((bf16[8,2,24,2048]{3,2,1,0:T(8,128)(2,1)}), bf16[8,2,24,2048]{3,2,1,0:T(8,128)(2,1)}, u32[]{:S(2)}, u32[]{:S(2)}) async-start(bf16[8,2,24,2048]{3,2,1,0:T(8,128)(2,1)} %pad_maximum_fusion.1), calls=%async_computation.3 | async-start | bytes 3145728 | tf_op jit(solution)/shard_map/all_to_all | solution.py:121
  164.4 1.8 fusion.93
  166.3 2.0 fusion.52
  169.0 1.6 multiply_convert_fusion.5
  173.1 2.3 %fusion.5 = bf16[1,1,2048,512]{2,3,1,0:T(8,128)(2,1)} fusion(f32[2048,512]{0,1:T(8,128)S(1)} %fusion.83, bf16[192,2048]{1,0:T(8,128)(2,1)S(1)} %copy-done.16, f32[512,2048]{1,0:T(8,128)S(1)} %copy-done, f32[512,2048]{1,0:T(8,128)S(1)} %fusion.52, bf16[192,256]{1,0:T(8,128)(2,1)S(1)} %get-tuple-element.41, bf16[192,256]{1,0:T(8,128)(2,1)S(1)} %get-tuple-element.40), kind=kOutput, calls=%fused_computation.13 | convolution fusion | flops 409337856 | bytes 15663104 | tf_op jit(solution)/shard_map/dot_general | solution.py:19
  175.4 3.9 %copy.35 = bf16[1,1,2048,512]{3,2,1,0:T(8,128)(2,1)} copy(bf16[1,1,2048,512]{2,3,1,0:T(8,128)(2,1)} %fusion.5) | data formatting | bytes 4194304
  179.3 1.9 fusion.94
  182.5 1.5 fusion.8
  184.0 18.2 %all-to-all-done.3 = bf16[8,2,24,2048]{3,2,1,0:T(8,128)(2,1)} async-done(((bf16[8,2,24,2048]{3,2,1,0:T(8,128)(2,1)}), bf16[8,2,24,2048]{3,2,1,0:T(8,128)(2,1)}, u32[]{:S(2)}, u32[]{:S(2)}) %all-to-all-start.3) | async-done | bytes 1572896 | tf_op jit(solution)/shard_map/all_to_all | solution.py:121
  202.2 2.9 %fusion.9 = bf16[2,1,96,2048]{3,2,1,0:T(8,128)(2,1)} fusion(pred[2,96,384]{2,1,0:T(32,128)(4,1)S(1)} %bitcast.213, bf16[384,2048,1]{1,0,2:T(8,128)(2,1)} %bitcast.53, bf16[1,96,2048]{2,1,0:T(8,128)(2,1)S(1)} %get-tuple-element.37, bf16[1,96,2048]{2,1,0:T(8,128)(2,1)S(1)} %get-tuple-element.36), kind=kOutput, calls=%fused_computation.21 | convolution fusion | flops 303562752 | bytes 3219456 | tf_op jit(solution)/shard_map/dot_general | solution.py:19
  (115 shorter events, 26.4 us)
Async XLA Ops:
  7.0 42.6 %all-to-all-start = ((bf16[8,2,24,2048]{3,2,1,0:T(8,128)(2,1)}), bf16[8,2,24,2048]{3,2,1,0:T(8,128)(2,1)S(1)}, u32[]{:S(2)}, u32[]{:S(2)}) async-start(bf16[8,2,24,2048]{3,2,1,0:T(8,128)(2,1)} %bitcast.13), calls=%async_computation | async-start | bytes 3145728 | tf_op jit(solution)/shard_map/all_to_all | solution.py:53
  13.3 4.6 %copy-start.1 = (bf16[2,2,1,1,192,2048]{5,4,3,2,1,0:T(8,128)(2,1)S(1)}, bf16[2,2,1,1,192,2048]{5,4,3,2,1,0:T(8,128)(2,1)}, u32[]{:S(2)}) copy-start(bf16[2,2,1,1,192,2048]{5,4,3,2,1,0:T(8,128)(2,1)} %param.12) | copy-start | bytes 9437188
  15.9 5.0 %copy-start.24 = (bf16[2,1,1,2048,512]{4,3,2,1,0:T(8,128)(2,1)S(1)}, bf16[2,1,1,2048,512]{4,3,2,1,0:T(8,128)(2,1)}, u32[]{:S(2)}) copy-start(bf16[2,1,1,2048,512]{4,3,2,1,0:T(8,128)(2,1)} %param.8) | copy-start | bytes 12582916
  15.9 33.8 %collective-permute-start = (bf16[192,2048]{1,0:T(8,128)(2,1)S(1)}, bf16[192,2048]{1,0:T(8,128)(2,1)S(1)}, u32[]{:S(2)}, u32[]{:S(2)}) collective-permute-start(bf16[192,2048]{1,0:T(8,128)(2,1)S(1)} %get-tuple-element.31), channel_id=1, source_target_pairs={{0,24},{8,16},{16,8},{24,0},{1,25},{9,17},{17,9},{25,1},{2,26},{10... | collective-permute-start | bytes 2359304 | tf_op jit(solution)/shard_map/ppermute | solution.py:15
  49.5 2.4 %copy-start.28 = (bf16[2,1,1,256,2048]{4,3,2,1,0:T(8,128)(2,1)S(1)}, bf16[2,1,1,256,2048]{4,3,2,1,0:T(8,128)(2,1)}, u32[]{:S(2)}) copy-start(bf16[2,1,1,256,2048]{4,3,2,1,0:T(8,128)(2,1)} %param.9) | copy-start | bytes 6291460
  49.5 2.5 %copy-start.32 = (f32[192,512]{1,0:T(8,128)S(1)}, f32[192,512]{1,0:T(8,128)}, u32[]{:S(2)}) copy-start(f32[192,512]{1,0:T(8,128)} %fusion.14) | copy-start | bytes 1179652
  49.6 3.4 %copy-start.3 = (bf16[8,1,24,2048]{3,2,1,0:T(8,128)(2,1)}, bf16[8,1,24,2048]{3,2,1,0:T(8,128)(2,1)S(1)}, u32[]{:S(2)}) copy-start(bf16[8,1,24,2048]{3,2,1,0:T(8,128)(2,1)S(1)} %get-tuple-element.35) | copy-start | bytes 2359300
  49.6 3.4 %copy-start.13 = (bf16[8,1,24,2048]{3,2,1,0:T(8,128)(2,1)}, bf16[8,1,24,2048]{3,2,1,0:T(8,128)(2,1)S(1)}, u32[]{:S(2)}) copy-start(bf16[8,1,24,2048]{3,2,1,0:T(8,128)(2,1)S(1)} %get-tuple-element.34) | copy-start | bytes 2359300
  49.7 2.9 %copy-start.17 = (f32[192,512]{1,0:T(8,128)S(1)}, f32[192,512]{1,0:T(8,128)}, u32[]{:S(2)}) copy-start(f32[192,512]{1,0:T(8,128)} %fusion.24) | copy-start | bytes 1179652
  49.7 3.4 %copy-start.14 = (bf16[192,2048]{1,0:T(8,128)(2,1)}, bf16[192,2048]{1,0:T(8,128)(2,1)S(1)}, u32[]{:S(2)}) copy-start(bf16[192,2048]{1,0:T(8,128)(2,1)S(1)} %collective-permute-done) | copy-start | bytes 2359300
  57.2 41.2 %copy-start.5 = (bf16[2,1,96,2048]{3,2,1,0:T(8,128)(2,1)S(1)}, bf16[2,1,96,2048]{3,2,1,0:T(8,128)(2,1)}, u32[]{:S(2)}) copy-start(bf16[2,1,96,2048]{3,2,1,0:T(8,128)(2,1)} %param.10) | copy-start | bytes 2359300
  57.2 41.1 %all-to-all-start.1 = ((bf16[8,2,24,2048]{3,2,1,0:T(8,128)(2,1)}), bf16[8,2,24,2048]{3,2,1,0:T(8,128)(2,1)S(1)}, u32[]{:S(2)}, u32[]{:S(2)}) async-start(bf16[8,2,24,2048]{3,2,1,0:T(8,128)(2,1)} %pad_maximum_fusion), calls=%async_computation.1 | async-start | bytes 3145728 | tf_op jit(solution)/shard_map/all_to_all | solution.py:121
  62.0 20.5 %collective-permute-start.1 = (bf16[192,2048]{1,0:T(8,128)(2,1)}, bf16[192,2048]{1,0:T(8,128)(2,1)S(1)}, u32[]{:S(2)}, u32[]{:S(2)}) collective-permute-start(bf16[192,2048]{1,0:T(8,128)(2,1)} %bitcast.208), channel_id=1, source_target_pairs={{0,24},{8,16},{16,8},{24,0},{1,25},{9,17},{17,9},{25,1},{2,26},{10... | collective-permute-start | bytes 2359304 | tf_op jit(solution)/shard_map/ppermute | solution.py:15
  82.4 16.6 %copy-start.9 = (bf16[192,2048]{1,0:T(8,128)(2,1)}, bf16[192,2048]{1,0:T(8,128)(2,1)S(1)}, u32[]{:S(2)}) copy-start(bf16[192,2048]{1,0:T(8,128)(2,1)S(1)} %collective-permute-done.1) | copy-start | bytes 2359300
  98.9 11.5 %copy-start.12 = (bf16[1,2,96,2048]{3,2,1,0:T(8,128)(2,1)S(1)}, bf16[1,2,96,2048]{3,2,1,0:T(8,128)(2,1)}, u32[]{:S(2)}) copy-start(bf16[1,2,96,2048]{3,2,1,0:T(8,128)(2,1)} %param.11) | copy-start | bytes 2359300
  99.0 10.2 %collective-permute-start.2 = (bf16[96,2048]{1,0:T(8,128)(2,1)S(1)}, bf16[96,2048]{1,0:T(8,128)(2,1)S(1)}, u32[]{:S(2)}, u32[]{:S(2)}) collective-permute-start(bf16[96,2048]{1,0:T(8,128)(2,1)S(1)} %get-tuple-element.38), channel_id=1, source_target_pairs={{8,0},{16,8},{24,16},{9,1},{17,9},{25,17},{10,2},{18,10},{26,18},{... | collective-permute-start | bytes 1179656 | tf_op jit(solution)/shard_map/ppermute | solution.py:10
  102.6 7.7 %collective-permute-start.3 = (bf16[96,2048]{1,0:T(8,128)(2,1)S(1)}, bf16[96,2048]{1,0:T(8,128)(2,1)S(1)}, u32[]{:S(2)}, u32[]{:S(2)}) collective-permute-start(bf16[96,2048]{1,0:T(8,128)(2,1)S(1)} %get-tuple-element.39), channel_id=1, source_target_pairs={{0,8},{8,16},{16,24},{1,9},{9,17},{17,25},{2,10},{10,18},{18,26},{... | collective-permute-start | bytes 1179656 | tf_op jit(solution)/shard_map/ppermute | solution.py:10
  112.4 37.9 %all-to-all-start.2 = ((bf16[8,2,24,2048]{3,2,1,0:T(8,128)(2,1)}), bf16[8,2,24,2048]{3,2,1,0:T(8,128)(2,1)S(1)}, u32[]{:S(2)}, u32[]{:S(2)}) async-start(bf16[8,2,24,2048]{3,2,1,0:T(8,128)(2,1)} %bitcast.43), calls=%async_computation.2 | async-start | bytes 3145728 | tf_op jit(solution)/shard_map/all_to_all | solution.py:53
  116.0 35.3 %collective-permute-start.4 = (bf16[192,2048]{1,0:T(8,128)(2,1)}, bf16[192,2048]{1,0:T(8,128)(2,1)S(1)}, u32[]{:S(2)}, u32[]{:S(2)}) collective-permute-start(bf16[192,2048]{1,0:T(8,128)(2,1)} %get-tuple-element.30), channel_id=1, source_target_pairs={{0,24},{8,16},{16,8},{24,0},{1,25},{9,17},{17,9},{25,1},{2,26},{10... | collective-permute-start | bytes 2359304 | tf_op jit(solution)/shard_map/ppermute | solution.py:15
  118.9 3.3 %copy-start.2 = (bf16[2,2,1,1,192,2048]{5,4,3,2,1,0:T(8,128)(2,1)S(1)}, bf16[2,2,1,1,192,2048]{5,4,3,2,1,0:T(8,128)(2,1)}, u32[]{:S(2)}) copy-start(bf16[2,2,1,1,192,2048]{5,4,3,2,1,0:T(8,128)(2,1)} %param.12) | copy-start | bytes 9437188
  118.9 6.3 %copy-start.26 = (bf16[2,1,1,2048,512]{4,3,2,1,0:T(8,128)(2,1)S(1)}, bf16[2,1,1,2048,512]{4,3,2,1,0:T(8,128)(2,1)}, u32[]{:S(2)}) copy-start(bf16[2,1,1,2048,512]{4,3,2,1,0:T(8,128)(2,1)} %param.8) | copy-start | bytes 12582916
  122.2 3.0 %copy-start.15 = (bf16[192,2048]{1,0:T(8,128)(2,1)S(1)}, bf16[192,2048]{1,0:T(8,128)(2,1)}, u32[]{:S(2)}) copy-start(bf16[192,2048]{1,0:T(8,128)(2,1)} %copy-done.14) | copy-start | bytes 2359300
  125.8 2.7 %copy-start.19 = (f32[192,512]{1,0:T(8,128)}, f32[192,512]{1,0:T(8,128)S(1)}, u32[]{:S(2)}) copy-start(f32[192,512]{1,0:T(8,128)S(1)} %fusion.18) | copy-start | bytes 1179652
  125.8 2.7 %copy-start.10 = (bf16[192,2048]{1,0:T(8,128)(2,1)S(1)}, bf16[192,2048]{1,0:T(8,128)(2,1)}, u32[]{:S(2)}) copy-start(bf16[192,2048]{1,0:T(8,128)(2,1)} %copy-done.9) | copy-start | bytes 2359300
  125.8 2.7 %copy-start.29 = (bf16[2,1,1,256,2048]{4,3,2,1,0:T(8,128)(2,1)S(1)}, bf16[2,1,1,256,2048]{4,3,2,1,0:T(8,128)(2,1)}, u32[]{:S(2)}) copy-start(bf16[2,1,1,256,2048]{4,3,2,1,0:T(8,128)(2,1)} %param.9) | copy-start | bytes 6291460
  150.4 4.2 %copy-start.27 = (bf16[2,1,1,2048,512]{4,3,2,1,0:T(8,128)(2,1)S(1)}, bf16[2,1,1,2048,512]{4,3,2,1,0:T(8,128)(2,1)}, u32[]{:S(2)}) copy-start(bf16[2,1,1,2048,512]{4,3,2,1,0:T(8,128)(2,1)} %param.8) | copy-start | bytes 12582916
  151.4 4.6 %copy-start.6 = (bf16[8,1,24,2048]{3,2,1,0:T(8,128)(2,1)}, bf16[8,1,24,2048]{3,2,1,0:T(8,128)(2,1)S(1)}, u32[]{:S(2)}) copy-start(bf16[8,1,24,2048]{3,2,1,0:T(8,128)(2,1)S(1)} %get-tuple-element.33) | copy-start | bytes 2359300
  151.4 4.6 %copy-start.7 = (bf16[192,2048]{1,0:T(8,128)(2,1)}, bf16[192,2048]{1,0:T(8,128)(2,1)S(1)}, u32[]{:S(2)}) copy-start(bf16[192,2048]{1,0:T(8,128)(2,1)S(1)} %collective-permute-done.4) | copy-start | bytes 2359300
  151.4 17.7 %collective-permute-start.5 = (bf16[192,2048]{1,0:T(8,128)(2,1)}, bf16[192,2048]{1,0:T(8,128)(2,1)}, u32[]{:S(2)}, u32[]{:S(2)}) collective-permute-start(bf16[192,2048]{1,0:T(8,128)(2,1)} %bitcast.45), channel_id=1, source_target_pairs={{0,24},{8,16},{16,8},{24,0},{1,25},{9,17},{17,9},{25,1},{2,26},{10... | collective-permute-start | bytes 2359304 | tf_op jit(solution)/shard_map/ppermute | solution.py:15
  159.9 42.3 %all-to-all-start.3 = ((bf16[8,2,24,2048]{3,2,1,0:T(8,128)(2,1)}), bf16[8,2,24,2048]{3,2,1,0:T(8,128)(2,1)}, u32[]{:S(2)}, u32[]{:S(2)}) async-start(bf16[8,2,24,2048]{3,2,1,0:T(8,128)(2,1)} %pad_maximum_fusion.1), calls=%async_computation.3 | async-start | bytes 3145728 | tf_op jit(solution)/shard_map/all_to_all | solution.py:121
  166.3 2.8 %copy-start.22 = (f32[192,512]{1,0:T(8,128)S(1)}, f32[192,512]{1,0:T(8,128)}, u32[]{:S(2)}) copy-start(f32[192,512]{1,0:T(8,128)} %fusion.16) | copy-start | bytes 1179652
  166.3 2.8 %copy-start.31 = (bf16[2,1,1,256,2048]{4,3,2,1,0:T(8,128)(2,1)S(1)}, bf16[2,1,1,256,2048]{4,3,2,1,0:T(8,128)(2,1)}, u32[]{:S(2)}) copy-start(bf16[2,1,1,256,2048]{4,3,2,1,0:T(8,128)(2,1)} %param.9) | copy-start | bytes 6291460
  (11 other events, 20.4 us)

commit v11 on v10

--- a/solution.py
+++ b/solution.py
@@ -93,6 +93,7 @@
         scaled = (probs[tick_id, :, 0][:, :, None] * current.astype(jnp.float32)).astype(jnp.bfloat16)
         blocks = jnp.dot(one_hot, scaled.reshape(-1, model_width), preferred_element_type=jnp.float32)
         blocks = blocks.astype(jnp.bfloat16).reshape(experts, 2, capacity, model_width)
+        blocks, tick_w_in, tick_w_out = lax.optimization_barrier((blocks, w_in[:, 0, 0], w_out[:, 0, 0]))
         if slope_mirror is not None:
             hidden_m, pair_grad_m = expert_grads(
                 slope_mirror, saved_mirror[tick_id - 1], w_in[0, 0, 0], w_out[0, 0, 0]
@@ -108,9 +109,9 @@
         for way_id in range(2):
             saved_rows = saved[tick_id, way_id, 0, 0]
             hidden, pair_grad = expert_grads(
-                slopes[way_id], saved_rows, w_in[way_id, 0, 0], w_out[way_id, 0, 0]
+                slopes[way_id], saved_rows, tick_w_in[way_id], tick_w_out[way_id]
             )
-            input_grad = right_product(pair_grad, w_in[way_id, 0, 0]).astype(jnp.bfloat16)
+            input_grad = right_product(pair_grad, tick_w_in[way_id]).astype(jnp.bfloat16)
             input_grads.append(input_grad.reshape(experts, 1, capacity, model_width))
             if way_id == 0:
                 part_in, part_out = weight_terms(saved_rows, slopes[0], hidden, pair_grad)

time: 206 us -> 206 us (level)
    all_to_all x2, waiting for transfers between devices: 34.1 us -> 30.9 us  [on_device(): lax.all_to_all(back_blocks, 'expert', split_axis=0, concat_axis=0, tiled=...]
    ppermute x4, waiting for transfers between devices: 19.1 us -> 21.4 us  [mirrored(): return lax.ppermute(block, axis, [(i, count - 1 - i) for i in range(count)])]
  transfers between devices with their start and end apart: 10 -> 10, of which waited for: 8 -> 8; matrix products, arithmetic and copies ran while one was open for 21% -> 19% of each run, Pallas kernels for 0% -> 0%
where the time goes in v11:
time: 206 us; the launch traced here: 205 us
  waiting for transfers between devices  106 us (51%)
  matrix products  42.5 us (21%)
  starting transfers between devices  33.2 us (16%)
  local copies, waits for them, and re-layouts  17.4 us (8%)
  other arithmetic  5.51 us (3%)
    all_to_all x2, waiting for transfers between devices, exchange(): lax.all_to_all(blocks, 'expert', split_axis=0, concat_axis=0, tiled=True)  48.7 us
    all_to_all x2, waiting for transfers between devices, on_device(): lax.all_to_all(back_blocks, 'expert', split_axis=0, concat_axis=0, tiled=...  30.9 us
    ppermute x4, waiting for transfers between devices, mirrored(): return lax.ppermute(block, axis, [(i, count - 1 - i) for i in range(count)])  21.4 us
    dot_general x10, matrix products, left_product(): lax.dot_general(left, right, (((0,), (0,)), ((), ())), preferred_element_...  17.2 us
    dot_general x6, matrix products, expert_grads(): gate_up = jnp.dot(saved_rows, weight_in, preferred_element_type=jnp.float32)  13 us
    unnamed x67, local copies, waits for them, and re-layouts  11.3 us
    all_to_all x2, starting transfers between devices, exchange(): lax.all_to_all(blocks, 'expert', split_axis=0, concat_axis=0, tiled=True)  9.95 us
    all_to_all x2, starting transfers between devices, on_device(): lax.all_to_all(back_blocks, 'expert', split_axis=0, concat_axis=0, tiled=...  9.25 us
  transfers between devices with their start and end apart: 10, of which 8 were waited for; matrix products, arithmetic and copies ran while one was open for 19% of the time, Pallas kernels for 0%

profile of v11, /device:TPU:1, one launch (start us, length us, event | category | flops | bytes accessed | tf_op | source)
XLA Modules:
  0.0 205.3 jit_solution(11805666908892869439)
XLA Ops:
  5.2 1.7 convolution_convert_fusion.1
  7.0 6.4 %all-to-all-start = ((bf16[8,2,24,2048]{3,2,1,0:T(8,128)(2,1)}), bf16[8,2,24,2048]{3,2,1,0:T(8,128)(2,1)S(1)}, u32[]{:S(2)}, u32[]{:S(2)}) async-start(bf16[8,2,24,2048]{3,2,1,0:T(8,128)(2,1)} %bitcast.13), calls=%async_computation | async-start | bytes 3145728 | tf_op jit(solution)/shard_map/all_to_all | solution.py:53
  13.3 2.5 %slice_bitcast_fusion = (bf16[192,2048]{1,0:T(8,128)(2,1)}, bf16[192,2048]{1,0:T(8,128)(2,1)S(1)}) fusion(bf16[2,2,1,1,192,2048]{5,4,3,2,1,0:T(8,128)(2,1)} %param.12), kind=kLoop, calls=%fused_computation.84 | loop fusion | bytes 3145728 | tf_op jit(solution)/shard_map/squeeze | solution.py:84
  15.9 2.1 %collective-permute-start = (bf16[192,2048]{1,0:T(8,128)(2,1)S(1)}, bf16[192,2048]{1,0:T(8,128)(2,1)S(1)}, u32[]{:S(2)}, u32[]{:S(2)}) collective-permute-start(bf16[192,2048]{1,0:T(8,128)(2,1)S(1)} %get-tuple-element.43), channel_id=1, source_target_pairs={{0,24},{8,16},{16,8},{24,0},{1,25},{9,17},{17,9},{25,1},{2,26},{10... | collective-permute-start | bytes 2359304 | tf_op jit(solution)/shard_map/ppermute | solution.py:15
  17.9 3.0 %fusion.38 = f32[192,512]{1,0:T(8,128)} fusion(bf16[2,2048,512]{2,1,0:T(8,128)(2,1)} %bitcast.239, bf16[2,2,1,1,192,2048]{5,4,3,2,1,0:T(8,128)(2,1)S(1)} %copy-done.1), kind=kOutput, calls=%fused_computation.54 | convolution fusion | flops 402653184 | bytes 3276800 | tf_op jit(solution)/shard_map/dot_general | solution.py:59
  22.2 27.3 %all-to-all-done = bf16[8,2,24,2048]{3,2,1,0:T(8,128)(2,1)S(1)} async-done(((bf16[8,2,24,2048]{3,2,1,0:T(8,128)(2,1)}), bf16[8,2,24,2048]{3,2,1,0:T(8,128)(2,1)S(1)}, u32[]{:S(2)}, u32[]{:S(2)}) %all-to-all-start) | async-done | bytes 1572896 | tf_op jit(solution)/shard_map/all_to_all | solution.py:53
  49.7 2.3 %copy-done.27 = bf16[2,1,1,256,2048]{4,3,2,1,0:T(8,128)(2,1)S(1)} copy-done((bf16[2,1,1,256,2048]{4,3,2,1,0:T(8,128)(2,1)S(1)}, bf16[2,1,1,256,2048]{4,3,2,1,0:T(8,128)(2,1)}, u32[]{:S(2)}) %copy-start.27) | copy-done | bytes 2097176
  57.2 4.8 %all-to-all-start.1 = ((bf16[8,2,24,2048]{3,2,1,0:T(8,128)(2,1)}), bf16[8,2,24,2048]{3,2,1,0:T(8,128)(2,1)S(1)}, u32[]{:S(2)}, u32[]{:S(2)}) async-start(bf16[8,2,24,2048]{3,2,1,0:T(8,128)(2,1)} %pad_maximum_fusion), calls=%async_computation.1 | async-start | bytes 3145728 | tf_op jit(solution)/shard_map/all_to_all | solution.py:122
  62.0 1.9 collective-permute-start.1
  64.1 18.3 %collective-permute-done.1 = bf16[192,2048]{1,0:T(8,128)(2,1)S(1)} collective-permute-done((bf16[192,2048]{1,0:T(8,128)(2,1)}, bf16[192,2048]{1,0:T(8,128)(2,1)S(1)}, u32[]{:S(2)}, u32[]{:S(2)}) %collective-permute-start.1) | collective-permute-done | bytes 786464 | tf_op jit(solution)/shard_map/ppermute | solution.py:15
  82.4 15.9 %all-to-all-done.1 = bf16[8,2,24,2048]{3,2,1,0:T(8,128)(2,1)S(1)} async-done(((bf16[8,2,24,2048]{3,2,1,0:T(8,128)(2,1)}), bf16[8,2,24,2048]{3,2,1,0:T(8,128)(2,1)S(1)}, u32[]{:S(2)}, u32[]{:S(2)}) %all-to-all-start.1) | async-done | bytes 1572896 | tf_op jit(solution)/shard_map/all_to_all | solution.py:122
  99.0 3.6 %collective-permute-start.2 = (bf16[96,2048]{1,0:T(8,128)(2,1)S(1)}, bf16[96,2048]{1,0:T(8,128)(2,1)S(1)}, u32[]{:S(2)}, u32[]{:S(2)}) collective-permute-start(bf16[96,2048]{1,0:T(8,128)(2,1)S(1)} %get-tuple-element.50), channel_id=1, source_target_pairs={{8,0},{16,8},{24,16},{9,1},{17,9},{25,17},{10,2},{18,10},{26,18},{... | collective-permute-start | bytes 1179656 | tf_op jit(solution)/shard_map/ppermute | solution.py:10
  102.6 3.0 %collective-permute-start.3 = (bf16[96,2048]{1,0:T(8,128)(2,1)S(1)}, bf16[96,2048]{1,0:T(8,128)(2,1)S(1)}, u32[]{:S(2)}, u32[]{:S(2)}) collective-permute-start(bf16[96,2048]{1,0:T(8,128)(2,1)S(1)} %get-tuple-element.51), channel_id=1, source_target_pairs={{0,8},{8,16},{16,24},{1,9},{9,17},{17,25},{2,10},{10,18},{18,26},{... | collective-permute-start | bytes 1179656 | tf_op jit(solution)/shard_map/ppermute | solution.py:10
  105.8 3.4 %collective-permute-done.2 = bf16[96,2048]{1,0:T(8,128)(2,1)S(1)} collective-permute-done((bf16[96,2048]{1,0:T(8,128)(2,1)S(1)}, bf16[96,2048]{1,0:T(8,128)(2,1)S(1)}, u32[]{:S(2)}, u32[]{:S(2)}) %collective-permute-start.2) | collective-permute-done | bytes 393248 | tf_op jit(solution)/shard_map/ppermute | solution.py:10
  110.7 1.7 convolution_convert_fusion
  112.4 3.6 %all-to-all-start.2 = ((bf16[8,2,24,2048]{3,2,1,0:T(8,128)(2,1)}), bf16[8,2,24,2048]{3,2,1,0:T(8,128)(2,1)S(1)}, u32[]{:S(2)}, u32[]{:S(2)}) async-start(bf16[8,2,24,2048]{3,2,1,0:T(8,128)(2,1)} %bitcast.47), calls=%async_computation.2 | async-start | bytes 3145728 | tf_op jit(solution)/shard_map/all_to_all | solution.py:53
  116.0 2.7 %collective-permute-start.4 = (bf16[192,2048]{1,0:T(8,128)(2,1)}, bf16[192,2048]{1,0:T(8,128)(2,1)S(1)}, u32[]{:S(2)}, u32[]{:S(2)}) collective-permute-start(bf16[192,2048]{1,0:T(8,128)(2,1)} %get-tuple-element.42), channel_id=1, source_target_pairs={{0,24},{8,16},{16,8},{24,0},{1,25},{9,17},{17,9},{25,1},{2,26},{10... | collective-permute-start | bytes 2359304 | tf_op jit(solution)/shard_map/ppermute | solution.py:15
  118.9 2.6 %fusion.12 = f32[192,512]{1,0:T(8,128)S(1)} fusion(bf16[192,2048]{1,0:T(8,128)(2,1)} %copy-done.14, bf16[2,1,1,2048,512]{4,3,2,1,0:T(8,128)(2,1)} %param.8), kind=kOutput, calls=%fused_computation.24 | convolution fusion | flops 402653184 | bytes 3276800 | tf_op jit(solution)/shard_map/dot_general | solution.py:59
  121.6 2.9 %fusion.71 = f32[512,2048]{1,0:T(8,128)} fusion(bf16[2,2,1,1,192,2048]{5,4,3,2,1,0:T(8,128)(2,1)S(1)} %copy-done.2, bf16[192,256]{1,0:T(8,128)(2,1)S(1)} %get-tuple-element.61, bf16[192,256]{1,0:T(8,128)(2,1)S(1)} %get-tuple-element.60), kind=kOutput, calls=%fused_computation.80 | convolution fusion | flops 403046400 | bytes 5177344 | tf_op jit(solution)/shard_map/dot_general | solution.py:19
  128.9 21.5 %all-to-all-done.2 = bf16[8,2,24,2048]{3,2,1,0:T(8,128)(2,1)S(1)} async-done(((bf16[8,2,24,2048]{3,2,1,0:T(8,128)(2,1)}), bf16[8,2,24,2048]{3,2,1,0:T(8,128)(2,1)S(1)}, u32[]{:S(2)}, u32[]{:S(2)}) %all-to-all-start.2) | async-done | bytes 1572896 | tf_op jit(solution)/shard_map/all_to_all | solution.py:53
  151.4 3.5 %fusion.10 = f32[192,512]{1,0:T(8,128)} fusion(bf16[192,2048]{1,0:T(8,128)(2,1)S(1)} %collective-permute-done.4, bf16[2,1,1,2048,512]{4,3,2,1,0:T(8,128)(2,1)} %param.8), kind=kOutput, calls=%fused_computation.22 | convolution fusion | flops 402653184 | bytes 3276800 | tf_op jit(solution)/shard_map/dot_general | solution.py:59
  155.6 1.8 fusion.82
  161.1 4.5 %all-to-all-start.3 = ((bf16[8,2,24,2048]{3,2,1,0:T(8,128)(2,1)}), bf16[8,2,24,2048]{3,2,1,0:T(8,128)(2,1)}, u32[]{:S(2)}, u32[]{:S(2)}) async-start(bf16[8,2,24,2048]{3,2,1,0:T(8,128)(2,1)} %pad_maximum_fusion.1), calls=%async_computation.3 | async-start | bytes 3145728 | tf_op jit(solution)/shard_map/all_to_all | solution.py:122
  165.6 1.8 fusion.105
  167.4 2.0 fusion.68
  169.5 3.1 %collective-permute-done.5 = bf16[192,2048]{1,0:T(8,128)(2,1)} collective-permute-done((bf16[192,2048]{1,0:T(8,128)(2,1)}, bf16[192,2048]{1,0:T(8,128)(2,1)}, u32[]{:S(2)}, u32[]{:S(2)}) %collective-permute-start.5) | collective-permute-done | bytes 786464 | tf_op jit(solution)/shard_map/ppermute | solution.py:15
  172.6 1.6 multiply_convert_fusion.5
  176.6 2.3 %fusion.5 = bf16[1,1,2048,512]{2,3,1,0:T(8,128)(2,1)} fusion(f32[2048,512]{0,1:T(8,128)S(1)} %fusion.95, bf16[192,2048]{1,0:T(8,128)(2,1)S(1)} %copy-done.15, f32[512,2048]{1,0:T(8,128)S(1)} %copy-done, f32[512,2048]{1,0:T(8,128)S(1)} %fusion.68, bf16[192,256]{1,0:T(8,128)(2,1)S(1)} %get-tuple-element.53, bf16[192,256]{1,0:T(8,128)(2,1)S(1)} %get-tuple-element.52), kind=kOutput, calls=%fused_computation.13 | convolution fusion | flops 409337856 | bytes 15663104 | tf_op jit(solution)/shard_map/dot_general | solution.py:19
  178.9 3.9 %copy.35 = bf16[1,1,2048,512]{3,2,1,0:T(8,128)(2,1)} copy(bf16[1,1,2048,512]{2,3,1,0:T(8,128)(2,1)} %fusion.5) | data formatting | bytes 4194304
  182.8 1.9 fusion.106
  187.5 14.9 %all-to-all-done.3 = bf16[8,2,24,2048]{3,2,1,0:T(8,128)(2,1)} async-done(((bf16[8,2,24,2048]{3,2,1,0:T(8,128)(2,1)}), bf16[8,2,24,2048]{3,2,1,0:T(8,128)(2,1)}, u32[]{:S(2)}, u32[]{:S(2)}) %all-to-all-start.3) | async-done | bytes 1572896 | tf_op jit(solution)/shard_map/all_to_all | solution.py:122
  202.5 2.9 %fusion.9 = bf16[2,1,96,2048]{3,2,1,0:T(8,128)(2,1)} fusion(pred[2,96,384]{2,1,0:T(32,128)(4,1)S(1)} %bitcast.237, bf16[384,2048,1]{1,0,2:T(8,128)(2,1)} %bitcast.63, bf16[1,96,2048]{2,1,0:T(8,128)(2,1)S(1)} %get-tuple-element.49, bf16[1,96,2048]{2,1,0:T(8,128)(2,1)S(1)} %get-tuple-element.48), kind=kOutput, calls=%fused_computation.21 | convolution fusion | flops 303562752 | bytes 3219456 | tf_op jit(solution)/shard_map/dot_general | solution.py:19
  (115 shorter events, 28.9 us)
Async XLA Ops:
  7.0 42.6 %all-to-all-start = ((bf16[8,2,24,2048]{3,2,1,0:T(8,128)(2,1)}), bf16[8,2,24,2048]{3,2,1,0:T(8,128)(2,1)S(1)}, u32[]{:S(2)}, u32[]{:S(2)}) async-start(bf16[8,2,24,2048]{3,2,1,0:T(8,128)(2,1)} %bitcast.13), calls=%async_computation | async-start | bytes 3145728 | tf_op jit(solution)/shard_map/all_to_all | solution.py:53
  13.3 4.6 %copy-start.1 = (bf16[2,2,1,1,192,2048]{5,4,3,2,1,0:T(8,128)(2,1)S(1)}, bf16[2,2,1,1,192,2048]{5,4,3,2,1,0:T(8,128)(2,1)}, u32[]{:S(2)}) copy-start(bf16[2,2,1,1,192,2048]{5,4,3,2,1,0:T(8,128)(2,1)} %param.12) | copy-start | bytes 9437188
  15.9 5.0 %copy-start.23 = (bf16[2,1,1,2048,512]{4,3,2,1,0:T(8,128)(2,1)S(1)}, bf16[2,1,1,2048,512]{4,3,2,1,0:T(8,128)(2,1)}, u32[]{:S(2)}) copy-start(bf16[2,1,1,2048,512]{4,3,2,1,0:T(8,128)(2,1)} %param.8) | copy-start | bytes 12582916
  15.9 33.8 %collective-permute-start = (bf16[192,2048]{1,0:T(8,128)(2,1)S(1)}, bf16[192,2048]{1,0:T(8,128)(2,1)S(1)}, u32[]{:S(2)}, u32[]{:S(2)}) collective-permute-start(bf16[192,2048]{1,0:T(8,128)(2,1)S(1)} %get-tuple-element.43), channel_id=1, source_target_pairs={{0,24},{8,16},{16,8},{24,0},{1,25},{9,17},{17,9},{25,1},{2,26},{10... | collective-permute-start | bytes 2359304 | tf_op jit(solution)/shard_map/ppermute | solution.py:15
  49.6 3.4 %copy-start.3 = (bf16[8,1,24,2048]{3,2,1,0:T(8,128)(2,1)}, bf16[8,1,24,2048]{3,2,1,0:T(8,128)(2,1)S(1)}, u32[]{:S(2)}) copy-start(bf16[8,1,24,2048]{3,2,1,0:T(8,128)(2,1)S(1)} %get-tuple-element.47) | copy-start | bytes 2359300
  49.6 3.4 %copy-start.13 = (bf16[8,1,24,2048]{3,2,1,0:T(8,128)(2,1)}, bf16[8,1,24,2048]{3,2,1,0:T(8,128)(2,1)S(1)}, u32[]{:S(2)}) copy-start(bf16[8,1,24,2048]{3,2,1,0:T(8,128)(2,1)S(1)} %get-tuple-element.46) | copy-start | bytes 2359300
  49.7 2.9 %copy-start.16 = (f32[192,512]{1,0:T(8,128)S(1)}, f32[192,512]{1,0:T(8,128)}, u32[]{:S(2)}) copy-start(f32[192,512]{1,0:T(8,128)} %fusion.38) | copy-start | bytes 1179652
  49.7 3.4 %copy-start.14 = (bf16[192,2048]{1,0:T(8,128)(2,1)}, bf16[192,2048]{1,0:T(8,128)(2,1)S(1)}, u32[]{:S(2)}) copy-start(bf16[192,2048]{1,0:T(8,128)(2,1)S(1)} %collective-permute-done) | copy-start | bytes 2359300
  57.2 41.2 %copy-start.5 = (bf16[2,1,96,2048]{3,2,1,0:T(8,128)(2,1)S(1)}, bf16[2,1,96,2048]{3,2,1,0:T(8,128)(2,1)}, u32[]{:S(2)}) copy-start(bf16[2,1,96,2048]{3,2,1,0:T(8,128)(2,1)} %param.10) | copy-start | bytes 2359300
  57.2 41.1 %all-to-all-start.1 = ((bf16[8,2,24,2048]{3,2,1,0:T(8,128)(2,1)}), bf16[8,2,24,2048]{3,2,1,0:T(8,128)(2,1)S(1)}, u32[]{:S(2)}, u32[]{:S(2)}) async-start(bf16[8,2,24,2048]{3,2,1,0:T(8,128)(2,1)} %pad_maximum_fusion), calls=%async_computation.1 | async-start | bytes 3145728 | tf_op jit(solution)/shard_map/all_to_all | solution.py:122
  62.0 20.5 %collective-permute-start.1 = (bf16[192,2048]{1,0:T(8,128)(2,1)}, bf16[192,2048]{1,0:T(8,128)(2,1)S(1)}, u32[]{:S(2)}, u32[]{:S(2)}) collective-permute-start(bf16[192,2048]{1,0:T(8,128)(2,1)} %bitcast.232), channel_id=1, source_target_pairs={{0,24},{8,16},{16,8},{24,0},{1,25},{9,17},{17,9},{25,1},{2,26},{10... | collective-permute-start | bytes 2359304 | tf_op jit(solution)/shard_map/ppermute | solution.py:15
  82.4 16.6 %copy-start.9 = (bf16[192,2048]{1,0:T(8,128)(2,1)}, bf16[192,2048]{1,0:T(8,128)(2,1)S(1)}, u32[]{:S(2)}) copy-start(bf16[192,2048]{1,0:T(8,128)(2,1)S(1)} %collective-permute-done.1) | copy-start | bytes 2359300
  98.9 11.5 %copy-start.12 = (bf16[1,2,96,2048]{3,2,1,0:T(8,128)(2,1)S(1)}, bf16[1,2,96,2048]{3,2,1,0:T(8,128)(2,1)}, u32[]{:S(2)}) copy-start(bf16[1,2,96,2048]{3,2,1,0:T(8,128)(2,1)} %param.11) | copy-start | bytes 2359300
  99.0 10.2 %collective-permute-start.2 = (bf16[96,2048]{1,0:T(8,128)(2,1)S(1)}, bf16[96,2048]{1,0:T(8,128)(2,1)S(1)}, u32[]{:S(2)}, u32[]{:S(2)}) collective-permute-start(bf16[96,2048]{1,0:T(8,128)(2,1)S(1)} %get-tuple-element.50), channel_id=1, source_target_pairs={{8,0},{16,8},{24,16},{9,1},{17,9},{25,17},{10,2},{18,10},{26,18},{... | collective-permute-start | bytes 1179656 | tf_op jit(solution)/shard_map/ppermute | solution.py:10
  102.6 7.7 %collective-permute-start.3 = (bf16[96,2048]{1,0:T(8,128)(2,1)S(1)}, bf16[96,2048]{1,0:T(8,128)(2,1)S(1)}, u32[]{:S(2)}, u32[]{:S(2)}) collective-permute-start(bf16[96,2048]{1,0:T(8,128)(2,1)S(1)} %get-tuple-element.51), channel_id=1, source_target_pairs={{0,8},{8,16},{16,24},{1,9},{9,17},{17,25},{2,10},{10,18},{18,26},{... | collective-permute-start | bytes 1179656 | tf_op jit(solution)/shard_map/ppermute | solution.py:10
  112.4 37.9 %all-to-all-start.2 = ((bf16[8,2,24,2048]{3,2,1,0:T(8,128)(2,1)}), bf16[8,2,24,2048]{3,2,1,0:T(8,128)(2,1)S(1)}, u32[]{:S(2)}, u32[]{:S(2)}) async-start(bf16[8,2,24,2048]{3,2,1,0:T(8,128)(2,1)} %bitcast.47), calls=%async_computation.2 | async-start | bytes 3145728 | tf_op jit(solution)/shard_map/all_to_all | solution.py:53
  116.0 35.3 %collective-permute-start.4 = (bf16[192,2048]{1,0:T(8,128)(2,1)}, bf16[192,2048]{1,0:T(8,128)(2,1)S(1)}, u32[]{:S(2)}, u32[]{:S(2)}) collective-permute-start(bf16[192,2048]{1,0:T(8,128)(2,1)} %get-tuple-element.42), channel_id=1, source_target_pairs={{0,24},{8,16},{16,8},{24,0},{1,25},{9,17},{17,9},{25,1},{2,26},{10... | collective-permute-start | bytes 2359304 | tf_op jit(solution)/shard_map/ppermute | solution.py:15
  118.8 2.8 %copy-start.2 = (bf16[2,2,1,1,192,2048]{5,4,3,2,1,0:T(8,128)(2,1)S(1)}, bf16[2,2,1,1,192,2048]{5,4,3,2,1,0:T(8,128)(2,1)}, u32[]{:S(2)}) copy-start(bf16[2,2,1,1,192,2048]{5,4,3,2,1,0:T(8,128)(2,1)} %param.12) | copy-start | bytes 9437188
  121.5 2.9 %copy-start.18 = (f32[192,512]{1,0:T(8,128)}, f32[192,512]{1,0:T(8,128)S(1)}, u32[]{:S(2)}) copy-start(f32[192,512]{1,0:T(8,128)S(1)} %fusion.12) | copy-start | bytes 1179652
  121.5 2.9 %copy-start.10 = (bf16[192,2048]{1,0:T(8,128)(2,1)S(1)}, bf16[192,2048]{1,0:T(8,128)(2,1)}, u32[]{:S(2)}) copy-start(bf16[192,2048]{1,0:T(8,128)(2,1)} %copy-done.9) | copy-start | bytes 2359300
  121.5 2.9 %copy-start.28 = (bf16[2,1,1,256,2048]{4,3,2,1,0:T(8,128)(2,1)S(1)}, bf16[2,1,1,256,2048]{4,3,2,1,0:T(8,128)(2,1)}, u32[]{:S(2)}) copy-start(bf16[2,1,1,256,2048]{4,3,2,1,0:T(8,128)(2,1)} %param.9) | copy-start | bytes 6291460
  121.5 4.7 %copy-start.25 = (bf16[2,1,1,2048,512]{4,3,2,1,0:T(8,128)(2,1)S(1)}, bf16[2,1,1,2048,512]{4,3,2,1,0:T(8,128)(2,1)}, u32[]{:S(2)}) copy-start(bf16[2,1,1,2048,512]{4,3,2,1,0:T(8,128)(2,1)} %param.8) | copy-start | bytes 12582916
  151.4 6.1 %copy-start.6 = (bf16[8,1,24,2048]{3,2,1,0:T(8,128)(2,1)}, bf16[8,1,24,2048]{3,2,1,0:T(8,128)(2,1)S(1)}, u32[]{:S(2)}) copy-start(bf16[8,1,24,2048]{3,2,1,0:T(8,128)(2,1)S(1)} %get-tuple-element.45) | copy-start | bytes 2359300
  151.4 4.3 %copy-start.29 = (bf16[2,1,1,256,2048]{4,3,2,1,0:T(8,128)(2,1)S(1)}, bf16[2,1,1,256,2048]{4,3,2,1,0:T(8,128)(2,1)}, u32[]{:S(2)}) copy-start(bf16[2,1,1,256,2048]{4,3,2,1,0:T(8,128)(2,1)} %param.9) | copy-start | bytes 6291460
  151.4 4.3 %copy-start.31 = (f32[192,512]{1,0:T(8,128)S(1)}, f32[192,512]{1,0:T(8,128)}, u32[]{:S(2)}) copy-start(f32[192,512]{1,0:T(8,128)} %fusion.47) | copy-start | bytes 1179652
  151.4 6.1 %copy-start.7 = (bf16[192,2048]{1,0:T(8,128)(2,1)}, bf16[192,2048]{1,0:T(8,128)(2,1)S(1)}, u32[]{:S(2)}) copy-start(bf16[192,2048]{1,0:T(8,128)(2,1)S(1)} %collective-permute-done.4) | copy-start | bytes 2359300
  154.9 2.6 %copy-start.21 = (f32[192,512]{1,0:T(8,128)S(1)}, f32[192,512]{1,0:T(8,128)}, u32[]{:S(2)}) copy-start(f32[192,512]{1,0:T(8,128)} %fusion.44) | copy-start | bytes 1179652
  154.9 17.7 %collective-permute-start.5 = (bf16[192,2048]{1,0:T(8,128)(2,1)}, bf16[192,2048]{1,0:T(8,128)(2,1)}, u32[]{:S(2)}, u32[]{:S(2)}) collective-permute-start(bf16[192,2048]{1,0:T(8,128)(2,1)} %bitcast.49), channel_id=1, source_target_pairs={{0,24},{8,16},{16,8},{24,0},{1,25},{9,17},{17,9},{25,1},{2,26},{10... | collective-permute-start | bytes 2359304 | tf_op jit(solution)/shard_map/ppermute | solution.py:15
  161.1 41.4 %all-to-all-start.3 = ((bf16[8,2,24,2048]{3,2,1,0:T(8,128)(2,1)}), bf16[8,2,24,2048]{3,2,1,0:T(8,128)(2,1)}, u32[]{:S(2)}, u32[]{:S(2)}) async-start(bf16[8,2,24,2048]{3,2,1,0:T(8,128)(2,1)} %pad_maximum_fusion.1), calls=%async_computation.3 | async-start | bytes 3145728 | tf_op jit(solution)/shard_map/all_to_all | solution.py:122
  167.4 5.2 %copy-start.20 = (f32[192,512]{1,0:T(8,128)S(1)}, f32[192,512]{1,0:T(8,128)}, u32[]{:S(2)}) copy-start(f32[192,512]{1,0:T(8,128)} %fusion.10) | copy-start | bytes 1179652
  167.4 5.2 %copy-start.30 = (bf16[2,1,1,256,2048]{4,3,2,1,0:T(8,128)(2,1)S(1)}, bf16[2,1,1,256,2048]{4,3,2,1,0:T(8,128)(2,1)}, u32[]{:S(2)}) copy-start(bf16[2,1,1,256,2048]{4,3,2,1,0:T(8,128)(2,1)} %param.9) | copy-start | bytes 6291460
  169.4 4.8 %copy-start.8 = (bf16[192,2048]{1,0:T(8,128)(2,1)S(1)}, bf16[192,2048]{1,0:T(8,128)(2,1)}, u32[]{:S(2)}) copy-start(bf16[192,2048]{1,0:T(8,128)(2,1)} %copy-done.7) | copy-start | bytes 2359300
  (11 other events, 22.2 us)

commit v12 on v5

--- a/solution.py
+++ b/solution.py
@@ -91,6 +91,7 @@
     for tick_id in range(ticks):
         one_hot = placement(routes[tick_id, :, 0], counts[tick_id, :, 0, 0], capacity)
         scaled = (probs[tick_id, :, 0][:, :, None] * current.astype(jnp.float32)).astype(jnp.bfloat16)
+        scaled = lax.optimization_barrier(scaled)
         blocks = jnp.dot(one_hot, scaled.reshape(-1, model_width), preferred_element_type=jnp.float32)
         blocks = blocks.astype(jnp.bfloat16).reshape(experts, 2, capacity, model_width)
         if slope_mirror is not None:

time: 205 us -> 205 us (level)
  no operation moved by 1% of the time
where the time goes in v12:
time: 205 us; the launch traced here: 204 us
  waiting for transfers between devices  104 us (51%)
  matrix products  44.8 us (22%)
  starting transfers between devices  30.4 us (15%)
  local copies, waits for them, and re-layouts  17.3 us (8%)
  other arithmetic  6.1 us (3%)
    all_to_all x2, waiting for transfers between devices, exchange(): lax.all_to_all(blocks, 'expert', split_axis=0, concat_axis=0, tiled=True)  48 us
    all_to_all x2, waiting for transfers between devices, on_device(): lax.all_to_all(back_blocks, 'expert', split_axis=0, concat_axis=0, tiled=...  31.2 us
    ppermute x3, waiting for transfers between devices, mirrored(): return lax.ppermute(block, axis, [(i, count - 1 - i) for i in range(count)])  20.5 us
    dot_general x10, matrix products, left_product(): lax.dot_general(left, right, (((0,), (0,)), ((), ())), preferred_element_...  16.8 us
    dot_general x6, matrix products, expert_grads(): gate_up = jnp.dot(saved_rows, weight_in, preferred_element_type=jnp.float32)  14.4 us
    unnamed x61, local copies, waits for them, and re-layouts  10.9 us
    dot_general x10, matrix products, right_product(): lax.dot_general(left, right, (((1,), (1,)), ((), ())), preferred_element_...  10.2 us
    all_to_all x2, starting transfers between devices, exchange(): lax.all_to_all(blocks, 'expert', split_axis=0, concat_axis=0, tiled=True)  9.95 us
  transfers between devices with their start and end apart: 9, of which 8 were waited for; matrix products, arithmetic and copies ran while one was open for 23% of the time, Pallas kernels for 0%

profile of v12, /device:TPU:1, one launch (start us, length us, event | category | flops | bytes accessed | tf_op | source)
XLA Modules:
  0.0 204.0 jit_solution(9333521491965721874)
XLA Ops:
  5.7 1.7 convolution_convert_fusion.1
  7.4 6.4 %all-to-all-start = ((bf16[8,2,24,2048]{3,2,1,0:T(8,128)(2,1)}), bf16[8,2,24,2048]{3,2,1,0:T(8,128)(2,1)S(1)}, u32[]{:S(2)}, u32[]{:S(2)}) async-start(bf16[8,2,24,2048]{3,2,1,0:T(8,128)(2,1)} %bitcast.15), calls=%async_computation | async-start | bytes 3145728 | tf_op jit(solution)/shard_map/all_to_all | solution.py:53
  13.8 2.9 %slice_bitcast_fusion = bf16[2,192,2048]{2,1,0:T(8,128)(2,1)} fusion(bf16[2,2,1,1,192,2048]{5,4,3,2,1,0:T(8,128)(2,1)} %param.12), kind=kLoop, calls=%fused_computation.44 | loop fusion | bytes 3145728 | tf_op jit(solution)/shard_map/squeeze | solution.py:84
  16.7 2.1 %collective-permute-start = (bf16[2,192,2048]{2,1,0:T(8,128)(2,1)}, bf16[2,192,2048]{2,1,0:T(8,128)(2,1)S(1)}, u32[]{:S(2)}, u32[]{:S(2)}) collective-permute-start(bf16[2,192,2048]{2,1,0:T(8,128)(2,1)} %slice_bitcast_fusion), channel_id=1, source_target_pairs={{0,24},{8,16},{16,8},{24,0},{1,25},{9,17},{17,9},{25,1},{2,26},{10... | collective-permute-start | bytes 4718600 | tf_op jit(solution)/shard_map/ppermute | solution.py:15
  18.8 3.0 %fusion.24 = f32[192,512]{1,0:T(8,128)} fusion(bf16[2,1,1,2048,512]{4,3,2,1,0:T(8,128)(2,1)} %param.8, bf16[2,2,1,1,192,2048]{5,4,3,2,1,0:T(8,128)(2,1)S(1)} %copy-done.1), kind=kOutput, calls=%fused_computation.36 | convolution fusion | flops 402653184 | bytes 3276800 | tf_op jit(solution)/shard_map/dot_general | solution.py:59
  23.0 26.9 %all-to-all-done = bf16[8,2,24,2048]{3,2,1,0:T(8,128)(2,1)S(1)} async-done(((bf16[8,2,24,2048]{3,2,1,0:T(8,128)(2,1)}), bf16[8,2,24,2048]{3,2,1,0:T(8,128)(2,1)S(1)}, u32[]{:S(2)}, u32[]{:S(2)}) %all-to-all-start) | async-done | bytes 1572896 | tf_op jit(solution)/shard_map/all_to_all | solution.py:53
  50.1 2.0 copy-done.25
  58.5 4.6 %all-to-all-start.1 = ((bf16[8,2,24,2048]{3,2,1,0:T(8,128)(2,1)}), bf16[8,2,24,2048]{3,2,1,0:T(8,128)(2,1)S(1)}, u32[]{:S(2)}, u32[]{:S(2)}) async-start(bf16[8,2,24,2048]{3,2,1,0:T(8,128)(2,1)} %pad_maximum_fusion), calls=%async_computation.1 | async-start | bytes 3145728 | tf_op jit(solution)/shard_map/all_to_all | solution.py:123
  63.1 1.9 collective-permute-start.1
  65.3 18.3 %collective-permute-done.1 = bf16[192,2048]{1,0:T(8,128)(2,1)S(1)} collective-permute-done((bf16[192,2048]{1,0:T(8,128)(2,1)}, bf16[192,2048]{1,0:T(8,128)(2,1)S(1)}, u32[]{:S(2)}, u32[]{:S(2)}) %collective-permute-start.1) | collective-permute-done | bytes 786464 | tf_op jit(solution)/shard_map/ppermute | solution.py:15
  83.6 15.9 %all-to-all-done.1 = bf16[8,2,24,2048]{3,2,1,0:T(8,128)(2,1)S(1)} async-done(((bf16[8,2,24,2048]{3,2,1,0:T(8,128)(2,1)}), bf16[8,2,24,2048]{3,2,1,0:T(8,128)(2,1)S(1)}, u32[]{:S(2)}, u32[]{:S(2)}) %all-to-all-start.1) | async-done | bytes 1572896 | tf_op jit(solution)/shard_map/all_to_all | solution.py:123
  100.2 3.6 %collective-permute-start.2 = (bf16[96,2048]{1,0:T(8,128)(2,1)S(1)}, bf16[96,2048]{1,0:T(8,128)(2,1)S(1)}, u32[]{:S(2)}, u32[]{:S(2)}) collective-permute-start(bf16[96,2048]{1,0:T(8,128)(2,1)S(1)} %get-tuple-element.26), channel_id=1, source_target_pairs={{8,0},{16,8},{24,16},{9,1},{17,9},{25,17},{10,2},{18,10},{26,18},{... | collective-permute-start | bytes 1179656 | tf_op jit(solution)/shard_map/ppermute | solution.py:10
  103.8 3.0 %collective-permute-start.3 = (bf16[96,2048]{1,0:T(8,128)(2,1)S(1)}, bf16[96,2048]{1,0:T(8,128)(2,1)S(1)}, u32[]{:S(2)}, u32[]{:S(2)}) collective-permute-start(bf16[96,2048]{1,0:T(8,128)(2,1)S(1)} %get-tuple-element.27), channel_id=1, source_target_pairs={{0,8},{8,16},{16,24},{1,9},{9,17},{17,25},{2,10},{10,18},{18,26},{... | collective-permute-start | bytes 1179656 | tf_op jit(solution)/shard_map/ppermute | solution.py:10
  106.9 3.5 %collective-permute-done.2 = bf16[96,2048]{1,0:T(8,128)(2,1)S(1)} collective-permute-done((bf16[96,2048]{1,0:T(8,128)(2,1)S(1)}, bf16[96,2048]{1,0:T(8,128)(2,1)S(1)}, u32[]{:S(2)}, u32[]{:S(2)}) %collective-permute-start.2) | collective-permute-done | bytes 393248 | tf_op jit(solution)/shard_map/ppermute | solution.py:10
  111.8 1.7 convolution_convert_fusion
  113.6 3.6 %all-to-all-start.2 = ((bf16[8,2,24,2048]{3,2,1,0:T(8,128)(2,1)}), bf16[8,2,24,2048]{3,2,1,0:T(8,128)(2,1)S(1)}, u32[]{:S(2)}, u32[]{:S(2)}) async-start(bf16[8,2,24,2048]{3,2,1,0:T(8,128)(2,1)} %bitcast.47), calls=%async_computation.2 | async-start | bytes 3145728 | tf_op jit(solution)/shard_map/all_to_all | solution.py:53
  117.4 2.6 %fusion.21 = f32[192,512]{1,0:T(8,128)S(1)} fusion(bf16[2,1,1,2048,512]{4,3,2,1,0:T(8,128)(2,1)} %param.8, bf16[2,2,1,1,192,2048]{5,4,3,2,1,0:T(8,128)(2,1)} %param.12), kind=kOutput, calls=%fused_computation.33 | convolution fusion | flops 402653184 | bytes 3276800 | tf_op jit(solution)/shard_map/dot_general | solution.py:59
  120.1 3.1 %fusion.11 = f32[192,512]{1,0:T(8,128)} fusion(bf16[2,1,1,2048,512]{4,3,2,1,0:T(8,128)(2,1)} %param.8, bf16[2,2,1,1,192,2048]{5,4,3,2,1,0:T(8,128)(2,1)S(1)} %copy-done.2), kind=kOutput, calls=%fused_computation.23 | convolution fusion | flops 402653184 | bytes 3276800 | tf_op jit(solution)/shard_map/dot_general | solution.py:59
  123.2 3.1 %fusion.16 = f32[192,512]{1,0:T(8,128)} fusion(bf16[2,1,1,2048,512]{4,3,2,1,0:T(8,128)(2,1)} %param.8, bf16[2,192,2048]{2,1,0:T(8,128)(2,1)S(1)} %copy-done.8), kind=kOutput, calls=%fused_computation.28 | convolution fusion | flops 402653184 | bytes 3276800 | tf_op jit(solution)/shard_map/dot_general | solution.py:59
  127.7 2.7 %fusion.61 = f32[512,2048]{1,0:T(8,128)} fusion(bf16[2,2,1,1,192,2048]{5,4,3,2,1,0:T(8,128)(2,1)S(1)} %copy-done.2, bf16[192,256]{1,0:T(8,128)(2,1)S(1)} %get-tuple-element.37, bf16[192,256]{1,0:T(8,128)(2,1)S(1)} %get-tuple-element.36), kind=kOutput, calls=%fused_computation.79 | convolution fusion | flops 403046400 | bytes 5177344 | tf_op jit(solution)/shard_map/dot_general | solution.py:19
  130.4 21.1 %all-to-all-done.2 = bf16[8,2,24,2048]{3,2,1,0:T(8,128)(2,1)S(1)} async-done(((bf16[8,2,24,2048]{3,2,1,0:T(8,128)(2,1)}), bf16[8,2,24,2048]{3,2,1,0:T(8,128)(2,1)S(1)}, u32[]{:S(2)}, u32[]{:S(2)}) %all-to-all-start.2) | async-done | bytes 1572896 | tf_op jit(solution)/shard_map/all_to_all | solution.py:53
  153.4 1.8 fusion.82
  158.9 4.5 %all-to-all-start.3 = ((bf16[8,2,24,2048]{3,2,1,0:T(8,128)(2,1)}), bf16[8,2,24,2048]{3,2,1,0:T(8,128)(2,1)}, u32[]{:S(2)}, u32[]{:S(2)}) async-start(bf16[8,2,24,2048]{3,2,1,0:T(8,128)(2,1)} %pad_maximum_fusion.1), calls=%async_computation.3 | async-start | bytes 3145728 | tf_op jit(solution)/shard_map/all_to_all | solution.py:123
  163.4 1.9 fusion.104
  165.3 1.9 multiply_convert_fusion.7
  168.0 2.2 %collective-permute-done.4 = bf16[192,2048]{1,0:T(8,128)(2,1)} collective-permute-done((bf16[192,2048]{1,0:T(8,128)(2,1)}, bf16[192,2048]{1,0:T(8,128)(2,1)}, u32[]{:S(2)}, u32[]{:S(2)}) %collective-permute-start.4) | collective-permute-done | bytes 786464 | tf_op jit(solution)/shard_map/ppermute | solution.py:15
  170.1 1.6 multiply_convert_fusion.5
  174.0 3.3 %fusion.1 = bf16[1,1,2048,512]{2,3,1,0:T(8,128)(2,1)} fusion(bf16[2048,512]{0,1:T(8,128)(2,1)S(1)} %add_convert_fusion, f32[512,2048]{1,0:T(8,128)S(1)} %copy-done, bf16[2,2,1,1,192,2048]{5,4,3,2,1,0:T(8,128)(2,1)} %param.12, bf16[192,256]{1,0:T(8,128)(2,1)S(1)} %get-tuple-element.33, bf16[192,256]{1,0:T(8,128)(2,1)S(1)} %get-tuple-element.32), kind=kOutput, calls=%fused_computation.5 | convolution fusion | flops 407240704 | bytes 9371648 | tf_op jit(solution)/shard_map/dot_general | solution.py:19
  177.3 3.9 %copy.35 = bf16[1,1,2048,512]{3,2,1,0:T(8,128)(2,1)} copy(bf16[1,1,2048,512]{2,3,1,0:T(8,128)(2,1)} %fusion.1) | data formatting | bytes 4194304
  181.2 1.9 fusion.105
  185.8 15.3 %all-to-all-done.3 = bf16[8,2,24,2048]{3,2,1,0:T(8,128)(2,1)} async-done(((bf16[8,2,24,2048]{3,2,1,0:T(8,128)(2,1)}), bf16[8,2,24,2048]{3,2,1,0:T(8,128)(2,1)}, u32[]{:S(2)}, u32[]{:S(2)}) %all-to-all-start.3) | async-done | bytes 1572896 | tf_op jit(solution)/shard_map/all_to_all | solution.py:123
  201.1 2.9 %fusion.9 = bf16[2,1,96,2048]{3,2,1,0:T(8,128)(2,1)} fusion(pred[2,96,384]{2,1,0:T(32,128)(4,1)S(1)} %bitcast.219, bf16[384,2048,1]{1,0,2:T(8,128)(2,1)} %bitcast.57, bf16[1,96,2048]{2,1,0:T(8,128)(2,1)S(1)} %get-tuple-element.25, bf16[1,96,2048]{2,1,0:T(8,128)(2,1)S(1)} %get-tuple-element.24), kind=kOutput, calls=%fused_computation.21 | convolution fusion | flops 303562752 | bytes 3219456 | tf_op jit(solution)/shard_map/dot_general | solution.py:19
  (103 shorter events, 28.1 us)
Async XLA Ops:
  7.4 42.6 %all-to-all-start = ((bf16[8,2,24,2048]{3,2,1,0:T(8,128)(2,1)}), bf16[8,2,24,2048]{3,2,1,0:T(8,128)(2,1)S(1)}, u32[]{:S(2)}, u32[]{:S(2)}) async-start(bf16[8,2,24,2048]{3,2,1,0:T(8,128)(2,1)} %bitcast.15), calls=%async_computation | async-start | bytes 3145728 | tf_op jit(solution)/shard_map/all_to_all | solution.py:53
  13.8 5.0 %copy-start.1 = (bf16[2,2,1,1,192,2048]{5,4,3,2,1,0:T(8,128)(2,1)S(1)}, bf16[2,2,1,1,192,2048]{5,4,3,2,1,0:T(8,128)(2,1)}, u32[]{:S(2)}) copy-start(bf16[2,2,1,1,192,2048]{5,4,3,2,1,0:T(8,128)(2,1)} %param.12) | copy-start | bytes 9437188
  16.7 5.0 %copy-start.21 = (bf16[2,1,1,2048,512]{4,3,2,1,0:T(8,128)(2,1)S(1)}, bf16[2,1,1,2048,512]{4,3,2,1,0:T(8,128)(2,1)}, u32[]{:S(2)}) copy-start(bf16[2,1,1,2048,512]{4,3,2,1,0:T(8,128)(2,1)} %param.8) | copy-start | bytes 12582916
  16.7 40.6 %collective-permute-start = (bf16[2,192,2048]{2,1,0:T(8,128)(2,1)}, bf16[2,192,2048]{2,1,0:T(8,128)(2,1)S(1)}, u32[]{:S(2)}, u32[]{:S(2)}) collective-permute-start(bf16[2,192,2048]{2,1,0:T(8,128)(2,1)} %slice_bitcast_fusion), channel_id=1, source_target_pairs={{0,24},{8,16},{16,8},{24,0},{1,25},{9,17},{17,9},{25,1},{2,26},{10... | collective-permute-start | bytes 4718600 | tf_op jit(solution)/shard_map/ppermute | solution.py:15
  49.9 2.2 %copy-start.25 = (bf16[2,1,1,256,2048]{4,3,2,1,0:T(8,128)(2,1)S(1)}, bf16[2,1,1,256,2048]{4,3,2,1,0:T(8,128)(2,1)}, u32[]{:S(2)}) copy-start(bf16[2,1,1,256,2048]{4,3,2,1,0:T(8,128)(2,1)} %param.9) | copy-start | bytes 6291460
  49.9 2.2 %copy-start.29 = (f32[192,512]{1,0:T(8,128)S(1)}, f32[192,512]{1,0:T(8,128)}, u32[]{:S(2)}) copy-start(f32[192,512]{1,0:T(8,128)} %fusion.14) | copy-start | bytes 1179652
  50.1 3.1 %copy-start.6 = (bf16[8,1,24,2048]{3,2,1,0:T(8,128)(2,1)}, bf16[8,1,24,2048]{3,2,1,0:T(8,128)(2,1)S(1)}, u32[]{:S(2)}) copy-start(bf16[8,1,24,2048]{3,2,1,0:T(8,128)(2,1)S(1)} %get-tuple-element.22) | copy-start | bytes 2359300
  50.1 3.1 %copy-start.14 = (bf16[8,1,24,2048]{3,2,1,0:T(8,128)(2,1)}, bf16[8,1,24,2048]{3,2,1,0:T(8,128)(2,1)S(1)}, u32[]{:S(2)}) copy-start(bf16[8,1,24,2048]{3,2,1,0:T(8,128)(2,1)S(1)} %get-tuple-element.23) | copy-start | bytes 2359300
  50.1 2.6 %copy-start.18 = (f32[192,512]{1,0:T(8,128)S(1)}, f32[192,512]{1,0:T(8,128)}, u32[]{:S(2)}) copy-start(f32[192,512]{1,0:T(8,128)} %fusion.24) | copy-start | bytes 1179652
  52.1 2.2 %copy-start.22 = (bf16[2,1,1,2048,512]{4,3,2,1,0:T(8,128)(2,1)S(1)}, bf16[2,1,1,2048,512]{4,3,2,1,0:T(8,128)(2,1)}, u32[]{:S(2)}) copy-start(bf16[2,1,1,2048,512]{4,3,2,1,0:T(8,128)(2,1)} %param.8) | copy-start | bytes 12582916
  57.3 7.7 %copy-start.20 = (s32[2,2,1,96]{3,2,1,0:T(1,128)S(1)}, s32[2,2,1,96]{3,2,1,0:T(1,128)}, u32[]{:S(2)}) copy-start(s32[2,2,1,96]{3,2,1,0:T(1,128)} %param.14) | copy-start | bytes 4612
  57.3 42.2 %copy-start.5 = (bf16[2,1,96,2048]{3,2,1,0:T(8,128)(2,1)S(1)}, bf16[2,1,96,2048]{3,2,1,0:T(8,128)(2,1)}, u32[]{:S(2)}) copy-start(bf16[2,1,96,2048]{3,2,1,0:T(8,128)(2,1)} %param.10) | copy-start | bytes 2359300
  58.5 41.0 %all-to-all-start.1 = ((bf16[8,2,24,2048]{3,2,1,0:T(8,128)(2,1)}), bf16[8,2,24,2048]{3,2,1,0:T(8,128)(2,1)S(1)}, u32[]{:S(2)}, u32[]{:S(2)}) async-start(bf16[8,2,24,2048]{3,2,1,0:T(8,128)(2,1)} %pad_maximum_fusion), calls=%async_computation.1 | async-start | bytes 3145728 | tf_op jit(solution)/shard_map/all_to_all | solution.py:123
  63.1 20.5 %collective-permute-start.1 = (bf16[192,2048]{1,0:T(8,128)(2,1)}, bf16[192,2048]{1,0:T(8,128)(2,1)S(1)}, u32[]{:S(2)}, u32[]{:S(2)}) collective-permute-start(bf16[192,2048]{1,0:T(8,128)(2,1)} %bitcast.214), channel_id=1, source_target_pairs={{0,24},{8,16},{16,8},{24,0},{1,25},{9,17},{17,9},{25,1},{2,26},{10... | collective-permute-start | bytes 2359304 | tf_op jit(solution)/shard_map/ppermute | solution.py:15
  83.6 16.6 %copy-start.10 = (bf16[192,2048]{1,0:T(8,128)(2,1)}, bf16[192,2048]{1,0:T(8,128)(2,1)S(1)}, u32[]{:S(2)}) copy-start(bf16[192,2048]{1,0:T(8,128)(2,1)S(1)} %collective-permute-done.1) | copy-start | bytes 2359300
  100.1 11.5 %copy-start.13 = (bf16[1,2,96,2048]{3,2,1,0:T(8,128)(2,1)S(1)}, bf16[1,2,96,2048]{3,2,1,0:T(8,128)(2,1)}, u32[]{:S(2)}) copy-start(bf16[1,2,96,2048]{3,2,1,0:T(8,128)(2,1)} %param.11) | copy-start | bytes 2359300
  100.2 10.2 %collective-permute-start.2 = (bf16[96,2048]{1,0:T(8,128)(2,1)S(1)}, bf16[96,2048]{1,0:T(8,128)(2,1)S(1)}, u32[]{:S(2)}, u32[]{:S(2)}) collective-permute-start(bf16[96,2048]{1,0:T(8,128)(2,1)S(1)} %get-tuple-element.26), channel_id=1, source_target_pairs={{8,0},{16,8},{24,16},{9,1},{17,9},{25,17},{10,2},{18,10},{26,18},{... | collective-permute-start | bytes 1179656 | tf_op jit(solution)/shard_map/ppermute | solution.py:10
  103.8 7.7 %collective-permute-start.3 = (bf16[96,2048]{1,0:T(8,128)(2,1)S(1)}, bf16[96,2048]{1,0:T(8,128)(2,1)S(1)}, u32[]{:S(2)}, u32[]{:S(2)}) collective-permute-start(bf16[96,2048]{1,0:T(8,128)(2,1)S(1)} %get-tuple-element.27), channel_id=1, source_target_pairs={{0,8},{8,16},{16,24},{1,9},{9,17},{17,25},{2,10},{10,18},{18,26},{... | collective-permute-start | bytes 1179656 | tf_op jit(solution)/shard_map/ppermute | solution.py:10
  113.6 37.9 %all-to-all-start.2 = ((bf16[8,2,24,2048]{3,2,1,0:T(8,128)(2,1)}), bf16[8,2,24,2048]{3,2,1,0:T(8,128)(2,1)S(1)}, u32[]{:S(2)}, u32[]{:S(2)}) async-start(bf16[8,2,24,2048]{3,2,1,0:T(8,128)(2,1)} %bitcast.47), calls=%async_computation.2 | async-start | bytes 3145728 | tf_op jit(solution)/shard_map/all_to_all | solution.py:53
  117.3 2.8 %copy-start.2 = (bf16[2,2,1,1,192,2048]{5,4,3,2,1,0:T(8,128)(2,1)S(1)}, bf16[2,2,1,1,192,2048]{5,4,3,2,1,0:T(8,128)(2,1)}, u32[]{:S(2)}) copy-start(bf16[2,2,1,1,192,2048]{5,4,3,2,1,0:T(8,128)(2,1)} %param.12) | copy-start | bytes 9437188
  120.1 35.1 %copy-start.15 = (f32[192,512]{1,0:T(8,128)}, f32[192,512]{1,0:T(8,128)S(1)}, u32[]{:S(2)}) copy-start(f32[192,512]{1,0:T(8,128)S(1)} %fusion.21) | copy-start | bytes 1179652
  120.1 3.1 %copy-start.8 = (bf16[2,192,2048]{2,1,0:T(8,128)(2,1)S(1)}, bf16[2,192,2048]{2,1,0:T(8,128)(2,1)}, u32[]{:S(2)}) copy-start(bf16[2,192,2048]{2,1,0:T(8,128)(2,1)} %copy-done.7) | copy-start | bytes 4718596
  123.2 3.1 %copy-start.23 = (bf16[2,1,1,2048,512]{4,3,2,1,0:T(8,128)(2,1)S(1)}, bf16[2,1,1,2048,512]{4,3,2,1,0:T(8,128)(2,1)}, u32[]{:S(2)}) copy-start(bf16[2,1,1,2048,512]{4,3,2,1,0:T(8,128)(2,1)} %param.8) | copy-start | bytes 12582916
  130.4 22.9 %copy-start.28 = (f32[192,512]{1,0:T(8,128)S(1)}, f32[192,512]{1,0:T(8,128)}, u32[]{:S(2)}) copy-start(f32[192,512]{1,0:T(8,128)} %fusion.11) | copy-start | bytes 1179652
  152.5 3.2 %copy-start.3 = (bf16[8,1,24,2048]{3,2,1,0:T(8,128)(2,1)}, bf16[8,1,24,2048]{3,2,1,0:T(8,128)(2,1)S(1)}, u32[]{:S(2)}) copy-start(bf16[8,1,24,2048]{3,2,1,0:T(8,128)(2,1)S(1)} %get-tuple-element.20) | copy-start | bytes 2359300
  152.5 17.7 %collective-permute-start.4 = (bf16[192,2048]{1,0:T(8,128)(2,1)}, bf16[192,2048]{1,0:T(8,128)(2,1)}, u32[]{:S(2)}, u32[]{:S(2)}) collective-permute-start(bf16[192,2048]{1,0:T(8,128)(2,1)} %bitcast.52), channel_id=1, source_target_pairs={{0,24},{8,16},{16,8},{24,0},{1,25},{9,17},{17,9},{25,1},{2,26},{10... | collective-permute-start | bytes 2359304 | tf_op jit(solution)/shard_map/ppermute | solution.py:15
  153.4 2.4 %copy-start.24 = (bf16[2,1,1,2048,512]{4,3,2,1,0:T(8,128)(2,1)S(1)}, bf16[2,1,1,2048,512]{4,3,2,1,0:T(8,128)(2,1)}, u32[]{:S(2)}) copy-start(bf16[2,1,1,2048,512]{4,3,2,1,0:T(8,128)(2,1)} %param.8) | copy-start | bytes 12582916
  158.9 42.3 %all-to-all-start.3 = ((bf16[8,2,24,2048]{3,2,1,0:T(8,128)(2,1)}), bf16[8,2,24,2048]{3,2,1,0:T(8,128)(2,1)}, u32[]{:S(2)}, u32[]{:S(2)}) async-start(bf16[8,2,24,2048]{3,2,1,0:T(8,128)(2,1)} %pad_maximum_fusion.1), calls=%async_computation.3 | async-start | bytes 3145728 | tf_op jit(solution)/shard_map/all_to_all | solution.py:123
  163.3 1.9 copy-start.11
  167.2 3.0 %copy-start.19 = (f32[192,512]{1,0:T(8,128)S(1)}, f32[192,512]{1,0:T(8,128)}, u32[]{:S(2)}) copy-start(f32[192,512]{1,0:T(8,128)} %fusion.16) | copy-start | bytes 1179652
  167.2 3.0 %copy-start.27 = (bf16[2,1,1,256,2048]{4,3,2,1,0:T(8,128)(2,1)S(1)}, bf16[2,1,1,256,2048]{4,3,2,1,0:T(8,128)(2,1)}, u32[]{:S(2)}) copy-start(bf16[2,1,1,256,2048]{4,3,2,1,0:T(8,128)(2,1)} %param.9) | copy-start | bytes 6291460
  171.8 2.2 %copy-start = (f32[512,2048]{1,0:T(8,128)S(1)}, f32[512,2048]{1,0:T(8,128)}, u32[]{:S(2)}) copy-start(f32[512,2048]{1,0:T(8,128)} %fusion.61) | copy-start | bytes 12582916
  (7 other events, 11.1 us)

commit v13 on v5

--- a/solution.py
+++ b/solution.py
@@ -27,22 +27,18 @@
     )
 
 
-def slot_table(route_ids, count_table, capacity, way_id, ways):
-    experts = count_table.shape[0]
-    labels = lax.iota(jnp.int32, experts)
-    below = jnp.sum(
-        jnp.where(labels[None, :] < labels[:, None], count_table[None, :], 0), axis=1
-    )
-    first_slot = jnp.sum(jnp.where(route_ids[:, None] == labels[None, :], below[None, :], 0), axis=1)
-    within = lax.iota(jnp.int32, route_ids.shape[0]) - first_slot
+def slot_table(route_ids, capacity, way_id, ways):
+    tokens = route_ids.shape[0]
+    positions = lax.iota(jnp.int32, tokens)
+    earlier = (positions[None, :] < positions[:, None]) & (route_ids[None, :] == route_ids[:, None])
+    within = jnp.sum(earlier.astype(jnp.int32), axis=1)
     return (route_ids * ways + way_id) * capacity + within
 
 
-def placement(route_ids, count_tables, capacity):
+def placement(route_ids, capacity, experts):
     ways, tokens = route_ids.shape
-    experts = count_tables.shape[1]
     slots = jnp.concatenate(
-        [slot_table(route_ids[w], count_tables[w], capacity, w, ways) for w in range(ways)]
+        [slot_table(route_ids[w], capacity, w, ways) for w in range(ways)]
     )
     rows = lax.iota(jnp.int32, ways * experts * capacity)
     return (rows[:, None] == slots[None, :]).astype(jnp.bfloat16)
@@ -89,7 +85,7 @@
     mirror_in, mirror_out = zeros_in, zeros_out
     slope_mirror = None
     for tick_id in range(ticks):
-        one_hot = placement(routes[tick_id, :, 0], counts[tick_id, :, 0, 0], capacity)
+        one_hot = placement(routes[tick_id, :, 0], capacity, experts)
         scaled = (probs[tick_id, :, 0][:, :, None] * current.astype(jnp.float32)).astype(jnp.bfloat16)
         blocks = jnp.dot(one_hot, scaled.reshape(-1, model_width), preferred_element_type=jnp.float32)
         blocks = blocks.astype(jnp.bfloat16).reshape(experts, 2, capacity, model_width)

time: 205 us -> 204 us (level)
  transfers between devices with their start and end apart: 9 -> 9, of which waited for: 8 -> 8; matrix products, arithmetic and copies ran while one was open for 23% -> 24% of each run, Pallas kernels for 0% -> 0%
where the time goes in v13:
time: 204 us; the launch traced here: 203 us
  waiting for transfers between devices  104 us (51%)
  matrix products  44.7 us (22%)
  starting transfers between devices  30.4 us (15%)
  local copies, waits for them, and re-layouts  16.7 us (8%)
  other arithmetic  5.5 us (3%)
    all_to_all x2, waiting for transfers between devices, exchange(): lax.all_to_all(blocks, 'expert', split_axis=0, concat_axis=0, tiled=True)  48.1 us
    all_to_all x2, waiting for transfers between devices, on_device(): lax.all_to_all(back_blocks, 'expert', split_axis=0, concat_axis=0, tiled=...  31.2 us
    ppermute x3, waiting for transfers between devices, mirrored(): return lax.ppermute(block, axis, [(i, count - 1 - i) for i in range(count)])  20.5 us
    dot_general x10, matrix products, left_product(): lax.dot_general(left, right, (((0,), (0,)), ((), ())), preferred_element_...  16.8 us
    dot_general x6, matrix products, expert_grads(): gate_up = jnp.dot(saved_rows, weight_in, preferred_element_type=jnp.float32)  14.3 us
    unnamed x61, local copies, waits for them, and re-layouts  10.9 us
    dot_general x10, matrix products, right_product(): lax.dot_general(left, right, (((1,), (1,)), ((), ())), preferred_element_...  10.2 us
    all_to_all x2, starting transfers between devices, exchange(): lax.all_to_all(blocks, 'expert', split_axis=0, concat_axis=0, tiled=True)  9.95 us
  transfers between devices with their start and end apart: 9, of which 8 were waited for; matrix products, arithmetic and copies ran while one was open for 24% of the time, Pallas kernels for 0%

profile of v13, /device:TPU:1, one launch (start us, length us, event | category | flops | bytes accessed | tf_op | source)
XLA Modules:
  0.0 202.8 jit_solution(4326790656929574386)
XLA Ops:
  4.5 1.7 convolution_convert_fusion.1
  6.2 6.4 %all-to-all-start = ((bf16[8,2,24,2048]{3,2,1,0:T(8,128)(2,1)}), bf16[8,2,24,2048]{3,2,1,0:T(8,128)(2,1)S(1)}, u32[]{:S(2)}, u32[]{:S(2)}) async-start(bf16[8,2,24,2048]{3,2,1,0:T(8,128)(2,1)} %bitcast.11), calls=%async_computation | async-start | bytes 3145728 | tf_op jit(solution)/shard_map/all_to_all | solution.py:49
  12.6 2.9 %slice_bitcast_fusion = bf16[2,192,2048]{2,1,0:T(8,128)(2,1)} fusion(bf16[2,2,1,1,192,2048]{5,4,3,2,1,0:T(8,128)(2,1)} %param.12), kind=kLoop, calls=%fused_computation.44 | loop fusion | bytes 3145728 | tf_op jit(solution)/shard_map/squeeze | solution.py:80
  15.5 2.1 %collective-permute-start = (bf16[2,192,2048]{2,1,0:T(8,128)(2,1)}, bf16[2,192,2048]{2,1,0:T(8,128)(2,1)S(1)}, u32[]{:S(2)}, u32[]{:S(2)}) collective-permute-start(bf16[2,192,2048]{2,1,0:T(8,128)(2,1)} %slice_bitcast_fusion), channel_id=1, source_target_pairs={{0,24},{8,16},{16,8},{24,0},{1,25},{9,17},{17,9},{25,1},{2,26},{10... | collective-permute-start | bytes 4718600 | tf_op jit(solution)/shard_map/ppermute | solution.py:15
  17.5 3.0 %fusion.24 = f32[192,512]{1,0:T(8,128)} fusion(bf16[2,1,1,2048,512]{4,3,2,1,0:T(8,128)(2,1)} %param.8, bf16[2,2,1,1,192,2048]{5,4,3,2,1,0:T(8,128)(2,1)S(1)} %copy-done.1), kind=kOutput, calls=%fused_computation.36 | convolution fusion | flops 402653184 | bytes 3276800 | tf_op jit(solution)/shard_map/dot_general | solution.py:55
  21.8 26.9 %all-to-all-done = bf16[8,2,24,2048]{3,2,1,0:T(8,128)(2,1)S(1)} async-done(((bf16[8,2,24,2048]{3,2,1,0:T(8,128)(2,1)}), bf16[8,2,24,2048]{3,2,1,0:T(8,128)(2,1)S(1)}, u32[]{:S(2)}, u32[]{:S(2)}) %all-to-all-start) | async-done | bytes 1572896 | tf_op jit(solution)/shard_map/all_to_all | solution.py:49
  48.9 2.0 copy-done.25
  57.3 4.6 %all-to-all-start.1 = ((bf16[8,2,24,2048]{3,2,1,0:T(8,128)(2,1)}), bf16[8,2,24,2048]{3,2,1,0:T(8,128)(2,1)S(1)}, u32[]{:S(2)}, u32[]{:S(2)}) async-start(bf16[8,2,24,2048]{3,2,1,0:T(8,128)(2,1)} %pad_maximum_fusion), calls=%async_computation.1 | async-start | bytes 3145728 | tf_op jit(solution)/shard_map/all_to_all | solution.py:118
  61.9 1.9 collective-permute-start.1
  64.1 18.3 %collective-permute-done.1 = bf16[192,2048]{1,0:T(8,128)(2,1)S(1)} collective-permute-done((bf16[192,2048]{1,0:T(8,128)(2,1)}, bf16[192,2048]{1,0:T(8,128)(2,1)S(1)}, u32[]{:S(2)}, u32[]{:S(2)}) %collective-permute-start.1) | collective-permute-done | bytes 786464 | tf_op jit(solution)/shard_map/ppermute | solution.py:15
  82.4 15.9 %all-to-all-done.1 = bf16[8,2,24,2048]{3,2,1,0:T(8,128)(2,1)S(1)} async-done(((bf16[8,2,24,2048]{3,2,1,0:T(8,128)(2,1)}), bf16[8,2,24,2048]{3,2,1,0:T(8,128)(2,1)S(1)}, u32[]{:S(2)}, u32[]{:S(2)}) %all-to-all-start.1) | async-done | bytes 1572896 | tf_op jit(solution)/shard_map/all_to_all | solution.py:118
  99.0 3.6 %collective-permute-start.2 = (bf16[96,2048]{1,0:T(8,128)(2,1)S(1)}, bf16[96,2048]{1,0:T(8,128)(2,1)S(1)}, u32[]{:S(2)}, u32[]{:S(2)}) collective-permute-start(bf16[96,2048]{1,0:T(8,128)(2,1)S(1)} %get-tuple-element.28), channel_id=1, source_target_pairs={{8,0},{16,8},{24,16},{9,1},{17,9},{25,17},{10,2},{18,10},{26,18},{... | collective-permute-start | bytes 1179656 | tf_op jit(solution)/shard_map/ppermute | solution.py:10
  102.6 3.0 %collective-permute-start.3 = (bf16[96,2048]{1,0:T(8,128)(2,1)S(1)}, bf16[96,2048]{1,0:T(8,128)(2,1)S(1)}, u32[]{:S(2)}, u32[]{:S(2)}) collective-permute-start(bf16[96,2048]{1,0:T(8,128)(2,1)S(1)} %get-tuple-element.29), channel_id=1, source_target_pairs={{0,8},{8,16},{16,24},{1,9},{9,17},{17,25},{2,10},{10,18},{18,26},{... | collective-permute-start | bytes 1179656 | tf_op jit(solution)/shard_map/ppermute | solution.py:10
  105.7 3.4 %collective-permute-done.2 = bf16[96,2048]{1,0:T(8,128)(2,1)S(1)} collective-permute-done((bf16[96,2048]{1,0:T(8,128)(2,1)S(1)}, bf16[96,2048]{1,0:T(8,128)(2,1)S(1)}, u32[]{:S(2)}, u32[]{:S(2)}) %collective-permute-start.2) | collective-permute-done | bytes 393248 | tf_op jit(solution)/shard_map/ppermute | solution.py:10
  110.7 1.7 convolution_convert_fusion
  112.4 3.6 %all-to-all-start.2 = ((bf16[8,2,24,2048]{3,2,1,0:T(8,128)(2,1)}), bf16[8,2,24,2048]{3,2,1,0:T(8,128)(2,1)S(1)}, u32[]{:S(2)}, u32[]{:S(2)}) async-start(bf16[8,2,24,2048]{3,2,1,0:T(8,128)(2,1)} %bitcast.40), calls=%async_computation.2 | async-start | bytes 3145728 | tf_op jit(solution)/shard_map/all_to_all | solution.py:49
  116.2 2.5 %fusion.21 = f32[192,512]{1,0:T(8,128)S(1)} fusion(bf16[2,1,1,2048,512]{4,3,2,1,0:T(8,128)(2,1)} %param.8, bf16[2,2,1,1,192,2048]{5,4,3,2,1,0:T(8,128)(2,1)} %param.12), kind=kOutput, calls=%fused_computation.33 | convolution fusion | flops 402653184 | bytes 3276800 | tf_op jit(solution)/shard_map/dot_general | solution.py:55
  119.0 3.1 %fusion.11 = f32[192,512]{1,0:T(8,128)} fusion(bf16[2,1,1,2048,512]{4,3,2,1,0:T(8,128)(2,1)} %param.8, bf16[2,2,1,1,192,2048]{5,4,3,2,1,0:T(8,128)(2,1)S(1)} %copy-done.2), kind=kOutput, calls=%fused_computation.23 | convolution fusion | flops 402653184 | bytes 3276800 | tf_op jit(solution)/shard_map/dot_general | solution.py:55
  122.1 3.1 %fusion.16 = f32[192,512]{1,0:T(8,128)} fusion(bf16[2,1,1,2048,512]{4,3,2,1,0:T(8,128)(2,1)} %param.8, bf16[2,192,2048]{2,1,0:T(8,128)(2,1)S(1)} %copy-done.8), kind=kOutput, calls=%fused_computation.28 | convolution fusion | flops 402653184 | bytes 3276800 | tf_op jit(solution)/shard_map/dot_general | solution.py:55
  126.5 2.7 %fusion.61 = f32[512,2048]{1,0:T(8,128)} fusion(bf16[2,2,1,1,192,2048]{5,4,3,2,1,0:T(8,128)(2,1)S(1)} %copy-done.2, bf16[192,256]{1,0:T(8,128)(2,1)S(1)} %get-tuple-element.39, bf16[192,256]{1,0:T(8,128)(2,1)S(1)} %get-tuple-element.38), kind=kOutput, calls=%fused_computation.79 | convolution fusion | flops 403046400 | bytes 5177344 | tf_op jit(solution)/shard_map/dot_general | solution.py:19
  129.2 21.1 %all-to-all-done.2 = bf16[8,2,24,2048]{3,2,1,0:T(8,128)(2,1)S(1)} async-done(((bf16[8,2,24,2048]{3,2,1,0:T(8,128)(2,1)}), bf16[8,2,24,2048]{3,2,1,0:T(8,128)(2,1)S(1)}, u32[]{:S(2)}, u32[]{:S(2)}) %all-to-all-start.2) | async-done | bytes 1572896 | tf_op jit(solution)/shard_map/all_to_all | solution.py:49
  152.2 1.8 fusion.82
  157.7 4.5 %all-to-all-start.3 = ((bf16[8,2,24,2048]{3,2,1,0:T(8,128)(2,1)}), bf16[8,2,24,2048]{3,2,1,0:T(8,128)(2,1)}, u32[]{:S(2)}, u32[]{:S(2)}) async-start(bf16[8,2,24,2048]{3,2,1,0:T(8,128)(2,1)} %pad_maximum_fusion.1), calls=%async_computation.3 | async-start | bytes 3145728 | tf_op jit(solution)/shard_map/all_to_all | solution.py:118
  162.2 1.9 fusion.104
  164.2 1.9 multiply_convert_fusion.7
  166.8 2.2 %collective-permute-done.4 = bf16[192,2048]{1,0:T(8,128)(2,1)} collective-permute-done((bf16[192,2048]{1,0:T(8,128)(2,1)}, bf16[192,2048]{1,0:T(8,128)(2,1)}, u32[]{:S(2)}, u32[]{:S(2)}) %collective-permute-start.4) | collective-permute-done | bytes 786464 | tf_op jit(solution)/shard_map/ppermute | solution.py:15
  169.0 1.6 multiply_convert_fusion.5
  172.8 3.3 %fusion.1 = bf16[1,1,2048,512]{2,3,1,0:T(8,128)(2,1)} fusion(bf16[2048,512]{0,1:T(8,128)(2,1)S(1)} %add_convert_fusion, f32[512,2048]{1,0:T(8,128)S(1)} %copy-done, bf16[2,2,1,1,192,2048]{5,4,3,2,1,0:T(8,128)(2,1)} %param.12, bf16[192,256]{1,0:T(8,128)(2,1)S(1)} %get-tuple-element.35, bf16[192,256]{1,0:T(8,128)(2,1)S(1)} %get-tuple-element.34), kind=kOutput, calls=%fused_computation.5 | convolution fusion | flops 407240704 | bytes 9371648 | tf_op jit(solution)/shard_map/dot_general | solution.py:19
  176.1 3.9 %copy.34 = bf16[1,1,2048,512]{3,2,1,0:T(8,128)(2,1)} copy(bf16[1,1,2048,512]{2,3,1,0:T(8,128)(2,1)} %fusion.1) | data formatting | bytes 4194304
  180.0 1.9 fusion.105
  184.7 15.3 %all-to-all-done.3 = bf16[8,2,24,2048]{3,2,1,0:T(8,128)(2,1)} async-done(((bf16[8,2,24,2048]{3,2,1,0:T(8,128)(2,1)}), bf16[8,2,24,2048]{3,2,1,0:T(8,128)(2,1)}, u32[]{:S(2)}, u32[]{:S(2)}) %all-to-all-start.3) | async-done | bytes 1572896 | tf_op jit(solution)/shard_map/all_to_all | solution.py:118
  200.0 2.9 %fusion.9 = bf16[2,1,96,2048]{3,2,1,0:T(8,128)(2,1)} fusion(pred[2,96,384]{2,1,0:T(32,128)(4,1)S(1)} %bitcast.205, bf16[384,2048,1]{1,0,2:T(8,128)(2,1)} %bitcast.50, bf16[1,96,2048]{2,1,0:T(8,128)(2,1)S(1)} %get-tuple-element.27, bf16[1,96,2048]{2,1,0:T(8,128)(2,1)S(1)} %get-tuple-element.26), kind=kOutput, calls=%fused_computation.21 | convolution fusion | flops 303562752 | bytes 3219456 | tf_op jit(solution)/shard_map/dot_general | solution.py:19
  (102 shorter events, 27.0 us)
Async XLA Ops:
  6.2 42.6 %all-to-all-start = ((bf16[8,2,24,2048]{3,2,1,0:T(8,128)(2,1)}), bf16[8,2,24,2048]{3,2,1,0:T(8,128)(2,1)S(1)}, u32[]{:S(2)}, u32[]{:S(2)}) async-start(bf16[8,2,24,2048]{3,2,1,0:T(8,128)(2,1)} %bitcast.11), calls=%async_computation | async-start | bytes 3145728 | tf_op jit(solution)/shard_map/all_to_all | solution.py:49
  12.6 5.0 %copy-start.1 = (bf16[2,2,1,1,192,2048]{5,4,3,2,1,0:T(8,128)(2,1)S(1)}, bf16[2,2,1,1,192,2048]{5,4,3,2,1,0:T(8,128)(2,1)}, u32[]{:S(2)}) copy-start(bf16[2,2,1,1,192,2048]{5,4,3,2,1,0:T(8,128)(2,1)} %param.12) | copy-start | bytes 9437188
  15.5 5.0 %copy-start.21 = (bf16[2,1,1,2048,512]{4,3,2,1,0:T(8,128)(2,1)S(1)}, bf16[2,1,1,2048,512]{4,3,2,1,0:T(8,128)(2,1)}, u32[]{:S(2)}) copy-start(bf16[2,1,1,2048,512]{4,3,2,1,0:T(8,128)(2,1)} %param.8) | copy-start | bytes 12582916
  15.5 40.7 %collective-permute-start = (bf16[2,192,2048]{2,1,0:T(8,128)(2,1)}, bf16[2,192,2048]{2,1,0:T(8,128)(2,1)S(1)}, u32[]{:S(2)}, u32[]{:S(2)}) collective-permute-start(bf16[2,192,2048]{2,1,0:T(8,128)(2,1)} %slice_bitcast_fusion), channel_id=1, source_target_pairs={{0,24},{8,16},{16,8},{24,0},{1,25},{9,17},{17,9},{25,1},{2,26},{10... | collective-permute-start | bytes 4718600 | tf_op jit(solution)/shard_map/ppermute | solution.py:15
  48.7 2.2 %copy-start.25 = (bf16[2,1,1,256,2048]{4,3,2,1,0:T(8,128)(2,1)S(1)}, bf16[2,1,1,256,2048]{4,3,2,1,0:T(8,128)(2,1)}, u32[]{:S(2)}) copy-start(bf16[2,1,1,256,2048]{4,3,2,1,0:T(8,128)(2,1)} %param.9) | copy-start | bytes 6291460
  48.7 2.2 %copy-start.29 = (f32[192,512]{1,0:T(8,128)S(1)}, f32[192,512]{1,0:T(8,128)}, u32[]{:S(2)}) copy-start(f32[192,512]{1,0:T(8,128)} %fusion.14) | copy-start | bytes 1179652
  48.9 3.1 %copy-start.6 = (bf16[8,1,24,2048]{3,2,1,0:T(8,128)(2,1)}, bf16[8,1,24,2048]{3,2,1,0:T(8,128)(2,1)S(1)}, u32[]{:S(2)}) copy-start(bf16[8,1,24,2048]{3,2,1,0:T(8,128)(2,1)S(1)} %get-tuple-element.24) | copy-start | bytes 2359300
  48.9 3.1 %copy-start.14 = (bf16[8,1,24,2048]{3,2,1,0:T(8,128)(2,1)}, bf16[8,1,24,2048]{3,2,1,0:T(8,128)(2,1)S(1)}, u32[]{:S(2)}) copy-start(bf16[8,1,24,2048]{3,2,1,0:T(8,128)(2,1)S(1)} %get-tuple-element.25) | copy-start | bytes 2359300
  48.9 2.6 %copy-start.18 = (f32[192,512]{1,0:T(8,128)S(1)}, f32[192,512]{1,0:T(8,128)}, u32[]{:S(2)}) copy-start(f32[192,512]{1,0:T(8,128)} %fusion.24) | copy-start | bytes 1179652
  50.9 2.2 %copy-start.22 = (bf16[2,1,1,2048,512]{4,3,2,1,0:T(8,128)(2,1)S(1)}, bf16[2,1,1,2048,512]{4,3,2,1,0:T(8,128)(2,1)}, u32[]{:S(2)}) copy-start(bf16[2,1,1,2048,512]{4,3,2,1,0:T(8,128)(2,1)} %param.8) | copy-start | bytes 12582916
  56.1 42.2 %copy-start.5 = (bf16[2,1,96,2048]{3,2,1,0:T(8,128)(2,1)S(1)}, bf16[2,1,96,2048]{3,2,1,0:T(8,128)(2,1)}, u32[]{:S(2)}) copy-start(bf16[2,1,96,2048]{3,2,1,0:T(8,128)(2,1)} %param.10) | copy-start | bytes 2359300
  57.3 41.0 %all-to-all-start.1 = ((bf16[8,2,24,2048]{3,2,1,0:T(8,128)(2,1)}), bf16[8,2,24,2048]{3,2,1,0:T(8,128)(2,1)S(1)}, u32[]{:S(2)}, u32[]{:S(2)}) async-start(bf16[8,2,24,2048]{3,2,1,0:T(8,128)(2,1)} %pad_maximum_fusion), calls=%async_computation.1 | async-start | bytes 3145728 | tf_op jit(solution)/shard_map/all_to_all | solution.py:118
  61.9 20.5 %collective-permute-start.1 = (bf16[192,2048]{1,0:T(8,128)(2,1)}, bf16[192,2048]{1,0:T(8,128)(2,1)S(1)}, u32[]{:S(2)}, u32[]{:S(2)}) collective-permute-start(bf16[192,2048]{1,0:T(8,128)(2,1)} %bitcast.200), channel_id=1, source_target_pairs={{0,24},{8,16},{16,8},{24,0},{1,25},{9,17},{17,9},{25,1},{2,26},{10... | collective-permute-start | bytes 2359304 | tf_op jit(solution)/shard_map/ppermute | solution.py:15
  82.4 16.6 %copy-start.10 = (bf16[192,2048]{1,0:T(8,128)(2,1)}, bf16[192,2048]{1,0:T(8,128)(2,1)S(1)}, u32[]{:S(2)}) copy-start(bf16[192,2048]{1,0:T(8,128)(2,1)S(1)} %collective-permute-done.1) | copy-start | bytes 2359300
  98.9 11.5 %copy-start.13 = (bf16[1,2,96,2048]{3,2,1,0:T(8,128)(2,1)S(1)}, bf16[1,2,96,2048]{3,2,1,0:T(8,128)(2,1)}, u32[]{:S(2)}) copy-start(bf16[1,2,96,2048]{3,2,1,0:T(8,128)(2,1)} %param.11) | copy-start | bytes 2359300
  99.0 10.2 %collective-permute-start.2 = (bf16[96,2048]{1,0:T(8,128)(2,1)S(1)}, bf16[96,2048]{1,0:T(8,128)(2,1)S(1)}, u32[]{:S(2)}, u32[]{:S(2)}) collective-permute-start(bf16[96,2048]{1,0:T(8,128)(2,1)S(1)} %get-tuple-element.28), channel_id=1, source_target_pairs={{8,0},{16,8},{24,16},{9,1},{17,9},{25,17},{10,2},{18,10},{26,18},{... | collective-permute-start | bytes 1179656 | tf_op jit(solution)/shard_map/ppermute | solution.py:10
  102.6 7.7 %collective-permute-start.3 = (bf16[96,2048]{1,0:T(8,128)(2,1)S(1)}, bf16[96,2048]{1,0:T(8,128)(2,1)S(1)}, u32[]{:S(2)}, u32[]{:S(2)}) collective-permute-start(bf16[96,2048]{1,0:T(8,128)(2,1)S(1)} %get-tuple-element.29), channel_id=1, source_target_pairs={{0,8},{8,16},{16,24},{1,9},{9,17},{17,25},{2,10},{10,18},{18,26},{... | collective-permute-start | bytes 1179656 | tf_op jit(solution)/shard_map/ppermute | solution.py:10
  112.4 37.9 %all-to-all-start.2 = ((bf16[8,2,24,2048]{3,2,1,0:T(8,128)(2,1)}), bf16[8,2,24,2048]{3,2,1,0:T(8,128)(2,1)S(1)}, u32[]{:S(2)}, u32[]{:S(2)}) async-start(bf16[8,2,24,2048]{3,2,1,0:T(8,128)(2,1)} %bitcast.40), calls=%async_computation.2 | async-start | bytes 3145728 | tf_op jit(solution)/shard_map/all_to_all | solution.py:49
  116.2 2.8 %copy-start.2 = (bf16[2,2,1,1,192,2048]{5,4,3,2,1,0:T(8,128)(2,1)S(1)}, bf16[2,2,1,1,192,2048]{5,4,3,2,1,0:T(8,128)(2,1)}, u32[]{:S(2)}) copy-start(bf16[2,2,1,1,192,2048]{5,4,3,2,1,0:T(8,128)(2,1)} %param.12) | copy-start | bytes 9437188
  119.0 35.1 %copy-start.15 = (f32[192,512]{1,0:T(8,128)}, f32[192,512]{1,0:T(8,128)S(1)}, u32[]{:S(2)}) copy-start(f32[192,512]{1,0:T(8,128)S(1)} %fusion.21) | copy-start | bytes 1179652
  119.0 3.1 %copy-start.8 = (bf16[2,192,2048]{2,1,0:T(8,128)(2,1)S(1)}, bf16[2,192,2048]{2,1,0:T(8,128)(2,1)}, u32[]{:S(2)}) copy-start(bf16[2,192,2048]{2,1,0:T(8,128)(2,1)} %copy-done.7) | copy-start | bytes 4718596
  122.1 3.1 %copy-start.23 = (bf16[2,1,1,2048,512]{4,3,2,1,0:T(8,128)(2,1)S(1)}, bf16[2,1,1,2048,512]{4,3,2,1,0:T(8,128)(2,1)}, u32[]{:S(2)}) copy-start(bf16[2,1,1,2048,512]{4,3,2,1,0:T(8,128)(2,1)} %param.8) | copy-start | bytes 12582916
  129.2 22.9 %copy-start.28 = (f32[192,512]{1,0:T(8,128)S(1)}, f32[192,512]{1,0:T(8,128)}, u32[]{:S(2)}) copy-start(f32[192,512]{1,0:T(8,128)} %fusion.11) | copy-start | bytes 1179652
  151.3 3.2 %copy-start.3 = (bf16[8,1,24,2048]{3,2,1,0:T(8,128)(2,1)}, bf16[8,1,24,2048]{3,2,1,0:T(8,128)(2,1)S(1)}, u32[]{:S(2)}) copy-start(bf16[8,1,24,2048]{3,2,1,0:T(8,128)(2,1)S(1)} %get-tuple-element.22) | copy-start | bytes 2359300
  151.3 17.7 %collective-permute-start.4 = (bf16[192,2048]{1,0:T(8,128)(2,1)}, bf16[192,2048]{1,0:T(8,128)(2,1)}, u32[]{:S(2)}, u32[]{:S(2)}) collective-permute-start(bf16[192,2048]{1,0:T(8,128)(2,1)} %bitcast.45), channel_id=1, source_target_pairs={{0,24},{8,16},{16,8},{24,0},{1,25},{9,17},{17,9},{25,1},{2,26},{10... | collective-permute-start | bytes 2359304 | tf_op jit(solution)/shard_map/ppermute | solution.py:15
  152.2 2.4 %copy-start.24 = (bf16[2,1,1,2048,512]{4,3,2,1,0:T(8,128)(2,1)S(1)}, bf16[2,1,1,2048,512]{4,3,2,1,0:T(8,128)(2,1)}, u32[]{:S(2)}) copy-start(bf16[2,1,1,2048,512]{4,3,2,1,0:T(8,128)(2,1)} %param.8) | copy-start | bytes 12582916
  157.7 42.3 %all-to-all-start.3 = ((bf16[8,2,24,2048]{3,2,1,0:T(8,128)(2,1)}), bf16[8,2,24,2048]{3,2,1,0:T(8,128)(2,1)}, u32[]{:S(2)}, u32[]{:S(2)}) async-start(bf16[8,2,24,2048]{3,2,1,0:T(8,128)(2,1)} %pad_maximum_fusion.1), calls=%async_computation.3 | async-start | bytes 3145728 | tf_op jit(solution)/shard_map/all_to_all | solution.py:118
  162.2 1.9 copy-start.11
  162.2 1.9 copy-start.17
  166.0 3.0 %copy-start.19 = (f32[192,512]{1,0:T(8,128)S(1)}, f32[192,512]{1,0:T(8,128)}, u32[]{:S(2)}) copy-start(f32[192,512]{1,0:T(8,128)} %fusion.16) | copy-start | bytes 1179652
  166.0 3.0 %copy-start.27 = (bf16[2,1,1,256,2048]{4,3,2,1,0:T(8,128)(2,1)S(1)}, bf16[2,1,1,256,2048]{4,3,2,1,0:T(8,128)(2,1)}, u32[]{:S(2)}) copy-start(bf16[2,1,1,256,2048]{4,3,2,1,0:T(8,128)(2,1)} %param.9) | copy-start | bytes 6291460
  170.6 2.2 %copy-start = (f32[512,2048]{1,0:T(8,128)S(1)}, f32[512,2048]{1,0:T(8,128)}, u32[]{:S(2)}) copy-start(f32[512,2048]{1,0:T(8,128)} %fusion.61) | copy-start | bytes 12582916
  (7 other events, 10.6 us)

commit v14 on v13

--- a/solution.py
+++ b/solution.py
@@ -41,7 +41,9 @@
         [slot_table(route_ids[w], capacity, w, ways) for w in range(ways)]
     )
     rows = lax.iota(jnp.int32, ways * experts * capacity)
-    return (rows[:, None] == slots[None, :]).astype(jnp.bfloat16)
+    scatter = (rows[:, None] == slots[None, :]).astype(jnp.bfloat16)
+    gather = (slots[:, None] == rows[None, :]).astype(jnp.bfloat16)
+    return scatter, gather
 
 
 def exchange(blocks):
@@ -85,7 +87,7 @@
     mirror_in, mirror_out = zeros_in, zeros_out
     slope_mirror = None
     for tick_id in range(ticks):
-        one_hot = placement(routes[tick_id, :, 0], capacity, experts)
+        one_hot, one_hot_back = placement(routes[tick_id, :, 0], capacity, experts)
         scaled = (probs[tick_id, :, 0][:, :, None] * current.astype(jnp.float32)).astype(jnp.bfloat16)
         blocks = jnp.dot(one_hot, scaled.reshape(-1, model_width), preferred_element_type=jnp.float32)
         blocks = blocks.astype(jnp.bfloat16).reshape(experts, 2, capacity, model_width)
@@ -118,7 +120,7 @@
         returned = lax.all_to_all(back_blocks, "expert", split_axis=0, concat_axis=0, tiled=True)
         if tick_id + 1 < ticks:
             returned, slope_mirror = lax.optimization_barrier((returned, slope_mirror))
-        back_rows = left_product(one_hot, returned.reshape(-1, model_width))
+        back_rows = jnp.dot(one_hot_back, returned.reshape(-1, model_width), preferred_element_type=jnp.float32)
         finished = (current.astype(jnp.float32) + back_rows.reshape(2, tokens, model_width)).astype(
             jnp.bfloat16
         )

time: 204 us -> 204 us (level)
    dot_general x0 -> x2, matrix products: none -> 3.53 us  [on_device(): jnp.dot(one_hot_back, returned.reshape(-1, model_width), preferred_elemen...]
    dot_general x10 -> x8, matrix products: 16.8 us -> 13.3 us  [left_product(): lax.dot_general(left, right, (((0,), (0,)), ((), ())), preferred_element_...]
    unnamed x61 -> x59, local copies, waits for them, and re-layouts: 10.9 us -> 11 us
  transfers between devices with their start and end apart: 9 -> 9, of which waited for: 8 -> 8; matrix products, arithmetic and copies ran while one was open for 24% -> 23% of each run, Pallas kernels for 0% -> 0%
where the time goes in v14:
time: 204 us; the launch traced here: 203 us
  waiting for transfers between devices  105 us (51%)
  matrix products  44.1 us (22%)
  starting transfers between devices  30.4 us (15%)
  local copies, waits for them, and re-layouts  16.8 us (8%)
  other arithmetic  4.89 us (2%)
    all_to_all x2, waiting for transfers between devices, exchange(): lax.all_to_all(blocks, 'expert', split_axis=0, concat_axis=0, tiled=True)  48.9 us
    all_to_all x2, waiting for transfers between devices, on_device(): lax.all_to_all(back_blocks, 'expert', split_axis=0, concat_axis=0, tiled=...  31.1 us
    ppermute x3, waiting for transfers between devices, mirrored(): return lax.ppermute(block, axis, [(i, count - 1 - i) for i in range(count)])  20.8 us
    dot_general x6, matrix products, expert_grads(): gate_up = jnp.dot(saved_rows, weight_in, preferred_element_type=jnp.float32)  13.6 us
    dot_general x8, matrix products, left_product(): lax.dot_general(left, right, (((0,), (0,)), ((), ())), preferred_element_...  13.3 us
    unnamed x59, local copies, waits for them, and re-layouts  11 us
    dot_general x10, matrix products, right_product(): lax.dot_general(left, right, (((1,), (1,)), ((), ())), preferred_element_...  10.2 us
    all_to_all x2, starting transfers between devices, exchange(): lax.all_to_all(blocks, 'expert', split_axis=0, concat_axis=0, tiled=True)  9.95 us
  transfers between devices with their start and end apart: 9, of which 8 were waited for; matrix products, arithmetic and copies ran while one was open for 23% of the time, Pallas kernels for 0%

profile of v14, /device:TPU:1, one launch (start us, length us, event | category | flops | bytes accessed | tf_op | source)
XLA Modules:
  0.0 202.6 jit_solution(2089749914458151956)
XLA Ops:
  4.1 1.7 convolution_convert_fusion.1
  5.8 6.4 %all-to-all-start = ((bf16[8,2,24,2048]{3,2,1,0:T(8,128)(2,1)}), bf16[8,2,24,2048]{3,2,1,0:T(8,128)(2,1)S(1)}, u32[]{:S(2)}, u32[]{:S(2)}) async-start(bf16[8,2,24,2048]{3,2,1,0:T(8,128)(2,1)} %bitcast.7), calls=%async_computation | async-start | bytes 3145728 | tf_op jit(solution)/shard_map/all_to_all | solution.py:51
  12.2 2.9 %slice_bitcast_fusion = bf16[2,192,2048]{2,1,0:T(8,128)(2,1)} fusion(bf16[2,2,1,1,192,2048]{5,4,3,2,1,0:T(8,128)(2,1)} %param.12), kind=kLoop, calls=%fused_computation.44 | loop fusion | bytes 3145728 | tf_op jit(solution)/shard_map/squeeze | solution.py:82
  15.1 2.1 %collective-permute-start = (bf16[2,192,2048]{2,1,0:T(8,128)(2,1)}, bf16[2,192,2048]{2,1,0:T(8,128)(2,1)S(1)}, u32[]{:S(2)}, u32[]{:S(2)}) collective-permute-start(bf16[2,192,2048]{2,1,0:T(8,128)(2,1)} %slice_bitcast_fusion), channel_id=1, source_target_pairs={{0,24},{8,16},{16,8},{24,0},{1,25},{9,17},{17,9},{25,1},{2,26},{10... | collective-permute-start | bytes 4718600 | tf_op jit(solution)/shard_map/ppermute | solution.py:15
  17.2 2.9 %fusion.24 = f32[192,512]{1,0:T(8,128)} fusion(bf16[2,1,1,2048,512]{4,3,2,1,0:T(8,128)(2,1)} %param.8, bf16[2,2,1,1,192,2048]{5,4,3,2,1,0:T(8,128)(2,1)S(1)} %copy-done.1), kind=kOutput, calls=%fused_computation.36 | convolution fusion | flops 402653184 | bytes 3276800 | tf_op jit(solution)/shard_map/dot_general | solution.py:57
  21.5 26.9 %all-to-all-done = bf16[8,2,24,2048]{3,2,1,0:T(8,128)(2,1)S(1)} async-done(((bf16[8,2,24,2048]{3,2,1,0:T(8,128)(2,1)}), bf16[8,2,24,2048]{3,2,1,0:T(8,128)(2,1)S(1)}, u32[]{:S(2)}, u32[]{:S(2)}) %all-to-all-start) | async-done | bytes 1572896 | tf_op jit(solution)/shard_map/all_to_all | solution.py:51
  48.5 2.0 copy-done.25
  57.0 4.6 %all-to-all-start.1 = ((bf16[8,2,24,2048]{3,2,1,0:T(8,128)(2,1)}), bf16[8,2,24,2048]{3,2,1,0:T(8,128)(2,1)S(1)}, u32[]{:S(2)}, u32[]{:S(2)}) async-start(bf16[8,2,24,2048]{3,2,1,0:T(8,128)(2,1)} %pad_maximum_fusion), calls=%async_computation.1 | async-start | bytes 3145728 | tf_op jit(solution)/shard_map/all_to_all | solution.py:120
  61.6 1.9 collective-permute-start.1
  63.6 18.5 %collective-permute-done.1 = bf16[192,2048]{1,0:T(8,128)(2,1)S(1)} collective-permute-done((bf16[192,2048]{1,0:T(8,128)(2,1)}, bf16[192,2048]{1,0:T(8,128)(2,1)S(1)}, u32[]{:S(2)}, u32[]{:S(2)}) %collective-permute-start.1) | collective-permute-done | bytes 786464 | tf_op jit(solution)/shard_map/ppermute | solution.py:15
  82.1 15.9 %all-to-all-done.1 = bf16[8,2,24,2048]{3,2,1,0:T(8,128)(2,1)S(1)} async-done(((bf16[8,2,24,2048]{3,2,1,0:T(8,128)(2,1)}), bf16[8,2,24,2048]{3,2,1,0:T(8,128)(2,1)S(1)}, u32[]{:S(2)}, u32[]{:S(2)}) %all-to-all-start.1) | async-done | bytes 1572896 | tf_op jit(solution)/shard_map/all_to_all | solution.py:120
  98.7 3.6 %collective-permute-start.2 = (bf16[96,2048]{1,0:T(8,128)(2,1)S(1)}, bf16[96,2048]{1,0:T(8,128)(2,1)S(1)}, u32[]{:S(2)}, u32[]{:S(2)}) collective-permute-start(bf16[96,2048]{1,0:T(8,128)(2,1)S(1)} %get-tuple-element.28), channel_id=1, source_target_pairs={{8,0},{16,8},{24,16},{9,1},{17,9},{25,17},{10,2},{18,10},{26,18},{... | collective-permute-start | bytes 1179656 | tf_op jit(solution)/shard_map/ppermute | solution.py:10
  102.4 3.0 %collective-permute-start.3 = (bf16[96,2048]{1,0:T(8,128)(2,1)S(1)}, bf16[96,2048]{1,0:T(8,128)(2,1)S(1)}, u32[]{:S(2)}, u32[]{:S(2)}) collective-permute-start(bf16[96,2048]{1,0:T(8,128)(2,1)S(1)} %get-tuple-element.29), channel_id=1, source_target_pairs={{0,8},{8,16},{16,24},{1,9},{9,17},{17,25},{2,10},{10,18},{18,26},{... | collective-permute-start | bytes 1179656 | tf_op jit(solution)/shard_map/ppermute | solution.py:10
  105.6 3.4 %collective-permute-done.2 = bf16[96,2048]{1,0:T(8,128)(2,1)S(1)} collective-permute-done((bf16[96,2048]{1,0:T(8,128)(2,1)S(1)}, bf16[96,2048]{1,0:T(8,128)(2,1)S(1)}, u32[]{:S(2)}, u32[]{:S(2)}) %collective-permute-start.2) | collective-permute-done | bytes 393248 | tf_op jit(solution)/shard_map/ppermute | solution.py:10
  110.5 1.7 convolution_convert_fusion
  112.2 3.6 %all-to-all-start.2 = ((bf16[8,2,24,2048]{3,2,1,0:T(8,128)(2,1)}), bf16[8,2,24,2048]{3,2,1,0:T(8,128)(2,1)S(1)}, u32[]{:S(2)}, u32[]{:S(2)}) async-start(bf16[8,2,24,2048]{3,2,1,0:T(8,128)(2,1)} %bitcast.32), calls=%async_computation.2 | async-start | bytes 3145728 | tf_op jit(solution)/shard_map/all_to_all | solution.py:51
  115.8 2.5 %fusion.21 = f32[192,512]{1,0:T(8,128)S(1)} fusion(bf16[2,1,1,2048,512]{4,3,2,1,0:T(8,128)(2,1)} %param.8, bf16[2,2,1,1,192,2048]{5,4,3,2,1,0:T(8,128)(2,1)} %param.12), kind=kOutput, calls=%fused_computation.33 | convolution fusion | flops 402653184 | bytes 3276800 | tf_op jit(solution)/shard_map/dot_general | solution.py:57
  118.6 2.3 %fusion.11 = f32[192,512]{1,0:T(8,128)S(1)} fusion(bf16[2,1,1,2048,512]{4,3,2,1,0:T(8,128)(2,1)} %param.8, bf16[2,2,1,1,192,2048]{5,4,3,2,1,0:T(8,128)(2,1)S(1)} %copy-done.2), kind=kOutput, calls=%fused_computation.23 | convolution fusion | flops 402653184 | bytes 3276800 | tf_op jit(solution)/shard_map/dot_general | solution.py:57
  121.0 3.1 %fusion.16 = f32[192,512]{1,0:T(8,128)} fusion(bf16[2,1,1,2048,512]{4,3,2,1,0:T(8,128)(2,1)} %param.8, bf16[2,192,2048]{2,1,0:T(8,128)(2,1)S(1)} %copy-done.8), kind=kOutput, calls=%fused_computation.28 | convolution fusion | flops 402653184 | bytes 3276800 | tf_op jit(solution)/shard_map/dot_general | solution.py:57
  125.4 2.7 %fusion.61 = f32[512,2048]{1,0:T(8,128)} fusion(bf16[2,2,1,1,192,2048]{5,4,3,2,1,0:T(8,128)(2,1)S(1)} %copy-done.2, bf16[192,256]{1,0:T(8,128)(2,1)S(1)} %get-tuple-element.39, bf16[192,256]{1,0:T(8,128)(2,1)S(1)} %get-tuple-element.38), kind=kOutput, calls=%fused_computation.79 | convolution fusion | flops 403046400 | bytes 5177344 | tf_op jit(solution)/shard_map/dot_general | solution.py:19
  128.1 22.0 %all-to-all-done.2 = bf16[8,2,24,2048]{3,2,1,0:T(8,128)(2,1)S(1)} async-done(((bf16[8,2,24,2048]{3,2,1,0:T(8,128)(2,1)}), bf16[8,2,24,2048]{3,2,1,0:T(8,128)(2,1)S(1)}, u32[]{:S(2)}, u32[]{:S(2)}) %all-to-all-start.2) | async-done | bytes 1572896 | tf_op jit(solution)/shard_map/all_to_all | solution.py:51
  152.0 1.8 fusion.86
  157.4 4.5 %all-to-all-start.3 = ((bf16[8,2,24,2048]{3,2,1,0:T(8,128)(2,1)}), bf16[8,2,24,2048]{3,2,1,0:T(8,128)(2,1)}, u32[]{:S(2)}, u32[]{:S(2)}) async-start(bf16[8,2,24,2048]{3,2,1,0:T(8,128)(2,1)} %pad_maximum_fusion.1), calls=%async_computation.3 | async-start | bytes 3145728 | tf_op jit(solution)/shard_map/all_to_all | solution.py:120
  161.9 1.9 fusion.110
  163.8 1.9 multiply_convert_fusion.7
  166.5 2.3 %collective-permute-done.4 = bf16[192,2048]{1,0:T(8,128)(2,1)} collective-permute-done((bf16[192,2048]{1,0:T(8,128)(2,1)}, bf16[192,2048]{1,0:T(8,128)(2,1)}, u32[]{:S(2)}, u32[]{:S(2)}) %collective-permute-start.4) | collective-permute-done | bytes 786464 | tf_op jit(solution)/shard_map/ppermute | solution.py:15
  168.8 1.6 multiply_convert_fusion.5
  172.6 3.3 %fusion.1 = bf16[1,1,2048,512]{2,3,1,0:T(8,128)(2,1)} fusion(bf16[2048,512]{0,1:T(8,128)(2,1)S(1)} %add_convert_fusion, f32[512,2048]{1,0:T(8,128)S(1)} %copy-done, bf16[2,2,1,1,192,2048]{5,4,3,2,1,0:T(8,128)(2,1)} %param.12, bf16[192,256]{1,0:T(8,128)(2,1)S(1)} %get-tuple-element.35, bf16[192,256]{1,0:T(8,128)(2,1)S(1)} %get-tuple-element.34), kind=kOutput, calls=%fused_computation.5 | convolution fusion | flops 407240704 | bytes 9371648 | tf_op jit(solution)/shard_map/dot_general | solution.py:19
  175.9 3.9 %copy.34 = bf16[1,1,2048,512]{3,2,1,0:T(8,128)(2,1)} copy(bf16[1,1,2048,512]{2,3,1,0:T(8,128)(2,1)} %fusion.1) | data formatting | bytes 4194304
  179.8 1.9 fusion.111
  184.5 15.2 %all-to-all-done.3 = bf16[8,2,24,2048]{3,2,1,0:T(8,128)(2,1)} async-done(((bf16[8,2,24,2048]{3,2,1,0:T(8,128)(2,1)}), bf16[8,2,24,2048]{3,2,1,0:T(8,128)(2,1)}, u32[]{:S(2)}, u32[]{:S(2)}) %all-to-all-start.3) | async-done | bytes 1572896 | tf_op jit(solution)/shard_map/all_to_all | solution.py:120
  199.6 2.9 %fusion.9 = bf16[2,1,96,2048]{3,2,1,0:T(8,128)(2,1)} fusion(bf16[384,2048,1]{1,0,2:T(8,128)(2,1)} %bitcast.42, s32[2,96]{1,0:T(2,128)S(1)} %eq.168, bf16[1,96,2048]{2,1,0:T(8,128)(2,1)S(1)} %get-tuple-element.27, bf16[1,96,2048]{2,1,0:T(8,128)(2,1)S(1)} %get-tuple-element.26), kind=kOutput, calls=%fused_computation.21 | convolution fusion | flops 303636480 | bytes 3146496 | tf_op jit(solution)/shard_map/dot_general | solution.py:123
  (95 shorter events, 26.5 us)
Async XLA Ops:
  0.6 3.2 %copy-start.20 = (s32[2,2,1,96]{3,2,1,0:T(1,128)S(1)}, s32[2,2,1,96]{3,2,1,0:T(1,128)}, u32[]{:S(2)}) copy-start(s32[2,2,1,96]{3,2,1,0:T(1,128)} %param.14) | copy-start | bytes 4612
  5.8 42.6 %all-to-all-start = ((bf16[8,2,24,2048]{3,2,1,0:T(8,128)(2,1)}), bf16[8,2,24,2048]{3,2,1,0:T(8,128)(2,1)S(1)}, u32[]{:S(2)}, u32[]{:S(2)}) async-start(bf16[8,2,24,2048]{3,2,1,0:T(8,128)(2,1)} %bitcast.7), calls=%async_computation | async-start | bytes 3145728 | tf_op jit(solution)/shard_map/all_to_all | solution.py:51
  12.2 5.0 %copy-start.1 = (bf16[2,2,1,1,192,2048]{5,4,3,2,1,0:T(8,128)(2,1)S(1)}, bf16[2,2,1,1,192,2048]{5,4,3,2,1,0:T(8,128)(2,1)}, u32[]{:S(2)}) copy-start(bf16[2,2,1,1,192,2048]{5,4,3,2,1,0:T(8,128)(2,1)} %param.12) | copy-start | bytes 9437188
  15.1 5.0 %copy-start.21 = (bf16[2,1,1,2048,512]{4,3,2,1,0:T(8,128)(2,1)S(1)}, bf16[2,1,1,2048,512]{4,3,2,1,0:T(8,128)(2,1)}, u32[]{:S(2)}) copy-start(bf16[2,1,1,2048,512]{4,3,2,1,0:T(8,128)(2,1)} %param.8) | copy-start | bytes 12582916
  15.1 40.6 %collective-permute-start = (bf16[2,192,2048]{2,1,0:T(8,128)(2,1)}, bf16[2,192,2048]{2,1,0:T(8,128)(2,1)S(1)}, u32[]{:S(2)}, u32[]{:S(2)}) collective-permute-start(bf16[2,192,2048]{2,1,0:T(8,128)(2,1)} %slice_bitcast_fusion), channel_id=1, source_target_pairs={{0,24},{8,16},{16,8},{24,0},{1,25},{9,17},{17,9},{25,1},{2,26},{10... | collective-permute-start | bytes 4718600 | tf_op jit(solution)/shard_map/ppermute | solution.py:15
  48.4 2.2 %copy-start.25 = (bf16[2,1,1,256,2048]{4,3,2,1,0:T(8,128)(2,1)S(1)}, bf16[2,1,1,256,2048]{4,3,2,1,0:T(8,128)(2,1)}, u32[]{:S(2)}) copy-start(bf16[2,1,1,256,2048]{4,3,2,1,0:T(8,128)(2,1)} %param.9) | copy-start | bytes 6291460
  48.4 2.2 %copy-start.28 = (f32[192,512]{1,0:T(8,128)S(1)}, f32[192,512]{1,0:T(8,128)}, u32[]{:S(2)}) copy-start(f32[192,512]{1,0:T(8,128)} %fusion.14) | copy-start | bytes 1179652
  48.5 3.1 %copy-start.6 = (bf16[8,1,24,2048]{3,2,1,0:T(8,128)(2,1)}, bf16[8,1,24,2048]{3,2,1,0:T(8,128)(2,1)S(1)}, u32[]{:S(2)}) copy-start(bf16[8,1,24,2048]{3,2,1,0:T(8,128)(2,1)S(1)} %get-tuple-element.24) | copy-start | bytes 2359300
  48.5 3.1 %copy-start.14 = (bf16[8,1,24,2048]{3,2,1,0:T(8,128)(2,1)}, bf16[8,1,24,2048]{3,2,1,0:T(8,128)(2,1)S(1)}, u32[]{:S(2)}) copy-start(bf16[8,1,24,2048]{3,2,1,0:T(8,128)(2,1)S(1)} %get-tuple-element.25) | copy-start | bytes 2359300
  48.5 2.6 %copy-start.18 = (f32[192,512]{1,0:T(8,128)S(1)}, f32[192,512]{1,0:T(8,128)}, u32[]{:S(2)}) copy-start(f32[192,512]{1,0:T(8,128)} %fusion.24) | copy-start | bytes 1179652
  50.6 2.2 %copy-start.22 = (bf16[2,1,1,2048,512]{4,3,2,1,0:T(8,128)(2,1)S(1)}, bf16[2,1,1,2048,512]{4,3,2,1,0:T(8,128)(2,1)}, u32[]{:S(2)}) copy-start(bf16[2,1,1,2048,512]{4,3,2,1,0:T(8,128)(2,1)} %param.8) | copy-start | bytes 12582916
  55.8 42.2 %copy-start.5 = (bf16[2,1,96,2048]{3,2,1,0:T(8,128)(2,1)S(1)}, bf16[2,1,96,2048]{3,2,1,0:T(8,128)(2,1)}, u32[]{:S(2)}) copy-start(bf16[2,1,96,2048]{3,2,1,0:T(8,128)(2,1)} %param.10) | copy-start | bytes 2359300
  57.0 41.0 %all-to-all-start.1 = ((bf16[8,2,24,2048]{3,2,1,0:T(8,128)(2,1)}), bf16[8,2,24,2048]{3,2,1,0:T(8,128)(2,1)S(1)}, u32[]{:S(2)}, u32[]{:S(2)}) async-start(bf16[8,2,24,2048]{3,2,1,0:T(8,128)(2,1)} %pad_maximum_fusion), calls=%async_computation.1 | async-start | bytes 3145728 | tf_op jit(solution)/shard_map/all_to_all | solution.py:120
  61.6 20.5 %collective-permute-start.1 = (bf16[192,2048]{1,0:T(8,128)(2,1)}, bf16[192,2048]{1,0:T(8,128)(2,1)S(1)}, u32[]{:S(2)}, u32[]{:S(2)}) collective-permute-start(bf16[192,2048]{1,0:T(8,128)(2,1)} %bitcast.186), channel_id=1, source_target_pairs={{0,24},{8,16},{16,8},{24,0},{1,25},{9,17},{17,9},{25,1},{2,26},{10... | collective-permute-start | bytes 2359304 | tf_op jit(solution)/shard_map/ppermute | solution.py:15
  82.1 16.6 %copy-start.10 = (bf16[192,2048]{1,0:T(8,128)(2,1)}, bf16[192,2048]{1,0:T(8,128)(2,1)S(1)}, u32[]{:S(2)}) copy-start(bf16[192,2048]{1,0:T(8,128)(2,1)S(1)} %collective-permute-done.1) | copy-start | bytes 2359300
  98.6 11.5 %copy-start.13 = (bf16[1,2,96,2048]{3,2,1,0:T(8,128)(2,1)S(1)}, bf16[1,2,96,2048]{3,2,1,0:T(8,128)(2,1)}, u32[]{:S(2)}) copy-start(bf16[1,2,96,2048]{3,2,1,0:T(8,128)(2,1)} %param.11) | copy-start | bytes 2359300
  98.7 10.2 %collective-permute-start.2 = (bf16[96,2048]{1,0:T(8,128)(2,1)S(1)}, bf16[96,2048]{1,0:T(8,128)(2,1)S(1)}, u32[]{:S(2)}, u32[]{:S(2)}) collective-permute-start(bf16[96,2048]{1,0:T(8,128)(2,1)S(1)} %get-tuple-element.28), channel_id=1, source_target_pairs={{8,0},{16,8},{24,16},{9,1},{17,9},{25,17},{10,2},{18,10},{26,18},{... | collective-permute-start | bytes 1179656 | tf_op jit(solution)/shard_map/ppermute | solution.py:10
  102.4 7.7 %collective-permute-start.3 = (bf16[96,2048]{1,0:T(8,128)(2,1)S(1)}, bf16[96,2048]{1,0:T(8,128)(2,1)S(1)}, u32[]{:S(2)}, u32[]{:S(2)}) collective-permute-start(bf16[96,2048]{1,0:T(8,128)(2,1)S(1)} %get-tuple-element.29), channel_id=1, source_target_pairs={{0,8},{8,16},{16,24},{1,9},{9,17},{17,25},{2,10},{10,18},{18,26},{... | collective-permute-start | bytes 1179656 | tf_op jit(solution)/shard_map/ppermute | solution.py:10
  112.2 37.9 %all-to-all-start.2 = ((bf16[8,2,24,2048]{3,2,1,0:T(8,128)(2,1)}), bf16[8,2,24,2048]{3,2,1,0:T(8,128)(2,1)S(1)}, u32[]{:S(2)}, u32[]{:S(2)}) async-start(bf16[8,2,24,2048]{3,2,1,0:T(8,128)(2,1)} %bitcast.32), calls=%async_computation.2 | async-start | bytes 3145728 | tf_op jit(solution)/shard_map/all_to_all | solution.py:51
  115.8 2.8 %copy-start.2 = (bf16[2,2,1,1,192,2048]{5,4,3,2,1,0:T(8,128)(2,1)S(1)}, bf16[2,2,1,1,192,2048]{5,4,3,2,1,0:T(8,128)(2,1)}, u32[]{:S(2)}) copy-start(bf16[2,2,1,1,192,2048]{5,4,3,2,1,0:T(8,128)(2,1)} %param.12) | copy-start | bytes 9437188
  118.6 35.2 %copy-start.15 = (f32[192,512]{1,0:T(8,128)}, f32[192,512]{1,0:T(8,128)S(1)}, u32[]{:S(2)}) copy-start(f32[192,512]{1,0:T(8,128)S(1)} %fusion.21) | copy-start | bytes 1179652
  118.6 2.4 %copy-start.8 = (bf16[2,192,2048]{2,1,0:T(8,128)(2,1)S(1)}, bf16[2,192,2048]{2,1,0:T(8,128)(2,1)}, u32[]{:S(2)}) copy-start(bf16[2,192,2048]{2,1,0:T(8,128)(2,1)} %copy-done.7) | copy-start | bytes 4718596
  121.0 3.1 %copy-start.23 = (bf16[2,1,1,2048,512]{4,3,2,1,0:T(8,128)(2,1)S(1)}, bf16[2,1,1,2048,512]{4,3,2,1,0:T(8,128)(2,1)}, u32[]{:S(2)}) copy-start(bf16[2,1,1,2048,512]{4,3,2,1,0:T(8,128)(2,1)} %param.8) | copy-start | bytes 12582916
  151.1 3.2 %copy-start.3 = (bf16[8,1,24,2048]{3,2,1,0:T(8,128)(2,1)}, bf16[8,1,24,2048]{3,2,1,0:T(8,128)(2,1)S(1)}, u32[]{:S(2)}) copy-start(bf16[8,1,24,2048]{3,2,1,0:T(8,128)(2,1)S(1)} %get-tuple-element.22) | copy-start | bytes 2359300
  151.1 17.7 %collective-permute-start.4 = (bf16[192,2048]{1,0:T(8,128)(2,1)}, bf16[192,2048]{1,0:T(8,128)(2,1)}, u32[]{:S(2)}, u32[]{:S(2)}) collective-permute-start(bf16[192,2048]{1,0:T(8,128)(2,1)} %bitcast.37), channel_id=1, source_target_pairs={{0,24},{8,16},{16,8},{24,0},{1,25},{9,17},{17,9},{25,1},{2,26},{10... | collective-permute-start | bytes 2359304 | tf_op jit(solution)/shard_map/ppermute | solution.py:15
  152.0 2.4 %copy-start.24 = (bf16[2,1,1,2048,512]{4,3,2,1,0:T(8,128)(2,1)S(1)}, bf16[2,1,1,2048,512]{4,3,2,1,0:T(8,128)(2,1)}, u32[]{:S(2)}) copy-start(bf16[2,1,1,2048,512]{4,3,2,1,0:T(8,128)(2,1)} %param.8) | copy-start | bytes 12582916
  157.4 42.3 %all-to-all-start.3 = ((bf16[8,2,24,2048]{3,2,1,0:T(8,128)(2,1)}), bf16[8,2,24,2048]{3,2,1,0:T(8,128)(2,1)}, u32[]{:S(2)}, u32[]{:S(2)}) async-start(bf16[8,2,24,2048]{3,2,1,0:T(8,128)(2,1)} %pad_maximum_fusion.1), calls=%async_computation.3 | async-start | bytes 3145728 | tf_op jit(solution)/shard_map/all_to_all | solution.py:120
  161.9 1.9 copy-start.11
  161.9 1.9 copy-start.17
  165.7 3.1 %copy-start.19 = (f32[192,512]{1,0:T(8,128)S(1)}, f32[192,512]{1,0:T(8,128)}, u32[]{:S(2)}) copy-start(f32[192,512]{1,0:T(8,128)} %fusion.16) | copy-start | bytes 1179652
  165.7 3.1 %copy-start.27 = (bf16[2,1,1,256,2048]{4,3,2,1,0:T(8,128)(2,1)S(1)}, bf16[2,1,1,256,2048]{4,3,2,1,0:T(8,128)(2,1)}, u32[]{:S(2)}) copy-start(bf16[2,1,1,256,2048]{4,3,2,1,0:T(8,128)(2,1)} %param.9) | copy-start | bytes 6291460
  170.4 2.2 %copy-start = (f32[512,2048]{1,0:T(8,128)S(1)}, f32[512,2048]{1,0:T(8,128)}, u32[]{:S(2)}) copy-start(f32[512,2048]{1,0:T(8,128)} %fusion.61) | copy-start | bytes 12582916
  (6 other events, 9.2 us)

commit v15 on v14

--- a/solution.py
+++ b/solution.py
@@ -49,7 +49,7 @@
 def exchange(blocks):
     experts, ways, capacity, model_width = blocks.shape
     arrived = lax.all_to_all(blocks, "expert", split_axis=0, concat_axis=0, tiled=True)
-    return [arrived[:, way_id].reshape(experts * capacity, model_width) for way_id in range(ways)]
+    return arrived, [arrived[:, way_id].reshape(experts * capacity, model_width) for way_id in range(ways)]
 
 
 def expert_grads(slope_rows, saved_rows, weight_in, weight_out):
@@ -100,7 +100,7 @@
             )
             mirror_in = mirror_in + part_in
             mirror_out = mirror_out + part_out
-        slopes = exchange(blocks)
+        arrived, slopes = exchange(blocks)
         input_grads = []
         for way_id in range(2):
             saved_rows = saved[tick_id, way_id, 0, 0]
@@ -113,8 +113,9 @@
                 part_in, part_out = weight_terms(saved_rows, slopes[0], hidden, pair_grad)
                 own_in = own_in + part_in
                 own_out = own_out + part_out
-        slope_mirror = mirrored(slopes[1], "section")
         back_blocks = jnp.concatenate(input_grads, axis=1)
+        back_blocks, arrived = lax.optimization_barrier((back_blocks, arrived))
+        slope_mirror = mirrored(arrived[:, 1].reshape(experts * capacity, model_width), "section")
         if tick_id == 0:
             back_blocks, saved_mirror = lax.optimization_barrier((back_blocks, saved_mirror))
         returned = lax.all_to_all(back_blocks, "expert", split_axis=0, concat_axis=0, tiled=True)

time: 204 us -> 204 us (level)
  local copies, waits for them, and re-layouts: 16.8 us -> 20.8 us
  matrix products: 44.1 us -> 41.2 us
    all_to_all x2, waiting for transfers between devices: 31.1 us -> 18.9 us  [on_device(): lax.all_to_all(back_blocks, 'expert', split_axis=0, concat_axis=0, tiled=...]
    ppermute x3, waiting for transfers between devices: 20.8 us -> 32.5 us  [mirrored(): return lax.ppermute(block, axis, [(i, count - 1 - i) for i in range(count)])]
    unnamed x59, local copies, waits for them, and re-layouts: 11 us -> 14.8 us
    dot_general x10, matrix products: 10.2 us -> 6.43 us  [right_product(): lax.dot_general(left, right, (((1,), (1,)), ((), ())), preferred_element_...]
  transfers between devices with their start and end apart: 9 -> 9, of which waited for: 8 -> 8; matrix products, arithmetic and copies ran while one was open for 23% -> 20% of each run, Pallas kernels for 0% -> 0%
where the time goes in v15:
time: 204 us; the launch traced here: 203 us
  waiting for transfers between devices  105 us (51%)
  matrix products  41.2 us (20%)
  starting transfers between devices  30.3 us (15%)
  local copies, waits for them, and re-layouts  20.8 us (10%)
  other arithmetic  4.89 us (2%)
    all_to_all x2, waiting for transfers between devices, exchange(): lax.all_to_all(blocks, 'expert', split_axis=0, concat_axis=0, tiled=True)  48.9 us
    ppermute x3, waiting for transfers between devices, mirrored(): return lax.ppermute(block, axis, [(i, count - 1 - i) for i in range(count)])  32.5 us
    all_to_all x2, waiting for transfers between devices, on_device(): lax.all_to_all(back_blocks, 'expert', split_axis=0, concat_axis=0, tiled=...  18.9 us
    unnamed x59, local copies, waits for them, and re-layouts  14.8 us
    dot_general x6, matrix products, expert_grads(): gate_up = jnp.dot(saved_rows, weight_in, preferred_element_type=jnp.float32)  13.6 us
    dot_general x8, matrix products, left_product(): lax.dot_general(left, right, (((0,), (0,)), ((), ())), preferred_element_...  13 us
    all_to_all x2, starting transfers between devices, exchange(): lax.all_to_all(blocks, 'expert', split_axis=0, concat_axis=0, tiled=True)  9.95 us
    all_to_all x2, starting transfers between devices, on_device(): lax.all_to_all(back_blocks, 'expert', split_axis=0, concat_axis=0, tiled=...  9.11 us
  transfers between devices with their start and end apart: 9, of which 8 were waited for; matrix products, arithmetic and copies ran while one was open for 20% of the time, Pallas kernels for 0%

profile of v15, /device:TPU:1, one launch (start us, length us, event | category | flops | bytes accessed | tf_op | source)
XLA Modules:
  0.0 203.1 jit_solution(5197952513933086380)
XLA Ops:
  4.1 1.7 convolution_convert_fusion.1
  5.8 6.4 %all-to-all-start = ((bf16[8,2,24,2048]{3,2,1,0:T(8,128)(2,1)}), bf16[8,2,24,2048]{3,2,1,0:T(8,128)(2,1)S(1)}, u32[]{:S(2)}, u32[]{:S(2)}) async-start(bf16[8,2,24,2048]{3,2,1,0:T(8,128)(2,1)} %bitcast.7), calls=%async_computation | async-start | bytes 3145728 | tf_op jit(solution)/shard_map/all_to_all | solution.py:51
  12.2 2.9 %slice_bitcast_fusion = bf16[2,192,2048]{2,1,0:T(8,128)(2,1)} fusion(bf16[2,2,1,1,192,2048]{5,4,3,2,1,0:T(8,128)(2,1)} %param.12), kind=kLoop, calls=%fused_computation.44 | loop fusion | bytes 3145728 | tf_op jit(solution)/shard_map/squeeze | solution.py:82
  15.1 2.1 %collective-permute-start = (bf16[2,192,2048]{2,1,0:T(8,128)(2,1)}, bf16[2,192,2048]{2,1,0:T(8,128)(2,1)S(1)}, u32[]{:S(2)}, u32[]{:S(2)}) collective-permute-start(bf16[2,192,2048]{2,1,0:T(8,128)(2,1)} %slice_bitcast_fusion), channel_id=1, source_target_pairs={{0,24},{8,16},{16,8},{24,0},{1,25},{9,17},{17,9},{25,1},{2,26},{10... | collective-permute-start | bytes 4718600 | tf_op jit(solution)/shard_map/ppermute | solution.py:15
  17.2 2.9 %fusion.24 = f32[192,512]{1,0:T(8,128)} fusion(bf16[2,1,1,2048,512]{4,3,2,1,0:T(8,128)(2,1)} %param.8, bf16[2,2,1,1,192,2048]{5,4,3,2,1,0:T(8,128)(2,1)S(1)} %copy-done.1), kind=kOutput, calls=%fused_computation.36 | convolution fusion | flops 402653184 | bytes 3276800 | tf_op jit(solution)/shard_map/dot_general | solution.py:57
  21.5 26.9 %all-to-all-done = bf16[8,2,24,2048]{3,2,1,0:T(8,128)(2,1)S(1)} async-done(((bf16[8,2,24,2048]{3,2,1,0:T(8,128)(2,1)}), bf16[8,2,24,2048]{3,2,1,0:T(8,128)(2,1)S(1)}, u32[]{:S(2)}, u32[]{:S(2)}) %all-to-all-start) | async-done | bytes 1572896 | tf_op jit(solution)/shard_map/all_to_all | solution.py:51
  48.5 1.7 copy-done.25
  56.7 4.6 %all-to-all-start.1 = ((bf16[8,2,24,2048]{3,2,1,0:T(8,128)(2,1)}), bf16[8,2,24,2048]{3,2,1,0:T(8,128)(2,1)S(1)}, u32[]{:S(2)}, u32[]{:S(2)}) async-start(bf16[8,2,24,2048]{3,2,1,0:T(8,128)(2,1)} %pad_maximum_fusion), calls=%async_computation.1 | async-start | bytes 3145728 | tf_op jit(solution)/shard_map/all_to_all | solution.py:121
  62.3 1.9 collective-permute-start.1
  64.2 18.5 %collective-permute-done.1 = bf16[192,2048]{1,0:T(8,128)(2,1)S(1)} collective-permute-done((bf16[192,2048]{1,0:T(8,128)(2,1)}, bf16[192,2048]{1,0:T(8,128)(2,1)S(1)}, u32[]{:S(2)}, u32[]{:S(2)}) %collective-permute-start.1) | collective-permute-done | bytes 786464 | tf_op jit(solution)/shard_map/ppermute | solution.py:15
  82.7 15.0 %all-to-all-done.1 = bf16[8,2,24,2048]{3,2,1,0:T(8,128)(2,1)S(1)} async-done(((bf16[8,2,24,2048]{3,2,1,0:T(8,128)(2,1)}), bf16[8,2,24,2048]{3,2,1,0:T(8,128)(2,1)S(1)}, u32[]{:S(2)}, u32[]{:S(2)}) %all-to-all-start.1) | async-done | bytes 1572896 | tf_op jit(solution)/shard_map/all_to_all | solution.py:121
  97.7 1.8 fusion.6
  99.6 3.5 %collective-permute-start.2 = (bf16[96,2048]{1,0:T(8,128)(2,1)S(1)}, bf16[96,2048]{1,0:T(8,128)(2,1)S(1)}, u32[]{:S(2)}, u32[]{:S(2)}) collective-permute-start(bf16[96,2048]{1,0:T(8,128)(2,1)S(1)} %get-tuple-element.36), channel_id=1, source_target_pairs={{8,0},{16,8},{24,16},{9,1},{17,9},{25,17},{10,2},{18,10},{26,18},{... | collective-permute-start | bytes 1179656 | tf_op jit(solution)/shard_map/ppermute | solution.py:10
  103.1 3.0 %collective-permute-start.3 = (bf16[96,2048]{1,0:T(8,128)(2,1)S(1)}, bf16[96,2048]{1,0:T(8,128)(2,1)S(1)}, u32[]{:S(2)}, u32[]{:S(2)}) collective-permute-start(bf16[96,2048]{1,0:T(8,128)(2,1)S(1)} %get-tuple-element.37), channel_id=1, source_target_pairs={{0,8},{8,16},{16,24},{1,9},{9,17},{17,25},{2,10},{10,18},{18,26},{... | collective-permute-start | bytes 1179656 | tf_op jit(solution)/shard_map/ppermute | solution.py:10
  106.3 3.4 %collective-permute-done.2 = bf16[96,2048]{1,0:T(8,128)(2,1)S(1)} collective-permute-done((bf16[96,2048]{1,0:T(8,128)(2,1)S(1)}, bf16[96,2048]{1,0:T(8,128)(2,1)S(1)}, u32[]{:S(2)}, u32[]{:S(2)}) %collective-permute-start.2) | collective-permute-done | bytes 393248 | tf_op jit(solution)/shard_map/ppermute | solution.py:10
  111.2 1.7 convolution_convert_fusion
  112.9 3.6 %all-to-all-start.2 = ((bf16[8,2,24,2048]{3,2,1,0:T(8,128)(2,1)}), bf16[8,2,24,2048]{3,2,1,0:T(8,128)(2,1)S(1)}, u32[]{:S(2)}, u32[]{:S(2)}) async-start(bf16[8,2,24,2048]{3,2,1,0:T(8,128)(2,1)} %bitcast.33), calls=%async_computation.2 | async-start | bytes 3145728 | tf_op jit(solution)/shard_map/all_to_all | solution.py:51
  116.6 2.5 %fusion.21 = f32[192,512]{1,0:T(8,128)S(1)} fusion(bf16[2,1,1,2048,512]{4,3,2,1,0:T(8,128)(2,1)} %param.8, bf16[2,2,1,1,192,2048]{5,4,3,2,1,0:T(8,128)(2,1)} %param.12), kind=kOutput, calls=%fused_computation.33 | convolution fusion | flops 402653184 | bytes 3276800 | tf_op jit(solution)/shard_map/dot_general | solution.py:57
  119.4 2.3 %fusion.11 = f32[192,512]{1,0:T(8,128)S(1)} fusion(bf16[2,1,1,2048,512]{4,3,2,1,0:T(8,128)(2,1)} %param.8, bf16[2,2,1,1,192,2048]{5,4,3,2,1,0:T(8,128)(2,1)S(1)} %copy-done.2), kind=kOutput, calls=%fused_computation.23 | convolution fusion | flops 402653184 | bytes 3276800 | tf_op jit(solution)/shard_map/dot_general | solution.py:57
  121.7 3.1 %fusion.16 = f32[192,512]{1,0:T(8,128)} fusion(bf16[2,1,1,2048,512]{4,3,2,1,0:T(8,128)(2,1)} %param.8, bf16[2,192,2048]{2,1,0:T(8,128)(2,1)S(1)} %copy-done.8), kind=kOutput, calls=%fused_computation.28 | convolution fusion | flops 402653184 | bytes 3276800 | tf_op jit(solution)/shard_map/dot_general | solution.py:57
  126.2 2.7 %fusion.61 = f32[512,2048]{1,0:T(8,128)} fusion(bf16[2,2,1,1,192,2048]{5,4,3,2,1,0:T(8,128)(2,1)S(1)} %copy-done.2, bf16[192,256]{1,0:T(8,128)(2,1)S(1)} %get-tuple-element.47, bf16[192,256]{1,0:T(8,128)(2,1)S(1)} %get-tuple-element.46), kind=kOutput, calls=%fused_computation.79 | convolution fusion | flops 403046400 | bytes 5177344 | tf_op jit(solution)/shard_map/dot_general | solution.py:19
  128.9 22.0 %all-to-all-done.2 = bf16[8,2,24,2048]{3,2,1,0:T(8,128)(2,1)S(1)} async-done(((bf16[8,2,24,2048]{3,2,1,0:T(8,128)(2,1)}), bf16[8,2,24,2048]{3,2,1,0:T(8,128)(2,1)S(1)}, u32[]{:S(2)}, u32[]{:S(2)}) %all-to-all-start.2) | async-done | bytes 1572896 | tf_op jit(solution)/shard_map/all_to_all | solution.py:51
  151.0 1.8 copy-done.26
  157.9 4.5 %all-to-all-start.3 = ((bf16[8,2,24,2048]{3,2,1,0:T(8,128)(2,1)}), bf16[8,2,24,2048]{3,2,1,0:T(8,128)(2,1)}, u32[]{:S(2)}, u32[]{:S(2)}) async-start(bf16[8,2,24,2048]{3,2,1,0:T(8,128)(2,1)} %pad_maximum_fusion.1), calls=%async_computation.3 | async-start | bytes 3145728 | tf_op jit(solution)/shard_map/all_to_all | solution.py:121
  163.6 1.6 fusion.110
  167.3 14.0 %collective-permute-done.4 = bf16[192,2048]{1,0:T(8,128)(2,1)S(1)} collective-permute-done((bf16[192,2048]{1,0:T(8,128)(2,1)S(1)}, bf16[192,2048]{1,0:T(8,128)(2,1)S(1)}, u32[]{:S(2)}, u32[]{:S(2)}) %collective-permute-start.4) | collective-permute-done | bytes 786464 | tf_op jit(solution)/shard_map/ppermute | solution.py:15
  184.4 3.3 %fusion.1 = bf16[1,1,2048,512]{2,3,1,0:T(8,128)(2,1)} fusion(bf16[2048,512]{0,1:T(8,128)(2,1)S(1)} %add_convert_fusion, f32[512,2048]{1,0:T(8,128)S(1)} %copy-done, bf16[2,2,1,1,192,2048]{5,4,3,2,1,0:T(8,128)(2,1)} %param.12, bf16[192,256]{1,0:T(8,128)(2,1)S(1)} %get-tuple-element.43, bf16[192,256]{1,0:T(8,128)(2,1)S(1)} %get-tuple-element.42), kind=kOutput, calls=%fused_computation.5 | convolution fusion | flops 407240704 | bytes 9371648 | tf_op jit(solution)/shard_map/dot_general | solution.py:19
  187.7 3.9 %copy.34 = bf16[1,1,2048,512]{3,2,1,0:T(8,128)(2,1)} copy(bf16[1,1,2048,512]{2,3,1,0:T(8,128)(2,1)} %fusion.1) | data formatting | bytes 4194304
  191.6 1.9 fusion.111
  194.7 1.5 fusion.8
  196.2 3.9 %all-to-all-done.3 = bf16[8,2,24,2048]{3,2,1,0:T(8,128)(2,1)} async-done(((bf16[8,2,24,2048]{3,2,1,0:T(8,128)(2,1)}), bf16[8,2,24,2048]{3,2,1,0:T(8,128)(2,1)}, u32[]{:S(2)}, u32[]{:S(2)}) %all-to-all-start.3) | async-done | bytes 1572896 | tf_op jit(solution)/shard_map/all_to_all | solution.py:121
  200.2 2.9 %fusion.9 = bf16[2,1,96,2048]{3,2,1,0:T(8,128)(2,1)} fusion(bf16[384,2048,1]{1,0,2:T(8,128)(2,1)} %bitcast.43, s32[2,96]{1,0:T(2,128)S(1)} %eq.168, bf16[1,96,2048]{2,1,0:T(8,128)(2,1)S(1)} %get-tuple-element.35, bf16[1,96,2048]{2,1,0:T(8,128)(2,1)S(1)} %get-tuple-element.34), kind=kOutput, calls=%fused_computation.21 | convolution fusion | flops 303636480 | bytes 3146496 | tf_op jit(solution)/shard_map/dot_general | solution.py:124
  (97 shorter events, 28.4 us)
Async XLA Ops:
  0.6 3.2 %copy-start.20 = (s32[2,2,1,96]{3,2,1,0:T(1,128)S(1)}, s32[2,2,1,96]{3,2,1,0:T(1,128)}, u32[]{:S(2)}) copy-start(s32[2,2,1,96]{3,2,1,0:T(1,128)} %param.14) | copy-start | bytes 4612
  5.8 42.6 %all-to-all-start = ((bf16[8,2,24,2048]{3,2,1,0:T(8,128)(2,1)}), bf16[8,2,24,2048]{3,2,1,0:T(8,128)(2,1)S(1)}, u32[]{:S(2)}, u32[]{:S(2)}) async-start(bf16[8,2,24,2048]{3,2,1,0:T(8,128)(2,1)} %bitcast.7), calls=%async_computation | async-start | bytes 3145728 | tf_op jit(solution)/shard_map/all_to_all | solution.py:51
  12.2 5.0 %copy-start.1 = (bf16[2,2,1,1,192,2048]{5,4,3,2,1,0:T(8,128)(2,1)S(1)}, bf16[2,2,1,1,192,2048]{5,4,3,2,1,0:T(8,128)(2,1)}, u32[]{:S(2)}) copy-start(bf16[2,2,1,1,192,2048]{5,4,3,2,1,0:T(8,128)(2,1)} %param.12) | copy-start | bytes 9437188
  15.1 5.0 %copy-start.21 = (bf16[2,1,1,2048,512]{4,3,2,1,0:T(8,128)(2,1)S(1)}, bf16[2,1,1,2048,512]{4,3,2,1,0:T(8,128)(2,1)}, u32[]{:S(2)}) copy-start(bf16[2,1,1,2048,512]{4,3,2,1,0:T(8,128)(2,1)} %param.8) | copy-start | bytes 12582916
  15.1 40.4 %collective-permute-start = (bf16[2,192,2048]{2,1,0:T(8,128)(2,1)}, bf16[2,192,2048]{2,1,0:T(8,128)(2,1)S(1)}, u32[]{:S(2)}, u32[]{:S(2)}) collective-permute-start(bf16[2,192,2048]{2,1,0:T(8,128)(2,1)} %slice_bitcast_fusion), channel_id=1, source_target_pairs={{0,24},{8,16},{16,8},{24,0},{1,25},{9,17},{17,9},{25,1},{2,26},{10... | collective-permute-start | bytes 4718600 | tf_op jit(solution)/shard_map/ppermute | solution.py:15
  48.4 1.9 copy-start.25
  48.4 1.9 copy-start.28
  48.5 2.8 %copy-start.5 = (bf16[8,1,24,2048]{3,2,1,0:T(8,128)(2,1)}, bf16[8,1,24,2048]{3,2,1,0:T(8,128)(2,1)S(1)}, u32[]{:S(2)}) copy-start(bf16[8,1,24,2048]{3,2,1,0:T(8,128)(2,1)S(1)} %get-tuple-element.32) | copy-start | bytes 2359300
  48.5 2.3 %copy-start.18 = (f32[192,512]{1,0:T(8,128)S(1)}, f32[192,512]{1,0:T(8,128)}, u32[]{:S(2)}) copy-start(f32[192,512]{1,0:T(8,128)} %fusion.24) | copy-start | bytes 1179652
  50.3 2.2 %copy-start.22 = (bf16[2,1,1,2048,512]{4,3,2,1,0:T(8,128)(2,1)S(1)}, bf16[2,1,1,2048,512]{4,3,2,1,0:T(8,128)(2,1)}, u32[]{:S(2)}) copy-start(bf16[2,1,1,2048,512]{4,3,2,1,0:T(8,128)(2,1)} %param.8) | copy-start | bytes 12582916
  56.7 41.0 %all-to-all-start.1 = ((bf16[8,2,24,2048]{3,2,1,0:T(8,128)(2,1)}), bf16[8,2,24,2048]{3,2,1,0:T(8,128)(2,1)S(1)}, u32[]{:S(2)}, u32[]{:S(2)}) async-start(bf16[8,2,24,2048]{3,2,1,0:T(8,128)(2,1)} %pad_maximum_fusion), calls=%async_computation.1 | async-start | bytes 3145728 | tf_op jit(solution)/shard_map/all_to_all | solution.py:121
  62.3 20.4 %collective-permute-start.1 = (bf16[192,2048]{1,0:T(8,128)(2,1)}, bf16[192,2048]{1,0:T(8,128)(2,1)S(1)}, u32[]{:S(2)}, u32[]{:S(2)}) collective-permute-start(bf16[192,2048]{1,0:T(8,128)(2,1)} %bitcast.21), channel_id=1, source_target_pairs={{0,24},{8,16},{16,8},{24,0},{1,25},{9,17},{17,9},{25,1},{2,26},{10... | collective-permute-start | bytes 2359304 | tf_op jit(solution)/shard_map/ppermute | solution.py:15
  82.7 16.9 %copy-start.10 = (bf16[192,2048]{1,0:T(8,128)(2,1)}, bf16[192,2048]{1,0:T(8,128)(2,1)S(1)}, u32[]{:S(2)}) copy-start(bf16[192,2048]{1,0:T(8,128)(2,1)S(1)} %collective-permute-done.1) | copy-start | bytes 2359300
  97.7 13.2 %copy-start.13 = (bf16[1,2,96,2048]{3,2,1,0:T(8,128)(2,1)S(1)}, bf16[1,2,96,2048]{3,2,1,0:T(8,128)(2,1)}, u32[]{:S(2)}) copy-start(bf16[1,2,96,2048]{3,2,1,0:T(8,128)(2,1)} %param.11) | copy-start | bytes 2359300
  99.6 10.1 %collective-permute-start.2 = (bf16[96,2048]{1,0:T(8,128)(2,1)S(1)}, bf16[96,2048]{1,0:T(8,128)(2,1)S(1)}, u32[]{:S(2)}, u32[]{:S(2)}) collective-permute-start(bf16[96,2048]{1,0:T(8,128)(2,1)S(1)} %get-tuple-element.36), channel_id=1, source_target_pairs={{8,0},{16,8},{24,16},{9,1},{17,9},{25,17},{10,2},{18,10},{26,18},{... | collective-permute-start | bytes 1179656 | tf_op jit(solution)/shard_map/ppermute | solution.py:10
  103.1 7.7 %collective-permute-start.3 = (bf16[96,2048]{1,0:T(8,128)(2,1)S(1)}, bf16[96,2048]{1,0:T(8,128)(2,1)S(1)}, u32[]{:S(2)}, u32[]{:S(2)}) collective-permute-start(bf16[96,2048]{1,0:T(8,128)(2,1)S(1)} %get-tuple-element.37), channel_id=1, source_target_pairs={{0,8},{8,16},{16,24},{1,9},{9,17},{17,25},{2,10},{10,18},{18,26},{... | collective-permute-start | bytes 1179656 | tf_op jit(solution)/shard_map/ppermute | solution.py:10
  112.9 37.9 %all-to-all-start.2 = ((bf16[8,2,24,2048]{3,2,1,0:T(8,128)(2,1)}), bf16[8,2,24,2048]{3,2,1,0:T(8,128)(2,1)S(1)}, u32[]{:S(2)}, u32[]{:S(2)}) async-start(bf16[8,2,24,2048]{3,2,1,0:T(8,128)(2,1)} %bitcast.33), calls=%async_computation.2 | async-start | bytes 3145728 | tf_op jit(solution)/shard_map/all_to_all | solution.py:51
  116.6 2.8 %copy-start.2 = (bf16[2,2,1,1,192,2048]{5,4,3,2,1,0:T(8,128)(2,1)S(1)}, bf16[2,2,1,1,192,2048]{5,4,3,2,1,0:T(8,128)(2,1)}, u32[]{:S(2)}) copy-start(bf16[2,2,1,1,192,2048]{5,4,3,2,1,0:T(8,128)(2,1)} %param.12) | copy-start | bytes 9437188
  119.4 33.9 %copy-start.15 = (f32[192,512]{1,0:T(8,128)}, f32[192,512]{1,0:T(8,128)S(1)}, u32[]{:S(2)}) copy-start(f32[192,512]{1,0:T(8,128)S(1)} %fusion.21) | copy-start | bytes 1179652
  119.4 2.4 %copy-start.8 = (bf16[2,192,2048]{2,1,0:T(8,128)(2,1)S(1)}, bf16[2,192,2048]{2,1,0:T(8,128)(2,1)}, u32[]{:S(2)}) copy-start(bf16[2,192,2048]{2,1,0:T(8,128)(2,1)} %copy-done.7) | copy-start | bytes 4718596
  121.7 3.1 %copy-start.23 = (bf16[2,1,1,2048,512]{4,3,2,1,0:T(8,128)(2,1)S(1)}, bf16[2,1,1,2048,512]{4,3,2,1,0:T(8,128)(2,1)}, u32[]{:S(2)}) copy-start(bf16[2,1,1,2048,512]{4,3,2,1,0:T(8,128)(2,1)} %param.8) | copy-start | bytes 12582916
  150.9 1.9 copy-start.26
  151.0 2.8 %copy-start.3 = (bf16[8,1,24,2048]{3,2,1,0:T(8,128)(2,1)}, bf16[8,1,24,2048]{3,2,1,0:T(8,128)(2,1)S(1)}, u32[]{:S(2)}) copy-start(bf16[8,1,24,2048]{3,2,1,0:T(8,128)(2,1)S(1)} %get-tuple-element.30) | copy-start | bytes 2359300
  152.8 2.2 %copy-start.24 = (bf16[2,1,1,2048,512]{4,3,2,1,0:T(8,128)(2,1)S(1)}, bf16[2,1,1,2048,512]{4,3,2,1,0:T(8,128)(2,1)}, u32[]{:S(2)}) copy-start(bf16[2,1,1,2048,512]{4,3,2,1,0:T(8,128)(2,1)} %param.8) | copy-start | bytes 12582916
  157.9 42.3 %all-to-all-start.3 = ((bf16[8,2,24,2048]{3,2,1,0:T(8,128)(2,1)}), bf16[8,2,24,2048]{3,2,1,0:T(8,128)(2,1)}, u32[]{:S(2)}, u32[]{:S(2)}) async-start(bf16[8,2,24,2048]{3,2,1,0:T(8,128)(2,1)} %pad_maximum_fusion.1), calls=%async_computation.3 | async-start | bytes 3145728 | tf_op jit(solution)/shard_map/all_to_all | solution.py:121
  162.4 2.7 %copy-start.11 = (bf16[192,2048]{1,0:T(8,128)(2,1)S(1)}, bf16[192,2048]{1,0:T(8,128)(2,1)}, u32[]{:S(2)}) copy-start(bf16[192,2048]{1,0:T(8,128)(2,1)} %copy-done.10) | copy-start | bytes 2359300
  162.4 2.7 %copy-start.17 = (f32[192,512]{1,0:T(8,128)S(1)}, f32[192,512]{1,0:T(8,128)}, u32[]{:S(2)}) copy-start(f32[192,512]{1,0:T(8,128)} %fusion.18) | copy-start | bytes 1179652
  162.4 2.7 %copy-start.27 = (bf16[2,1,1,256,2048]{4,3,2,1,0:T(8,128)(2,1)S(1)}, bf16[2,1,1,256,2048]{4,3,2,1,0:T(8,128)(2,1)}, u32[]{:S(2)}) copy-start(bf16[2,1,1,256,2048]{4,3,2,1,0:T(8,128)(2,1)} %param.9) | copy-start | bytes 6291460
  162.5 18.8 %collective-permute-start.4 = (bf16[192,2048]{1,0:T(8,128)(2,1)S(1)}, bf16[192,2048]{1,0:T(8,128)(2,1)S(1)}, u32[]{:S(2)}, u32[]{:S(2)}) collective-permute-start(bf16[192,2048]{1,0:T(8,128)(2,1)S(1)} %bitcast.187), channel_id=1, source_target_pairs={{0,24},{8,16},{16,8},{24,0},{1,25},{9,17},{17,9},{25,1},{2,26},{10... | collective-permute-start | bytes 2359304 | tf_op jit(solution)/shard_map/ppermute | solution.py:15
  166.6 14.7 %copy-start.19 = (f32[192,512]{1,0:T(8,128)S(1)}, f32[192,512]{1,0:T(8,128)}, u32[]{:S(2)}) copy-start(f32[192,512]{1,0:T(8,128)} %fusion.16) | copy-start | bytes 1179652
  182.2 2.2 %copy-start = (f32[512,2048]{1,0:T(8,128)S(1)}, f32[512,2048]{1,0:T(8,128)}, u32[]{:S(2)}) copy-start(f32[512,2048]{1,0:T(8,128)} %fusion.61) | copy-start | bytes 12582916
  191.6 1.9 copy-start.12
  (6 other events, 7.0 us)

commit v16 on v14

--- a/solution.py
+++ b/solution.py
@@ -79,7 +79,7 @@
     capacity = 2 * tokens // experts
     hidden_width = w_out.shape[-2]
     ticks = saved.shape[0]
-    saved_mirror = mirrored(saved[:, 1, 0, 0], "section")
+    saved_mirror = [mirrored(saved[tick_id, 1, 0, 0], "section") for tick_id in range(saved.shape[0])]
     current = grads[:, 0]
     zeros_in = jnp.zeros((model_width, 2 * hidden_width), jnp.float32)
     zeros_out = jnp.zeros((hidden_width, model_width), jnp.float32)
@@ -116,10 +116,12 @@
         slope_mirror = mirrored(slopes[1], "section")
         back_blocks = jnp.concatenate(input_grads, axis=1)
         if tick_id == 0:
-            back_blocks, saved_mirror = lax.optimization_barrier((back_blocks, saved_mirror))
+            back_blocks, saved_mirror[0] = lax.optimization_barrier((back_blocks, saved_mirror[0]))
         returned = lax.all_to_all(back_blocks, "expert", split_axis=0, concat_axis=0, tiled=True)
         if tick_id + 1 < ticks:
-            returned, slope_mirror = lax.optimization_barrier((returned, slope_mirror))
+            returned, slope_mirror, saved_mirror[tick_id + 1] = lax.optimization_barrier(
+                (returned, slope_mirror, saved_mirror[tick_id + 1])
+            )
         back_rows = jnp.dot(one_hot_back, returned.reshape(-1, model_width), preferred_element_type=jnp.float32)
         finished = (current.astype(jnp.float32) + back_rows.reshape(2, tokens, model_width)).astype(
             jnp.bfloat16

time: 204 us -> 207 us (1.015)
  matrix products: 44.1 us -> 46.2 us
    ppermute x3 -> x4, waiting for transfers between devices: 20.8 us -> 38.4 us  [mirrored(): return lax.ppermute(block, axis, [(i, count - 1 - i) for i in range(count)])]
    all_to_all x2, waiting for transfers between devices: 31.1 us -> 15 us  [on_device(): lax.all_to_all(back_blocks, 'expert', split_axis=0, concat_axis=0, tiled=...]
    unnamed x59 -> x61, local copies, waits for them, and re-layouts: 11 us -> 8.15 us
    dot_general x10, matrix products: 10.2 us -> 12.5 us  [right_product(): lax.dot_general(left, right, (((1,), (1,)), ((), ())), preferred_element_...]
    ppermute x3 -> x4, starting transfers between devices: 4.69 us -> 4.42 us  [mirrored(): return lax.ppermute(block, axis, [(i, count - 1 - i) for i in range(count)])]
  transfers between devices with their start and end apart: 9 -> 10, of which waited for: 8 -> 8; matrix products, arithmetic and copies ran while one was open for 23% -> 24% of each run, Pallas kernels for 0% -> 0%
where the time goes in v16:
time: 207 us; the launch traced here: 205 us
  waiting for transfers between devices  107 us (52%)
  matrix products  46.2 us (22%)
  starting transfers between devices  31.4 us (15%)
  local copies, waits for them, and re-layouts  15.2 us (7%)
  other arithmetic  4.91 us (2%)
    all_to_all x2, waiting for transfers between devices, exchange(): lax.all_to_all(blocks, 'expert', split_axis=0, concat_axis=0, tiled=True)  48.7 us
    ppermute x4, waiting for transfers between devices, mirrored(): return lax.ppermute(block, axis, [(i, count - 1 - i) for i in range(count)])  38.4 us
    all_to_all x2, waiting for transfers between devices, on_device(): lax.all_to_all(back_blocks, 'expert', split_axis=0, concat_axis=0, tiled=...  15 us
    dot_general x8, matrix products, left_product(): lax.dot_general(left, right, (((0,), (0,)), ((), ())), preferred_element_...  13.4 us
    dot_general x6, matrix products, expert_grads(): gate_up = jnp.dot(saved_rows, weight_in, preferred_element_type=jnp.float32)  13.3 us
    dot_general x10, matrix products, right_product(): lax.dot_general(left, right, (((1,), (1,)), ((), ())), preferred_element_...  12.5 us
    all_to_all x2, starting transfers between devices, exchange(): lax.all_to_all(blocks, 'expert', split_axis=0, concat_axis=0, tiled=True)  12 us
    all_to_all x2, starting transfers between devices, on_device(): lax.all_to_all(back_blocks, 'expert', split_axis=0, concat_axis=0, tiled=...  9.26 us
  transfers between devices with their start and end apart: 10, of which 8 were waited for; matrix products, arithmetic and copies ran while one was open for 24% of the time, Pallas kernels for 0%

profile of v16, /device:TPU:1, one launch (start us, length us, event | category | flops | bytes accessed | tf_op | source)
XLA Modules:
  0.0 205.5 jit_solution(10442838776457781821)
XLA Ops:
  4.1 1.7 convolution_convert_fusion.1
  5.8 6.4 %all-to-all-start = ((bf16[8,2,24,2048]{3,2,1,0:T(8,128)(2,1)}), bf16[8,2,24,2048]{3,2,1,0:T(8,128)(2,1)S(1)}, u32[]{:S(2)}, u32[]{:S(2)}) async-start(bf16[8,2,24,2048]{3,2,1,0:T(8,128)(2,1)} %bitcast.7), calls=%async_computation | async-start | bytes 3145728 | tf_op jit(solution)/shard_map/all_to_all | solution.py:51
  12.2 2.5 %slice_bitcast_fusion = (bf16[192,2048]{1,0:T(8,128)(2,1)}, bf16[192,2048]{1,0:T(8,128)(2,1)S(1)}) fusion(bf16[2,2,1,1,192,2048]{5,4,3,2,1,0:T(8,128)(2,1)} %param.12), kind=kLoop, calls=%fused_computation.76 | loop fusion | bytes 3145728 | tf_op jit(solution)/shard_map/squeeze | solution.py:82
  14.7 2.1 %collective-permute-start = (bf16[192,2048]{1,0:T(8,128)(2,1)S(1)}, bf16[192,2048]{1,0:T(8,128)(2,1)S(1)}, u32[]{:S(2)}, u32[]{:S(2)}) collective-permute-start(bf16[192,2048]{1,0:T(8,128)(2,1)S(1)} %get-tuple-element.25), channel_id=1, source_target_pairs={{0,24},{8,16},{16,8},{24,0},{1,25},{9,17},{17,9},{25,1},{2,26},{10... | collective-permute-start | bytes 2359304 | tf_op jit(solution)/shard_map/ppermute | solution.py:15
  16.8 2.9 %fusion.24 = f32[192,512]{1,0:T(8,128)} fusion(bf16[2,1,1,2048,512]{4,3,2,1,0:T(8,128)(2,1)} %param.8, bf16[2,2,1,1,192,2048]{5,4,3,2,1,0:T(8,128)(2,1)S(1)} %copy-done.1), kind=kOutput, calls=%fused_computation.36 | convolution fusion | flops 402653184 | bytes 3276800 | tf_op jit(solution)/shard_map/dot_general | solution.py:57
  21.1 27.3 %all-to-all-done = bf16[8,2,24,2048]{3,2,1,0:T(8,128)(2,1)S(1)} async-done(((bf16[8,2,24,2048]{3,2,1,0:T(8,128)(2,1)}), bf16[8,2,24,2048]{3,2,1,0:T(8,128)(2,1)S(1)}, u32[]{:S(2)}, u32[]{:S(2)}) %all-to-all-start) | async-done | bytes 1572896 | tf_op jit(solution)/shard_map/all_to_all | solution.py:51
  49.4 2.6 %fusion.77 = (bf16[192,256]{1,0:T(8,128)(2,1)S(1)}, bf16[192,256]{1,0:T(8,128)(2,1)S(1)}) fusion(f32[192,512]{1,0:T(8,128)} %fusion.14, bf16[192,2048]{1,0:T(8,128)(2,1)S(1)} %bitcast.177, bf16[2,1,1,256,2048]{4,3,2,1,0:T(8,128)(2,1)} %param.9), kind=kOutput, calls=%fused_computation.105 | convolution fusion | flops 201965568 | bytes 2424832 | tf_op jit(solution)/shard_map/dot_general | solution.py:25
  56.5 4.8 %all-to-all-start.1 = ((bf16[8,2,24,2048]{3,2,1,0:T(8,128)(2,1)}), bf16[8,2,24,2048]{3,2,1,0:T(8,128)(2,1)S(1)}, u32[]{:S(2)}, u32[]{:S(2)}) async-start(bf16[8,2,24,2048]{3,2,1,0:T(8,128)(2,1)} %pad_maximum_fusion), calls=%async_computation.1 | async-start | bytes 3145728 | tf_op jit(solution)/shard_map/all_to_all | solution.py:120
  61.2 1.9 collective-permute-start.2
  63.3 18.5 %collective-permute-done.2 = bf16[192,2048]{1,0:T(8,128)(2,1)S(1)} collective-permute-done((bf16[192,2048]{1,0:T(8,128)(2,1)}, bf16[192,2048]{1,0:T(8,128)(2,1)S(1)}, u32[]{:S(2)}, u32[]{:S(2)}) %collective-permute-start.2) | collective-permute-done | bytes 786464 | tf_op jit(solution)/shard_map/ppermute | solution.py:15
  81.9 16.8 %collective-permute-done.1 = bf16[192,2048]{1,0:T(8,128)(2,1)} collective-permute-done((bf16[192,2048]{1,0:T(8,128)(2,1)}, bf16[192,2048]{1,0:T(8,128)(2,1)}, u32[]{:S(2)}, u32[]{:S(2)}) %collective-permute-start.1) | collective-permute-done | bytes 786464 | tf_op jit(solution)/shard_map/ppermute | solution.py:15
  99.4 2.6 %collective-permute-start.3 = (bf16[96,2048]{1,0:T(8,128)(2,1)S(1)}, bf16[96,2048]{1,0:T(8,128)(2,1)S(1)}, u32[]{:S(2)}, u32[]{:S(2)}) collective-permute-start(bf16[96,2048]{1,0:T(8,128)(2,1)S(1)} %get-tuple-element.32), channel_id=1, source_target_pairs={{8,0},{16,8},{24,16},{9,1},{17,9},{25,17},{10,2},{18,10},{26,18},{... | collective-permute-start | bytes 1179656 | tf_op jit(solution)/shard_map/ppermute | solution.py:10
  102.0 3.1 %collective-permute-start.4 = (bf16[96,2048]{1,0:T(8,128)(2,1)S(1)}, bf16[96,2048]{1,0:T(8,128)(2,1)S(1)}, u32[]{:S(2)}, u32[]{:S(2)}) collective-permute-start(bf16[96,2048]{1,0:T(8,128)(2,1)S(1)} %get-tuple-element.33), channel_id=1, source_target_pairs={{0,8},{8,16},{16,24},{1,9},{9,17},{17,25},{2,10},{10,18},{18,26},{... | collective-permute-start | bytes 1179656 | tf_op jit(solution)/shard_map/ppermute | solution.py:10
  105.2 3.4 %collective-permute-done.3 = bf16[96,2048]{1,0:T(8,128)(2,1)S(1)} collective-permute-done((bf16[96,2048]{1,0:T(8,128)(2,1)S(1)}, bf16[96,2048]{1,0:T(8,128)(2,1)S(1)}, u32[]{:S(2)}, u32[]{:S(2)}) %collective-permute-start.3) | collective-permute-done | bytes 393248 | tf_op jit(solution)/shard_map/ppermute | solution.py:10
  110.1 1.7 convolution_convert_fusion
  111.9 5.6 %all-to-all-start.2 = ((bf16[8,2,24,2048]{3,2,1,0:T(8,128)(2,1)}), bf16[8,2,24,2048]{3,2,1,0:T(8,128)(2,1)}, u32[]{:S(2)}, u32[]{:S(2)}) async-start(bf16[8,2,24,2048]{3,2,1,0:T(8,128)(2,1)} %bitcast.32), calls=%async_computation.2 | async-start | bytes 3145728 | tf_op jit(solution)/shard_map/all_to_all | solution.py:51
  117.6 3.3 %fusion.21 = f32[192,512]{1,0:T(8,128)} fusion(bf16[2,1,1,2048,512]{4,3,2,1,0:T(8,128)(2,1)} %param.8, bf16[2,2,1,1,192,2048]{5,4,3,2,1,0:T(8,128)(2,1)} %param.12), kind=kOutput, calls=%fused_computation.33 | convolution fusion | flops 402653184 | bytes 3276800 | tf_op jit(solution)/shard_map/dot_general | solution.py:57
  120.9 3.1 %fusion.11 = f32[192,512]{1,0:T(8,128)} fusion(bf16[2,1,1,2048,512]{4,3,2,1,0:T(8,128)(2,1)} %param.8, bf16[2,2,1,1,192,2048]{5,4,3,2,1,0:T(8,128)(2,1)S(1)} %copy-done.2), kind=kOutput, calls=%fused_computation.23 | convolution fusion | flops 402653184 | bytes 3276800 | tf_op jit(solution)/shard_map/dot_general | solution.py:57
  126.5 2.7 %fusion.55 = f32[512,2048]{1,0:T(8,128)} fusion(bf16[2,2,1,1,192,2048]{5,4,3,2,1,0:T(8,128)(2,1)S(1)} %copy-done.2, bf16[192,256]{1,0:T(8,128)(2,1)S(1)} %get-tuple-element.43, bf16[192,256]{1,0:T(8,128)(2,1)S(1)} %get-tuple-element.42), kind=kOutput, calls=%fused_computation.72 | convolution fusion | flops 403046400 | bytes 5177344 | tf_op jit(solution)/shard_map/dot_general | solution.py:19
  130.6 21.4 %all-to-all-done.2 = bf16[8,2,24,2048]{3,2,1,0:T(8,128)(2,1)} async-done(((bf16[8,2,24,2048]{3,2,1,0:T(8,128)(2,1)}), bf16[8,2,24,2048]{3,2,1,0:T(8,128)(2,1)}, u32[]{:S(2)}, u32[]{:S(2)}) %all-to-all-start.2) | async-done | bytes 1572896 | tf_op jit(solution)/shard_map/all_to_all | solution.py:51
  152.0 2.6 %fusion.121 = (bf16[8,1,24,2048]{3,2,1,0:T(8,128)(2,1)S(1)}, bf16[8,1,24,2048]{3,2,1,0:T(8,128)(2,1)}) fusion(bf16[8,2,24,2048]{3,2,1,0:T(8,128)(2,1)} %all-to-all-done.2), kind=kLoop, calls=%fused_computation.184 | loop fusion | bytes 3145728 | tf_op jit(solution)/shard_map/slice | solution.py:52
  154.9 1.8 fusion.74
  160.4 4.5 %all-to-all-start.3 = ((bf16[8,2,24,2048]{3,2,1,0:T(8,128)(2,1)}), bf16[8,2,24,2048]{3,2,1,0:T(8,128)(2,1)}, u32[]{:S(2)}, u32[]{:S(2)}) async-start(bf16[8,2,24,2048]{3,2,1,0:T(8,128)(2,1)} %pad_maximum_fusion.1), calls=%async_computation.3 | async-start | bytes 3145728 | tf_op jit(solution)/shard_map/all_to_all | solution.py:120
  164.9 2.1 multiply_convert_fusion.7
  167.0 2.0 fusion.52
  169.0 3.1 %collective-permute-done.5 = bf16[192,2048]{1,0:T(8,128)(2,1)} collective-permute-done((bf16[192,2048]{1,0:T(8,128)(2,1)}, bf16[192,2048]{1,0:T(8,128)(2,1)}, u32[]{:S(2)}, u32[]{:S(2)}) %collective-permute-start.5) | collective-permute-done | bytes 786464 | tf_op jit(solution)/shard_map/ppermute | solution.py:15
  176.2 2.3 %fusion.5 = bf16[1,1,2048,512]{2,3,1,0:T(8,128)(2,1)} fusion(f32[2048,512]{0,1:T(8,128)S(1)} %fusion.87, bf16[192,2048]{1,0:T(8,128)(2,1)S(1)} %copy-done.15, f32[512,2048]{1,0:T(8,128)S(1)} %copy-done, f32[512,2048]{1,0:T(8,128)S(1)} %fusion.52, bf16[192,256]{1,0:T(8,128)(2,1)S(1)} %get-tuple-element.35, bf16[192,256]{1,0:T(8,128)(2,1)S(1)} %get-tuple-element.34), kind=kOutput, calls=%fused_computation.13 | convolution fusion | flops 409337856 | bytes 15663104 | tf_op jit(solution)/shard_map/dot_general | solution.py:19
  178.5 3.9 %copy.34 = bf16[1,1,2048,512]{3,2,1,0:T(8,128)(2,1)} copy(bf16[1,1,2048,512]{2,3,1,0:T(8,128)(2,1)} %fusion.5) | data formatting | bytes 4194304
  182.4 1.9 fusion.100
  184.3 1.7 fusion.4
  187.6 15.0 %all-to-all-done.3 = bf16[8,2,24,2048]{3,2,1,0:T(8,128)(2,1)} async-done(((bf16[8,2,24,2048]{3,2,1,0:T(8,128)(2,1)}), bf16[8,2,24,2048]{3,2,1,0:T(8,128)(2,1)}, u32[]{:S(2)}, u32[]{:S(2)}) %all-to-all-start.3) | async-done | bytes 1572896 | tf_op jit(solution)/shard_map/all_to_all | solution.py:120
  202.6 2.9 %fusion.9 = bf16[2,1,96,2048]{3,2,1,0:T(8,128)(2,1)} fusion(bf16[384,2048,1]{1,0,2:T(8,128)(2,1)} %bitcast.41, s32[2,96]{1,0:T(2,128)S(1)} %eq.168, bf16[1,96,2048]{2,1,0:T(8,128)(2,1)S(1)} %get-tuple-element.31, bf16[1,96,2048]{2,1,0:T(8,128)(2,1)S(1)} %get-tuple-element.30), kind=kOutput, calls=%fused_computation.21 | convolution fusion | flops 303636480 | bytes 3146496 | tf_op jit(solution)/shard_map/dot_general | solution.py:125
  (99 shorter events, 26.2 us)
Async XLA Ops:
  0.6 3.2 %copy-start.21 = (s32[2,2,1,96]{3,2,1,0:T(1,128)S(1)}, s32[2,2,1,96]{3,2,1,0:T(1,128)}, u32[]{:S(2)}) copy-start(s32[2,2,1,96]{3,2,1,0:T(1,128)} %param.14) | copy-start | bytes 4612
  5.8 42.6 %all-to-all-start = ((bf16[8,2,24,2048]{3,2,1,0:T(8,128)(2,1)}), bf16[8,2,24,2048]{3,2,1,0:T(8,128)(2,1)S(1)}, u32[]{:S(2)}, u32[]{:S(2)}) async-start(bf16[8,2,24,2048]{3,2,1,0:T(8,128)(2,1)} %bitcast.7), calls=%async_computation | async-start | bytes 3145728 | tf_op jit(solution)/shard_map/all_to_all | solution.py:51
  12.2 4.6 %copy-start.1 = (bf16[2,2,1,1,192,2048]{5,4,3,2,1,0:T(8,128)(2,1)S(1)}, bf16[2,2,1,1,192,2048]{5,4,3,2,1,0:T(8,128)(2,1)}, u32[]{:S(2)}) copy-start(bf16[2,2,1,1,192,2048]{5,4,3,2,1,0:T(8,128)(2,1)} %param.12) | copy-start | bytes 9437188
  14.7 5.0 %copy-start.22 = (bf16[2,1,1,2048,512]{4,3,2,1,0:T(8,128)(2,1)S(1)}, bf16[2,1,1,2048,512]{4,3,2,1,0:T(8,128)(2,1)}, u32[]{:S(2)}) copy-start(bf16[2,1,1,2048,512]{4,3,2,1,0:T(8,128)(2,1)} %param.8) | copy-start | bytes 12582916
  14.7 41.7 %collective-permute-start = (bf16[192,2048]{1,0:T(8,128)(2,1)S(1)}, bf16[192,2048]{1,0:T(8,128)(2,1)S(1)}, u32[]{:S(2)}, u32[]{:S(2)}) collective-permute-start(bf16[192,2048]{1,0:T(8,128)(2,1)S(1)} %get-tuple-element.25), channel_id=1, source_target_pairs={{0,24},{8,16},{16,8},{24,0},{1,25},{9,17},{17,9},{25,1},{2,26},{10... | collective-permute-start | bytes 2359304 | tf_op jit(solution)/shard_map/ppermute | solution.py:15
  48.4 3.7 %copy-start.23 = (bf16[2,1,1,2048,512]{4,3,2,1,0:T(8,128)(2,1)S(1)}, bf16[2,1,1,2048,512]{4,3,2,1,0:T(8,128)(2,1)}, u32[]{:S(2)}) copy-start(bf16[2,1,1,2048,512]{4,3,2,1,0:T(8,128)(2,1)} %param.8) | copy-start | bytes 12582916
  48.5 4.4 %copy-start.6 = (bf16[8,1,24,2048]{3,2,1,0:T(8,128)(2,1)}, bf16[8,1,24,2048]{3,2,1,0:T(8,128)(2,1)S(1)}, u32[]{:S(2)}) copy-start(bf16[8,1,24,2048]{3,2,1,0:T(8,128)(2,1)S(1)} %get-tuple-element.28) | copy-start | bytes 2359300
  56.5 42.2 %copy-start.5 = (bf16[2,1,96,2048]{3,2,1,0:T(8,128)(2,1)S(1)}, bf16[2,1,96,2048]{3,2,1,0:T(8,128)(2,1)}, u32[]{:S(2)}) copy-start(bf16[2,1,96,2048]{3,2,1,0:T(8,128)(2,1)} %param.10) | copy-start | bytes 2359300
  56.5 4.8 %copy-start.13 = (bf16[192,2048]{1,0:T(8,128)(2,1)}, bf16[192,2048]{1,0:T(8,128)(2,1)S(1)}, u32[]{:S(2)}) copy-start(bf16[192,2048]{1,0:T(8,128)(2,1)S(1)} %collective-permute-done) | copy-start | bytes 2359300
  56.5 42.2 %all-to-all-start.1 = ((bf16[8,2,24,2048]{3,2,1,0:T(8,128)(2,1)}), bf16[8,2,24,2048]{3,2,1,0:T(8,128)(2,1)S(1)}, u32[]{:S(2)}, u32[]{:S(2)}) async-start(bf16[8,2,24,2048]{3,2,1,0:T(8,128)(2,1)} %pad_maximum_fusion), calls=%async_computation.1 | async-start | bytes 3145728 | tf_op jit(solution)/shard_map/all_to_all | solution.py:120
  61.2 20.6 %collective-permute-start.2 = (bf16[192,2048]{1,0:T(8,128)(2,1)}, bf16[192,2048]{1,0:T(8,128)(2,1)S(1)}, u32[]{:S(2)}, u32[]{:S(2)}) collective-permute-start(bf16[192,2048]{1,0:T(8,128)(2,1)} %get-tuple-element.24), channel_id=1, source_target_pairs={{0,24},{8,16},{16,8},{24,0},{1,25},{9,17},{17,9},{25,1},{2,26},{10... | collective-permute-start | bytes 2359304 | tf_op jit(solution)/shard_map/ppermute | solution.py:15
  63.2 35.5 %collective-permute-start.1 = (bf16[192,2048]{1,0:T(8,128)(2,1)}, bf16[192,2048]{1,0:T(8,128)(2,1)}, u32[]{:S(2)}, u32[]{:S(2)}) collective-permute-start(bf16[192,2048]{1,0:T(8,128)(2,1)} %bitcast.178), channel_id=1, source_target_pairs={{0,24},{8,16},{16,8},{24,0},{1,25},{9,17},{17,9},{25,1},{2,26},{10... | collective-permute-start | bytes 2359304 | tf_op jit(solution)/shard_map/ppermute | solution.py:15
  81.9 17.5 %copy-start.8 = (bf16[192,2048]{1,0:T(8,128)(2,1)}, bf16[192,2048]{1,0:T(8,128)(2,1)S(1)}, u32[]{:S(2)}) copy-start(bf16[192,2048]{1,0:T(8,128)(2,1)S(1)} %collective-permute-done.2) | copy-start | bytes 2359300
  99.3 10.5 %copy-start.11 = (bf16[1,2,96,2048]{3,2,1,0:T(8,128)(2,1)S(1)}, bf16[1,2,96,2048]{3,2,1,0:T(8,128)(2,1)}, u32[]{:S(2)}) copy-start(bf16[1,2,96,2048]{3,2,1,0:T(8,128)(2,1)} %param.11) | copy-start | bytes 2359300
  99.4 9.2 %collective-permute-start.3 = (bf16[96,2048]{1,0:T(8,128)(2,1)S(1)}, bf16[96,2048]{1,0:T(8,128)(2,1)S(1)}, u32[]{:S(2)}, u32[]{:S(2)}) collective-permute-start(bf16[96,2048]{1,0:T(8,128)(2,1)S(1)} %get-tuple-element.32), channel_id=1, source_target_pairs={{8,0},{16,8},{24,16},{9,1},{17,9},{25,17},{10,2},{18,10},{26,18},{... | collective-permute-start | bytes 1179656 | tf_op jit(solution)/shard_map/ppermute | solution.py:10
  102.0 7.8 %collective-permute-start.4 = (bf16[96,2048]{1,0:T(8,128)(2,1)S(1)}, bf16[96,2048]{1,0:T(8,128)(2,1)S(1)}, u32[]{:S(2)}, u32[]{:S(2)}) collective-permute-start(bf16[96,2048]{1,0:T(8,128)(2,1)S(1)} %get-tuple-element.33), channel_id=1, source_target_pairs={{0,8},{8,16},{16,24},{1,9},{9,17},{17,25},{2,10},{10,18},{18,26},{... | collective-permute-start | bytes 1179656 | tf_op jit(solution)/shard_map/ppermute | solution.py:10
  111.9 40.1 %all-to-all-start.2 = ((bf16[8,2,24,2048]{3,2,1,0:T(8,128)(2,1)}), bf16[8,2,24,2048]{3,2,1,0:T(8,128)(2,1)}, u32[]{:S(2)}, u32[]{:S(2)}) async-start(bf16[8,2,24,2048]{3,2,1,0:T(8,128)(2,1)} %bitcast.32), calls=%async_computation.2 | async-start | bytes 3145728 | tf_op jit(solution)/shard_map/all_to_all | solution.py:51
  117.6 3.3 %copy-start.2 = (bf16[2,2,1,1,192,2048]{5,4,3,2,1,0:T(8,128)(2,1)S(1)}, bf16[2,2,1,1,192,2048]{5,4,3,2,1,0:T(8,128)(2,1)}, u32[]{:S(2)}) copy-start(bf16[2,2,1,1,192,2048]{5,4,3,2,1,0:T(8,128)(2,1)} %param.12) | copy-start | bytes 9437188
  120.9 3.1 %copy-start.7 = (bf16[8,1,24,2048]{3,2,1,0:T(8,128)(2,1)S(1)}, bf16[8,1,24,2048]{3,2,1,0:T(8,128)(2,1)}, u32[]{:S(2)}) copy-start(bf16[8,1,24,2048]{3,2,1,0:T(8,128)(2,1)} %copy-done.6) | copy-start | bytes 2359300
  120.9 3.1 %copy-start.19 = (f32[192,512]{1,0:T(8,128)S(1)}, f32[192,512]{1,0:T(8,128)}, u32[]{:S(2)}) copy-start(f32[192,512]{1,0:T(8,128)} %fusion.24) | copy-start | bytes 1179652
  120.9 3.6 %copy-start.24 = (bf16[2,1,1,2048,512]{4,3,2,1,0:T(8,128)(2,1)S(1)}, bf16[2,1,1,2048,512]{4,3,2,1,0:T(8,128)(2,1)}, u32[]{:S(2)}) copy-start(bf16[2,1,1,2048,512]{4,3,2,1,0:T(8,128)(2,1)} %param.8) | copy-start | bytes 12582916
  126.5 2.7 %copy-start.9 = (bf16[192,2048]{1,0:T(8,128)(2,1)S(1)}, bf16[192,2048]{1,0:T(8,128)(2,1)}, u32[]{:S(2)}) copy-start(bf16[192,2048]{1,0:T(8,128)(2,1)} %copy-done.8) | copy-start | bytes 2359300
  152.0 2.9 %copy-start.27 = (bf16[2,1,1,256,2048]{4,3,2,1,0:T(8,128)(2,1)S(1)}, bf16[2,1,1,256,2048]{4,3,2,1,0:T(8,128)(2,1)}, u32[]{:S(2)}) copy-start(bf16[2,1,1,256,2048]{4,3,2,1,0:T(8,128)(2,1)} %param.9) | copy-start | bytes 6291460
  152.0 2.9 %copy-start.29 = (f32[192,512]{1,0:T(8,128)S(1)}, f32[192,512]{1,0:T(8,128)}, u32[]{:S(2)}) copy-start(f32[192,512]{1,0:T(8,128)} %fusion.11) | copy-start | bytes 1179652
  154.5 2.7 %copy-start.3 = (bf16[8,1,24,2048]{3,2,1,0:T(8,128)(2,1)}, bf16[8,1,24,2048]{3,2,1,0:T(8,128)(2,1)S(1)}, u32[]{:S(2)}) copy-start(bf16[8,1,24,2048]{3,2,1,0:T(8,128)(2,1)S(1)} %get-tuple-element.26) | copy-start | bytes 2359300
  154.5 17.6 %collective-permute-start.5 = (bf16[192,2048]{1,0:T(8,128)(2,1)}, bf16[192,2048]{1,0:T(8,128)(2,1)}, u32[]{:S(2)}, u32[]{:S(2)}) collective-permute-start(bf16[192,2048]{1,0:T(8,128)(2,1)} %bitcast.37), channel_id=1, source_target_pairs={{0,24},{8,16},{16,8},{24,0},{1,25},{9,17},{17,9},{25,1},{2,26},{10... | collective-permute-start | bytes 2359304 | tf_op jit(solution)/shard_map/ppermute | solution.py:15
  154.9 2.5 %copy-start.25 = (bf16[2,1,1,2048,512]{4,3,2,1,0:T(8,128)(2,1)S(1)}, bf16[2,1,1,2048,512]{4,3,2,1,0:T(8,128)(2,1)}, u32[]{:S(2)}) copy-start(bf16[2,1,1,2048,512]{4,3,2,1,0:T(8,128)(2,1)} %param.8) | copy-start | bytes 12582916
  160.4 42.2 %all-to-all-start.3 = ((bf16[8,2,24,2048]{3,2,1,0:T(8,128)(2,1)}), bf16[8,2,24,2048]{3,2,1,0:T(8,128)(2,1)}, u32[]{:S(2)}, u32[]{:S(2)}) async-start(bf16[8,2,24,2048]{3,2,1,0:T(8,128)(2,1)} %pad_maximum_fusion.1), calls=%async_computation.3 | async-start | bytes 3145728 | tf_op jit(solution)/shard_map/all_to_all | solution.py:120
  167.0 5.2 %copy-start.20 = (f32[192,512]{1,0:T(8,128)S(1)}, f32[192,512]{1,0:T(8,128)}, u32[]{:S(2)}) copy-start(f32[192,512]{1,0:T(8,128)} %fusion.16) | copy-start | bytes 1179652
  167.0 5.1 %copy-start.28 = (bf16[2,1,1,256,2048]{4,3,2,1,0:T(8,128)(2,1)S(1)}, bf16[2,1,1,256,2048]{4,3,2,1,0:T(8,128)(2,1)}, u32[]{:S(2)}) copy-start(bf16[2,1,1,256,2048]{4,3,2,1,0:T(8,128)(2,1)} %param.9) | copy-start | bytes 6291460
  169.0 4.8 %copy-start.10 = (bf16[192,2048]{1,0:T(8,128)(2,1)S(1)}, bf16[192,2048]{1,0:T(8,128)(2,1)}, u32[]{:S(2)}) copy-start(bf16[192,2048]{1,0:T(8,128)(2,1)} %copy-done.8) | copy-start | bytes 2359300
  173.8 2.4 %copy-start.15 = (bf16[192,2048]{1,0:T(8,128)(2,1)S(1)}, bf16[192,2048]{1,0:T(8,128)(2,1)}, u32[]{:S(2)}) copy-start(bf16[192,2048]{1,0:T(8,128)(2,1)} %copy-done.13) | copy-start | bytes 2359300
  (8 other events, 12.7 us)

commit v17 on v14

--- a/solution.py
+++ b/solution.py
@@ -89,7 +89,9 @@
     for tick_id in range(ticks):
         one_hot, one_hot_back = placement(routes[tick_id, :, 0], capacity, experts)
         scaled = (probs[tick_id, :, 0][:, :, None] * current.astype(jnp.float32)).astype(jnp.bfloat16)
-        blocks = jnp.dot(one_hot, scaled.reshape(-1, model_width), preferred_element_type=jnp.float32)
+        blocks = jnp.dot(
+            one_hot[:, :tokens], scaled[0], preferred_element_type=jnp.float32
+        ) + jnp.dot(one_hot[:, tokens:], scaled[1], preferred_element_type=jnp.float32)
         blocks = blocks.astype(jnp.bfloat16).reshape(experts, 2, capacity, model_width)
         if slope_mirror is not None:
             hidden_m, pair_grad_m = expert_grads(

time: 204 us -> 206 us (level)
    dot_general x2 -> x4, matrix products: 3.43 us -> 4.66 us  [the longest x2 3.55 us: on_device(): jnp.dot(one_hot[:, tokens:], scaled[1], preferred_element_type=jnp.float32)]
    unnamed x59 -> x57, local copies, waits for them, and re-layouts: 11 us -> 11 us
where the time goes in v17:
time: 206 us; the launch traced here: 204 us
  waiting for transfers between devices  105 us (51%)
  matrix products  45.3 us (22%)
  starting transfers between devices  30.4 us (15%)
  local copies, waits for them, and re-layouts  16.7 us (8%)
  other arithmetic  5.55 us (3%)
    all_to_all x2, waiting for transfers between devices, exchange(): lax.all_to_all(blocks, 'expert', split_axis=0, concat_axis=0, tiled=True)  48.9 us
    all_to_all x2, waiting for transfers between devices, on_device(): lax.all_to_all(back_blocks, 'expert', split_axis=0, concat_axis=0, tiled=...  31.1 us
    ppermute x3, waiting for transfers between devices, mirrored(): return lax.ppermute(block, axis, [(i, count - 1 - i) for i in range(count)])  20.7 us
    dot_general x6, matrix products, expert_grads(): gate_up = jnp.dot(saved_rows, weight_in, preferred_element_type=jnp.float32)  13.6 us
    dot_general x8, matrix products, left_product(): lax.dot_general(left, right, (((0,), (0,)), ((), ())), preferred_element_...  13.3 us
    unnamed x57, local copies, waits for them, and re-layouts  11 us
    dot_general x10, matrix products, right_product(): lax.dot_general(left, right, (((1,), (1,)), ((), ())), preferred_element_...  10.2 us
    all_to_all x2, starting transfers between devices, exchange(): lax.all_to_all(blocks, 'expert', split_axis=0, concat_axis=0, tiled=True)  9.95 us
  transfers between devices with their start and end apart: 9, of which 8 were waited for; matrix products, arithmetic and copies ran while one was open for 23% of the time, Pallas kernels for 0%

profile of v17, /device:TPU:1, one launch (start us, length us, event | category | flops | bytes accessed | tf_op | source)
XLA Modules:
  0.0 204.3 jit_solution(3207410458999331639)
XLA Ops:
  5.2 1.8 add_convert_fusion.2
  6.9 6.4 %all-to-all-start = ((bf16[8,2,24,2048]{3,2,1,0:T(8,128)(2,1)}), bf16[8,2,24,2048]{3,2,1,0:T(8,128)(2,1)S(1)}, u32[]{:S(2)}, u32[]{:S(2)}) async-start(bf16[8,2,24,2048]{3,2,1,0:T(8,128)(2,1)} %bitcast.10), calls=%async_computation | async-start | bytes 3145728 | tf_op jit(solution)/shard_map/all_to_all | solution.py:51
  13.3 2.9 %slice_bitcast_fusion = bf16[2,192,2048]{2,1,0:T(8,128)(2,1)} fusion(bf16[2,2,1,1,192,2048]{5,4,3,2,1,0:T(8,128)(2,1)} %param.12), kind=kLoop, calls=%fused_computation.44 | loop fusion | bytes 3145728 | tf_op jit(solution)/shard_map/squeeze | solution.py:82
  16.2 2.1 %collective-permute-start = (bf16[2,192,2048]{2,1,0:T(8,128)(2,1)}, bf16[2,192,2048]{2,1,0:T(8,128)(2,1)S(1)}, u32[]{:S(2)}, u32[]{:S(2)}) collective-permute-start(bf16[2,192,2048]{2,1,0:T(8,128)(2,1)} %slice_bitcast_fusion), channel_id=1, source_target_pairs={{0,24},{8,16},{16,8},{24,0},{1,25},{9,17},{17,9},{25,1},{2,26},{10... | collective-permute-start | bytes 4718600 | tf_op jit(solution)/shard_map/ppermute | solution.py:15
  18.3 3.0 %fusion.24 = f32[192,512]{1,0:T(8,128)} fusion(bf16[2,1,1,2048,512]{4,3,2,1,0:T(8,128)(2,1)} %param.8, bf16[2,2,1,1,192,2048]{5,4,3,2,1,0:T(8,128)(2,1)S(1)} %copy-done.1), kind=kOutput, calls=%fused_computation.36 | convolution fusion | flops 402653184 | bytes 3276800 | tf_op jit(solution)/shard_map/dot_general | solution.py:57
  22.6 26.9 %all-to-all-done = bf16[8,2,24,2048]{3,2,1,0:T(8,128)(2,1)S(1)} async-done(((bf16[8,2,24,2048]{3,2,1,0:T(8,128)(2,1)}), bf16[8,2,24,2048]{3,2,1,0:T(8,128)(2,1)S(1)}, u32[]{:S(2)}, u32[]{:S(2)}) %all-to-all-start) | async-done | bytes 1572896 | tf_op jit(solution)/shard_map/all_to_all | solution.py:51
  58.2 4.6 %all-to-all-start.1 = ((bf16[8,2,24,2048]{3,2,1,0:T(8,128)(2,1)}), bf16[8,2,24,2048]{3,2,1,0:T(8,128)(2,1)S(1)}, u32[]{:S(2)}, u32[]{:S(2)}) async-start(bf16[8,2,24,2048]{3,2,1,0:T(8,128)(2,1)} %pad_maximum_fusion), calls=%async_computation.1 | async-start | bytes 3145728 | tf_op jit(solution)/shard_map/all_to_all | solution.py:122
  62.8 1.9 collective-permute-start.1
  64.8 18.5 %collective-permute-done.1 = bf16[192,2048]{1,0:T(8,128)(2,1)S(1)} collective-permute-done((bf16[192,2048]{1,0:T(8,128)(2,1)}, bf16[192,2048]{1,0:T(8,128)(2,1)S(1)}, u32[]{:S(2)}, u32[]{:S(2)}) %collective-permute-start.1) | collective-permute-done | bytes 786464 | tf_op jit(solution)/shard_map/ppermute | solution.py:15
  83.3 15.9 %all-to-all-done.1 = bf16[8,2,24,2048]{3,2,1,0:T(8,128)(2,1)S(1)} async-done(((bf16[8,2,24,2048]{3,2,1,0:T(8,128)(2,1)}), bf16[8,2,24,2048]{3,2,1,0:T(8,128)(2,1)S(1)}, u32[]{:S(2)}, u32[]{:S(2)}) %all-to-all-start.1) | async-done | bytes 1572896 | tf_op jit(solution)/shard_map/all_to_all | solution.py:122
  99.9 3.6 %collective-permute-start.2 = (bf16[96,2048]{1,0:T(8,128)(2,1)S(1)}, bf16[96,2048]{1,0:T(8,128)(2,1)S(1)}, u32[]{:S(2)}, u32[]{:S(2)}) collective-permute-start(bf16[96,2048]{1,0:T(8,128)(2,1)S(1)} %get-tuple-element.26), channel_id=1, source_target_pairs={{8,0},{16,8},{24,16},{9,1},{17,9},{25,17},{10,2},{18,10},{26,18},{... | collective-permute-start | bytes 1179656 | tf_op jit(solution)/shard_map/ppermute | solution.py:10
  103.6 3.0 %collective-permute-start.3 = (bf16[96,2048]{1,0:T(8,128)(2,1)S(1)}, bf16[96,2048]{1,0:T(8,128)(2,1)S(1)}, u32[]{:S(2)}, u32[]{:S(2)}) collective-permute-start(bf16[96,2048]{1,0:T(8,128)(2,1)S(1)} %get-tuple-element.27), channel_id=1, source_target_pairs={{0,8},{8,16},{16,24},{1,9},{9,17},{17,25},{2,10},{10,18},{18,26},{... | collective-permute-start | bytes 1179656 | tf_op jit(solution)/shard_map/ppermute | solution.py:10
  106.8 3.4 %collective-permute-done.2 = bf16[96,2048]{1,0:T(8,128)(2,1)S(1)} collective-permute-done((bf16[96,2048]{1,0:T(8,128)(2,1)S(1)}, bf16[96,2048]{1,0:T(8,128)(2,1)S(1)}, u32[]{:S(2)}, u32[]{:S(2)}) %collective-permute-start.2) | collective-permute-done | bytes 393248 | tf_op jit(solution)/shard_map/ppermute | solution.py:10
  112.1 1.8 add_convert_fusion.1
  113.9 3.6 %all-to-all-start.2 = ((bf16[8,2,24,2048]{3,2,1,0:T(8,128)(2,1)}), bf16[8,2,24,2048]{3,2,1,0:T(8,128)(2,1)S(1)}, u32[]{:S(2)}, u32[]{:S(2)}) async-start(bf16[8,2,24,2048]{3,2,1,0:T(8,128)(2,1)} %bitcast.37), calls=%async_computation.2 | async-start | bytes 3145728 | tf_op jit(solution)/shard_map/all_to_all | solution.py:51
  117.6 2.5 %fusion.21 = f32[192,512]{1,0:T(8,128)S(1)} fusion(bf16[2,1,1,2048,512]{4,3,2,1,0:T(8,128)(2,1)} %param.8, bf16[2,2,1,1,192,2048]{5,4,3,2,1,0:T(8,128)(2,1)} %param.12), kind=kOutput, calls=%fused_computation.33 | convolution fusion | flops 402653184 | bytes 3276800 | tf_op jit(solution)/shard_map/dot_general | solution.py:57
  120.4 2.3 %fusion.11 = f32[192,512]{1,0:T(8,128)S(1)} fusion(bf16[2,1,1,2048,512]{4,3,2,1,0:T(8,128)(2,1)} %param.8, bf16[2,2,1,1,192,2048]{5,4,3,2,1,0:T(8,128)(2,1)S(1)} %copy-done.2), kind=kOutput, calls=%fused_computation.23 | convolution fusion | flops 402653184 | bytes 3276800 | tf_op jit(solution)/shard_map/dot_general | solution.py:57
  122.7 3.1 %fusion.16 = f32[192,512]{1,0:T(8,128)} fusion(bf16[2,1,1,2048,512]{4,3,2,1,0:T(8,128)(2,1)} %param.8, bf16[2,192,2048]{2,1,0:T(8,128)(2,1)S(1)} %copy-done.8), kind=kOutput, calls=%fused_computation.28 | convolution fusion | flops 402653184 | bytes 3276800 | tf_op jit(solution)/shard_map/dot_general | solution.py:57
  127.2 2.7 %fusion.61 = f32[512,2048]{1,0:T(8,128)} fusion(bf16[2,2,1,1,192,2048]{5,4,3,2,1,0:T(8,128)(2,1)S(1)} %copy-done.2, bf16[192,256]{1,0:T(8,128)(2,1)S(1)} %get-tuple-element.37, bf16[192,256]{1,0:T(8,128)(2,1)S(1)} %get-tuple-element.36), kind=kOutput, calls=%fused_computation.79 | convolution fusion | flops 403046400 | bytes 5177344 | tf_op jit(solution)/shard_map/dot_general | solution.py:19
  129.9 22.0 %all-to-all-done.2 = bf16[8,2,24,2048]{3,2,1,0:T(8,128)(2,1)S(1)} async-done(((bf16[8,2,24,2048]{3,2,1,0:T(8,128)(2,1)}), bf16[8,2,24,2048]{3,2,1,0:T(8,128)(2,1)S(1)}, u32[]{:S(2)}, u32[]{:S(2)}) %all-to-all-start.2) | async-done | bytes 1572896 | tf_op jit(solution)/shard_map/all_to_all | solution.py:51
  153.7 1.8 fusion.88
  159.1 4.5 %all-to-all-start.3 = ((bf16[8,2,24,2048]{3,2,1,0:T(8,128)(2,1)}), bf16[8,2,24,2048]{3,2,1,0:T(8,128)(2,1)}, u32[]{:S(2)}, u32[]{:S(2)}) async-start(bf16[8,2,24,2048]{3,2,1,0:T(8,128)(2,1)} %pad_maximum_fusion.1), calls=%async_computation.3 | async-start | bytes 3145728 | tf_op jit(solution)/shard_map/all_to_all | solution.py:122
  163.7 1.9 fusion.114
  165.6 1.9 multiply_convert_fusion.7
  168.2 2.3 %collective-permute-done.4 = bf16[192,2048]{1,0:T(8,128)(2,1)} collective-permute-done((bf16[192,2048]{1,0:T(8,128)(2,1)}, bf16[192,2048]{1,0:T(8,128)(2,1)}, u32[]{:S(2)}, u32[]{:S(2)}) %collective-permute-start.4) | collective-permute-done | bytes 786464 | tf_op jit(solution)/shard_map/ppermute | solution.py:15
  170.5 1.6 multiply_convert_fusion.5
  174.4 3.3 %fusion.1 = bf16[1,1,2048,512]{2,3,1,0:T(8,128)(2,1)} fusion(bf16[2048,512]{0,1:T(8,128)(2,1)S(1)} %add_convert_fusion, f32[512,2048]{1,0:T(8,128)S(1)} %copy-done, bf16[2,2,1,1,192,2048]{5,4,3,2,1,0:T(8,128)(2,1)} %param.12, bf16[192,256]{1,0:T(8,128)(2,1)S(1)} %get-tuple-element.33, bf16[192,256]{1,0:T(8,128)(2,1)S(1)} %get-tuple-element.32), kind=kOutput, calls=%fused_computation.5 | convolution fusion | flops 407240704 | bytes 9371648 | tf_op jit(solution)/shard_map/dot_general | solution.py:19
  177.6 3.9 %copy.34 = bf16[1,1,2048,512]{3,2,1,0:T(8,128)(2,1)} copy(bf16[1,1,2048,512]{2,3,1,0:T(8,128)(2,1)} %fusion.1) | data formatting | bytes 4194304
  181.5 1.9 fusion.115
  184.7 1.5 fusion.8
  186.2 15.2 %all-to-all-done.3 = bf16[8,2,24,2048]{3,2,1,0:T(8,128)(2,1)} async-done(((bf16[8,2,24,2048]{3,2,1,0:T(8,128)(2,1)}), bf16[8,2,24,2048]{3,2,1,0:T(8,128)(2,1)}, u32[]{:S(2)}, u32[]{:S(2)}) %all-to-all-start.3) | async-done | bytes 1572896 | tf_op jit(solution)/shard_map/all_to_all | solution.py:122
  201.4 2.9 %fusion.9 = bf16[2,1,96,2048]{3,2,1,0:T(8,128)(2,1)} fusion(bf16[384,2048,1]{1,0,2:T(8,128)(2,1)} %bitcast.47, bf16[1,96,2048]{2,1,0:T(8,128)(2,1)S(1)} %get-tuple-element.25, bf16[1,96,2048]{2,1,0:T(8,128)(2,1)S(1)} %get-tuple-element.24, s32[2,96]{1,0:T(2,128)S(1)} %eq.168), kind=kOutput, calls=%fused_computation.21 | convolution fusion | flops 303636480 | bytes 3146496 | tf_op jit(solution)/shard_map/dot_general | solution.py:125
  (93 shorter events, 28.7 us)
Async XLA Ops:
  6.9 42.6 %all-to-all-start = ((bf16[8,2,24,2048]{3,2,1,0:T(8,128)(2,1)}), bf16[8,2,24,2048]{3,2,1,0:T(8,128)(2,1)S(1)}, u32[]{:S(2)}, u32[]{:S(2)}) async-start(bf16[8,2,24,2048]{3,2,1,0:T(8,128)(2,1)} %bitcast.10), calls=%async_computation | async-start | bytes 3145728 | tf_op jit(solution)/shard_map/all_to_all | solution.py:51
  13.3 5.0 %copy-start.1 = (bf16[2,2,1,1,192,2048]{5,4,3,2,1,0:T(8,128)(2,1)S(1)}, bf16[2,2,1,1,192,2048]{5,4,3,2,1,0:T(8,128)(2,1)}, u32[]{:S(2)}) copy-start(bf16[2,2,1,1,192,2048]{5,4,3,2,1,0:T(8,128)(2,1)} %param.12) | copy-start | bytes 9437188
  16.2 5.0 %copy-start.20 = (bf16[2,1,1,2048,512]{4,3,2,1,0:T(8,128)(2,1)S(1)}, bf16[2,1,1,2048,512]{4,3,2,1,0:T(8,128)(2,1)}, u32[]{:S(2)}) copy-start(bf16[2,1,1,2048,512]{4,3,2,1,0:T(8,128)(2,1)} %param.8) | copy-start | bytes 12582916
  16.2 40.7 %collective-permute-start = (bf16[2,192,2048]{2,1,0:T(8,128)(2,1)}, bf16[2,192,2048]{2,1,0:T(8,128)(2,1)S(1)}, u32[]{:S(2)}, u32[]{:S(2)}) collective-permute-start(bf16[2,192,2048]{2,1,0:T(8,128)(2,1)} %slice_bitcast_fusion), channel_id=1, source_target_pairs={{0,24},{8,16},{16,8},{24,0},{1,25},{9,17},{17,9},{25,1},{2,26},{10... | collective-permute-start | bytes 4718600 | tf_op jit(solution)/shard_map/ppermute | solution.py:15
  49.5 2.3 %copy-start.24 = (bf16[2,1,1,256,2048]{4,3,2,1,0:T(8,128)(2,1)S(1)}, bf16[2,1,1,256,2048]{4,3,2,1,0:T(8,128)(2,1)}, u32[]{:S(2)}) copy-start(bf16[2,1,1,256,2048]{4,3,2,1,0:T(8,128)(2,1)} %param.9) | copy-start | bytes 6291460
  49.6 3.2 %copy-start.6 = (bf16[8,1,24,2048]{3,2,1,0:T(8,128)(2,1)}, bf16[8,1,24,2048]{3,2,1,0:T(8,128)(2,1)S(1)}, u32[]{:S(2)}) copy-start(bf16[8,1,24,2048]{3,2,1,0:T(8,128)(2,1)S(1)} %get-tuple-element.22) | copy-start | bytes 2359300
  49.6 3.2 %copy-start.14 = (bf16[8,1,24,2048]{3,2,1,0:T(8,128)(2,1)}, bf16[8,1,24,2048]{3,2,1,0:T(8,128)(2,1)S(1)}, u32[]{:S(2)}) copy-start(bf16[8,1,24,2048]{3,2,1,0:T(8,128)(2,1)S(1)} %get-tuple-element.23) | copy-start | bytes 2359300
  49.6 2.7 %copy-start.27 = (f32[192,512]{1,0:T(8,128)S(1)}, f32[192,512]{1,0:T(8,128)}, u32[]{:S(2)}) copy-start(f32[192,512]{1,0:T(8,128)} %fusion.14) | copy-start | bytes 1179652
  51.8 2.2 %copy-start.21 = (bf16[2,1,1,2048,512]{4,3,2,1,0:T(8,128)(2,1)S(1)}, bf16[2,1,1,2048,512]{4,3,2,1,0:T(8,128)(2,1)}, u32[]{:S(2)}) copy-start(bf16[2,1,1,2048,512]{4,3,2,1,0:T(8,128)(2,1)} %param.8) | copy-start | bytes 12582916
  57.0 42.2 %copy-start.5 = (bf16[2,1,96,2048]{3,2,1,0:T(8,128)(2,1)S(1)}, bf16[2,1,96,2048]{3,2,1,0:T(8,128)(2,1)}, u32[]{:S(2)}) copy-start(bf16[2,1,96,2048]{3,2,1,0:T(8,128)(2,1)} %param.10) | copy-start | bytes 2359300
  58.2 41.0 %all-to-all-start.1 = ((bf16[8,2,24,2048]{3,2,1,0:T(8,128)(2,1)}), bf16[8,2,24,2048]{3,2,1,0:T(8,128)(2,1)S(1)}, u32[]{:S(2)}, u32[]{:S(2)}) async-start(bf16[8,2,24,2048]{3,2,1,0:T(8,128)(2,1)} %pad_maximum_fusion), calls=%async_computation.1 | async-start | bytes 3145728 | tf_op jit(solution)/shard_map/all_to_all | solution.py:122
  62.8 20.5 %collective-permute-start.1 = (bf16[192,2048]{1,0:T(8,128)(2,1)}, bf16[192,2048]{1,0:T(8,128)(2,1)S(1)}, u32[]{:S(2)}, u32[]{:S(2)}) collective-permute-start(bf16[192,2048]{1,0:T(8,128)(2,1)} %bitcast.190), channel_id=1, source_target_pairs={{0,24},{8,16},{16,8},{24,0},{1,25},{9,17},{17,9},{25,1},{2,26},{10... | collective-permute-start | bytes 2359304 | tf_op jit(solution)/shard_map/ppermute | solution.py:15
  83.3 16.6 %copy-start.10 = (bf16[192,2048]{1,0:T(8,128)(2,1)}, bf16[192,2048]{1,0:T(8,128)(2,1)S(1)}, u32[]{:S(2)}) copy-start(bf16[192,2048]{1,0:T(8,128)(2,1)S(1)} %collective-permute-done.1) | copy-start | bytes 2359300
  99.8 11.5 %copy-start.13 = (bf16[1,2,96,2048]{3,2,1,0:T(8,128)(2,1)S(1)}, bf16[1,2,96,2048]{3,2,1,0:T(8,128)(2,1)}, u32[]{:S(2)}) copy-start(bf16[1,2,96,2048]{3,2,1,0:T(8,128)(2,1)} %param.11) | copy-start | bytes 2359300
  99.9 10.2 %collective-permute-start.2 = (bf16[96,2048]{1,0:T(8,128)(2,1)S(1)}, bf16[96,2048]{1,0:T(8,128)(2,1)S(1)}, u32[]{:S(2)}, u32[]{:S(2)}) collective-permute-start(bf16[96,2048]{1,0:T(8,128)(2,1)S(1)} %get-tuple-element.26), channel_id=1, source_target_pairs={{8,0},{16,8},{24,16},{9,1},{17,9},{25,17},{10,2},{18,10},{26,18},{... | collective-permute-start | bytes 1179656 | tf_op jit(solution)/shard_map/ppermute | solution.py:10
  103.6 7.7 %collective-permute-start.3 = (bf16[96,2048]{1,0:T(8,128)(2,1)S(1)}, bf16[96,2048]{1,0:T(8,128)(2,1)S(1)}, u32[]{:S(2)}, u32[]{:S(2)}) collective-permute-start(bf16[96,2048]{1,0:T(8,128)(2,1)S(1)} %get-tuple-element.27), channel_id=1, source_target_pairs={{0,8},{8,16},{16,24},{1,9},{9,17},{17,25},{2,10},{10,18},{18,26},{... | collective-permute-start | bytes 1179656 | tf_op jit(solution)/shard_map/ppermute | solution.py:10
  113.9 37.9 %all-to-all-start.2 = ((bf16[8,2,24,2048]{3,2,1,0:T(8,128)(2,1)}), bf16[8,2,24,2048]{3,2,1,0:T(8,128)(2,1)S(1)}, u32[]{:S(2)}, u32[]{:S(2)}) async-start(bf16[8,2,24,2048]{3,2,1,0:T(8,128)(2,1)} %bitcast.37), calls=%async_computation.2 | async-start | bytes 3145728 | tf_op jit(solution)/shard_map/all_to_all | solution.py:51
  117.6 2.8 %copy-start.2 = (bf16[2,2,1,1,192,2048]{5,4,3,2,1,0:T(8,128)(2,1)S(1)}, bf16[2,2,1,1,192,2048]{5,4,3,2,1,0:T(8,128)(2,1)}, u32[]{:S(2)}) copy-start(bf16[2,2,1,1,192,2048]{5,4,3,2,1,0:T(8,128)(2,1)} %param.12) | copy-start | bytes 9437188
  120.4 35.2 %copy-start.15 = (f32[192,512]{1,0:T(8,128)}, f32[192,512]{1,0:T(8,128)S(1)}, u32[]{:S(2)}) copy-start(f32[192,512]{1,0:T(8,128)S(1)} %fusion.21) | copy-start | bytes 1179652
  120.4 2.4 %copy-start.8 = (bf16[2,192,2048]{2,1,0:T(8,128)(2,1)S(1)}, bf16[2,192,2048]{2,1,0:T(8,128)(2,1)}, u32[]{:S(2)}) copy-start(bf16[2,192,2048]{2,1,0:T(8,128)(2,1)} %copy-done.7) | copy-start | bytes 4718596
  122.7 3.1 %copy-start.22 = (bf16[2,1,1,2048,512]{4,3,2,1,0:T(8,128)(2,1)S(1)}, bf16[2,1,1,2048,512]{4,3,2,1,0:T(8,128)(2,1)}, u32[]{:S(2)}) copy-start(bf16[2,1,1,2048,512]{4,3,2,1,0:T(8,128)(2,1)} %param.8) | copy-start | bytes 12582916
  151.9 1.9 copy-start.25
  152.8 3.2 %copy-start.3 = (bf16[8,1,24,2048]{3,2,1,0:T(8,128)(2,1)}, bf16[8,1,24,2048]{3,2,1,0:T(8,128)(2,1)S(1)}, u32[]{:S(2)}) copy-start(bf16[8,1,24,2048]{3,2,1,0:T(8,128)(2,1)S(1)} %get-tuple-element.20) | copy-start | bytes 2359300
  152.9 17.7 %collective-permute-start.4 = (bf16[192,2048]{1,0:T(8,128)(2,1)}, bf16[192,2048]{1,0:T(8,128)(2,1)}, u32[]{:S(2)}, u32[]{:S(2)}) collective-permute-start(bf16[192,2048]{1,0:T(8,128)(2,1)} %bitcast.42), channel_id=1, source_target_pairs={{0,24},{8,16},{16,8},{24,0},{1,25},{9,17},{17,9},{25,1},{2,26},{10... | collective-permute-start | bytes 2359304 | tf_op jit(solution)/shard_map/ppermute | solution.py:15
  153.7 2.4 %copy-start.23 = (bf16[2,1,1,2048,512]{4,3,2,1,0:T(8,128)(2,1)S(1)}, bf16[2,1,1,2048,512]{4,3,2,1,0:T(8,128)(2,1)}, u32[]{:S(2)}) copy-start(bf16[2,1,1,2048,512]{4,3,2,1,0:T(8,128)(2,1)} %param.8) | copy-start | bytes 12582916
  159.1 42.3 %all-to-all-start.3 = ((bf16[8,2,24,2048]{3,2,1,0:T(8,128)(2,1)}), bf16[8,2,24,2048]{3,2,1,0:T(8,128)(2,1)}, u32[]{:S(2)}, u32[]{:S(2)}) async-start(bf16[8,2,24,2048]{3,2,1,0:T(8,128)(2,1)} %pad_maximum_fusion.1), calls=%async_computation.3 | async-start | bytes 3145728 | tf_op jit(solution)/shard_map/all_to_all | solution.py:122
  163.6 1.9 copy-start.11
  163.6 1.9 copy-start.17
  167.5 3.1 %copy-start.19 = (f32[192,512]{1,0:T(8,128)S(1)}, f32[192,512]{1,0:T(8,128)}, u32[]{:S(2)}) copy-start(f32[192,512]{1,0:T(8,128)} %fusion.16) | copy-start | bytes 1179652
  167.5 3.0 %copy-start.26 = (bf16[2,1,1,256,2048]{4,3,2,1,0:T(8,128)(2,1)S(1)}, bf16[2,1,1,256,2048]{4,3,2,1,0:T(8,128)(2,1)}, u32[]{:S(2)}) copy-start(bf16[2,1,1,256,2048]{4,3,2,1,0:T(8,128)(2,1)} %param.9) | copy-start | bytes 6291460
  172.2 2.2 %copy-start = (f32[512,2048]{1,0:T(8,128)S(1)}, f32[512,2048]{1,0:T(8,128)}, u32[]{:S(2)}) copy-start(f32[512,2048]{1,0:T(8,128)} %fusion.61) | copy-start | bytes 12582916
  181.5 1.9 copy-start.12
  (5 other events, 6.5 us)
